TPU v7x, 256 devices: a whole 4x4x8 slice. The times are simulated.
256 devices in a mesh: shard: 32 (over z, x), tensor: 4 (over y), section: 2 (over core).
Axes of the slice: x: 4, y: 4, z: 8, core: 2. Of those that a mesh axis runs over, the one named last changes fastest.
Arguments:
- gradient: bfloat16 [32, 512, 2048], P(('tensor', 'section'), 'shard'), may hold values from -48 to 48
- momentum: float32 [32, 512, 2048], P(('tensor', 'section'), 'shard'), may hold values from -8 to 8
- normed: bfloat16 [32768, 512], P(('shard', 'section'), 'tensor'), may hold values from -6 to 6
- ln_gain: float32 [512], P('tensor'), may hold values from 0.5 to 1.5
- ln_bias: float32 [512], P('tensor'), may hold values from -3 to 3
- ln_cotangent: bfloat16 [32768, 512], P(('shard', 'section'), 'tensor'), may hold values from -0.125 to 0.125
- router_cotangent: bfloat16 [32768, 32], P(('shard', 'section')), may hold values from -0.125 to 0.125
- first_moment: float32 [34, 512], P(None, 'tensor'), may hold values from -3 to 3
- second_moment: float32 [34, 512], P(None, 'tensor'), may hold values from 0.5 to 5
Outputs:
- next_momentum: float32 [32, 512, 2048], P(('tensor', 'section'), 'shard')
- update: float32 [32, 512, 2048], P(('tensor', 'section'), 'shard')
- next_first: float32 [34, 512], P(None, 'tensor')
- next_second: float32 [34, 512], P(None, 'tensor')
- adam_step: float32 [34, 512], P(None, 'tensor')
All inputs are finite; a program needn't handle non-finite values.
Results may differ from a plain program's by a relative error of at most 0.035.
Values may be sent and summed in bfloat16 or wider, within the bound.
No kernel may reach another device: no remote copies, remote signals or barrier semaphores. Data moves between devices by JAX's collectives and lax.ppermute only.
A program may use at most 64 MiB of HBM per device.

v0:
```python
import math

import jax
import jax.numpy as jnp
from jax import lax
from jax.sharding import PartitionSpec as P

FF = 2048
ITERS = 5


MUON_DECAY = 0.95
LINEAR_TERM = 3.4445
CUBIC_TERM = -4.775
QUINTIC_TERM = 2.0315
NORM_EPSILON = 1e-07
ADAM_FIRST = 0.9
ADAM_SECOND = 0.95
ADAM_EPSILON = 1e-08


def keep_local(value):
    return value


def orthogonalize(blocks, join_sums, join_grams):
    squares = jnp.sum(jnp.square(blocks.astype(jnp.float32)), axis=(1, 2))
    total = jnp.sqrt(join_sums(squares))
    iterate = (blocks.astype(jnp.float32) / (total + NORM_EPSILON)[:, None, None]).astype(
        jnp.bfloat16
    )
    for repeat in range(ITERS):
        gram = join_grams(
            jnp.einsum("kij,klj->kil", iterate, iterate, preferred_element_type=jnp.float32)
        )
        gram_half = gram.astype(jnp.bfloat16)
        square_term = jnp.einsum(
            "kij,kjl->kil", gram_half, gram_half, preferred_element_type=jnp.float32
        )
        poly = (CUBIC_TERM * gram + QUINTIC_TERM * square_term).astype(jnp.bfloat16)
        product = jnp.einsum("kij,kjl->kil", poly, iterate, preferred_element_type=jnp.float32)
        iterate = (LINEAR_TERM * iterate.astype(jnp.float32) + product).astype(jnp.bfloat16)
    return iterate


def on_device(
    gradient,
    momentum,
    normed,
    ln_gain,
    ln_bias,
    ln_cotangent,
    router_cotangent,
    first_moment,
    second_moment,
):
    grad_float = gradient.astype(jnp.float32)
    next_momentum = MUON_DECAY * momentum + grad_float
    nesterov = (grad_float + MUON_DECAY * next_momentum).astype(jnp.bfloat16)
    count_all, rows_piece, cols_full = nesterov.shape
    shard_count = lax.axis_size("shard")
    normed_float = normed.astype(jnp.float32)
    cot_float = ln_cotangent.astype(jnp.float32)
    ln_out = (ln_gain[None, :] * normed_float + ln_bias[None, :]).astype(jnp.bfloat16)
    gain_local = jnp.sum(cot_float * normed_float, axis=0)
    bias_local = jnp.sum(cot_float, axis=0)
    router_local = lax.dot_general(
        router_cotangent, ln_out, (((0,), (0,)), ((), ())), preferred_element_type=jnp.float32
    )
    gain_grad, bias_grad, router_grad = lax.psum(
        (gain_local, bias_local, router_local), ("shard", "section")
    )
    vec_grad = jnp.concatenate([gain_grad[None, :], bias_grad[None, :], router_grad], axis=0)
    next_first = ADAM_FIRST * first_moment + (1.0 - ADAM_FIRST) * vec_grad
    next_second = ADAM_SECOND * second_moment + (1.0 - ADAM_SECOND) * vec_grad * vec_grad
    adam_step = next_first / (jnp.sqrt(next_second) + ADAM_EPSILON)
    slots = -(-count_all // shard_count)
    padded = jnp.pad(nesterov, ((0, slots * shard_count - count_all), (0, 0), (0, 0)))
    outgoing = padded.reshape(slots, shard_count, rows_piece, cols_full).transpose(1, 0, 2, 3)
    received = lax.all_to_all(outgoing, "shard", split_axis=0, concat_axis=0, tiled=True)
    items = received.shape[1]
    blocks = received.transpose(1, 0, 2, 3).reshape(items, shard_count * rows_piece, cols_full)
    result = orthogonalize(blocks, keep_local, keep_local)
    returned = lax.all_to_all(
        result.reshape(items, shard_count, rows_piece, cols_full).transpose(1, 0, 2, 3),
        "shard",
        split_axis=0,
        concat_axis=0,
        tiled=True,
    )
    ordered = returned.transpose(1, 0, 2, 3).reshape(slots * shard_count, rows_piece, cols_full)
    update = ordered[:count_all].astype(jnp.float32) * math.sqrt(FF)
    return (next_momentum, update, next_first, next_second, adam_step)


def solution(mesh):
    return jax.shard_map(
        on_device,
        mesh=mesh,
        in_specs=(
            P(("tensor", "section"), "shard", None),
            P(("tensor", "section"), "shard", None),
            P(("shard", "section"), "tensor"),
            P("tensor"),
            P("tensor"),
            P(("shard", "section"), "tensor"),
            P(("shard", "section"), None),
            P(None, "tensor"),
            P(None, "tensor"),
        ),
        out_specs=(
            P(("tensor", "section"), "shard", None),
            P(("tensor", "section"), "shard", None),
            P(None, "tensor"),
            P(None, "tensor"),
            P(None, "tensor"),
        ),
        check_vma=False,
    )
```

profile of v0, /device:TPU:16, one launch (start us, length us, event | category | flops | bytes accessed | tf_op | source)
XLA Modules:
  0.0 389.4 jit_solution(11584441895327626136)
XLA Ops:
  0.6 0.0 copy-start
  0.6 2.0 fusion.12
  2.7 0.2 pad_bitcast_fusion
  2.9 61.6 %all_to_all.10 = bf16[32,1,16,2048]{3,2,1,0:T(8,128)(2,1)S(1)} all-to-all(bf16[32,1,16,2048]{3,2,1,0:T(8,128)(2,1)S(1)} %pad_bitcast_fusion), channel_id=1, replica_groups=mesh['shard'=32,'tensor'=4,'section'=2] {'shard'}, dimensions={0} | all-to-all | bytes 4194304 | tf_op jit(solution)/shard_map/all_to_all | solution.py:80
  64.5 1.7 fusion
  66.9 0.4 fusion.1
  67.3 1.3 copy-done.1
  68.7 1.3 fusion.51
  70.0 3.8 add_convert_fusion.4
  73.7 1.3 fusion.52
  75.0 2.9 add_convert_fusion.3
  77.9 3.6 fusion.53
  81.6 2.9 add_convert_fusion.2
  84.5 3.6 fusion.54
  88.2 2.9 add_convert_fusion.1
  91.1 3.6 fusion.55
  94.8 2.9 add_convert_fusion
  97.7 0.0 copy-start.4
  97.7 5.7 %all-to-all-start.1 = ((bf16[32,1,16,2048]{3,2,1,0:T(8,128)(2,1)}), bf16[32,1,16,2048]{3,2,1,0:T(8,128)(2,1)S(1)}, u32[]{:S(2)}, u32[]{:S(2)}) async-start(bf16[32,1,16,2048]{3,2,1,0:T(8,128)(2,1)} %bitcast.28), calls=%async_computation.1 | async-start | bytes 4194304 | tf_op jit(solution)/shard_map/all_to_all | solution.py:84
  103.5 0.1 fusion.33
  103.6 0.2 convolution_bitcast_fusion
  103.7 284.2 %all-reduce.1 = (f32[32,128]{1,0:T(8,128)S(1)}, f32[1,128]{1,0:T(1,128)S(1)}, f32[1,128]{1,0:T(1,128)S(1)}) all-reduce(f32[32,128]{1,0:T(8,128)S(1)} %convolution_bitcast_fusion, f32[1,128]{1,0:T(1,128)S(1)} %bitcast.32, f32[1,128]{1,0:T(1,128)S(1)} %bitcast.31), channel_id=1, replica_groups=mesh['shard'=32,'tensor'=4,'section'=2] {'shard','section'}, use_global_device_ids=true, to_apply=%region_5.6 | all-reduce | flops 4352 | bytes 34816 | tf_op jit(solution)/shard_map/psum | solution.py:70
  387.9 0.6 add_divide_fusion
  388.6 0.8 multiply_bitcast_fusion
  (20 shorter events, 0.0 us)
Async XLA Ops:
  0.6 102.9 %copy-start = (bf16[512,32]{0,1:T(8,128)(2,1)S(1)}, bf16[512,32]{0,1:T(8,128)(2,1)}, u32[]{:S(2)}) copy-start(bf16[512,32]{0,1:T(8,128)(2,1)} %param.15) | copy-start | bytes 98308
  67.3 1.3 copy-start.1
  77.9 3.7 copy-start.8
  84.5 3.7 copy-start.9
  91.1 3.7 copy-start.10
  97.7 5.8 %copy-start.2 = (bf16[512,128]{1,0:T(8,128)(2,1)S(1)}, bf16[512,128]{1,0:T(8,128)(2,1)}, u32[]{:S(2)}) copy-start(bf16[512,128]{1,0:T(8,128)(2,1)} %param.14) | copy-start | bytes 393220
  97.7 5.8 %copy-start.3 = (bf16[512,128]{1,0:T(8,128)(2,1)S(1)}, bf16[512,128]{1,0:T(8,128)(2,1)}, u32[]{:S(2)}) copy-start(bf16[512,128]{1,0:T(8,128)(2,1)} %param.11) | copy-start | bytes 393220
  97.7 5.9 %copy-start.6 = (f32[128]{0:T(128)S(1)}, f32[128]{0:T(128)}, u32[]{:S(2)}) copy-start(f32[128]{0:T(128)} %param.13) | copy-start | bytes 1540
  97.7 5.9 %copy-start.7 = (f32[128]{0:T(128)S(1)}, f32[128]{0:T(128)}, u32[]{:S(2)}) copy-start(f32[128]{0:T(128)} %param.12) | copy-start | bytes 1540
  97.7 290.3 %copy-start.4 = (f32[34,128]{1,0:T(8,128)S(1)}, f32[34,128]{1,0:T(8,128)}, u32[]{:S(2)}) copy-start(f32[34,128]{1,0:T(8,128)} %param.17) | copy-start | bytes 52228
  97.7 290.2 %copy-start.5 = (f32[34,128]{1,0:T(8,128)S(1)}, f32[34,128]{1,0:T(8,128)}, u32[]{:S(2)}) copy-start(f32[34,128]{1,0:T(8,128)} %param.16) | copy-start | bytes 52228
  97.7 290.9 %all-to-all-start.1 = ((bf16[32,1,16,2048]{3,2,1,0:T(8,128)(2,1)}), bf16[32,1,16,2048]{3,2,1,0:T(8,128)(2,1)S(1)}, u32[]{:S(2)}, u32[]{:S(2)}) async-start(bf16[32,1,16,2048]{3,2,1,0:T(8,128)(2,1)} %bitcast.28), calls=%async_computation.1 | async-start | bytes 4194304 | tf_op jit(solution)/shard_map/all_to_all | solution.py:84
where the time goes:
time: 391 us; the launch traced here: 389 us
  blocking collectives  346 us (88%)
  matrix products  29.1 us (7%)
  starting transfers between devices  5.72 us (1%)
  other arithmetic  5.67 us (1%)
    psum x1, blocking collectives, on_device(): lax.psum((gain_local, bias_local, router_local), ('shard', 'section'))  284 us
    all_to_all x1, blocking collectives, on_device(): lax.all_to_all(outgoing, 'shard', split_axis=0, concat_axis=0, tiled=True)  61.6 us
    dot_general x5, matrix products, orthogonalize(): jnp.einsum('kij,kjl->kil', poly, iterate, preferred_element_type=jnp.floa...  15.4 us
    dot_general x5, matrix products, orthogonalize(): jnp.einsum('kij,klj->kil', iterate, iterate, preferred_element_type=jnp.f...  13.5 us
  transfers between devices with their start and end apart: 1, of which 0 were waited for; matrix products, arithmetic and copies ran while one was open for 0% of the time, Pallas kernels for 0%

commit v1 on v0

v1 whole, which is shorter than its diff:
```python
import math

import jax
import jax.numpy as jnp
import numpy as np
from jax import lax
from jax.sharding import Mesh
from jax.sharding import PartitionSpec as P

FF = 2048
ITERS = 5


MUON_DECAY = 0.95
LINEAR_TERM = 3.4445
CUBIC_TERM = -4.775
QUINTIC_TERM = 2.0315
NORM_EPSILON = 1e-07
ADAM_FIRST = 0.9
ADAM_SECOND = 0.95
ADAM_EPSILON = 1e-08

SHARD = ("outer", "inner")


def orthogonalize(blocks):
    squares = jnp.sum(jnp.square(blocks.astype(jnp.float32)), axis=(1, 2))
    total = jnp.sqrt(squares)
    iterate = (blocks.astype(jnp.float32) / (total + NORM_EPSILON)[:, None, None]).astype(
        jnp.bfloat16
    )
    for repeat in range(ITERS):
        gram = jnp.einsum("kij,klj->kil", iterate, iterate, preferred_element_type=jnp.float32)
        gram_half = gram.astype(jnp.bfloat16)
        square_term = jnp.einsum(
            "kij,kjl->kil", gram_half, gram_half, preferred_element_type=jnp.float32
        )
        poly = (CUBIC_TERM * gram + QUINTIC_TERM * square_term).astype(jnp.bfloat16)
        product = jnp.einsum("kij,kjl->kil", poly, iterate, preferred_element_type=jnp.float32)
        iterate = (LINEAR_TERM * iterate.astype(jnp.float32) + product).astype(jnp.bfloat16)
    return iterate


def vector_step(normed, ln_gain, ln_bias, ln_cotangent, router_cotangent, first_moment, second_moment):
    normed_float = normed.astype(jnp.float32)
    cot_float = ln_cotangent.astype(jnp.float32)
    ln_out = (ln_gain[None, :] * normed_float + ln_bias[None, :]).astype(jnp.bfloat16)
    gain_local = jnp.sum(cot_float * normed_float, axis=0)
    bias_local = jnp.sum(cot_float, axis=0)
    router_local = lax.dot_general(
        router_cotangent, ln_out, (((0,), (0,)), ((), ())), preferred_element_type=jnp.float32
    )
    local = jnp.concatenate([gain_local[None, :], bias_local[None, :], router_local], axis=0)
    vec_grad = lax.psum(local, SHARD + ("section",))
    next_first = ADAM_FIRST * first_moment + (1.0 - ADAM_FIRST) * vec_grad
    next_second = ADAM_SECOND * second_moment + (1.0 - ADAM_SECOND) * vec_grad * vec_grad
    adam_step = next_first / (jnp.sqrt(next_second) + ADAM_EPSILON)
    return next_first, next_second, adam_step


def on_device(
    gradient,
    momentum,
    normed,
    ln_gain,
    ln_bias,
    ln_cotangent,
    router_cotangent,
    first_moment,
    second_moment,
):
    next_first, next_second, adam_step = vector_step(
        normed, ln_gain, ln_bias, ln_cotangent, router_cotangent, first_moment, second_moment
    )
    grad_float = gradient.astype(jnp.float32)
    next_momentum = MUON_DECAY * momentum + grad_float
    nesterov = (grad_float + MUON_DECAY * next_momentum).astype(jnp.bfloat16)
    nesterov, next_first, next_second, adam_step = lax.optimization_barrier(
        (nesterov, next_first, next_second, adam_step)
    )
    count_all, rows_piece, cols_full = nesterov.shape
    inner = lax.axis_size("inner")
    outer = lax.axis_size("outer")
    slots = -(-count_all // inner)
    padded = jnp.pad(nesterov, ((0, slots * inner - count_all), (0, 0), (0, 0)))
    strip = lax.all_to_all(padded, "inner", split_axis=0, concat_axis=1, tiled=True)
    blocks = lax.all_gather(strip, "outer", axis=1, tiled=True)
    result = orthogonalize(blocks)
    strip_rows = inner * rows_piece
    mine = lax.dynamic_slice_in_dim(result, lax.axis_index("outer") * strip_rows, strip_rows, axis=1)
    outgoing = mine.reshape(slots, inner, rows_piece, cols_full).transpose(1, 0, 2, 3)
    returned = lax.all_to_all(outgoing, "inner", split_axis=0, concat_axis=0, tiled=True)
    ordered = returned.reshape(slots * inner, rows_piece, cols_full)
    update = ordered[:count_all].astype(jnp.float32) * math.sqrt(FF)
    return (next_momentum, update, next_first, next_second, adam_step)


def inner_size(mesh):
    row = np.asarray(mesh.devices)[:, 0, 0]
    try:
        size = len({tuple(device.coords)[0] for device in row})
    except (AttributeError, TypeError):
        size = 0
    if size <= 1 or row.size % size:
        size = math.gcd(row.size, 4)
    return size


def solution(mesh):
    devices = np.asarray(mesh.devices)
    shard, tensor, section = devices.shape
    inner = inner_size(mesh)
    split = Mesh(
        devices.reshape(shard // inner, inner, tensor, section),
        ("outer", "inner", "tensor", "section"),
    )
    return jax.shard_map(
        on_device,
        mesh=split,
        in_specs=(
            P(("tensor", "section"), SHARD, None),
            P(("tensor", "section"), SHARD, None),
            P((*SHARD, "section"), "tensor"),
            P("tensor"),
            P("tensor"),
            P((*SHARD, "section"), "tensor"),
            P((*SHARD, "section"), None),
            P(None, "tensor"),
            P(None, "tensor"),
        ),
        out_specs=(
            P(("tensor", "section"), SHARD, None),
            P(("tensor", "section"), SHARD, None),
            P(None, "tensor"),
            P(None, "tensor"),
            P(None, "tensor"),
        ),
        check_vma=False,
    )
```

time: 391 us -> 365 us (0.934)
  blocking collectives: 346 us -> 274 us
  waiting for transfers between devices: 0.01 us -> 36.3 us
  between operations: 1.49 us -> 14.8 us
  starting transfers between devices: 5.72 us -> 0.04 us
    all_to_all x1 -> x2, blocking collectives: 61.6 us -> 20.5 us  [the longest x1 10.7 us: on_device(): lax.all_to_all(outgoing, 'inner', split_axis=0, concat_axis=0, tiled=True)]
    all_gather x0 -> x1, waiting for transfers between devices: none -> 36.3 us  [on_device(): blocks = lax.all_gather(strip, 'outer', axis=1, tiled=True)]
    psum x1, blocking collectives: 284 us -> 254 us  [vector_step(): vec_grad = lax.psum(local, SHARD + ('section',))]
    all_to_all x1 -> x0, starting transfers between devices: 5.72 us -> none  [on_device(): lax.all_to_all(result.reshape(items, shard_count, rows_piece, cols_full)....]
  transfers between devices with their start and end apart: 1 -> 1, of which waited for: 0 -> 1; matrix products, arithmetic and copies ran while one was open for 0% -> 0% of each run, Pallas kernels for 0% -> 0%
where the time goes in v1:
time: 365 us
  blocking collectives  274 us (75%)
  waiting for transfers between devices  36.3 us (10%)
  matrix products  30.6 us (8%)
  between operations  14.8 us (4%)
  other arithmetic  9.08 us (2%)
    psum x1, blocking collectives, vector_step(): vec_grad = lax.psum(local, SHARD + ('section',))  254 us
    all_gather x1, waiting for transfers between devices, on_device(): blocks = lax.all_gather(strip, 'outer', axis=1, tiled=True)  36.3 us
    dot_general x5, matrix products, orthogonalize(): jnp.einsum('kij,kjl->kil', poly, iterate, preferred_element_type=jnp.floa...  16.1 us
    dot_general x5, matrix products, orthogonalize(): jnp.einsum('kij,klj->kil', iterate, iterate, preferred_element_type=jnp.f...  13.4 us
    all_to_all x1, blocking collectives, on_device(): lax.all_to_all(outgoing, 'inner', split_axis=0, concat_axis=0, tiled=True)  10.7 us
    all_to_all x1, blocking collectives, on_device(): lax.all_to_all(padded, 'inner', split_axis=0, concat_axis=1, tiled=True)  9.74 us
  transfers between devices with their start and end apart: 1, of which 1 were waited for; matrix products, arithmetic and copies ran while one was open for 0% of the time, Pallas kernels for 0%

profile of v1, /device:TPU:16, one launch (start us, length us, event | category | flops | bytes accessed | tf_op | source)
XLA Modules:
  0.0 364.9 jit_solution(559402803805379701)
XLA Ops:
  7.2 0.0 copy-start
  7.2 0.0 all-gather.2.cloned.1.call-start
  7.2 1.1 fusion.53
  8.3 1.1 convolution_bitcast_fusion.1
  9.4 253.6 %psum.7 = f32[34,128]{1,0:T(8,128)S(1)} all-reduce(f32[34,128]{1,0:T(8,128)S(1)} %pad_maximum_fusion), channel_id=1, replica_groups=mesh['outer'=8,'inner'=4,'tensor'=4,'section'=2] {'outer','inner','secti..., use_global_device_ids=true, to_apply=%region_2.0 | all-reduce | flops 4352 | bytes 34816 | tf_op jit(solution)/shard_map/psum | solution.py:54
  263.0 2.0 fusion.31
  265.0 0.6 add_divide_fusion
  265.7 9.7 %all_to_all.17 = bf16[4,16,2048]{2,1,0:T(8,128)(2,1)} all-to-all(bf16[4,16,2048]{2,1,0:T(8,128)(2,1)S(1)} %get-tuple-element.9), channel_id=1, replica_groups=mesh['outer'=8,'inner'=4,'tensor'=4,'section'=2] {'inner'}, dimensions={0} | all-to-all | bytes 524288 | tf_op jit(solution)/shard_map/all_to_all | solution.py:86
  275.4 0.0 all-gather.2.cloned.1.call-update
  275.4 36.3 %all-gather.2.cloned.1.call-done = bf16[1,512,2048]{2,1,0:T(8,128)(2,1)} async-done(((bf16[1,64,2048]{2,1,0:T(8,128)(2,1)}), bf16[1,512,2048]{2,1,0:T(8,128)(2,1)}) %all-gather.2.cloned.1.call-update) | async-done | bytes 2097168 | tf_op jit(solution)/shard_map/all_gather | solution.py:87
  311.7 3.4 fusion
  315.8 1.3 fusion.19
  317.1 3.0 fusion.5
  320.2 3.6 fusion.16
  323.8 2.9 fusion.4
  326.7 3.7 %fusion.13 = f32[512,512]{1,0:T(8,128)S(1)} fusion(bf16[1,512,2048]{2,1,0:T(8,128)(2,1)} %fusion.4), kind=kOutput, calls=%fused_computation.20 | convolution fusion | flops 1073741824 | bytes 3145728 | tf_op jit(solution)/shard_map/kij,klj->kil/dot_general | solution.py:33
  330.4 2.9 fusion.3
  333.3 3.5 fusion.10
  336.8 3.8 %fusion.2 = bf16[1,512,2048]{2,1,0:T(8,128)(2,1)S(1)} fusion(bf16[1,512,2048]{2,1,0:T(8,128)(2,1)} %fusion.3, f32[512,512]{1,0:T(8,128)S(1)} %fusion.10), kind=kOutput, calls=%fused_computation.5 | convolution fusion | flops 1347682304 | bytes 5242880 | tf_op jit(solution)/shard_map/kij,kjl->kil/dot_general | solution.py:39
  340.6 1.3 fusion.7
  341.9 3.5 convolution_bitcast_fusion
  345.4 1.1 fusion.32
  346.5 10.7 %all_to_all.18 = bf16[4,1,16,2048]{3,2,1,0:T(8,128)(2,1)S(1)} all-to-all(bf16[4,1,16,2048]{3,2,1,0:T(8,128)(2,1)S(1)} %bitcast.53), channel_id=1, replica_groups=mesh['outer'=8,'inner'=4,'tensor'=4,'section'=2] {'inner'}, dimensions={0} | all-to-all | bytes 524288 | tf_op jit(solution)/shard_map/all_to_all | solution.py:92
  357.2 0.8 multiply_bitcast_fusion
  (12 shorter events, 0.0 us)
Async XLA Ops:
  7.2 1.1 copy-start
  7.2 257.8 %copy-start.2 = (f32[34,128]{1,0:T(8,128)S(1)}, f32[34,128]{1,0:T(8,128)}, u32[]{:S(2)}) copy-start(f32[34,128]{1,0:T(8,128)} %param.17) | copy-start | bytes 52228
  7.2 257.8 %copy-start.3 = (f32[34,128]{1,0:T(8,128)S(1)}, f32[34,128]{1,0:T(8,128)}, u32[]{:S(2)}) copy-start(f32[34,128]{1,0:T(8,128)} %param.16) | copy-start | bytes 52228
  7.2 304.5 %all-gather.2.cloned.1.call-start = ((), (), s32[]{:S(2)}) async-start(), calls=%async_computation.2 | async-start | bytes 2359296 | tf_op jit(solution)/shard_map/all_gather | solution.py:87
  311.7 4.1 %copy-start.1 = (bf16[1,512,2048]{2,1,0:T(8,128)(2,1)S(1)}, bf16[1,512,2048]{2,1,0:T(8,128)(2,1)}, u32[]{:S(2)}) copy-start(bf16[1,512,2048]{2,1,0:T(8,128)(2,1)} %all-gather.2.cloned.1.call-done) | copy-start | bytes 6291460
  320.1 3.7 %copy-start.4 = (bf16[1,512,2048]{2,1,0:T(8,128)(2,1)S(1)}, bf16[1,512,2048]{2,1,0:T(8,128)(2,1)}, u32[]{:S(2)}) copy-start(bf16[1,512,2048]{2,1,0:T(8,128)(2,1)} %fusion.5) | copy-start | bytes 6291460
  326.7 3.7 %copy-start.5 = (bf16[1,512,2048]{2,1,0:T(8,128)(2,1)S(1)}, bf16[1,512,2048]{2,1,0:T(8,128)(2,1)}, u32[]{:S(2)}) copy-start(bf16[1,512,2048]{2,1,0:T(8,128)(2,1)} %fusion.4) | copy-start | bytes 6291460
Sparse Core Ops, SparseCore 0:
  275.5 36.0 all-gather.1

commit v2 on v1

--- a/solution.py
+++ b/solution.py
@@ -41,7 +41,9 @@
     return iterate
 
 
-def vector_step(normed, ln_gain, ln_bias, ln_cotangent, router_cotangent, first_moment, second_moment):
+def vector_step(
+    normed, ln_gain, ln_bias, ln_cotangent, router_cotangent, first_moment, second_moment, after
+):
     normed_float = normed.astype(jnp.float32)
     cot_float = ln_cotangent.astype(jnp.float32)
     ln_out = (ln_gain[None, :] * normed_float + ln_bias[None, :]).astype(jnp.bfloat16)
@@ -51,7 +53,9 @@
         router_cotangent, ln_out, (((0,), (0,)), ((), ())), preferred_element_type=jnp.float32
     )
     local = jnp.concatenate([gain_local[None, :], bias_local[None, :], router_local], axis=0)
-    vec_grad = lax.psum(local, SHARD + ("section",))
+    local, after = lax.optimization_barrier((local, after))
+    everyone = lax.all_gather(local, SHARD + ("section",), axis=0, tiled=False)
+    vec_grad = jnp.sum(everyone, axis=0)
     next_first = ADAM_FIRST * first_moment + (1.0 - ADAM_FIRST) * vec_grad
     next_second = ADAM_SECOND * second_moment + (1.0 - ADAM_SECOND) * vec_grad * vec_grad
     adam_step = next_first / (jnp.sqrt(next_second) + ADAM_EPSILON)
@@ -69,15 +73,9 @@
     first_moment,
     second_moment,
 ):
-    next_first, next_second, adam_step = vector_step(
-        normed, ln_gain, ln_bias, ln_cotangent, router_cotangent, first_moment, second_moment
-    )
     grad_float = gradient.astype(jnp.float32)
     next_momentum = MUON_DECAY * momentum + grad_float
     nesterov = (grad_float + MUON_DECAY * next_momentum).astype(jnp.bfloat16)
-    nesterov, next_first, next_second, adam_step = lax.optimization_barrier(
-        (nesterov, next_first, next_second, adam_step)
-    )
     count_all, rows_piece, cols_full = nesterov.shape
     inner = lax.axis_size("inner")
     outer = lax.axis_size("outer")
@@ -85,6 +83,9 @@
     padded = jnp.pad(nesterov, ((0, slots * inner - count_all), (0, 0), (0, 0)))
     strip = lax.all_to_all(padded, "inner", split_axis=0, concat_axis=1, tiled=True)
     blocks = lax.all_gather(strip, "outer", axis=1, tiled=True)
+    next_first, next_second, adam_step = vector_step(
+        normed, ln_gain, ln_bias, ln_cotangent, router_cotangent, first_moment, second_moment, blocks
+    )
     result = orthogonalize(blocks)
     strip_rows = inner * rows_piece
     mine = lax.dynamic_slice_in_dim(result, lax.axis_index("outer") * strip_rows, strip_rows, axis=1)

time: 365 us -> 152 us (0.42)
  blocking collectives: 274 us -> 21.6 us
  waiting for transfers between devices: 36.3 us -> 74.1 us
    psum x1 -> x0, blocking collectives: 254 us -> none  [vector_step(): vec_grad = lax.psum(local, SHARD + ('section',))]
    all_gather x0 -> x1, waiting for transfers between devices: none -> 33.1 us  [vector_step(): everyone = lax.all_gather(local, SHARD + ('section',), axis=0, tiled=False)]
    all_gather x1, waiting for transfers between devices: 36.3 us -> 41 us  [on_device(): blocks = lax.all_gather(strip, 'outer', axis=1, tiled=True)]
  transfers between devices with their start and end apart: 1 -> 2, of which waited for: 1 -> 2; matrix products, arithmetic and copies ran while one was open for 0% -> 22% of each run, Pallas kernels for 0% -> 0%
where the time goes in v2:
time: 152 us; the launch traced here: 151 us
  waiting for transfers between devices  74.1 us (49%)
  matrix products  29.9 us (20%)
  blocking collectives  21.6 us (14%)
  between operations  14.9 us (10%)
  other arithmetic  10.2 us (7%)
    all_gather x1, waiting for transfers between devices, on_device(): blocks = lax.all_gather(strip, 'outer', axis=1, tiled=True)  41 us
    all_gather x1, waiting for transfers between devices, vector_step(): everyone = lax.all_gather(local, SHARD + ('section',), axis=0, tiled=False)  33.1 us
    dot_general x5, matrix products, orthogonalize(): jnp.einsum('kij,kjl->kil', poly, iterate, preferred_element_type=jnp.floa...  16.4 us
    dot_general x5, matrix products, orthogonalize(): jnp.einsum('kij,klj->kil', iterate, iterate, preferred_element_type=jnp.f...  13.4 us
    all_to_all x1, blocking collectives, on_device(): lax.all_to_all(padded, 'inner', split_axis=0, concat_axis=1, tiled=True)  10.9 us
    all_to_all x1, blocking collectives, on_device(): lax.all_to_all(outgoing, 'inner', split_axis=0, concat_axis=0, tiled=True)  10.7 us
    reduce_sum x1, other arithmetic, orthogonalize(): squares = jnp.sum(jnp.square(blocks.astype(jnp.float32)), axis=(1, 2))  3.42 us
  transfers between devices with their start and end apart: 2, of which 2 were waited for; matrix products, arithmetic and copies ran while one was open for 22% of the time, Pallas kernels for 0%

profile of v2, /device:TPU:16, one launch (start us, length us, event | category | flops | bytes accessed | tf_op | source)
XLA Modules:
  0.0 150.8 jit_solution(5409121314503021347)
XLA Ops:
  7.3 2.1 %fusion.31 = (bf16[4,16,2048]{2,1,0:T(8,128)(2,1)S(1)}, f32[4,16,2048]{2,1,0:T(8,128)}) fusion(bf16[4,16,2048]{2,1,0:T(8,128)(2,1)} %param.9, f32[4,16,2048]{2,1,0:T(8,128)} %param.10), kind=kLoop, calls=%fused_computation.46 | loop fusion | flops 786432 | bytes 1572864 | tf_op jit(solution)/shard_map/convert_element_type | solution.py:78
  9.3 10.9 %all_to_all.17 = bf16[4,16,2048]{2,1,0:T(8,128)(2,1)} all-to-all(bf16[4,16,2048]{2,1,0:T(8,128)(2,1)S(1)} %get-tuple-element.12), channel_id=1, replica_groups=mesh['outer'=8,'inner'=4,'tensor'=4,'section'=2] {'inner'}, dimensions={0} | all-to-all | bytes 524288 | tf_op jit(solution)/shard_map/all_to_all | solution.py:84
  20.2 0.0 all-gather.7.cloned.1.call-start
  20.3 0.1 fusion.53
  20.4 0.2 convolution_bitcast_fusion.1
  20.5 0.6 pad_maximum_fusion
  21.2 41.0 %all-gather.5.cloned.1.call-done = bf16[1,512,2048]{2,1,0:T(8,128)(2,1)} async-done(((bf16[1,64,2048]{2,1,0:T(8,128)(2,1)}), bf16[1,512,2048]{2,1,0:T(8,128)(2,1)}) %all-gather.5.cloned.1.call-update) | async-done | bytes 2097168 | tf_op jit(solution)/shard_map/all_gather | solution.py:85
  62.2 3.4 %fusion = f32[]{:T(128)} fusion(bf16[1,512,2048]{2,1,0:T(8,128)(2,1)} %all-gather.5.cloned.1.call-done), kind=kLoop, calls=%fused_computation.2 | loop fusion | flops 3145727 | bytes 2097156 | tf_op jit(solution)/shard_map/reduce_sum | solution.py:27
  66.3 1.3 fusion.19
  67.6 3.1 %fusion.5 = bf16[1,512,2048]{2,1,0:T(8,128)(2,1)} fusion(f32[512,512]{1,0:T(8,128)S(1)} %fusion.19, f32[]{:T(128)S(6)} %add.70, bf16[1,512,2048]{2,1,0:T(8,128)(2,1)S(1)} %copy-done.1), kind=kOutput, calls=%fused_computation.11 | convolution fusion | flops 1353973760 | bytes 5242884 | tf_op jit(solution)/shard_map/kij,kjl->kil/dot_general | solution.py:39
  70.7 3.6 %fusion.16 = f32[512,512]{1,0:T(8,128)S(1)} fusion(bf16[1,512,2048]{2,1,0:T(8,128)(2,1)} %fusion.5), kind=kOutput, calls=%fused_computation.23 | convolution fusion | flops 1073741824 | bytes 3145728 | tf_op jit(solution)/shard_map/kij,klj->kil/dot_general | solution.py:33
  74.4 3.0 %fusion.4 = bf16[1,512,2048]{2,1,0:T(8,128)(2,1)} fusion(bf16[1,512,2048]{2,1,0:T(8,128)(2,1)S(1)} %copy-done.8, f32[512,512]{1,0:T(8,128)S(1)} %fusion.16), kind=kOutput, calls=%fused_computation.9 | convolution fusion | flops 1347682304 | bytes 5242880 | tf_op jit(solution)/shard_map/kij,kjl->kil/dot_general | solution.py:39
  77.4 3.7 %fusion.13 = f32[512,512]{1,0:T(8,128)S(1)} fusion(bf16[1,512,2048]{2,1,0:T(8,128)(2,1)} %fusion.4), kind=kOutput, calls=%fused_computation.20 | convolution fusion | flops 1073741824 | bytes 3145728 | tf_op jit(solution)/shard_map/kij,klj->kil/dot_general | solution.py:33
  81.0 3.0 %fusion.3 = bf16[1,512,2048]{2,1,0:T(8,128)(2,1)} fusion(bf16[1,512,2048]{2,1,0:T(8,128)(2,1)S(1)} %copy-done.9, f32[512,512]{1,0:T(8,128)S(1)} %fusion.13), kind=kOutput, calls=%fused_computation.7 | convolution fusion | flops 1347682304 | bytes 5242880 | tf_op jit(solution)/shard_map/kij,kjl->kil/dot_general | solution.py:39
  84.0 3.5 %fusion.10 = f32[512,512]{1,0:T(8,128)S(1)} fusion(bf16[1,512,2048]{2,1,0:T(8,128)(2,1)} %fusion.3), kind=kOutput, calls=%fused_computation.17 | convolution fusion | flops 1073741824 | bytes 3145728 | tf_op jit(solution)/shard_map/kij,klj->kil/dot_general | solution.py:33
  87.5 3.8 %fusion.2 = bf16[1,512,2048]{2,1,0:T(8,128)(2,1)S(1)} fusion(bf16[1,512,2048]{2,1,0:T(8,128)(2,1)} %fusion.3, f32[512,512]{1,0:T(8,128)S(1)} %fusion.10), kind=kOutput, calls=%fused_computation.5 | convolution fusion | flops 1347682304 | bytes 5242880 | tf_op jit(solution)/shard_map/kij,kjl->kil/dot_general | solution.py:39
  91.3 1.3 fusion.7
  92.6 3.5 %convolution_bitcast_fusion = f32[1,512,2048]{2,1,0:T(8,128)} fusion(bf16[1,512,2048]{2,1,0:T(8,128)(2,1)S(1)} %fusion.2, f32[512,512]{1,0:T(8,128)S(1)} %fusion.7), kind=kOutput, calls=%fused_computation.12 | convolution fusion | flops 1343488000 | bytes 7340032 | tf_op jit(solution)/shard_map/kij,kjl->kil/dot_general | solution.py:39
  96.1 1.1 fusion.32
  97.2 10.7 %all_to_all.18 = bf16[4,1,16,2048]{3,2,1,0:T(8,128)(2,1)S(1)} all-to-all(bf16[4,1,16,2048]{3,2,1,0:T(8,128)(2,1)S(1)} %bitcast.54), channel_id=1, replica_groups=mesh['outer'=8,'inner'=4,'tensor'=4,'section'=2] {'inner'}, dimensions={0} | all-to-all | bytes 524288 | tf_op jit(solution)/shard_map/all_to_all | solution.py:93
  108.0 0.8 multiply_bitcast_fusion
  108.8 33.1 %all-gather.7.cloned.1.call-done = f32[64,34,128]{2,1,0:T(8,128)} async-done(((f32[1,34,128]{2,1,0:T(8,128)}), f32[64,34,128]{2,1,0:T(8,128)}) %all-gather.7.cloned.1.call-update) | async-done | bytes 1114128 | tf_op jit(solution)/shard_map/all_gather | solution.py:57
  141.9 1.4 reduce_sum.39
  143.3 0.6 add_divide_fusion
  (23 shorter events, 0.1 us)
Async XLA Ops:
  7.2 13.2 %copy-start = (bf16[512,32]{0,1:T(8,128)(2,1)S(1)}, bf16[512,32]{0,1:T(8,128)(2,1)}, u32[]{:S(2)}) copy-start(bf16[512,32]{0,1:T(8,128)(2,1)} %param.15) | copy-start | bytes 98308
  7.2 13.1 %copy-start.3 = (bf16[512,128]{1,0:T(8,128)(2,1)S(1)}, bf16[512,128]{1,0:T(8,128)(2,1)}, u32[]{:S(2)}) copy-start(bf16[512,128]{1,0:T(8,128)(2,1)} %param.11) | copy-start | bytes 393220
  7.2 13.1 %copy-start.2 = (bf16[512,128]{1,0:T(8,128)(2,1)S(1)}, bf16[512,128]{1,0:T(8,128)(2,1)}, u32[]{:S(2)}) copy-start(bf16[512,128]{1,0:T(8,128)(2,1)} %param.14) | copy-start | bytes 393220
  7.2 13.2 %copy-start.6 = (f32[128]{0:T(128)S(1)}, f32[128]{0:T(128)}, u32[]{:S(2)}) copy-start(f32[128]{0:T(128)} %param.13) | copy-start | bytes 1540
  7.2 13.2 %copy-start.7 = (f32[128]{0:T(128)S(1)}, f32[128]{0:T(128)}, u32[]{:S(2)}) copy-start(f32[128]{0:T(128)} %param.12) | copy-start | bytes 1540
  7.2 54.9 %all-gather.5.cloned.1.call-start = ((), (), s32[]{:S(2)}) async-start(), calls=%async_computation.2 | async-start | bytes 2359296 | tf_op jit(solution)/shard_map/all_gather | solution.py:85
  20.2 121.6 %all-gather.7.cloned.1.call-start = ((), (), s32[]{:S(2)}) async-start(), calls=%async_computation.3 | async-start | bytes 1331200 | tf_op jit(solution)/shard_map/all_gather | solution.py:57
  62.2 4.1 %copy-start.1 = (bf16[1,512,2048]{2,1,0:T(8,128)(2,1)S(1)}, bf16[1,512,2048]{2,1,0:T(8,128)(2,1)}, u32[]{:S(2)}) copy-start(bf16[1,512,2048]{2,1,0:T(8,128)(2,1)} %all-gather.5.cloned.1.call-done) | copy-start | bytes 6291460
  70.7 3.7 %copy-start.8 = (bf16[1,512,2048]{2,1,0:T(8,128)(2,1)S(1)}, bf16[1,512,2048]{2,1,0:T(8,128)(2,1)}, u32[]{:S(2)}) copy-start(bf16[1,512,2048]{2,1,0:T(8,128)(2,1)} %fusion.5) | copy-start | bytes 6291460
  77.4 3.7 %copy-start.9 = (bf16[1,512,2048]{2,1,0:T(8,128)(2,1)S(1)}, bf16[1,512,2048]{2,1,0:T(8,128)(2,1)}, u32[]{:S(2)}) copy-start(bf16[1,512,2048]{2,1,0:T(8,128)(2,1)} %fusion.4) | copy-start | bytes 6291460
  96.1 47.2 %copy-start.4 = (f32[34,128]{1,0:T(8,128)S(1)}, f32[34,128]{1,0:T(8,128)}, u32[]{:S(2)}) copy-start(f32[34,128]{1,0:T(8,128)} %param.17) | copy-start | bytes 52228
  96.1 47.2 %copy-start.5 = (f32[34,128]{1,0:T(8,128)S(1)}, f32[34,128]{1,0:T(8,128)}, u32[]{:S(2)}) copy-start(f32[34,128]{1,0:T(8,128)} %param.16) | copy-start | bytes 52228
Sparse Core Ops, SparseCore 0:
  20.3 41.7 all-gather.4
  66.4 75.3 all-gather.6

commit v3 on v2

--- a/solution.py
+++ b/solution.py
@@ -41,9 +41,19 @@
     return iterate
 
 
-def vector_step(
-    normed, ln_gain, ln_bias, ln_cotangent, router_cotangent, first_moment, second_moment, after
-):
+def butterfly_sum(value, axis):
+    size = lax.axis_size(axis)
+    if size & (size - 1):
+        return jnp.sum(lax.all_gather(value, axis, axis=0, tiled=False), axis=0)
+    step = 1
+    while step < size:
+        partner = lax.ppermute(value, axis, [(i, i ^ step) for i in range(size)])
+        value = value + partner
+        step *= 2
+    return value
+
+
+def vector_step(normed, ln_gain, ln_bias, ln_cotangent, router_cotangent, first_moment, second_moment):
     normed_float = normed.astype(jnp.float32)
     cot_float = ln_cotangent.astype(jnp.float32)
     ln_out = (ln_gain[None, :] * normed_float + ln_bias[None, :]).astype(jnp.bfloat16)
@@ -53,9 +63,9 @@
         router_cotangent, ln_out, (((0,), (0,)), ((), ())), preferred_element_type=jnp.float32
     )
     local = jnp.concatenate([gain_local[None, :], bias_local[None, :], router_local], axis=0)
-    local, after = lax.optimization_barrier((local, after))
-    everyone = lax.all_gather(local, SHARD + ("section",), axis=0, tiled=False)
-    vec_grad = jnp.sum(everyone, axis=0)
+    vec_grad = local
+    for axis in ("section",) + SHARD:
+        vec_grad = butterfly_sum(vec_grad, axis)
     next_first = ADAM_FIRST * first_moment + (1.0 - ADAM_FIRST) * vec_grad
     next_second = ADAM_SECOND * second_moment + (1.0 - ADAM_SECOND) * vec_grad * vec_grad
     adam_step = next_first / (jnp.sqrt(next_second) + ADAM_EPSILON)
@@ -84,7 +94,7 @@
     strip = lax.all_to_all(padded, "inner", split_axis=0, concat_axis=1, tiled=True)
     blocks = lax.all_gather(strip, "outer", axis=1, tiled=True)
     next_first, next_second, adam_step = vector_step(
-        normed, ln_gain, ln_bias, ln_cotangent, router_cotangent, first_moment, second_moment, blocks
+        normed, ln_gain, ln_bias, ln_cotangent, router_cotangent, first_moment, second_moment
     )
     result = orthogonalize(blocks)
     strip_rows = inner * rows_piece

time: 152 us -> 117 us (0.77)
  waiting for transfers between devices: 74.1 us -> 34 us
  starting transfers between devices: 0.08 us -> 18.3 us
  blocking collectives: 21.6 us -> 10.9 us
    all_gather x1 -> x0, waiting for transfers between devices: 33.1 us -> none  [vector_step(): everyone = lax.all_gather(local, SHARD + ('section',), axis=0, tiled=False)]
    all_gather x1, waiting for transfers between devices: 41 us -> 17.9 us  [on_device(): blocks = lax.all_gather(strip, 'outer', axis=1, tiled=True)]
    ppermute x0 -> x6, starting transfers between devices: none -> 13.5 us  [butterfly_sum(): partner = lax.ppermute(value, axis, [(i, i ^ step) for i in range(size)])]
    all_to_all x1 -> x0, blocking collectives: 10.7 us -> none  [on_device(): lax.all_to_all(outgoing, 'inner', split_axis=0, concat_axis=0, tiled=True)]
    ppermute x0 -> x6, waiting for transfers between devices: none -> 10.1 us  [butterfly_sum(): partner = lax.ppermute(value, axis, [(i, i ^ step) for i in range(size)])]
    all_to_all x0 -> x1, waiting for transfers between devices: none -> 6.03 us  [on_device(): lax.all_to_all(outgoing, 'inner', split_axis=0, concat_axis=0, tiled=True)]
    all_to_all x0 -> x1, starting transfers between devices: none -> 4.79 us  [on_device(): lax.all_to_all(outgoing, 'inner', split_axis=0, concat_axis=0, tiled=True)]
  transfers between devices with their start and end apart: 2 -> 8, of which waited for: 2 -> 7; matrix products, arithmetic and copies ran while one was open for 22% -> 31% of each run, Pallas kernels for 0% -> 0%
where the time goes in v3:
time: 117 us
  waiting for transfers between devices  34 us (29%)
  matrix products  29.8 us (25%)
  starting transfers between devices  18.3 us (16%)
  between operations  14.9 us (13%)
  blocking collectives  10.9 us (9%)
  other arithmetic  8.89 us (8%)
    all_gather x1, waiting for transfers between devices, on_device(): blocks = lax.all_gather(strip, 'outer', axis=1, tiled=True)  17.9 us
    dot_general x5, matrix products, orthogonalize(): jnp.einsum('kij,kjl->kil', poly, iterate, preferred_element_type=jnp.floa...  16.3 us
    ppermute x6, starting transfers between devices, butterfly_sum(): partner = lax.ppermute(value, axis, [(i, i ^ step) for i in range(size)])  13.5 us
    dot_general x5, matrix products, orthogonalize(): jnp.einsum('kij,klj->kil', iterate, iterate, preferred_element_type=jnp.f...  13.4 us
    all_to_all x1, blocking collectives, on_device(): lax.all_to_all(padded, 'inner', split_axis=0, concat_axis=1, tiled=True)  10.9 us
    ppermute x6, waiting for transfers between devices, butterfly_sum(): partner = lax.ppermute(value, axis, [(i, i ^ step) for i in range(size)])  10.1 us
    all_to_all x1, waiting for transfers between devices, on_device(): lax.all_to_all(outgoing, 'inner', split_axis=0, concat_axis=0, tiled=True)  6.03 us
    all_to_all x1, starting transfers between devices, on_device(): lax.all_to_all(outgoing, 'inner', split_axis=0, concat_axis=0, tiled=True)  4.79 us
  transfers between devices with their start and end apart: 8, of which 7 were waited for; matrix products, arithmetic and copies ran while one was open for 31% of the time, Pallas kernels for 0%

profile of v3, /device:TPU:16, one launch (start us, length us, event | category | flops | bytes accessed | tf_op | source)
XLA Modules:
  0.0 116.8 jit_solution(6073687290194067642)
XLA Ops:
  7.3 2.1 %fusion.31 = (bf16[4,16,2048]{2,1,0:T(8,128)(2,1)S(1)}, f32[4,16,2048]{2,1,0:T(8,128)}) fusion(bf16[4,16,2048]{2,1,0:T(8,128)(2,1)} %param.9, f32[4,16,2048]{2,1,0:T(8,128)} %param.10), kind=kLoop, calls=%fused_computation.46 | loop fusion | flops 786432 | bytes 1572864 | tf_op jit(solution)/shard_map/convert_element_type | solution.py:88
  9.3 10.9 %all_to_all.17 = bf16[4,16,2048]{2,1,0:T(8,128)(2,1)} all-to-all(bf16[4,16,2048]{2,1,0:T(8,128)(2,1)S(1)} %get-tuple-element.10), channel_id=1, replica_groups=mesh['outer'=8,'inner'=4,'tensor'=4,'section'=2] {'inner'}, dimensions={0} | all-to-all | bytes 524288 | tf_op jit(solution)/shard_map/all_to_all | solution.py:94
  21.8 2.0 %collective-permute-start.1 = (f32[34,128]{1,0:T(8,128)S(1)}, f32[34,128]{1,0:T(8,128)S(1)}, u32[]{:S(2)}, u32[]{:S(2)}) collective-permute-start(f32[34,128]{1,0:T(8,128)S(1)} %fusion.70), channel_id=1, source_target_pairs={{0,32},{32,0},{64,96},{96,64},{128,160},{160,128},{192,224},{224,1... | collective-permute-start | bytes 52232 | tf_op jit(solution)/shard_map/ppermute | solution.py:50
  23.8 1.9 %collective-permute-done.1 = f32[34,128]{1,0:T(8,128)S(1)} collective-permute-done((f32[34,128]{1,0:T(8,128)S(1)}, f32[34,128]{1,0:T(8,128)S(1)}, u32[]{:S(2)}, u32[]{:S(2)}) %collective-permute-start.1) | collective-permute-done | bytes 17440 | tf_op jit(solution)/shard_map/ppermute | solution.py:50
  25.7 3.3 %collective-permute-start.2 = (f32[34,128]{1,0:T(8,128)S(1)}, f32[34,128]{1,0:T(8,128)S(1)}, u32[]{:S(2)}, u32[]{:S(2)}) collective-permute-start(f32[34,128]{1,0:T(8,128)S(1)} %add.103), channel_id=1, source_target_pairs={{0,64},{32,96},{64,0},{96,32},{128,192},{160,224},{192,128},{224,1... | collective-permute-start | bytes 52232 | tf_op jit(solution)/shard_map/ppermute | solution.py:50
  28.9 1.8 %collective-permute-done.2 = f32[34,128]{1,0:T(8,128)S(1)} collective-permute-done((f32[34,128]{1,0:T(8,128)S(1)}, f32[34,128]{1,0:T(8,128)S(1)}, u32[]{:S(2)}, u32[]{:S(2)}) %collective-permute-start.2) | collective-permute-done | bytes 17440 | tf_op jit(solution)/shard_map/ppermute | solution.py:50
  30.7 6.9 %collective-permute-start.3 = (f32[34,128]{1,0:T(8,128)S(1)}, f32[34,128]{1,0:T(8,128)S(1)}, u32[]{:S(2)}, u32[]{:S(2)}) collective-permute-start(f32[34,128]{1,0:T(8,128)S(1)} %add.104), channel_id=1, source_target_pairs={{0,128},{32,160},{64,192},{96,224},{128,0},{160,32},{192,64},{224,... | collective-permute-start | bytes 52232 | tf_op jit(solution)/shard_map/ppermute | solution.py:50
  37.6 2.0 %collective-permute-done.3 = f32[34,128]{1,0:T(8,128)S(1)} collective-permute-done((f32[34,128]{1,0:T(8,128)S(1)}, f32[34,128]{1,0:T(8,128)S(1)}, u32[]{:S(2)}, u32[]{:S(2)}) %collective-permute-start.3) | collective-permute-done | bytes 17440 | tf_op jit(solution)/shard_map/ppermute | solution.py:50
  40.1 3.3 %collective-permute-done.4 = f32[34,128]{1,0:T(8,128)S(1)} collective-permute-done((f32[34,128]{1,0:T(8,128)S(1)}, f32[34,128]{1,0:T(8,128)S(1)}, u32[]{:S(2)}, u32[]{:S(2)}) %collective-permute-start.4) | collective-permute-done | bytes 17440 | tf_op jit(solution)/shard_map/ppermute | solution.py:50
  44.1 17.9 %all-gather.2.cloned.1.call-done = bf16[1,512,2048]{2,1,0:T(8,128)(2,1)} async-done(((bf16[1,64,2048]{2,1,0:T(8,128)(2,1)}), bf16[1,512,2048]{2,1,0:T(8,128)(2,1)}) %all-gather.2.cloned.1.call-update) | async-done | bytes 2097168 | tf_op jit(solution)/shard_map/all_gather | solution.py:95
  62.0 3.4 %fusion = f32[]{:T(128)} fusion(bf16[1,512,2048]{2,1,0:T(8,128)(2,1)} %all-gather.2.cloned.1.call-done), kind=kLoop, calls=%fused_computation.2 | loop fusion | flops 3145727 | bytes 2097156 | tf_op jit(solution)/shard_map/reduce_sum | solution.py:27
  66.2 1.3 %fusion.19 = f32[512,512]{1,0:T(8,128)S(1)} fusion(bf16[1,512,2048]{2,1,0:T(8,128)(2,1)S(1)} %copy-done.1, f32[]{:T(128)S(6)} %add.88), kind=kOutput, calls=%fused_computation.26 | convolution fusion | flops 1076887552 | bytes 3145732 | tf_op jit(solution)/shard_map/kij,klj->kil/dot_general | solution.py:33
  67.5 3.1 %fusion.5 = bf16[1,512,2048]{2,1,0:T(8,128)(2,1)} fusion(f32[512,512]{1,0:T(8,128)S(1)} %fusion.19, f32[]{:T(128)S(6)} %add.88, bf16[1,512,2048]{2,1,0:T(8,128)(2,1)S(1)} %copy-done.1), kind=kOutput, calls=%fused_computation.11 | convolution fusion | flops 1353973760 | bytes 5242884 | tf_op jit(solution)/shard_map/kij,kjl->kil/dot_general | solution.py:39
  70.5 3.7 %fusion.16 = f32[512,512]{1,0:T(8,128)S(1)} fusion(bf16[1,512,2048]{2,1,0:T(8,128)(2,1)} %fusion.5), kind=kOutput, calls=%fused_computation.23 | convolution fusion | flops 1073741824 | bytes 3145728 | tf_op jit(solution)/shard_map/kij,klj->kil/dot_general | solution.py:33
  74.2 2.9 %fusion.4 = bf16[1,512,2048]{2,1,0:T(8,128)(2,1)} fusion(bf16[1,512,2048]{2,1,0:T(8,128)(2,1)S(1)} %copy-done.8, f32[512,512]{1,0:T(8,128)S(1)} %fusion.16), kind=kOutput, calls=%fused_computation.9 | convolution fusion | flops 1347682304 | bytes 5242880 | tf_op jit(solution)/shard_map/kij,kjl->kil/dot_general | solution.py:39
  77.1 3.6 %fusion.13 = f32[512,512]{1,0:T(8,128)S(1)} fusion(bf16[1,512,2048]{2,1,0:T(8,128)(2,1)} %fusion.4), kind=kOutput, calls=%fused_computation.20 | convolution fusion | flops 1073741824 | bytes 3145728 | tf_op jit(solution)/shard_map/kij,klj->kil/dot_general | solution.py:33
  80.8 2.9 %fusion.3 = bf16[1,512,2048]{2,1,0:T(8,128)(2,1)} fusion(bf16[1,512,2048]{2,1,0:T(8,128)(2,1)S(1)} %copy-done.9, f32[512,512]{1,0:T(8,128)S(1)} %fusion.13), kind=kOutput, calls=%fused_computation.7 | convolution fusion | flops 1347682304 | bytes 5242880 | tf_op jit(solution)/shard_map/kij,kjl->kil/dot_general | solution.py:39
  83.7 3.5 %fusion.10 = f32[512,512]{1,0:T(8,128)S(1)} fusion(bf16[1,512,2048]{2,1,0:T(8,128)(2,1)} %fusion.3), kind=kOutput, calls=%fused_computation.17 | convolution fusion | flops 1073741824 | bytes 3145728 | tf_op jit(solution)/shard_map/kij,klj->kil/dot_general | solution.py:33
  87.3 3.8 %fusion.2 = bf16[1,512,2048]{2,1,0:T(8,128)(2,1)S(1)} fusion(bf16[1,512,2048]{2,1,0:T(8,128)(2,1)} %fusion.3, f32[512,512]{1,0:T(8,128)S(1)} %fusion.10), kind=kOutput, calls=%fused_computation.5 | convolution fusion | flops 1347682304 | bytes 5242880 | tf_op jit(solution)/shard_map/kij,kjl->kil/dot_general | solution.py:39
  91.0 1.3 %fusion.7 = f32[512,512]{1,0:T(8,128)S(1)} fusion(bf16[1,512,2048]{2,1,0:T(8,128)(2,1)S(1)} %fusion.2), kind=kOutput, calls=%fused_computation.14 | convolution fusion | flops 1073741824 | bytes 3145728 | tf_op jit(solution)/shard_map/kij,klj->kil/dot_general | solution.py:33
  92.4 3.5 %convolution_bitcast_fusion = f32[1,512,2048]{2,1,0:T(8,128)} fusion(bf16[1,512,2048]{2,1,0:T(8,128)(2,1)S(1)} %fusion.2, f32[512,512]{1,0:T(8,128)S(1)} %fusion.7), kind=kOutput, calls=%fused_computation.12 | convolution fusion | flops 1343488000 | bytes 7340032 | tf_op jit(solution)/shard_map/kij,kjl->kil/dot_general | solution.py:39
  95.9 1.8 %fusion.32 = bf16[1,64,2048]{2,1,0:T(8,128)(2,1)} fusion(f32[1,512,2048]{2,1,0:T(8,128)} %convolution_bitcast_fusion, s32[]{:T(128)S(6)} %select_n.3, bf16[1,512,2048]{2,1,0:T(8,128)(2,1)S(1)} %fusion.2), kind=kLoop, calls=%fused_computation.48 | loop fusion | flops 524288 | bytes 1048580 | tf_op jit(solution)/shard_map/convert_element_type | solution.py:40
  97.7 4.8 %all-to-all-start.1 = ((bf16[4,1,16,2048]{3,2,1,0:T(8,128)(2,1)}), bf16[4,1,16,2048]{3,2,1,0:T(8,128)(2,1)S(1)}, u32[]{:S(2)}, u32[]{:S(2)}) async-start(bf16[4,1,16,2048]{3,2,1,0:T(8,128)(2,1)} %bitcast.11), calls=%async_computation.1 | async-start | bytes 524288 | tf_op jit(solution)/shard_map/all_to_all | solution.py:103
  103.1 6.0 %all-to-all-done.1 = bf16[4,1,16,2048]{3,2,1,0:T(8,128)(2,1)S(1)} async-done(((bf16[4,1,16,2048]{3,2,1,0:T(8,128)(2,1)}), bf16[4,1,16,2048]{3,2,1,0:T(8,128)(2,1)S(1)}, u32[]{:S(2)}, u32[]{:S(2)}) %all-to-all-start.1) | async-done | bytes 262176 | tf_op jit(solution)/shard_map/all_to_all | solution.py:103
  (37 shorter events, 4.3 us)
Async XLA Ops:
  7.2 13.2 %copy-start = (bf16[512,32]{0,1:T(8,128)(2,1)S(1)}, bf16[512,32]{0,1:T(8,128)(2,1)}, u32[]{:S(2)}) copy-start(bf16[512,32]{0,1:T(8,128)(2,1)} %param.15) | copy-start | bytes 98308
  7.2 13.0 %copy-start.3 = (bf16[512,128]{1,0:T(8,128)(2,1)S(1)}, bf16[512,128]{1,0:T(8,128)(2,1)}, u32[]{:S(2)}) copy-start(bf16[512,128]{1,0:T(8,128)(2,1)} %param.11) | copy-start | bytes 393220
  7.2 13.0 %copy-start.2 = (bf16[512,128]{1,0:T(8,128)(2,1)S(1)}, bf16[512,128]{1,0:T(8,128)(2,1)}, u32[]{:S(2)}) copy-start(bf16[512,128]{1,0:T(8,128)(2,1)} %param.14) | copy-start | bytes 393220
  7.2 13.1 %copy-start.6 = (f32[128]{0:T(128)S(1)}, f32[128]{0:T(128)}, u32[]{:S(2)}) copy-start(f32[128]{0:T(128)} %param.13) | copy-start | bytes 1540
  7.2 13.1 %copy-start.7 = (f32[128]{0:T(128)S(1)}, f32[128]{0:T(128)}, u32[]{:S(2)}) copy-start(f32[128]{0:T(128)} %param.12) | copy-start | bytes 1540
  7.2 54.8 %all-gather.2.cloned.1.call-start = ((), (), s32[]{:S(2)}) async-start(), calls=%async_computation.2 | async-start | bytes 2359296 | tf_op jit(solution)/shard_map/all_gather | solution.py:95
  20.5 1.3 %collective-permute-start = (f32[34,128]{1,0:T(8,128)S(1)}, f32[34,128]{1,0:T(8,128)S(1)}, u32[]{:S(2)}, u32[]{:S(2)}) collective-permute-start(f32[34,128]{1,0:T(8,128)S(1)} %pad_maximum_fusion), channel_id=1, source_target_pairs={{0,1},{1,0},{2,3},{3,2},{4,5},{5,4},{6,7},{7,6},{8,9},{9,8},{10,11... | collective-permute-start | bytes 52232 | tf_op jit(solution)/shard_map/ppermute | solution.py:50
  21.8 3.9 %collective-permute-start.1 = (f32[34,128]{1,0:T(8,128)S(1)}, f32[34,128]{1,0:T(8,128)S(1)}, u32[]{:S(2)}, u32[]{:S(2)}) collective-permute-start(f32[34,128]{1,0:T(8,128)S(1)} %fusion.70), channel_id=1, source_target_pairs={{0,32},{32,0},{64,96},{96,64},{128,160},{160,128},{192,224},{224,1... | collective-permute-start | bytes 52232 | tf_op jit(solution)/shard_map/ppermute | solution.py:50
  25.7 5.0 %collective-permute-start.2 = (f32[34,128]{1,0:T(8,128)S(1)}, f32[34,128]{1,0:T(8,128)S(1)}, u32[]{:S(2)}, u32[]{:S(2)}) collective-permute-start(f32[34,128]{1,0:T(8,128)S(1)} %add.103), channel_id=1, source_target_pairs={{0,64},{32,96},{64,0},{96,32},{128,192},{160,224},{192,128},{224,1... | collective-permute-start | bytes 52232 | tf_op jit(solution)/shard_map/ppermute | solution.py:50
  30.7 8.9 %collective-permute-start.3 = (f32[34,128]{1,0:T(8,128)S(1)}, f32[34,128]{1,0:T(8,128)S(1)}, u32[]{:S(2)}, u32[]{:S(2)}) collective-permute-start(f32[34,128]{1,0:T(8,128)S(1)} %add.104), channel_id=1, source_target_pairs={{0,128},{32,160},{64,192},{96,224},{128,0},{160,32},{192,64},{224,... | collective-permute-start | bytes 52232 | tf_op jit(solution)/shard_map/ppermute | solution.py:50
  39.6 3.8 %collective-permute-start.4 = (f32[34,128]{1,0:T(8,128)S(1)}, f32[34,128]{1,0:T(8,128)S(1)}, u32[]{:S(2)}, u32[]{:S(2)}) collective-permute-start(f32[34,128]{1,0:T(8,128)S(1)} %add.105), channel_id=1, source_target_pairs={{0,8},{8,0},{16,24},{24,16},{1,9},{9,1},{17,25},{25,17},{2,10},{10... | collective-permute-start | bytes 52232 | tf_op jit(solution)/shard_map/ppermute | solution.py:50
  43.4 59.1 %collective-permute-start.5 = (f32[34,128]{1,0:T(8,128)S(1)}, f32[34,128]{1,0:T(8,128)S(1)}, u32[]{:S(2)}, u32[]{:S(2)}) collective-permute-start(f32[34,128]{1,0:T(8,128)S(1)} %add.106), channel_id=1, source_target_pairs={{0,16},{8,24},{16,0},{24,8},{1,17},{9,25},{17,1},{25,9},{2,18},{10... | collective-permute-start | bytes 52232 | tf_op jit(solution)/shard_map/ppermute | solution.py:50
  62.0 4.1 %copy-start.1 = (bf16[1,512,2048]{2,1,0:T(8,128)(2,1)S(1)}, bf16[1,512,2048]{2,1,0:T(8,128)(2,1)}, u32[]{:S(2)}) copy-start(bf16[1,512,2048]{2,1,0:T(8,128)(2,1)} %all-gather.2.cloned.1.call-done) | copy-start | bytes 6291460
  70.5 3.7 %copy-start.8 = (bf16[1,512,2048]{2,1,0:T(8,128)(2,1)S(1)}, bf16[1,512,2048]{2,1,0:T(8,128)(2,1)}, u32[]{:S(2)}) copy-start(bf16[1,512,2048]{2,1,0:T(8,128)(2,1)} %fusion.5) | copy-start | bytes 6291460
  77.1 3.7 %copy-start.9 = (bf16[1,512,2048]{2,1,0:T(8,128)(2,1)S(1)}, bf16[1,512,2048]{2,1,0:T(8,128)(2,1)}, u32[]{:S(2)}) copy-start(bf16[1,512,2048]{2,1,0:T(8,128)(2,1)} %fusion.4) | copy-start | bytes 6291460
  92.3 10.1 %copy-start.4 = (f32[34,128]{1,0:T(8,128)S(1)}, f32[34,128]{1,0:T(8,128)}, u32[]{:S(2)}) copy-start(f32[34,128]{1,0:T(8,128)} %param.17) | copy-start | bytes 52228
  92.3 10.1 %copy-start.5 = (f32[34,128]{1,0:T(8,128)S(1)}, f32[34,128]{1,0:T(8,128)}, u32[]{:S(2)}) copy-start(f32[34,128]{1,0:T(8,128)} %param.16) | copy-start | bytes 52228
  97.7 11.5 %all-to-all-start.1 = ((bf16[4,1,16,2048]{3,2,1,0:T(8,128)(2,1)}), bf16[4,1,16,2048]{3,2,1,0:T(8,128)(2,1)S(1)}, u32[]{:S(2)}, u32[]{:S(2)}) async-start(bf16[4,1,16,2048]{3,2,1,0:T(8,128)(2,1)} %bitcast.11), calls=%async_computation.1 | async-start | bytes 524288 | tf_op jit(solution)/shard_map/all_to_all | solution.py:103
Sparse Core Ops, SparseCore 0:
  20.3 41.6 all-gather.1

commit v4 on v3

--- a/solution.py
+++ b/solution.py
@@ -21,6 +21,32 @@
 ADAM_EPSILON = 1e-08
 
 SHARD = ("outer", "inner")
+
+
+def shift(value, axis, k):
+    size = lax.axis_size(axis)
+    if k % size == 0:
+        return value
+    return lax.ppermute(value, axis, [(i, (i + k) % size) for i in range(size)])
+
+
+def ring_gather(strip, axis):
+    size = lax.axis_size(axis)
+    cols = strip.shape[-1]
+    ahead, behind = [], []
+    from_behind = from_ahead = strip
+    for distance in range(1, size // 2 + 1):
+        if 2 * distance == size:
+            half = cols // 2
+            first = shift(from_behind[..., :half], axis, 1)
+            second = shift(from_ahead[..., half:], axis, -1)
+            ahead.append(jnp.concatenate([first, second], axis=-1))
+            break
+        from_behind = shift(from_behind, axis, 1)
+        from_ahead = shift(from_ahead, axis, -1)
+        ahead.append(from_ahead)
+        behind.append(from_behind)
+    return jnp.concatenate([strip] + ahead + behind[::-1], axis=1)
 
 
 def orthogonalize(blocks):
@@ -88,20 +114,27 @@
     nesterov = (grad_float + MUON_DECAY * next_momentum).astype(jnp.bfloat16)
     count_all, rows_piece, cols_full = nesterov.shape
     inner = lax.axis_size("inner")
-    outer = lax.axis_size("outer")
     slots = -(-count_all // inner)
     padded = jnp.pad(nesterov, ((0, slots * inner - count_all), (0, 0), (0, 0)))
-    strip = lax.all_to_all(padded, "inner", split_axis=0, concat_axis=1, tiled=True)
-    blocks = lax.all_gather(strip, "outer", axis=1, tiled=True)
+    by_owner = padded.reshape(inner, slots, rows_piece, cols_full)
+    here = lax.axis_index("inner")
+    strip = jnp.concatenate(
+        [shift(lax.dynamic_index_in_dim(by_owner, (here + k) % inner, 0, keepdims=False), "inner", k)
+         for k in range(inner)],
+        axis=1,
+    )
+    blocks = ring_gather(strip, "outer")
     next_first, next_second, adam_step = vector_step(
         normed, ln_gain, ln_bias, ln_cotangent, router_cotangent, first_moment, second_moment
     )
     result = orthogonalize(blocks)
-    strip_rows = inner * rows_piece
-    mine = lax.dynamic_slice_in_dim(result, lax.axis_index("outer") * strip_rows, strip_rows, axis=1)
-    outgoing = mine.reshape(slots, inner, rows_piece, cols_full).transpose(1, 0, 2, 3)
-    returned = lax.all_to_all(outgoing, "inner", split_axis=0, concat_axis=0, tiled=True)
-    ordered = returned.reshape(slots * inner, rows_piece, cols_full)
+    back = jnp.stack(
+        [shift(result[:, k * rows_piece:(k + 1) * rows_piece], "inner", -k) for k in range(inner)],
+        axis=0,
+    )
+    twice = jnp.concatenate([back, back], axis=0)
+    ordered = lax.dynamic_slice_in_dim(twice, (inner - here) % inner, inner, axis=0)
+    ordered = ordered.reshape(inner * slots, rows_piece, cols_full)
     update = ordered[:count_all].astype(jnp.float32) * math.sqrt(FF)
     return (next_momentum, update, next_first, next_second, adam_step)
 

time: 117 us -> 114 us (0.974)
  starting transfers between devices: 18.3 us -> 32.7 us
  between operations: 14.9 us -> 1.65 us
  blocking collectives: 10.9 us -> 0 us
  local copies, waits for them, and re-layouts: 0.05 us -> 7.06 us
  matrix products: 29.8 us -> 35.1 us
  waiting for transfers between devices: 34 us -> 29.9 us
  other arithmetic: 8.89 us -> 7 us
    ppermute x0 -> x14, waiting for transfers between devices: none -> 20.8 us  [shift(): return lax.ppermute(value, axis, [(i, (i + k) % size) for i in range(size)])]
    ppermute x0 -> x14, starting transfers between devices: none -> 20.2 us  [shift(): return lax.ppermute(value, axis, [(i, (i + k) % size) for i in range(size)])]
    all_gather x1 -> x0, waiting for transfers between devices: 17.9 us -> none  [on_device(): blocks = lax.all_gather(strip, 'outer', axis=1, tiled=True)]
    all_to_all x1 -> x0, blocking collectives: 10.9 us -> none  [on_device(): lax.all_to_all(padded, 'inner', split_axis=0, concat_axis=1, tiled=True)]
    unnamed x20 -> x40, local copies, waits for them, and re-layouts: 0.05 us -> 6.26 us
    all_to_all x1 -> x0, waiting for transfers between devices: 6.03 us -> none  [on_device(): lax.all_to_all(outgoing, 'inner', split_axis=0, concat_axis=0, tiled=True)]
    all_to_all x1 -> x0, starting transfers between devices: 4.79 us -> none  [on_device(): lax.all_to_all(outgoing, 'inner', split_axis=0, concat_axis=0, tiled=True)]
    dot_general x5, matrix products: 13.4 us -> 18.1 us  [orthogonalize(): jnp.einsum('kij,klj->kil', iterate, iterate, preferred_element_type=jnp.f...]
  transfers between devices with their start and end apart: 8 -> 20, of which waited for: 7 -> 10; matrix products, arithmetic and copies ran while one was open for 31% -> 7% of each run, Pallas kernels for 0% -> 0%
where the time goes in v4:
time: 114 us; the launch traced here: 113 us
  matrix products  35.1 us (31%)
  starting transfers between devices  32.7 us (29%)
  waiting for transfers between devices  29.9 us (26%)
  local copies, waits for them, and re-layouts  7.06 us (6%)
  other arithmetic  7 us (6%)
  between operations  1.65 us (1%)
    ppermute x14, waiting for transfers between devices, shift(): return lax.ppermute(value, axis, [(i, (i + k) % size) for i in range(size)])  20.8 us
    ppermute x14, starting transfers between devices, shift(): return lax.ppermute(value, axis, [(i, (i + k) % size) for i in range(size)])  20.2 us
    dot_general x5, matrix products, orthogonalize(): jnp.einsum('kij,klj->kil', iterate, iterate, preferred_element_type=jnp.f...  18.1 us
    dot_general x5, matrix products, orthogonalize(): jnp.einsum('kij,kjl->kil', poly, iterate, preferred_element_type=jnp.floa...  15.9 us
    ppermute x6, starting transfers between devices, butterfly_sum(): partner = lax.ppermute(value, axis, [(i, i ^ step) for i in range(size)])  12.6 us
    ppermute x6, waiting for transfers between devices, butterfly_sum(): partner = lax.ppermute(value, axis, [(i, i ^ step) for i in range(size)])  9.11 us
    unnamed x40, local copies, waits for them, and re-layouts  6.26 us
  transfers between devices with their start and end apart: 20, of which 10 were waited for; matrix products, arithmetic and copies ran while one was open for 7% of the time, Pallas kernels for 0%

profile of v4, /device:TPU:16, one launch (start us, length us, event | category | flops | bytes accessed | tf_op | source)
XLA Modules:
  0.0 113.4 jit_solution(175148847109134642)
XLA Ops:
  2.9 2.0 %fusion.9 = (bf16[4,16,2048]{2,1,0:T(8,128)(2,1)S(1)}, f32[4,16,2048]{2,1,0:T(8,128)}) fusion(bf16[4,16,2048]{2,1,0:T(8,128)(2,1)} %param.9, f32[4,16,2048]{2,1,0:T(8,128)} %param.10), kind=kLoop, calls=%fused_computation.25 | loop fusion | flops 786432 | bytes 1572864 | tf_op jit(solution)/shard_map/convert_element_type | solution.py:114
  8.6 2.7 %collective-permute-start.1 = (bf16[1,16,2048]{2,1,0:T(8,128)(2,1)S(1)}, bf16[1,16,2048]{2,1,0:T(8,128)(2,1)S(1)}, u32[]{:S(2)}, u32[]{:S(2)}) collective-permute-start(bf16[1,16,2048]{2,1,0:T(8,128)(2,1)S(1)} %get-tuple-element.18), channel_id=1, source_target_pairs={{0,16},{8,24},{16,0},{24,8},{1,17},{9,25},{17,1},{25,9},{2,18},{10... | collective-permute-start | bytes 196616 | tf_op jit(solution)/shard_map/ppermute | solution.py:30
  12.7 3.4 %collective-permute-start.16 = (f32[34,128]{1,0:T(8,128)S(1)}, f32[34,128]{1,0:T(8,128)S(1)}, u32[]{:S(2)}, u32[]{:S(2)}) collective-permute-start(f32[34,128]{1,0:T(8,128)S(1)} %add.158), channel_id=1, source_target_pairs={{0,64},{32,96},{64,0},{96,32},{128,192},{160,224},{192,128},{224,1... | collective-permute-start | bytes 52232 | tf_op jit(solution)/shard_map/ppermute | solution.py:76
  17.9 5.9 %collective-permute-start.17 = (f32[34,128]{1,0:T(8,128)S(1)}, f32[34,128]{1,0:T(8,128)S(1)}, u32[]{:S(2)}, u32[]{:S(2)}) collective-permute-start(f32[34,128]{1,0:T(8,128)S(1)} %add.159), channel_id=1, source_target_pairs={{0,128},{32,160},{64,192},{96,224},{128,0},{160,32},{192,64},{224,... | collective-permute-start | bytes 52232 | tf_op jit(solution)/shard_map/ppermute | solution.py:76
  23.9 2.0 %collective-permute-start.6 = (bf16[1,64,2048]{2,1,0:T(8,128)(2,1)S(1)}, bf16[1,64,2048]{2,1,0:T(8,128)(2,1)S(1)}, u32[]{:S(2)}, u32[]{:S(2)}) collective-permute-start(bf16[1,64,2048]{2,1,0:T(8,128)(2,1)S(1)} %pad_maximum_fusion), channel_id=1, source_target_pairs={{0,32},{32,64},{64,96},{96,128},{128,160},{160,192},{192,224},{224... | collective-permute-start | bytes 786440 | tf_op jit(solution)/shard_map/ppermute | solution.py:30
  28.5 3.2 %collective-permute-done.18 = f32[34,128]{1,0:T(8,128)S(1)} collective-permute-done((f32[34,128]{1,0:T(8,128)S(1)}, f32[34,128]{1,0:T(8,128)S(1)}, u32[]{:S(2)}, u32[]{:S(2)}) %collective-permute-start.18) | collective-permute-done | bytes 17440 | tf_op jit(solution)/shard_map/ppermute | solution.py:76
  32.2 4.8 %collective-permute-done.19 = f32[34,128]{1,0:T(8,128)S(1)} collective-permute-done((f32[34,128]{1,0:T(8,128)S(1)}, f32[34,128]{1,0:T(8,128)S(1)}, u32[]{:S(2)}, u32[]{:S(2)}) %collective-permute-start.19) | collective-permute-done | bytes 17440 | tf_op jit(solution)/shard_map/ppermute | solution.py:76
  37.6 2.4 %collective-permute-start.4 = (bf16[1,64,2048]{2,1,0:T(8,128)(2,1)S(1)}, bf16[1,64,2048]{2,1,0:T(8,128)(2,1)S(1)}, u32[]{:S(2)}, u32[]{:S(2)}) collective-permute-start(bf16[1,64,2048]{2,1,0:T(8,128)(2,1)S(1)} %collective-permute-done.3), channel_id=1, source_target_pairs={{0,224},{32,0},{64,32},{96,64},{128,96},{160,128},{192,160},{224,1... | collective-permute-start | bytes 786440 | tf_op jit(solution)/shard_map/ppermute | solution.py:30
  40.8 5.6 %collective-permute-done.4 = bf16[1,64,2048]{2,1,0:T(8,128)(2,1)S(1)} collective-permute-done((bf16[1,64,2048]{2,1,0:T(8,128)(2,1)S(1)}, bf16[1,64,2048]{2,1,0:T(8,128)(2,1)S(1)}, u32[]{:S(2)}, u32[]{:S(2)}) %collective-permute-start.4) | collective-permute-done | bytes 262176 | tf_op jit(solution)/shard_map/ppermute | solution.py:30
  46.5 3.6 %collective-permute-start.5 = (bf16[1,64,2048]{2,1,0:T(8,128)(2,1)S(1)}, bf16[1,64,2048]{2,1,0:T(8,128)(2,1)S(1)}, u32[]{:S(2)}, u32[]{:S(2)}) collective-permute-start(bf16[1,64,2048]{2,1,0:T(8,128)(2,1)S(1)} %collective-permute-done.4), channel_id=1, source_target_pairs={{0,224},{32,0},{64,32},{96,64},{128,96},{160,128},{192,160},{224,1... | collective-permute-start | bytes 786440 | tf_op jit(solution)/shard_map/ppermute | solution.py:30
  51.1 7.5 %collective-permute-done.8 = bf16[1,64,2048]{2,1,0:T(8,128)(2,1)S(1)} collective-permute-done((bf16[1,64,2048]{2,1,0:T(8,128)(2,1)S(1)}, bf16[1,64,2048]{2,1,0:T(8,128)(2,1)S(1)}, u32[]{:S(2)}, u32[]{:S(2)}) %collective-permute-start.8) | collective-permute-done | bytes 262176 | tf_op jit(solution)/shard_map/ppermute | solution.py:30
  58.7 3.5 %collective-permute-start.10 = (bf16[1,64,1024]{2,1,0:T(8,128)(2,1)S(1)}, bf16[1,64,1024]{2,1,0:T(8,128)(2,1)S(1)}, u32[]{:S(2)}, u32[]{:S(2)}) collective-permute-start(bf16[1,64,1024]{2,1,0:T(8,128)(2,1)S(1)} %slice.25), channel_id=1, source_target_pairs={{0,224},{32,0},{64,32},{96,64},{128,96},{160,128},{192,160},{224,1... | collective-permute-start | bytes 393224 | tf_op jit(solution)/shard_map/ppermute | solution.py:30
  70.2 3.7 %fusion.49 = f32[512,512]{1,0:T(8,128)S(1)} fusion(bf16[512,2048]{1,0:T(8,128)(2,1)} %bitcast_dynamic-update-slice_fusion, f32[]{:T(128)S(6)} %add.142), kind=kOutput, calls=%fused_computation.104 | convolution fusion | flops 1076887552 | bytes 3145732 | tf_op jit(solution)/shard_map/kij,klj->kil/dot_general | solution.py:59
  73.9 3.1 %add_convert_fusion.4 = bf16[512,2048]{1,0:T(8,128)(2,1)} fusion(f32[512,512]{1,0:T(8,128)S(1)} %fusion.49, f32[]{:T(128)S(6)} %add.142, bf16[512,2048]{1,0:T(8,128)(2,1)S(1)} %copy-done.3), kind=kOutput, calls=%fused_computation.4 | convolution fusion | flops 1353973760 | bytes 5242884 | tf_op jit(solution)/shard_map/kij,kjl->kil/dot_general | solution.py:65
  77.0 3.6 %fusion.52 = f32[512,512]{1,0:T(8,128)S(1)} fusion(bf16[512,2048]{1,0:T(8,128)(2,1)} %add_convert_fusion.4), kind=kOutput, calls=%fused_computation.106 | convolution fusion | flops 1073741824 | bytes 3145728 | tf_op jit(solution)/shard_map/kij,klj->kil/dot_general | solution.py:59
  80.6 2.9 %add_convert_fusion.3 = bf16[512,2048]{1,0:T(8,128)(2,1)} fusion(bf16[512,2048]{1,0:T(8,128)(2,1)S(1)} %copy-done.4, f32[512,512]{1,0:T(8,128)S(1)} %fusion.52), kind=kOutput, calls=%fused_computation.3 | convolution fusion | flops 1347682304 | bytes 5242880 | tf_op jit(solution)/shard_map/kij,kjl->kil/dot_general | solution.py:65
  83.6 3.6 %fusion.53 = f32[512,512]{1,0:T(8,128)S(1)} fusion(bf16[512,2048]{1,0:T(8,128)(2,1)} %add_convert_fusion.3), kind=kOutput, calls=%fused_computation.107 | convolution fusion | flops 1073741824 | bytes 3145728 | tf_op jit(solution)/shard_map/kij,klj->kil/dot_general | solution.py:59
  87.2 2.9 %add_convert_fusion.2 = bf16[512,2048]{1,0:T(8,128)(2,1)} fusion(bf16[512,2048]{1,0:T(8,128)(2,1)S(1)} %copy-done.5, f32[512,512]{1,0:T(8,128)S(1)} %fusion.53), kind=kOutput, calls=%fused_computation.2 | convolution fusion | flops 1347682304 | bytes 5242880 | tf_op jit(solution)/shard_map/kij,kjl->kil/dot_general | solution.py:65
  90.2 3.6 %fusion.54 = f32[512,512]{1,0:T(8,128)S(1)} fusion(bf16[512,2048]{1,0:T(8,128)(2,1)} %add_convert_fusion.2), kind=kOutput, calls=%fused_computation.108 | convolution fusion | flops 1073741824 | bytes 3145728 | tf_op jit(solution)/shard_map/kij,klj->kil/dot_general | solution.py:59
  93.8 2.9 %add_convert_fusion.1 = bf16[512,2048]{1,0:T(8,128)(2,1)} fusion(bf16[512,2048]{1,0:T(8,128)(2,1)S(1)} %copy-done.6, f32[512,512]{1,0:T(8,128)S(1)} %fusion.54), kind=kOutput, calls=%fused_computation.1 | convolution fusion | flops 1347682304 | bytes 5242880 | tf_op jit(solution)/shard_map/kij,kjl->kil/dot_general | solution.py:65
  96.8 3.5 %fusion.55 = f32[512,512]{1,0:T(8,128)S(1)} fusion(bf16[512,2048]{1,0:T(8,128)(2,1)} %add_convert_fusion.1), kind=kOutput, calls=%fused_computation.109 | convolution fusion | flops 1073741824 | bytes 3145728 | tf_op jit(solution)/shard_map/kij,klj->kil/dot_general | solution.py:59
  100.3 4.0 %fusion = bf16[1,512,2048]{2,1,0:T(8,128)(2,1)S(1)} fusion(bf16[512,2048]{1,0:T(8,128)(2,1)} %add_convert_fusion.1, f32[512,512]{1,0:T(8,128)S(1)} %fusion.55), kind=kOutput, calls=%fused_computation.7 | convolution fusion | flops 1347682304 | bytes 5242880 | tf_op jit(solution)/shard_map/kij,kjl->kil/dot_general | solution.py:65
  104.4 2.6 %collective-permute-start.12 = (bf16[1,16,2048]{2,1,0:T(8,128)(2,1)S(1)}, bf16[1,16,2048]{2,1,0:T(8,128)(2,1)S(1)}, u32[]{:S(2)}, u32[]{:S(2)}) collective-permute-start(bf16[1,16,2048]{2,1,0:T(8,128)(2,1)S(1)} %get-tuple-element.15), channel_id=1, source_target_pairs={{0,16},{8,24},{16,0},{24,8},{1,17},{9,25},{17,1},{25,9},{2,18},{10... | collective-permute-start | bytes 196616 | tf_op jit(solution)/shard_map/ppermute | solution.py:30
  110.3 2.3 %collective-permute-done.13 = bf16[1,16,2048]{2,1,0:T(8,128)(2,1)S(1)} collective-permute-done((bf16[1,16,2048]{2,1,0:T(8,128)(2,1)S(1)}, bf16[1,16,2048]{2,1,0:T(8,128)(2,1)S(1)}, u32[]{:S(2)}, u32[]{:S(2)}) %collective-permute-start.13) | collective-permute-done | bytes 65568 | tf_op jit(solution)/shard_map/ppermute | solution.py:30
  (87 shorter events, 26.2 us)
Async XLA Ops:
  2.8 34.2 %copy-start.1 = (f32[34,128]{1,0:T(8,128)S(1)}, f32[34,128]{1,0:T(8,128)}, u32[]{:S(2)}) copy-start(f32[34,128]{1,0:T(8,128)} %param.17) | copy-start | bytes 52228
  2.8 34.2 %copy-start.2 = (f32[34,128]{1,0:T(8,128)S(1)}, f32[34,128]{1,0:T(8,128)}, u32[]{:S(2)}) copy-start(f32[34,128]{1,0:T(8,128)} %param.16) | copy-start | bytes 52228
  2.8 2.1 %collective-permute-start.14 = (f32[34,128]{1,0:T(8,128)S(1)}, f32[34,128]{1,0:T(8,128)S(1)}, u32[]{:S(2)}, u32[]{:S(2)}) collective-permute-start(f32[34,128]{1,0:T(8,128)S(1)} %pad_maximum_fusion.1), channel_id=1, source_target_pairs={{0,1},{1,0},{2,3},{3,2},{4,5},{5,4},{6,7},{7,6},{8,9},{9,8},{10,11... | collective-permute-start | bytes 52232 | tf_op jit(solution)/shard_map/ppermute | solution.py:76
  5.0 7.8 %collective-permute-start.15 = (f32[34,128]{1,0:T(8,128)S(1)}, f32[34,128]{1,0:T(8,128)S(1)}, u32[]{:S(2)}, u32[]{:S(2)}) collective-permute-start(f32[34,128]{1,0:T(8,128)S(1)} %fusion.48), channel_id=1, source_target_pairs={{0,32},{32,0},{64,96},{96,64},{128,160},{160,128},{192,224},{224,1... | collective-permute-start | bytes 52232 | tf_op jit(solution)/shard_map/ppermute | solution.py:76
  7.0 16.8 %collective-permute-start = (bf16[1,16,2048]{2,1,0:T(8,128)(2,1)S(1)}, bf16[1,16,2048]{2,1,0:T(8,128)(2,1)S(1)}, u32[]{:S(2)}, u32[]{:S(2)}) collective-permute-start(bf16[1,16,2048]{2,1,0:T(8,128)(2,1)S(1)} %get-tuple-element.19), channel_id=1, source_target_pairs={{0,8},{8,16},{16,24},{24,0},{1,9},{9,17},{17,25},{25,1},{2,10},{10... | collective-permute-start | bytes 196616 | tf_op jit(solution)/shard_map/ppermute | solution.py:30
  8.6 15.2 %collective-permute-start.1 = (bf16[1,16,2048]{2,1,0:T(8,128)(2,1)S(1)}, bf16[1,16,2048]{2,1,0:T(8,128)(2,1)S(1)}, u32[]{:S(2)}, u32[]{:S(2)}) collective-permute-start(bf16[1,16,2048]{2,1,0:T(8,128)(2,1)S(1)} %get-tuple-element.18), channel_id=1, source_target_pairs={{0,16},{8,24},{16,0},{24,8},{1,17},{9,25},{17,1},{25,9},{2,18},{10... | collective-permute-start | bytes 196616 | tf_op jit(solution)/shard_map/ppermute | solution.py:30
  11.3 12.5 %collective-permute-start.2 = (bf16[1,16,2048]{2,1,0:T(8,128)(2,1)S(1)}, bf16[1,16,2048]{2,1,0:T(8,128)(2,1)S(1)}, u32[]{:S(2)}, u32[]{:S(2)}) collective-permute-start(bf16[1,16,2048]{2,1,0:T(8,128)(2,1)S(1)} %get-tuple-element.17), channel_id=1, source_target_pairs={{0,24},{8,0},{16,8},{24,16},{1,25},{9,1},{17,9},{25,17},{2,26},{10... | collective-permute-start | bytes 196616 | tf_op jit(solution)/shard_map/ppermute | solution.py:30
  12.7 5.1 %collective-permute-start.16 = (f32[34,128]{1,0:T(8,128)S(1)}, f32[34,128]{1,0:T(8,128)S(1)}, u32[]{:S(2)}, u32[]{:S(2)}) collective-permute-start(f32[34,128]{1,0:T(8,128)S(1)} %add.158), channel_id=1, source_target_pairs={{0,64},{32,96},{64,0},{96,32},{128,192},{160,224},{192,128},{224,1... | collective-permute-start | bytes 52232 | tf_op jit(solution)/shard_map/ppermute | solution.py:76
  17.9 10.0 %collective-permute-start.17 = (f32[34,128]{1,0:T(8,128)S(1)}, f32[34,128]{1,0:T(8,128)S(1)}, u32[]{:S(2)}, u32[]{:S(2)}) collective-permute-start(f32[34,128]{1,0:T(8,128)S(1)} %add.159), channel_id=1, source_target_pairs={{0,128},{32,160},{64,192},{96,224},{128,0},{160,32},{192,64},{224,... | collective-permute-start | bytes 52232 | tf_op jit(solution)/shard_map/ppermute | solution.py:76
  23.8 13.8 %collective-permute-start.3 = (bf16[1,64,2048]{2,1,0:T(8,128)(2,1)S(1)}, bf16[1,64,2048]{2,1,0:T(8,128)(2,1)S(1)}, u32[]{:S(2)}, u32[]{:S(2)}) collective-permute-start(bf16[1,64,2048]{2,1,0:T(8,128)(2,1)S(1)} %pad_maximum_fusion), channel_id=1, source_target_pairs={{0,224},{32,0},{64,32},{96,64},{128,96},{160,128},{192,160},{224,1... | collective-permute-start | bytes 786440 | tf_op jit(solution)/shard_map/ppermute | solution.py:30
  23.9 16.2 %collective-permute-start.6 = (bf16[1,64,2048]{2,1,0:T(8,128)(2,1)S(1)}, bf16[1,64,2048]{2,1,0:T(8,128)(2,1)S(1)}, u32[]{:S(2)}, u32[]{:S(2)}) collective-permute-start(bf16[1,64,2048]{2,1,0:T(8,128)(2,1)S(1)} %pad_maximum_fusion), channel_id=1, source_target_pairs={{0,32},{32,64},{64,96},{96,128},{128,160},{160,192},{192,224},{224... | collective-permute-start | bytes 786440 | tf_op jit(solution)/shard_map/ppermute | solution.py:30
  27.8 3.9 %collective-permute-start.18 = (f32[34,128]{1,0:T(8,128)S(1)}, f32[34,128]{1,0:T(8,128)S(1)}, u32[]{:S(2)}, u32[]{:S(2)}) collective-permute-start(f32[34,128]{1,0:T(8,128)S(1)} %add.160), channel_id=1, source_target_pairs={{0,8},{8,0},{16,24},{24,16},{1,9},{9,1},{17,25},{25,17},{2,10},{10... | collective-permute-start | bytes 52232 | tf_op jit(solution)/shard_map/ppermute | solution.py:76
  31.7 5.3 %collective-permute-start.19 = (f32[34,128]{1,0:T(8,128)S(1)}, f32[34,128]{1,0:T(8,128)S(1)}, u32[]{:S(2)}, u32[]{:S(2)}) collective-permute-start(f32[34,128]{1,0:T(8,128)S(1)} %add.161), channel_id=1, source_target_pairs={{0,16},{8,24},{16,0},{24,8},{1,17},{9,25},{17,1},{25,9},{2,18},{10... | collective-permute-start | bytes 52232 | tf_op jit(solution)/shard_map/ppermute | solution.py:76
  37.6 8.8 %collective-permute-start.4 = (bf16[1,64,2048]{2,1,0:T(8,128)(2,1)S(1)}, bf16[1,64,2048]{2,1,0:T(8,128)(2,1)S(1)}, u32[]{:S(2)}, u32[]{:S(2)}) collective-permute-start(bf16[1,64,2048]{2,1,0:T(8,128)(2,1)S(1)} %collective-permute-done.3), channel_id=1, source_target_pairs={{0,224},{32,0},{64,32},{96,64},{128,96},{160,128},{192,160},{224,1... | collective-permute-start | bytes 786440 | tf_op jit(solution)/shard_map/ppermute | solution.py:30
  40.1 10.3 %collective-permute-start.7 = (bf16[1,64,2048]{2,1,0:T(8,128)(2,1)S(1)}, bf16[1,64,2048]{2,1,0:T(8,128)(2,1)S(1)}, u32[]{:S(2)}, u32[]{:S(2)}) collective-permute-start(bf16[1,64,2048]{2,1,0:T(8,128)(2,1)S(1)} %collective-permute-done.6), channel_id=1, source_target_pairs={{0,32},{32,64},{64,96},{96,128},{128,160},{160,192},{192,224},{224... | collective-permute-start | bytes 786440 | tf_op jit(solution)/shard_map/ppermute | solution.py:30
  46.5 12.2 %collective-permute-start.5 = (bf16[1,64,2048]{2,1,0:T(8,128)(2,1)S(1)}, bf16[1,64,2048]{2,1,0:T(8,128)(2,1)S(1)}, u32[]{:S(2)}, u32[]{:S(2)}) collective-permute-start(bf16[1,64,2048]{2,1,0:T(8,128)(2,1)S(1)} %collective-permute-done.4), channel_id=1, source_target_pairs={{0,224},{32,0},{64,32},{96,64},{128,96},{160,128},{192,160},{224,1... | collective-permute-start | bytes 786440 | tf_op jit(solution)/shard_map/ppermute | solution.py:30
  50.4 8.2 %collective-permute-start.8 = (bf16[1,64,2048]{2,1,0:T(8,128)(2,1)S(1)}, bf16[1,64,2048]{2,1,0:T(8,128)(2,1)S(1)}, u32[]{:S(2)}, u32[]{:S(2)}) collective-permute-start(bf16[1,64,2048]{2,1,0:T(8,128)(2,1)S(1)} %collective-permute-done.7), channel_id=1, source_target_pairs={{0,32},{32,64},{64,96},{96,128},{128,160},{160,192},{192,224},{224... | collective-permute-start | bytes 786440 | tf_op jit(solution)/shard_map/ppermute | solution.py:30
  58.6 6.3 %collective-permute-start.9 = (bf16[1,64,1024]{2,1,0:T(8,128)(2,1)S(1)}, bf16[1,64,1024]{2,1,0:T(8,128)(2,1)S(1)}, u32[]{:S(2)}, u32[]{:S(2)}) collective-permute-start(bf16[1,64,1024]{2,1,0:T(8,128)(2,1)S(1)} %slice.24), channel_id=1, source_target_pairs={{0,32},{32,64},{64,96},{96,128},{128,160},{160,192},{192,224},{224... | collective-permute-start | bytes 393224 | tf_op jit(solution)/shard_map/ppermute | solution.py:30
  58.7 6.2 %collective-permute-start.10 = (bf16[1,64,1024]{2,1,0:T(8,128)(2,1)S(1)}, bf16[1,64,1024]{2,1,0:T(8,128)(2,1)S(1)}, u32[]{:S(2)}, u32[]{:S(2)}) collective-permute-start(bf16[1,64,1024]{2,1,0:T(8,128)(2,1)S(1)} %slice.25), channel_id=1, source_target_pairs={{0,224},{32,0},{64,32},{96,64},{128,96},{160,128},{192,160},{224,1... | collective-permute-start | bytes 393224 | tf_op jit(solution)/shard_map/ppermute | solution.py:30
  70.2 3.7 %copy-start.3 = (bf16[512,2048]{1,0:T(8,128)(2,1)S(1)}, bf16[512,2048]{1,0:T(8,128)(2,1)}, u32[]{:S(2)}) copy-start(bf16[512,2048]{1,0:T(8,128)(2,1)} %bitcast_dynamic-update-slice_fusion) | copy-start | bytes 6291460
  83.6 3.7 %copy-start.5 = (bf16[512,2048]{1,0:T(8,128)(2,1)S(1)}, bf16[512,2048]{1,0:T(8,128)(2,1)}, u32[]{:S(2)}) copy-start(bf16[512,2048]{1,0:T(8,128)(2,1)} %add_convert_fusion.3) | copy-start | bytes 6291460
  104.3 4.3 %collective-permute-start.11 = (bf16[1,16,2048]{2,1,0:T(8,128)(2,1)S(1)}, bf16[1,16,2048]{2,1,0:T(8,128)(2,1)S(1)}, u32[]{:S(2)}, u32[]{:S(2)}) collective-permute-start(bf16[1,16,2048]{2,1,0:T(8,128)(2,1)S(1)} %get-tuple-element.16), channel_id=1, source_target_pairs={{0,24},{8,0},{16,8},{24,16},{1,25},{9,1},{17,9},{25,17},{2,26},{10... | collective-permute-start | bytes 196616 | tf_op jit(solution)/shard_map/ppermute | solution.py:30
  104.4 5.9 %collective-permute-start.12 = (bf16[1,16,2048]{2,1,0:T(8,128)(2,1)S(1)}, bf16[1,16,2048]{2,1,0:T(8,128)(2,1)S(1)}, u32[]{:S(2)}, u32[]{:S(2)}) collective-permute-start(bf16[1,16,2048]{2,1,0:T(8,128)(2,1)S(1)} %get-tuple-element.15), channel_id=1, source_target_pairs={{0,16},{8,24},{16,0},{24,8},{1,17},{9,25},{17,1},{25,9},{2,18},{10... | collective-permute-start | bytes 196616 | tf_op jit(solution)/shard_map/ppermute | solution.py:30
  107.1 5.5 %collective-permute-start.13 = (bf16[1,16,2048]{2,1,0:T(8,128)(2,1)S(1)}, bf16[1,16,2048]{2,1,0:T(8,128)(2,1)S(1)}, u32[]{:S(2)}, u32[]{:S(2)}) collective-permute-start(bf16[1,16,2048]{2,1,0:T(8,128)(2,1)S(1)} %get-tuple-element.14), channel_id=1, source_target_pairs={{0,8},{8,16},{16,24},{24,0},{1,9},{9,17},{17,25},{25,1},{2,10},{10... | collective-permute-start | bytes 196616 | tf_op jit(solution)/shard_map/ppermute | solution.py:30
  (3 other events, 8.4 us)

commit v5 on v4

--- a/solution.py
+++ b/solution.py
@@ -49,13 +49,16 @@
     return jnp.concatenate([strip] + ahead + behind[::-1], axis=1)
 
 
-def orthogonalize(blocks):
+def orthogonalize(blocks, carried, rounds):
     squares = jnp.sum(jnp.square(blocks.astype(jnp.float32)), axis=(1, 2))
     total = jnp.sqrt(squares)
     iterate = (blocks.astype(jnp.float32) / (total + NORM_EPSILON)[:, None, None]).astype(
         jnp.bfloat16
     )
     for repeat in range(ITERS):
+        carried, iterate = lax.optimization_barrier((carried, iterate))
+        for step in rounds[repeat] if repeat < len(rounds) else ():
+            carried = step(carried)
         gram = jnp.einsum("kij,klj->kil", iterate, iterate, preferred_element_type=jnp.float32)
         gram_half = gram.astype(jnp.bfloat16)
         square_term = jnp.einsum(
@@ -64,22 +67,26 @@
         poly = (CUBIC_TERM * gram + QUINTIC_TERM * square_term).astype(jnp.bfloat16)
         product = jnp.einsum("kij,kjl->kil", poly, iterate, preferred_element_type=jnp.float32)
         iterate = (LINEAR_TERM * iterate.astype(jnp.float32) + product).astype(jnp.bfloat16)
-    return iterate
+    for group in rounds[ITERS:]:
+        for step in group:
+            carried = step(carried)
+    return iterate, carried
 
 
-def butterfly_sum(value, axis):
+def butterfly_rounds(axis):
     size = lax.axis_size(axis)
     if size & (size - 1):
-        return jnp.sum(lax.all_gather(value, axis, axis=0, tiled=False), axis=0)
-    step = 1
-    while step < size:
-        partner = lax.ppermute(value, axis, [(i, i ^ step) for i in range(size)])
-        value = value + partner
-        step *= 2
-    return value
+        return [lambda value: jnp.sum(lax.all_gather(value, axis, axis=0, tiled=False), axis=0)]
+    steps = []
+    distance = 1
+    while distance < size:
+        perm = [(i, i ^ distance) for i in range(size)]
+        steps.append(lambda value, perm=perm: value + lax.ppermute(value, axis, perm))
+        distance *= 2
+    return steps
 
 
-def vector_step(normed, ln_gain, ln_bias, ln_cotangent, router_cotangent, first_moment, second_moment):
+def vector_partials(normed, ln_gain, ln_bias, ln_cotangent, router_cotangent):
     normed_float = normed.astype(jnp.float32)
     cot_float = ln_cotangent.astype(jnp.float32)
     ln_out = (ln_gain[None, :] * normed_float + ln_bias[None, :]).astype(jnp.bfloat16)
@@ -88,10 +95,10 @@
     router_local = lax.dot_general(
         router_cotangent, ln_out, (((0,), (0,)), ((), ())), preferred_element_type=jnp.float32
     )
-    local = jnp.concatenate([gain_local[None, :], bias_local[None, :], router_local], axis=0)
-    vec_grad = local
-    for axis in ("section",) + SHARD:
-        vec_grad = butterfly_sum(vec_grad, axis)
+    return jnp.concatenate([gain_local[None, :], bias_local[None, :], router_local], axis=0)
+
+
+def adam(vec_grad, first_moment, second_moment):
     next_first = ADAM_FIRST * first_moment + (1.0 - ADAM_FIRST) * vec_grad
     next_second = ADAM_SECOND * second_moment + (1.0 - ADAM_SECOND) * vec_grad * vec_grad
     adam_step = next_first / (jnp.sqrt(next_second) + ADAM_EPSILON)
@@ -124,10 +131,11 @@
         axis=1,
     )
     blocks = ring_gather(strip, "outer")
-    next_first, next_second, adam_step = vector_step(
-        normed, ln_gain, ln_bias, ln_cotangent, router_cotangent, first_moment, second_moment
-    )
-    result = orthogonalize(blocks)
+    local = vector_partials(normed, ln_gain, ln_bias, ln_cotangent, router_cotangent)
+    steps = [step for axis in ("section",) + SHARD for step in butterfly_rounds(axis)]
+    rounds = [steps[:2]] + [[step] for step in steps[2:]]
+    result, vec_grad = orthogonalize(blocks, local, rounds)
+    next_first, next_second, adam_step = adam(vec_grad, first_moment, second_moment)
     back = jnp.stack(
         [shift(result[:, k * rows_piece:(k + 1) * rows_piece], "inner", -k) for k in range(inner)],
         axis=0,

time: 114 us -> 97.4 us (0.85)
  local copies, waits for them, and re-layouts: 7.06 us -> 0.29 us
  matrix products: 35.1 us -> 29.6 us
  waiting for transfers between devices: 29.9 us -> 26.6 us
  other arithmetic: 7 us -> 5.81 us
    ppermute x6, waiting for transfers between devices: 9.11 us -> 0.8 us  [butterfly_rounds(): lax.ppermute(value, axis, perm)]
    unnamed x40 -> x35, local copies, waits for them, and re-layouts: 6.26 us -> 0.21 us
    dot_general x5, matrix products: 18.1 us -> 13.1 us  [orthogonalize(): jnp.einsum('kij,klj->kil', iterate, iterate, preferred_element_type=jnp.f...]
    ppermute x14, waiting for transfers between devices: 20.8 us -> 25.8 us  [shift(): return lax.ppermute(value, axis, [(i, (i + k) % size) for i in range(size)])]
    ppermute x14, starting transfers between devices: 20.2 us -> 25 us  [shift(): return lax.ppermute(value, axis, [(i, (i + k) % size) for i in range(size)])]
    ppermute x6, starting transfers between devices: 12.6 us -> 8.19 us  [butterfly_rounds(): lax.ppermute(value, axis, perm)]
  transfers between devices with their start and end apart: 20 -> 20, of which waited for: 10 -> 14; matrix products, arithmetic and copies ran while one was open for 7% -> 24% of each run, Pallas kernels for 0% -> 0%
where the time goes in v5:
time: 97.4 us; the launch traced here: 97.2 us
  starting transfers between devices  33.2 us (34%)
  matrix products  29.6 us (30%)
  waiting for transfers between devices  26.6 us (27%)
  other arithmetic  5.81 us (6%)
  between operations  1.76 us (2%)
    ppermute x14, waiting for transfers between devices, shift(): return lax.ppermute(value, axis, [(i, (i + k) % size) for i in range(size)])  25.8 us
    ppermute x14, starting transfers between devices, shift(): return lax.ppermute(value, axis, [(i, (i + k) % size) for i in range(size)])  25 us
    dot_general x5, matrix products, orthogonalize(): jnp.einsum('kij,kjl->kil', poly, iterate, preferred_element_type=jnp.floa...  16.4 us
    dot_general x5, matrix products, orthogonalize(): jnp.einsum('kij,klj->kil', iterate, iterate, preferred_element_type=jnp.f...  13.1 us
    ppermute x6, starting transfers between devices, butterfly_rounds(): lax.ppermute(value, axis, perm)  8.19 us
    convert_element_type x1, other arithmetic, on_device(): nesterov = (grad_float + MUON_DECAY * next_momentum).astype(jnp.bfloat16)  2.08 us
  transfers between devices with their start and end apart: 20, of which 14 were waited for; matrix products, arithmetic and copies ran while one was open for 24% of the time, Pallas kernels for 0%

profile of v5, /device:TPU:16, one launch (start us, length us, event | category | flops | bytes accessed | tf_op | source)
XLA Modules:
  0.0 97.2 jit_solution(8300059658688715680)
XLA Ops:
  0.7 2.1 %fusion.32 = (bf16[4,16,2048]{2,1,0:T(8,128)(2,1)S(1)}, f32[4,16,2048]{2,1,0:T(8,128)}) fusion(bf16[4,16,2048]{2,1,0:T(8,128)(2,1)} %param.9, f32[4,16,2048]{2,1,0:T(8,128)} %param.10), kind=kLoop, calls=%fused_computation.47 | loop fusion | flops 786432 | bytes 1572864 | tf_op jit(solution)/shard_map/convert_element_type | solution.py:121
  2.9 1.6 %collective-permute-start = (bf16[1,16,2048]{2,1,0:T(8,128)(2,1)S(1)}, bf16[1,16,2048]{2,1,0:T(8,128)(2,1)S(1)}, u32[]{:S(2)}, u32[]{:S(2)}) collective-permute-start(bf16[1,16,2048]{2,1,0:T(8,128)(2,1)S(1)} %get-tuple-element.39), channel_id=1, source_target_pairs={{0,8},{8,16},{16,24},{24,0},{1,9},{9,17},{17,25},{25,1},{2,10},{10... | collective-permute-start | bytes 196616 | tf_op jit(solution)/shard_map/ppermute | solution.py:30
  4.4 2.7 %collective-permute-start.1 = (bf16[1,16,2048]{2,1,0:T(8,128)(2,1)S(1)}, bf16[1,16,2048]{2,1,0:T(8,128)(2,1)S(1)}, u32[]{:S(2)}, u32[]{:S(2)}) collective-permute-start(bf16[1,16,2048]{2,1,0:T(8,128)(2,1)S(1)} %get-tuple-element.38), channel_id=1, source_target_pairs={{0,16},{8,24},{16,0},{24,8},{1,17},{9,25},{17,1},{25,9},{2,18},{10... | collective-permute-start | bytes 196616 | tf_op jit(solution)/shard_map/ppermute | solution.py:30
  11.4 5.9 %collective-permute-start.3 = (bf16[1,64,2048]{2,1,0:T(8,128)(2,1)S(1)}, bf16[1,64,2048]{2,1,0:T(8,128)(2,1)S(1)}, u32[]{:S(2)}, u32[]{:S(2)}) collective-permute-start(bf16[1,64,2048]{2,1,0:T(8,128)(2,1)S(1)} %pad_maximum_fusion), channel_id=1, source_target_pairs={{0,224},{32,0},{64,32},{96,64},{128,96},{160,128},{192,160},{224,1... | collective-permute-start | bytes 786440 | tf_op jit(solution)/shard_map/ppermute | solution.py:30
  17.4 4.3 %collective-permute-done.3 = bf16[1,64,2048]{2,1,0:T(8,128)(2,1)S(1)} collective-permute-done((bf16[1,64,2048]{2,1,0:T(8,128)(2,1)S(1)}, bf16[1,64,2048]{2,1,0:T(8,128)(2,1)S(1)}, u32[]{:S(2)}, u32[]{:S(2)}) %collective-permute-start.3) | collective-permute-done | bytes 262176 | tf_op jit(solution)/shard_map/ppermute | solution.py:30
  21.8 3.7 %collective-permute-start.4 = (bf16[1,64,2048]{2,1,0:T(8,128)(2,1)S(1)}, bf16[1,64,2048]{2,1,0:T(8,128)(2,1)S(1)}, u32[]{:S(2)}, u32[]{:S(2)}) collective-permute-start(bf16[1,64,2048]{2,1,0:T(8,128)(2,1)S(1)} %collective-permute-done.3), channel_id=1, source_target_pairs={{0,224},{32,0},{64,32},{96,64},{128,96},{160,128},{192,160},{224,1... | collective-permute-start | bytes 786440 | tf_op jit(solution)/shard_map/ppermute | solution.py:30
  25.5 3.9 %collective-permute-done.4 = bf16[1,64,2048]{2,1,0:T(8,128)(2,1)S(1)} collective-permute-done((bf16[1,64,2048]{2,1,0:T(8,128)(2,1)S(1)}, bf16[1,64,2048]{2,1,0:T(8,128)(2,1)S(1)}, u32[]{:S(2)}, u32[]{:S(2)}) %collective-permute-start.4) | collective-permute-done | bytes 262176 | tf_op jit(solution)/shard_map/ppermute | solution.py:30
  29.3 3.7 %collective-permute-start.5 = (bf16[1,64,2048]{2,1,0:T(8,128)(2,1)S(1)}, bf16[1,64,2048]{2,1,0:T(8,128)(2,1)S(1)}, u32[]{:S(2)}, u32[]{:S(2)}) collective-permute-start(bf16[1,64,2048]{2,1,0:T(8,128)(2,1)S(1)} %collective-permute-done.4), channel_id=1, source_target_pairs={{0,224},{32,0},{64,32},{96,64},{128,96},{160,128},{192,160},{224,1... | collective-permute-start | bytes 786440 | tf_op jit(solution)/shard_map/ppermute | solution.py:30
  33.1 4.4 %collective-permute-done.5 = bf16[1,64,2048]{2,1,0:T(8,128)(2,1)S(1)} collective-permute-done((bf16[1,64,2048]{2,1,0:T(8,128)(2,1)S(1)}, bf16[1,64,2048]{2,1,0:T(8,128)(2,1)S(1)}, u32[]{:S(2)}, u32[]{:S(2)}) %collective-permute-start.5) | collective-permute-done | bytes 262176 | tf_op jit(solution)/shard_map/ppermute | solution.py:30
  37.5 3.8 %collective-permute-start.10 = (bf16[1,64,1024]{2,1,0:T(8,128)(2,1)S(1)}, bf16[1,64,1024]{2,1,0:T(8,128)(2,1)S(1)}, u32[]{:S(2)}, u32[]{:S(2)}) collective-permute-start(bf16[1,64,1024]{2,1,0:T(8,128)(2,1)S(1)} %slice.25), channel_id=1, source_target_pairs={{0,224},{32,0},{64,32},{96,64},{128,96},{160,128},{192,160},{224,1... | collective-permute-start | bytes 393224 | tf_op jit(solution)/shard_map/ppermute | solution.py:30
  41.5 2.3 %collective-permute-done.10 = bf16[1,64,1024]{2,1,0:T(8,128)(2,1)S(1)} collective-permute-done((bf16[1,64,1024]{2,1,0:T(8,128)(2,1)S(1)}, bf16[1,64,1024]{2,1,0:T(8,128)(2,1)S(1)}, u32[]{:S(2)}, u32[]{:S(2)}) %collective-permute-start.10) | collective-permute-done | bytes 131104 | tf_op jit(solution)/shard_map/ppermute | solution.py:30
  43.8 3.8 %collective-permute-done.9 = bf16[1,64,1024]{2,1,0:T(8,128)(2,1)S(1)} collective-permute-done((bf16[1,64,1024]{2,1,0:T(8,128)(2,1)S(1)}, bf16[1,64,1024]{2,1,0:T(8,128)(2,1)S(1)}, u32[]{:S(2)}, u32[]{:S(2)}) %collective-permute-start.9) | collective-permute-done | bytes 131104 | tf_op jit(solution)/shard_map/ppermute | solution.py:30
  47.8 1.7 %fusion = f32[]{:T(128)} fusion(bf16[1,512,2048]{2,1,0:T(8,128)(2,1)S(1)} %constant_dynamic-update-slice_fusion), kind=kLoop, calls=%fused_computation.2 | loop fusion | flops 3145727 | bytes 2097156 | tf_op jit(solution)/shard_map/reduce_sum | solution.py:53
  52.3 3.8 %fusion.6 = bf16[1,512,2048]{2,1,0:T(8,128)(2,1)S(1)} fusion(bf16[1,512,2048]{2,1,0:T(8,128)(2,1)} %copy-done.1, f32[512,512]{1,0:T(8,128)S(1)} %fusion.20), kind=kOutput, calls=%fused_computation.13 | convolution fusion | flops 1347682304 | bytes 5242880 | tf_op jit(solution)/shard_map/kij,kjl->kil/dot_general | solution.py:68
  57.5 2.9 %fusion.5 = bf16[1,512,2048]{2,1,0:T(8,128)(2,1)} fusion(bf16[1,512,2048]{2,1,0:T(8,128)(2,1)S(1)} %fusion.6, f32[512,512]{1,0:T(8,128)S(1)} %fusion.17), kind=kOutput, calls=%fused_computation.11 | convolution fusion | flops 1347682304 | bytes 5242880 | tf_op jit(solution)/shard_map/kij,kjl->kil/dot_general | solution.py:68
  60.9 3.2 %collective-permute-start.14 = (f32[34,128]{1,0:T(8,128)S(1)}, f32[34,128]{1,0:T(8,128)S(1)}, u32[]{:S(2)}, u32[]{:S(2)}) collective-permute-start(f32[34,128]{1,0:T(8,128)S(1)} %add.144), channel_id=1, source_target_pairs={{0,128},{32,160},{64,192},{96,224},{128,0},{160,32},{192,64},{224,... | collective-permute-start | bytes 52232 | tf_op jit(solution)/shard_map/ppermute | solution.py:84
  64.1 3.5 %fusion.14 = f32[512,512]{1,0:T(8,128)S(1)} fusion(bf16[1,512,2048]{2,1,0:T(8,128)(2,1)} %fusion.5), kind=kOutput, calls=%fused_computation.21 | convolution fusion | flops 1073741824 | bytes 3145728 | tf_op jit(solution)/shard_map/kij,klj->kil/dot_general | solution.py:62
  67.7 2.9 %fusion.4 = bf16[1,512,2048]{2,1,0:T(8,128)(2,1)} fusion(bf16[1,512,2048]{2,1,0:T(8,128)(2,1)S(1)} %copy-done.8, f32[512,512]{1,0:T(8,128)S(1)} %fusion.14), kind=kOutput, calls=%fused_computation.9 | convolution fusion | flops 1347682304 | bytes 5242880 | tf_op jit(solution)/shard_map/kij,kjl->kil/dot_general | solution.py:68
  72.1 3.5 %fusion.11 = f32[512,512]{1,0:T(8,128)S(1)} fusion(bf16[1,512,2048]{2,1,0:T(8,128)(2,1)} %fusion.4), kind=kOutput, calls=%fused_computation.18 | convolution fusion | flops 1073741824 | bytes 3145728 | tf_op jit(solution)/shard_map/kij,klj->kil/dot_general | solution.py:62
  75.7 2.9 %fusion.3 = bf16[1,512,2048]{2,1,0:T(8,128)(2,1)} fusion(bf16[1,512,2048]{2,1,0:T(8,128)(2,1)S(1)} %copy-done.9, f32[512,512]{1,0:T(8,128)S(1)} %fusion.11), kind=kOutput, calls=%fused_computation.7 | convolution fusion | flops 1347682304 | bytes 5242880 | tf_op jit(solution)/shard_map/kij,kjl->kil/dot_general | solution.py:68
  78.6 3.5 %fusion.8 = f32[512,512]{1,0:T(8,128)S(1)} fusion(bf16[1,512,2048]{2,1,0:T(8,128)(2,1)} %fusion.3), kind=kOutput, calls=%fused_computation.15 | convolution fusion | flops 1073741824 | bytes 3145728 | tf_op jit(solution)/shard_map/kij,klj->kil/dot_general | solution.py:62
  82.1 3.8 %fusion.2 = bf16[1,512,2048]{2,1,0:T(8,128)(2,1)S(1)} fusion(bf16[1,512,2048]{2,1,0:T(8,128)(2,1)} %fusion.3, f32[512,512]{1,0:T(8,128)S(1)} %fusion.8), kind=kOutput, calls=%fused_computation.5 | convolution fusion | flops 1347682304 | bytes 5242880 | tf_op jit(solution)/shard_map/kij,kjl->kil/dot_general | solution.py:68
  86.0 3.0 %collective-permute-start.19 = (f32[34,128]{1,0:T(8,128)S(1)}, f32[34,128]{1,0:T(8,128)S(1)}, u32[]{:S(2)}, u32[]{:S(2)}) collective-permute-start(f32[34,128]{1,0:T(8,128)S(1)} %add.150), channel_id=1, source_target_pairs={{0,16},{8,24},{16,0},{24,8},{1,17},{9,25},{17,1},{25,9},{2,18},{10... | collective-permute-start | bytes 52232 | tf_op jit(solution)/shard_map/ppermute | solution.py:84
  93.2 2.4 %collective-permute-done.17 = bf16[1,16,2048]{2,1,0:T(8,128)(2,1)S(1)} collective-permute-done((bf16[1,16,2048]{2,1,0:T(8,128)(2,1)S(1)}, bf16[1,16,2048]{2,1,0:T(8,128)(2,1)S(1)}, u32[]{:S(2)}, u32[]{:S(2)}) %collective-permute-start.17) | collective-permute-done | bytes 65568 | tf_op jit(solution)/shard_map/ppermute | solution.py:30
  (82 shorter events, 16.0 us)
Async XLA Ops:
  0.6 8.0 %copy-start = (bf16[512,32]{0,1:T(8,128)(2,1)S(1)}, bf16[512,32]{0,1:T(8,128)(2,1)}, u32[]{:S(2)}) copy-start(bf16[512,32]{0,1:T(8,128)(2,1)} %param.15) | copy-start | bytes 98308
  0.7 8.1 %copy-start.3 = (bf16[512,128]{1,0:T(8,128)(2,1)S(1)}, bf16[512,128]{1,0:T(8,128)(2,1)}, u32[]{:S(2)}) copy-start(bf16[512,128]{1,0:T(8,128)(2,1)} %param.14) | copy-start | bytes 393220
  2.9 6.1 %collective-permute-start = (bf16[1,16,2048]{2,1,0:T(8,128)(2,1)S(1)}, bf16[1,16,2048]{2,1,0:T(8,128)(2,1)S(1)}, u32[]{:S(2)}, u32[]{:S(2)}) collective-permute-start(bf16[1,16,2048]{2,1,0:T(8,128)(2,1)S(1)} %get-tuple-element.39), channel_id=1, source_target_pairs={{0,8},{8,16},{16,24},{24,0},{1,9},{9,17},{17,25},{25,1},{2,10},{10... | collective-permute-start | bytes 196616 | tf_op jit(solution)/shard_map/ppermute | solution.py:30
  4.4 5.9 %collective-permute-start.1 = (bf16[1,16,2048]{2,1,0:T(8,128)(2,1)S(1)}, bf16[1,16,2048]{2,1,0:T(8,128)(2,1)S(1)}, u32[]{:S(2)}, u32[]{:S(2)}) collective-permute-start(bf16[1,16,2048]{2,1,0:T(8,128)(2,1)S(1)} %get-tuple-element.38), channel_id=1, source_target_pairs={{0,16},{8,24},{16,0},{24,8},{1,17},{9,25},{17,1},{25,9},{2,18},{10... | collective-permute-start | bytes 196616 | tf_op jit(solution)/shard_map/ppermute | solution.py:30
  7.1 4.3 %collective-permute-start.2 = (bf16[1,16,2048]{2,1,0:T(8,128)(2,1)S(1)}, bf16[1,16,2048]{2,1,0:T(8,128)(2,1)S(1)}, u32[]{:S(2)}, u32[]{:S(2)}) collective-permute-start(bf16[1,16,2048]{2,1,0:T(8,128)(2,1)S(1)} %get-tuple-element.37), channel_id=1, source_target_pairs={{0,24},{8,0},{16,8},{24,16},{1,25},{9,1},{17,9},{25,17},{2,26},{10... | collective-permute-start | bytes 196616 | tf_op jit(solution)/shard_map/ppermute | solution.py:30
  11.4 10.3 %collective-permute-start.3 = (bf16[1,64,2048]{2,1,0:T(8,128)(2,1)S(1)}, bf16[1,64,2048]{2,1,0:T(8,128)(2,1)S(1)}, u32[]{:S(2)}, u32[]{:S(2)}) collective-permute-start(bf16[1,64,2048]{2,1,0:T(8,128)(2,1)S(1)} %pad_maximum_fusion), channel_id=1, source_target_pairs={{0,224},{32,0},{64,32},{96,64},{128,96},{160,128},{192,160},{224,1... | collective-permute-start | bytes 786440 | tf_op jit(solution)/shard_map/ppermute | solution.py:30
  17.4 8.1 %collective-permute-start.6 = (bf16[1,64,2048]{2,1,0:T(8,128)(2,1)S(1)}, bf16[1,64,2048]{2,1,0:T(8,128)(2,1)S(1)}, u32[]{:S(2)}, u32[]{:S(2)}) collective-permute-start(bf16[1,64,2048]{2,1,0:T(8,128)(2,1)S(1)} %pad_maximum_fusion), channel_id=1, source_target_pairs={{0,32},{32,64},{64,96},{96,128},{128,160},{160,192},{192,224},{224... | collective-permute-start | bytes 786440 | tf_op jit(solution)/shard_map/ppermute | solution.py:30
  21.8 7.6 %collective-permute-start.4 = (bf16[1,64,2048]{2,1,0:T(8,128)(2,1)S(1)}, bf16[1,64,2048]{2,1,0:T(8,128)(2,1)S(1)}, u32[]{:S(2)}, u32[]{:S(2)}) collective-permute-start(bf16[1,64,2048]{2,1,0:T(8,128)(2,1)S(1)} %collective-permute-done.3), channel_id=1, source_target_pairs={{0,224},{32,0},{64,32},{96,64},{128,96},{160,128},{192,160},{224,1... | collective-permute-start | bytes 786440 | tf_op jit(solution)/shard_map/ppermute | solution.py:30
  25.5 7.6 %collective-permute-start.7 = (bf16[1,64,2048]{2,1,0:T(8,128)(2,1)S(1)}, bf16[1,64,2048]{2,1,0:T(8,128)(2,1)S(1)}, u32[]{:S(2)}, u32[]{:S(2)}) collective-permute-start(bf16[1,64,2048]{2,1,0:T(8,128)(2,1)S(1)} %collective-permute-done.6), channel_id=1, source_target_pairs={{0,32},{32,64},{64,96},{96,128},{128,160},{160,192},{192,224},{224... | collective-permute-start | bytes 786440 | tf_op jit(solution)/shard_map/ppermute | solution.py:30
  29.3 8.2 %collective-permute-start.5 = (bf16[1,64,2048]{2,1,0:T(8,128)(2,1)S(1)}, bf16[1,64,2048]{2,1,0:T(8,128)(2,1)S(1)}, u32[]{:S(2)}, u32[]{:S(2)}) collective-permute-start(bf16[1,64,2048]{2,1,0:T(8,128)(2,1)S(1)} %collective-permute-done.4), channel_id=1, source_target_pairs={{0,224},{32,0},{64,32},{96,64},{128,96},{160,128},{192,160},{224,1... | collective-permute-start | bytes 786440 | tf_op jit(solution)/shard_map/ppermute | solution.py:30
  33.0 8.4 %collective-permute-start.8 = (bf16[1,64,2048]{2,1,0:T(8,128)(2,1)S(1)}, bf16[1,64,2048]{2,1,0:T(8,128)(2,1)S(1)}, u32[]{:S(2)}, u32[]{:S(2)}) collective-permute-start(bf16[1,64,2048]{2,1,0:T(8,128)(2,1)S(1)} %collective-permute-done.7), channel_id=1, source_target_pairs={{0,32},{32,64},{64,96},{96,128},{128,160},{160,192},{192,224},{224... | collective-permute-start | bytes 786440 | tf_op jit(solution)/shard_map/ppermute | solution.py:30
  37.5 6.3 %collective-permute-start.10 = (bf16[1,64,1024]{2,1,0:T(8,128)(2,1)S(1)}, bf16[1,64,1024]{2,1,0:T(8,128)(2,1)S(1)}, u32[]{:S(2)}, u32[]{:S(2)}) collective-permute-start(bf16[1,64,1024]{2,1,0:T(8,128)(2,1)S(1)} %slice.25), channel_id=1, source_target_pairs={{0,224},{32,0},{64,32},{96,64},{128,96},{160,128},{192,160},{224,1... | collective-permute-start | bytes 393224 | tf_op jit(solution)/shard_map/ppermute | solution.py:30
  41.4 6.3 %collective-permute-start.9 = (bf16[1,64,1024]{2,1,0:T(8,128)(2,1)S(1)}, bf16[1,64,1024]{2,1,0:T(8,128)(2,1)S(1)}, u32[]{:S(2)}, u32[]{:S(2)}) collective-permute-start(bf16[1,64,1024]{2,1,0:T(8,128)(2,1)S(1)} %slice.24), channel_id=1, source_target_pairs={{0,32},{32,64},{64,96},{96,128},{128,160},{160,192},{192,224},{224... | collective-permute-start | bytes 393224 | tf_op jit(solution)/shard_map/ppermute | solution.py:30
  50.6 1.4 %collective-permute-start.11 = (f32[34,128]{1,0:T(8,128)S(1)}, f32[34,128]{1,0:T(8,128)S(1)}, u32[]{:S(2)}, u32[]{:S(2)}) collective-permute-start(f32[34,128]{1,0:T(8,128)S(1)} %pad_maximum_fusion.1), channel_id=1, source_target_pairs={{0,1},{1,0},{2,3},{3,2},{4,5},{5,4},{6,7},{7,6},{8,9},{9,8},{10,11... | collective-permute-start | bytes 52232 | tf_op jit(solution)/shard_map/ppermute | solution.py:84
  52.0 4.1 %collective-permute-start.12 = (f32[34,128]{1,0:T(8,128)S(1)}, f32[34,128]{1,0:T(8,128)S(1)}, u32[]{:S(2)}, u32[]{:S(2)}) collective-permute-start(f32[34,128]{1,0:T(8,128)S(1)} %add.140), channel_id=1, source_target_pairs={{0,32},{32,0},{64,96},{96,64},{128,160},{160,128},{192,224},{224,1... | collective-permute-start | bytes 52232 | tf_op jit(solution)/shard_map/ppermute | solution.py:84
  56.1 4.8 %collective-permute-start.13 = (f32[34,128]{1,0:T(8,128)S(1)}, f32[34,128]{1,0:T(8,128)S(1)}, u32[]{:S(2)}, u32[]{:S(2)}) collective-permute-start(f32[34,128]{1,0:T(8,128)S(1)} %add.141), channel_id=1, source_target_pairs={{0,64},{32,96},{64,0},{96,32},{128,192},{160,224},{192,128},{224,1... | collective-permute-start | bytes 52232 | tf_op jit(solution)/shard_map/ppermute | solution.py:84
  60.9 9.7 %collective-permute-start.14 = (f32[34,128]{1,0:T(8,128)S(1)}, f32[34,128]{1,0:T(8,128)S(1)}, u32[]{:S(2)}, u32[]{:S(2)}) collective-permute-start(f32[34,128]{1,0:T(8,128)S(1)} %add.144), channel_id=1, source_target_pairs={{0,128},{32,160},{64,192},{96,224},{128,0},{160,32},{192,64},{224,... | collective-permute-start | bytes 52232 | tf_op jit(solution)/shard_map/ppermute | solution.py:84
  70.6 8.0 %collective-permute-start.15 = (f32[34,128]{1,0:T(8,128)S(1)}, f32[34,128]{1,0:T(8,128)S(1)}, u32[]{:S(2)}, u32[]{:S(2)}) collective-permute-start(f32[34,128]{1,0:T(8,128)S(1)} %add.147), channel_id=1, source_target_pairs={{0,8},{8,0},{16,24},{24,16},{1,9},{9,1},{17,25},{25,17},{2,10},{10... | collective-permute-start | bytes 52232 | tf_op jit(solution)/shard_map/ppermute | solution.py:84
  82.1 9.2 %copy-start.4 = (f32[34,128]{1,0:T(8,128)S(1)}, f32[34,128]{1,0:T(8,128)}, u32[]{:S(2)}) copy-start(f32[34,128]{1,0:T(8,128)} %param.17) | copy-start | bytes 52228
  82.1 9.2 %copy-start.5 = (f32[34,128]{1,0:T(8,128)S(1)}, f32[34,128]{1,0:T(8,128)}, u32[]{:S(2)}) copy-start(f32[34,128]{1,0:T(8,128)} %param.16) | copy-start | bytes 52228
  86.0 5.4 %collective-permute-start.19 = (f32[34,128]{1,0:T(8,128)S(1)}, f32[34,128]{1,0:T(8,128)S(1)}, u32[]{:S(2)}, u32[]{:S(2)}) collective-permute-start(f32[34,128]{1,0:T(8,128)S(1)} %add.150), channel_id=1, source_target_pairs={{0,16},{8,24},{16,0},{24,8},{1,17},{9,25},{17,1},{25,9},{2,18},{10... | collective-permute-start | bytes 52232 | tf_op jit(solution)/shard_map/ppermute | solution.py:84
  88.9 4.3 %collective-permute-start.16 = (bf16[1,16,2048]{2,1,0:T(8,128)(2,1)S(1)}, bf16[1,16,2048]{2,1,0:T(8,128)(2,1)S(1)}, u32[]{:S(2)}, u32[]{:S(2)}) collective-permute-start(bf16[1,16,2048]{2,1,0:T(8,128)(2,1)S(1)} %get-tuple-element.36), channel_id=1, source_target_pairs={{0,24},{8,0},{16,8},{24,16},{1,25},{9,1},{17,9},{25,17},{2,26},{10... | collective-permute-start | bytes 196616 | tf_op jit(solution)/shard_map/ppermute | solution.py:30
  89.5 6.1 %collective-permute-start.17 = (bf16[1,16,2048]{2,1,0:T(8,128)(2,1)S(1)}, bf16[1,16,2048]{2,1,0:T(8,128)(2,1)S(1)}, u32[]{:S(2)}, u32[]{:S(2)}) collective-permute-start(bf16[1,16,2048]{2,1,0:T(8,128)(2,1)S(1)} %get-tuple-element.35), channel_id=1, source_target_pairs={{0,16},{8,24},{16,0},{24,8},{1,17},{9,25},{17,1},{25,9},{2,18},{10... | collective-permute-start | bytes 196616 | tf_op jit(solution)/shard_map/ppermute | solution.py:30
  90.6 5.7 %collective-permute-start.18 = (bf16[1,16,2048]{2,1,0:T(8,128)(2,1)S(1)}, bf16[1,16,2048]{2,1,0:T(8,128)(2,1)S(1)}, u32[]{:S(2)}, u32[]{:S(2)}) collective-permute-start(bf16[1,16,2048]{2,1,0:T(8,128)(2,1)S(1)} %get-tuple-element.34), channel_id=1, source_target_pairs={{0,8},{8,16},{16,24},{24,0},{1,9},{9,17},{17,25},{25,1},{2,10},{10... | collective-permute-start | bytes 196616 | tf_op jit(solution)/shard_map/ppermute | solution.py:30
  (6 other events, 37.0 us)

commit v6 on v5

--- a/solution.py
+++ b/solution.py
@@ -4,6 +4,7 @@
 import jax.numpy as jnp
 import numpy as np
 from jax import lax
+from jax.experimental import pallas as pl
 from jax.sharding import Mesh
 from jax.sharding import PartitionSpec as P
 
@@ -49,6 +50,30 @@
     return jnp.concatenate([strip] + ahead + behind[::-1], axis=1)
 
 
+def ns_step_kernel(iterate_ref, out_ref):
+    iterate = iterate_ref[...]
+    gram = lax.dot_general(
+        iterate, iterate, (((1,), (1,)), ((), ())), preferred_element_type=jnp.float32
+    )
+    gram_half = gram.astype(jnp.bfloat16)
+    square_term = jnp.dot(gram_half, gram_half, preferred_element_type=jnp.float32)
+    poly = (CUBIC_TERM * gram + QUINTIC_TERM * square_term).astype(jnp.bfloat16)
+    product = jnp.dot(poly, iterate, preferred_element_type=jnp.float32)
+    out_ref[...] = (LINEAR_TERM * iterate.astype(jnp.float32) + product).astype(jnp.bfloat16)
+
+
+def ns_step(iterate):
+    count, rows, cols = iterate.shape
+    spec = pl.BlockSpec((None, rows, cols), lambda k: (k, 0, 0))
+    return pl.pallas_call(
+        ns_step_kernel,
+        out_shape=jax.ShapeDtypeStruct(iterate.shape, iterate.dtype),
+        grid=(count,),
+        in_specs=[spec],
+        out_specs=spec,
+    )(iterate)
+
+
 def orthogonalize(blocks, carried, rounds):
     squares = jnp.sum(jnp.square(blocks.astype(jnp.float32)), axis=(1, 2))
     total = jnp.sqrt(squares)
@@ -59,14 +84,7 @@
         carried, iterate = lax.optimization_barrier((carried, iterate))
         for step in rounds[repeat] if repeat < len(rounds) else ():
             carried = step(carried)
-        gram = jnp.einsum("kij,klj->kil", iterate, iterate, preferred_element_type=jnp.float32)
-        gram_half = gram.astype(jnp.bfloat16)
-        square_term = jnp.einsum(
-            "kij,kjl->kil", gram_half, gram_half, preferred_element_type=jnp.float32
-        )
-        poly = (CUBIC_TERM * gram + QUINTIC_TERM * square_term).astype(jnp.bfloat16)
-        product = jnp.einsum("kij,kjl->kil", poly, iterate, preferred_element_type=jnp.float32)
-        iterate = (LINEAR_TERM * iterate.astype(jnp.float32) + product).astype(jnp.bfloat16)
+        iterate = ns_step(iterate)
     for group in rounds[ITERS:]:
         for step in group:
             carried = step(carried)

time: 97.4 us -> 101 us (1.037)
  matrix products: 29.6 us -> 0.15 us
  Pallas kernels: 0 us -> 28.2 us
  local copies, waits for them, and re-layouts: 0.29 us -> 2.85 us
  other arithmetic: 5.81 us -> 7.11 us
    dot_general x10 -> x0, matrix products: 29.5 us -> none  [the longest x5 16.4 us: orthogonalize(): jnp.einsum('kij,kjl->kil', poly, iterate, preferred_element_type=jnp.floa...]
    pallas_call x0 -> x5, Pallas kernels: none -> 28.2 us  [ns_step(): pl.pallas_call(ns_step_kernel, out_shape=jax.ShapeDtypeStruct(iterate.sha...]
    unnamed x35 -> x29, local copies, waits for them, and re-layouts: 0.21 us -> 1.87 us
    convert_element_type x1, other arithmetic: 0.42 us -> 1.72 us  [orthogonalize(): (blocks.astype(jnp.float32) / (total + NORM_EPSILON)[:, None, None]).asty...]
  transfers between devices with their start and end apart: 20 -> 20, of which waited for: 14 -> 13; matrix products, arithmetic and copies ran while one was open for 24% -> 3% of each run, Pallas kernels for 0% -> 28%
where the time goes in v6:
time: 101 us; the launch traced here: 100 us
  starting transfers between devices  33.3 us (33%)
  Pallas kernels  28.2 us (28%)
  waiting for transfers between devices  27 us (27%)
  other arithmetic  7.11 us (7%)
  local copies, waits for them, and re-layouts  2.85 us (3%)
  between operations  1.62 us (2%)
    pallas_call x5, Pallas kernels, ns_step(): pl.pallas_call(ns_step_kernel, out_shape=jax.ShapeDtypeStruct(iterate.sha...  28.2 us
    ppermute x14, waiting for transfers between devices, shift(): return lax.ppermute(value, axis, [(i, (i + k) % size) for i in range(size)])  25.8 us
    ppermute x14, starting transfers between devices, shift(): return lax.ppermute(value, axis, [(i, (i + k) % size) for i in range(size)])  25 us
    ppermute x6, starting transfers between devices, butterfly_rounds(): lax.ppermute(value, axis, perm)  8.3 us
    convert_element_type x1, other arithmetic, on_device(): nesterov = (grad_float + MUON_DECAY * next_momentum).astype(jnp.bfloat16)  2.08 us
  transfers between devices with their start and end apart: 20, of which 13 were waited for; matrix products, arithmetic and copies ran while one was open for 3% of the time, Pallas kernels for 28%

profile of v6, /device:TPU:16, one launch (start us, length us, event | category | flops | bytes accessed | tf_op | source)
XLA Modules:
  0.0 100.2 jit_solution(3437985623234197607)
XLA Ops:
  0.7 2.1 %fusion.2 = (bf16[4,16,2048]{2,1,0:T(8,128)(2,1)S(1)}, f32[4,16,2048]{2,1,0:T(8,128)}) fusion(bf16[4,16,2048]{2,1,0:T(8,128)(2,1)} %param.9, f32[4,16,2048]{2,1,0:T(8,128)} %param.10), kind=kLoop, calls=%fused_computation.7 | loop fusion | flops 786432 | bytes 1572864 | tf_op jit(solution)/shard_map/convert_element_type | solution.py:139
  2.8 1.6 %collective-permute-start = (bf16[1,16,2048]{2,1,0:T(8,128)(2,1)S(1)}, bf16[1,16,2048]{2,1,0:T(8,128)(2,1)S(1)}, u32[]{:S(2)}, u32[]{:S(2)}) collective-permute-start(bf16[1,16,2048]{2,1,0:T(8,128)(2,1)S(1)} %get-tuple-element.39), channel_id=1, source_target_pairs={{0,8},{8,16},{16,24},{24,0},{1,9},{9,17},{17,25},{25,1},{2,10},{10... | collective-permute-start | bytes 196616 | tf_op jit(solution)/shard_map/ppermute | solution.py:31
  4.4 2.7 %collective-permute-start.1 = (bf16[1,16,2048]{2,1,0:T(8,128)(2,1)S(1)}, bf16[1,16,2048]{2,1,0:T(8,128)(2,1)S(1)}, u32[]{:S(2)}, u32[]{:S(2)}) collective-permute-start(bf16[1,16,2048]{2,1,0:T(8,128)(2,1)S(1)} %get-tuple-element.38), channel_id=1, source_target_pairs={{0,16},{8,24},{16,0},{24,8},{1,17},{9,25},{17,1},{25,9},{2,18},{10... | collective-permute-start | bytes 196616 | tf_op jit(solution)/shard_map/ppermute | solution.py:31
  7.1 1.4 %collective-permute-start.2 = (bf16[1,16,2048]{2,1,0:T(8,128)(2,1)S(1)}, bf16[1,16,2048]{2,1,0:T(8,128)(2,1)S(1)}, u32[]{:S(2)}, u32[]{:S(2)}) collective-permute-start(bf16[1,16,2048]{2,1,0:T(8,128)(2,1)S(1)} %get-tuple-element.37), channel_id=1, source_target_pairs={{0,24},{8,0},{16,8},{24,16},{1,25},{9,1},{17,9},{25,17},{2,26},{10... | collective-permute-start | bytes 196616 | tf_op jit(solution)/shard_map/ppermute | solution.py:31
  11.4 5.9 %collective-permute-start.3 = (bf16[1,64,2048]{2,1,0:T(8,128)(2,1)S(1)}, bf16[1,64,2048]{2,1,0:T(8,128)(2,1)S(1)}, u32[]{:S(2)}, u32[]{:S(2)}) collective-permute-start(bf16[1,64,2048]{2,1,0:T(8,128)(2,1)S(1)} %pad_maximum_fusion), channel_id=1, source_target_pairs={{0,224},{32,0},{64,32},{96,64},{128,96},{160,128},{192,160},{224,1... | collective-permute-start | bytes 786440 | tf_op jit(solution)/shard_map/ppermute | solution.py:31
  17.4 4.4 %collective-permute-done.3 = bf16[1,64,2048]{2,1,0:T(8,128)(2,1)S(1)} collective-permute-done((bf16[1,64,2048]{2,1,0:T(8,128)(2,1)S(1)}, bf16[1,64,2048]{2,1,0:T(8,128)(2,1)S(1)}, u32[]{:S(2)}, u32[]{:S(2)}) %collective-permute-start.3) | collective-permute-done | bytes 262176 | tf_op jit(solution)/shard_map/ppermute | solution.py:31
  21.8 3.7 %collective-permute-start.4 = (bf16[1,64,2048]{2,1,0:T(8,128)(2,1)S(1)}, bf16[1,64,2048]{2,1,0:T(8,128)(2,1)S(1)}, u32[]{:S(2)}, u32[]{:S(2)}) collective-permute-start(bf16[1,64,2048]{2,1,0:T(8,128)(2,1)S(1)} %collective-permute-done.3), channel_id=1, source_target_pairs={{0,224},{32,0},{64,32},{96,64},{128,96},{160,128},{192,160},{224,1... | collective-permute-start | bytes 786440 | tf_op jit(solution)/shard_map/ppermute | solution.py:31
  25.5 3.9 %collective-permute-done.4 = bf16[1,64,2048]{2,1,0:T(8,128)(2,1)S(1)} collective-permute-done((bf16[1,64,2048]{2,1,0:T(8,128)(2,1)S(1)}, bf16[1,64,2048]{2,1,0:T(8,128)(2,1)S(1)}, u32[]{:S(2)}, u32[]{:S(2)}) %collective-permute-start.4) | collective-permute-done | bytes 262176 | tf_op jit(solution)/shard_map/ppermute | solution.py:31
  29.3 3.7 %collective-permute-start.5 = (bf16[1,64,2048]{2,1,0:T(8,128)(2,1)S(1)}, bf16[1,64,2048]{2,1,0:T(8,128)(2,1)S(1)}, u32[]{:S(2)}, u32[]{:S(2)}) collective-permute-start(bf16[1,64,2048]{2,1,0:T(8,128)(2,1)S(1)} %collective-permute-done.4), channel_id=1, source_target_pairs={{0,224},{32,0},{64,32},{96,64},{128,96},{160,128},{192,160},{224,1... | collective-permute-start | bytes 786440 | tf_op jit(solution)/shard_map/ppermute | solution.py:31
  33.1 4.4 %collective-permute-done.5 = bf16[1,64,2048]{2,1,0:T(8,128)(2,1)S(1)} collective-permute-done((bf16[1,64,2048]{2,1,0:T(8,128)(2,1)S(1)}, bf16[1,64,2048]{2,1,0:T(8,128)(2,1)S(1)}, u32[]{:S(2)}, u32[]{:S(2)}) %collective-permute-start.5) | collective-permute-done | bytes 262176 | tf_op jit(solution)/shard_map/ppermute | solution.py:31
  37.5 3.8 %collective-permute-start.10 = (bf16[1,64,1024]{2,1,0:T(8,128)(2,1)S(1)}, bf16[1,64,1024]{2,1,0:T(8,128)(2,1)S(1)}, u32[]{:S(2)}, u32[]{:S(2)}) collective-permute-start(bf16[1,64,1024]{2,1,0:T(8,128)(2,1)S(1)} %slice.25), channel_id=1, source_target_pairs={{0,224},{32,0},{64,32},{96,64},{128,96},{160,128},{192,160},{224,1... | collective-permute-start | bytes 393224 | tf_op jit(solution)/shard_map/ppermute | solution.py:31
  41.5 2.3 %collective-permute-done.10 = bf16[1,64,1024]{2,1,0:T(8,128)(2,1)S(1)} collective-permute-done((bf16[1,64,1024]{2,1,0:T(8,128)(2,1)S(1)}, bf16[1,64,1024]{2,1,0:T(8,128)(2,1)S(1)}, u32[]{:S(2)}, u32[]{:S(2)}) %collective-permute-start.10) | collective-permute-done | bytes 131104 | tf_op jit(solution)/shard_map/ppermute | solution.py:31
  43.8 3.8 %collective-permute-done.9 = bf16[1,64,1024]{2,1,0:T(8,128)(2,1)S(1)} collective-permute-done((bf16[1,64,1024]{2,1,0:T(8,128)(2,1)S(1)}, bf16[1,64,1024]{2,1,0:T(8,128)(2,1)S(1)}, u32[]{:S(2)}, u32[]{:S(2)}) %collective-permute-start.9) | collective-permute-done | bytes 131104 | tf_op jit(solution)/shard_map/ppermute | solution.py:31
  47.8 1.7 %fusion = f32[]{:T(128)} fusion(bf16[1,512,2048]{2,1,0:T(8,128)(2,1)S(1)} %constant_dynamic-update-slice_fusion), kind=kLoop, calls=%fused_computation.2 | loop fusion | flops 3145727 | bytes 2097156 | tf_op jit(solution)/shard_map/reduce_sum | solution.py:78
  50.2 1.7 %fusion.1.iterate_ref = bf16[1,512,2048]{2,1,0:T(8,128)(2,1)} fusion(bf16[1,512,2048]{2,1,0:T(8,128)(2,1)S(1)} %constant_dynamic-update-slice_fusion, f32[]{:T(128)S(6)} %add.104), kind=kLoop, calls=%fused_computation.3 | loop fusion | flops 3145728 | bytes 4194308 | tf_op jit(solution)/shard_map/convert_element_type | solution.py:80
  53.1 5.6 %shard_map.128.iterate_ref = bf16[1,512,2048]{2,1,0:T(8,128)(2,1)} custom-call(bf16[1,512,2048]{2,1,0:T(8,128)(2,1)} %fusion.1.iterate_ref), custom_call_target="tpu_custom_call" | custom-call | tf_op jit(solution)/shard_map/pallas_call | solution.py:68
  58.8 5.6 %shard_map.129.iterate_ref = bf16[1,512,2048]{2,1,0:T(8,128)(2,1)} custom-call(bf16[1,512,2048]{2,1,0:T(8,128)(2,1)} %shard_map.128.iterate_ref), custom_call_target="tpu_custom_call" | custom-call | tf_op jit(solution)/shard_map/pallas_call | solution.py:68
  64.5 3.7 %collective-permute-start.14 = (f32[34,128]{1,0:T(8,128)S(1)}, f32[34,128]{1,0:T(8,128)S(1)}, u32[]{:S(2)}, u32[]{:S(2)}) collective-permute-start(f32[34,128]{1,0:T(8,128)S(1)} %add.107), channel_id=1, source_target_pairs={{0,128},{32,160},{64,192},{96,224},{128,0},{160,32},{192,64},{224,... | collective-permute-start | bytes 52232 | tf_op jit(solution)/shard_map/ppermute | solution.py:102
  68.2 5.6 %shard_map.130.iterate_ref = bf16[1,512,2048]{2,1,0:T(8,128)(2,1)} custom-call(bf16[1,512,2048]{2,1,0:T(8,128)(2,1)} %shard_map.129.iterate_ref), custom_call_target="tpu_custom_call" | custom-call | tf_op jit(solution)/shard_map/pallas_call | solution.py:68
  75.1 5.6 %shard_map.131.iterate_ref = bf16[1,512,2048]{2,1,0:T(8,128)(2,1)} custom-call(bf16[1,512,2048]{2,1,0:T(8,128)(2,1)} %shard_map.130.iterate_ref), custom_call_target="tpu_custom_call" | custom-call | tf_op jit(solution)/shard_map/pallas_call | solution.py:68
  80.8 3.2 %collective-permute-start.19 = (f32[34,128]{1,0:T(8,128)S(1)}, f32[34,128]{1,0:T(8,128)S(1)}, u32[]{:S(2)}, u32[]{:S(2)}) collective-permute-start(f32[34,128]{1,0:T(8,128)S(1)} %add.109), channel_id=1, source_target_pairs={{0,16},{8,24},{16,0},{24,8},{1,17},{9,25},{17,1},{25,9},{2,18},{10... | collective-permute-start | bytes 52232 | tf_op jit(solution)/shard_map/ppermute | solution.py:102
  84.0 5.6 %shard_map.132 = bf16[1,512,2048]{2,1,0:T(8,128)(2,1)} custom-call(bf16[1,512,2048]{2,1,0:T(8,128)(2,1)} %shard_map.131.iterate_ref), custom_call_target="tpu_custom_call" | custom-call | tf_op jit(solution)/shard_map/pallas_call | solution.py:68
  94.1 1.5 %collective-permute-done.16 = bf16[1,16,2048]{2,1,0:T(8,128)(2,1)S(1)} collective-permute-done((bf16[1,16,2048]{2,1,0:T(8,128)(2,1)S(1)}, bf16[1,16,2048]{2,1,0:T(8,128)(2,1)S(1)}, u32[]{:S(2)}, u32[]{:S(2)}) %collective-permute-start.16) | collective-permute-done | bytes 65568 | tf_op jit(solution)/shard_map/ppermute | solution.py:31
  95.6 2.1 %collective-permute-done.17 = bf16[1,16,2048]{2,1,0:T(8,128)(2,1)S(1)} collective-permute-done((bf16[1,16,2048]{2,1,0:T(8,128)(2,1)S(1)}, bf16[1,16,2048]{2,1,0:T(8,128)(2,1)S(1)}, u32[]{:S(2)}, u32[]{:S(2)}) %collective-permute-start.17) | collective-permute-done | bytes 65568 | tf_op jit(solution)/shard_map/ppermute | solution.py:31
  (71 shorter events, 12.8 us)
Async XLA Ops:
  0.6 8.0 %copy-start = (bf16[512,32]{0,1:T(8,128)(2,1)S(1)}, bf16[512,32]{0,1:T(8,128)(2,1)}, u32[]{:S(2)}) copy-start(bf16[512,32]{0,1:T(8,128)(2,1)} %param.15) | copy-start | bytes 98308
  0.7 8.1 %copy-start.2 = (bf16[512,128]{1,0:T(8,128)(2,1)S(1)}, bf16[512,128]{1,0:T(8,128)(2,1)}, u32[]{:S(2)}) copy-start(bf16[512,128]{1,0:T(8,128)(2,1)} %param.14) | copy-start | bytes 393220
  2.8 6.1 %collective-permute-start = (bf16[1,16,2048]{2,1,0:T(8,128)(2,1)S(1)}, bf16[1,16,2048]{2,1,0:T(8,128)(2,1)S(1)}, u32[]{:S(2)}, u32[]{:S(2)}) collective-permute-start(bf16[1,16,2048]{2,1,0:T(8,128)(2,1)S(1)} %get-tuple-element.39), channel_id=1, source_target_pairs={{0,8},{8,16},{16,24},{24,0},{1,9},{9,17},{17,25},{25,1},{2,10},{10... | collective-permute-start | bytes 196616 | tf_op jit(solution)/shard_map/ppermute | solution.py:31
  4.4 5.9 %collective-permute-start.1 = (bf16[1,16,2048]{2,1,0:T(8,128)(2,1)S(1)}, bf16[1,16,2048]{2,1,0:T(8,128)(2,1)S(1)}, u32[]{:S(2)}, u32[]{:S(2)}) collective-permute-start(bf16[1,16,2048]{2,1,0:T(8,128)(2,1)S(1)} %get-tuple-element.38), channel_id=1, source_target_pairs={{0,16},{8,24},{16,0},{24,8},{1,17},{9,25},{17,1},{25,9},{2,18},{10... | collective-permute-start | bytes 196616 | tf_op jit(solution)/shard_map/ppermute | solution.py:31
  7.1 4.3 %collective-permute-start.2 = (bf16[1,16,2048]{2,1,0:T(8,128)(2,1)S(1)}, bf16[1,16,2048]{2,1,0:T(8,128)(2,1)S(1)}, u32[]{:S(2)}, u32[]{:S(2)}) collective-permute-start(bf16[1,16,2048]{2,1,0:T(8,128)(2,1)S(1)} %get-tuple-element.37), channel_id=1, source_target_pairs={{0,24},{8,0},{16,8},{24,16},{1,25},{9,1},{17,9},{25,17},{2,26},{10... | collective-permute-start | bytes 196616 | tf_op jit(solution)/shard_map/ppermute | solution.py:31
  11.4 10.3 %collective-permute-start.3 = (bf16[1,64,2048]{2,1,0:T(8,128)(2,1)S(1)}, bf16[1,64,2048]{2,1,0:T(8,128)(2,1)S(1)}, u32[]{:S(2)}, u32[]{:S(2)}) collective-permute-start(bf16[1,64,2048]{2,1,0:T(8,128)(2,1)S(1)} %pad_maximum_fusion), channel_id=1, source_target_pairs={{0,224},{32,0},{64,32},{96,64},{128,96},{160,128},{192,160},{224,1... | collective-permute-start | bytes 786440 | tf_op jit(solution)/shard_map/ppermute | solution.py:31
  17.4 8.1 %collective-permute-start.6 = (bf16[1,64,2048]{2,1,0:T(8,128)(2,1)S(1)}, bf16[1,64,2048]{2,1,0:T(8,128)(2,1)S(1)}, u32[]{:S(2)}, u32[]{:S(2)}) collective-permute-start(bf16[1,64,2048]{2,1,0:T(8,128)(2,1)S(1)} %pad_maximum_fusion), channel_id=1, source_target_pairs={{0,32},{32,64},{64,96},{96,128},{128,160},{160,192},{192,224},{224... | collective-permute-start | bytes 786440 | tf_op jit(solution)/shard_map/ppermute | solution.py:31
  21.8 7.6 %collective-permute-start.4 = (bf16[1,64,2048]{2,1,0:T(8,128)(2,1)S(1)}, bf16[1,64,2048]{2,1,0:T(8,128)(2,1)S(1)}, u32[]{:S(2)}, u32[]{:S(2)}) collective-permute-start(bf16[1,64,2048]{2,1,0:T(8,128)(2,1)S(1)} %collective-permute-done.3), channel_id=1, source_target_pairs={{0,224},{32,0},{64,32},{96,64},{128,96},{160,128},{192,160},{224,1... | collective-permute-start | bytes 786440 | tf_op jit(solution)/shard_map/ppermute | solution.py:31
  25.5 7.6 %collective-permute-start.7 = (bf16[1,64,2048]{2,1,0:T(8,128)(2,1)S(1)}, bf16[1,64,2048]{2,1,0:T(8,128)(2,1)S(1)}, u32[]{:S(2)}, u32[]{:S(2)}) collective-permute-start(bf16[1,64,2048]{2,1,0:T(8,128)(2,1)S(1)} %collective-permute-done.6), channel_id=1, source_target_pairs={{0,32},{32,64},{64,96},{96,128},{128,160},{160,192},{192,224},{224... | collective-permute-start | bytes 786440 | tf_op jit(solution)/shard_map/ppermute | solution.py:31
  29.3 8.2 %collective-permute-start.5 = (bf16[1,64,2048]{2,1,0:T(8,128)(2,1)S(1)}, bf16[1,64,2048]{2,1,0:T(8,128)(2,1)S(1)}, u32[]{:S(2)}, u32[]{:S(2)}) collective-permute-start(bf16[1,64,2048]{2,1,0:T(8,128)(2,1)S(1)} %collective-permute-done.4), channel_id=1, source_target_pairs={{0,224},{32,0},{64,32},{96,64},{128,96},{160,128},{192,160},{224,1... | collective-permute-start | bytes 786440 | tf_op jit(solution)/shard_map/ppermute | solution.py:31
  33.0 8.4 %collective-permute-start.8 = (bf16[1,64,2048]{2,1,0:T(8,128)(2,1)S(1)}, bf16[1,64,2048]{2,1,0:T(8,128)(2,1)S(1)}, u32[]{:S(2)}, u32[]{:S(2)}) collective-permute-start(bf16[1,64,2048]{2,1,0:T(8,128)(2,1)S(1)} %collective-permute-done.7), channel_id=1, source_target_pairs={{0,32},{32,64},{64,96},{96,128},{128,160},{160,192},{192,224},{224... | collective-permute-start | bytes 786440 | tf_op jit(solution)/shard_map/ppermute | solution.py:31
  37.5 6.3 %collective-permute-start.10 = (bf16[1,64,1024]{2,1,0:T(8,128)(2,1)S(1)}, bf16[1,64,1024]{2,1,0:T(8,128)(2,1)S(1)}, u32[]{:S(2)}, u32[]{:S(2)}) collective-permute-start(bf16[1,64,1024]{2,1,0:T(8,128)(2,1)S(1)} %slice.25), channel_id=1, source_target_pairs={{0,224},{32,0},{64,32},{96,64},{128,96},{160,128},{192,160},{224,1... | collective-permute-start | bytes 393224 | tf_op jit(solution)/shard_map/ppermute | solution.py:31
  41.4 6.3 %collective-permute-start.9 = (bf16[1,64,1024]{2,1,0:T(8,128)(2,1)S(1)}, bf16[1,64,1024]{2,1,0:T(8,128)(2,1)S(1)}, u32[]{:S(2)}, u32[]{:S(2)}) collective-permute-start(bf16[1,64,1024]{2,1,0:T(8,128)(2,1)S(1)} %slice.24), channel_id=1, source_target_pairs={{0,32},{32,64},{64,96},{96,128},{128,160},{160,192},{192,224},{224... | collective-permute-start | bytes 393224 | tf_op jit(solution)/shard_map/ppermute | solution.py:31
  51.9 1.2 %collective-permute-start.11 = (f32[34,128]{1,0:T(8,128)S(1)}, f32[34,128]{1,0:T(8,128)S(1)}, u32[]{:S(2)}, u32[]{:S(2)}) collective-permute-start(f32[34,128]{1,0:T(8,128)S(1)} %pad_maximum_fusion.1), channel_id=1, source_target_pairs={{0,1},{1,0},{2,3},{3,2},{4,5},{5,4},{6,7},{7,6},{8,9},{9,8},{10,11... | collective-permute-start | bytes 52232 | tf_op jit(solution)/shard_map/ppermute | solution.py:102
  53.1 5.7 %collective-permute-start.12 = (f32[34,128]{1,0:T(8,128)S(1)}, f32[34,128]{1,0:T(8,128)S(1)}, u32[]{:S(2)}, u32[]{:S(2)}) collective-permute-start(f32[34,128]{1,0:T(8,128)S(1)} %add.105), channel_id=1, source_target_pairs={{0,32},{32,0},{64,96},{96,64},{128,160},{160,128},{192,224},{224,1... | collective-permute-start | bytes 52232 | tf_op jit(solution)/shard_map/ppermute | solution.py:102
  58.7 5.7 %collective-permute-start.13 = (f32[34,128]{1,0:T(8,128)S(1)}, f32[34,128]{1,0:T(8,128)S(1)}, u32[]{:S(2)}, u32[]{:S(2)}) collective-permute-start(f32[34,128]{1,0:T(8,128)S(1)} %add.106), channel_id=1, source_target_pairs={{0,64},{32,96},{64,0},{96,32},{128,192},{160,224},{192,128},{224,1... | collective-permute-start | bytes 52232 | tf_op jit(solution)/shard_map/ppermute | solution.py:102
  64.5 9.3 %collective-permute-start.14 = (f32[34,128]{1,0:T(8,128)S(1)}, f32[34,128]{1,0:T(8,128)S(1)}, u32[]{:S(2)}, u32[]{:S(2)}) collective-permute-start(f32[34,128]{1,0:T(8,128)S(1)} %add.107), channel_id=1, source_target_pairs={{0,128},{32,160},{64,192},{96,224},{128,0},{160,32},{192,64},{224,... | collective-permute-start | bytes 52232 | tf_op jit(solution)/shard_map/ppermute | solution.py:102
  73.8 6.9 %collective-permute-start.15 = (f32[34,128]{1,0:T(8,128)S(1)}, f32[34,128]{1,0:T(8,128)S(1)}, u32[]{:S(2)}, u32[]{:S(2)}) collective-permute-start(f32[34,128]{1,0:T(8,128)S(1)} %add.108), channel_id=1, source_target_pairs={{0,8},{8,0},{16,24},{24,16},{1,9},{9,1},{17,25},{25,17},{2,10},{10... | collective-permute-start | bytes 52232 | tf_op jit(solution)/shard_map/ppermute | solution.py:102
  80.8 12.7 %copy-start.3 = (f32[34,128]{1,0:T(8,128)S(1)}, f32[34,128]{1,0:T(8,128)}, u32[]{:S(2)}) copy-start(f32[34,128]{1,0:T(8,128)} %param.17) | copy-start | bytes 52228
  80.8 12.7 %copy-start.4 = (f32[34,128]{1,0:T(8,128)S(1)}, f32[34,128]{1,0:T(8,128)}, u32[]{:S(2)}) copy-start(f32[34,128]{1,0:T(8,128)} %param.16) | copy-start | bytes 52228
  80.8 12.7 %collective-permute-start.19 = (f32[34,128]{1,0:T(8,128)S(1)}, f32[34,128]{1,0:T(8,128)S(1)}, u32[]{:S(2)}, u32[]{:S(2)}) collective-permute-start(f32[34,128]{1,0:T(8,128)S(1)} %add.109), channel_id=1, source_target_pairs={{0,16},{8,24},{16,0},{24,8},{1,17},{9,25},{17,1},{25,9},{2,18},{10... | collective-permute-start | bytes 52232 | tf_op jit(solution)/shard_map/ppermute | solution.py:102
  91.4 4.3 %collective-permute-start.16 = (bf16[1,16,2048]{2,1,0:T(8,128)(2,1)S(1)}, bf16[1,16,2048]{2,1,0:T(8,128)(2,1)S(1)}, u32[]{:S(2)}, u32[]{:S(2)}) collective-permute-start(bf16[1,16,2048]{2,1,0:T(8,128)(2,1)S(1)} %get-tuple-element.36), channel_id=1, source_target_pairs={{0,24},{8,0},{16,8},{24,16},{1,25},{9,1},{17,9},{25,17},{2,26},{10... | collective-permute-start | bytes 196616 | tf_op jit(solution)/shard_map/ppermute | solution.py:31
  92.0 5.8 %collective-permute-start.17 = (bf16[1,16,2048]{2,1,0:T(8,128)(2,1)S(1)}, bf16[1,16,2048]{2,1,0:T(8,128)(2,1)S(1)}, u32[]{:S(2)}, u32[]{:S(2)}) collective-permute-start(bf16[1,16,2048]{2,1,0:T(8,128)(2,1)S(1)} %get-tuple-element.35), channel_id=1, source_target_pairs={{0,16},{8,24},{16,0},{24,8},{1,17},{9,25},{17,1},{25,9},{2,18},{10... | collective-permute-start | bytes 196616 | tf_op jit(solution)/shard_map/ppermute | solution.py:31
  92.9 5.6 %collective-permute-start.18 = (bf16[1,16,2048]{2,1,0:T(8,128)(2,1)S(1)}, bf16[1,16,2048]{2,1,0:T(8,128)(2,1)S(1)}, u32[]{:S(2)}, u32[]{:S(2)}) collective-permute-start(bf16[1,16,2048]{2,1,0:T(8,128)(2,1)S(1)} %get-tuple-element.34), channel_id=1, source_target_pairs={{0,8},{8,16},{16,24},{24,0},{1,9},{9,17},{17,25},{25,1},{2,10},{10... | collective-permute-start | bytes 196616 | tf_op jit(solution)/shard_map/ppermute | solution.py:31
  (3 other events, 23.8 us)

commit v7 on v5

--- a/solution.py
+++ b/solution.py
@@ -30,23 +30,35 @@
     return lax.ppermute(value, axis, [(i, (i + k) % size) for i in range(size)])
 
 
-def ring_gather(strip, axis):
+def ring_gather(strip, extra, axis):
     size = lax.axis_size(axis)
     cols = strip.shape[-1]
     ahead, behind = [], []
-    from_behind = from_ahead = strip
+    from_behind = from_ahead = (strip, extra)
     for distance in range(1, size // 2 + 1):
         if 2 * distance == size:
             half = cols // 2
-            first = shift(from_behind[..., :half], axis, 1)
-            second = shift(from_ahead[..., half:], axis, -1)
-            ahead.append(jnp.concatenate([first, second], axis=-1))
+            first, far_extra = shift((from_behind[0][..., :half], from_behind[1]), axis, 1)
+            second = shift(from_ahead[0][..., half:], axis, -1)
+            ahead.append((jnp.concatenate([first, second], axis=-1), far_extra))
             break
         from_behind = shift(from_behind, axis, 1)
         from_ahead = shift(from_ahead, axis, -1)
         ahead.append(from_ahead)
         behind.append(from_behind)
-    return jnp.concatenate([strip] + ahead + behind[::-1], axis=1)
+    pieces = [(strip, extra)] + ahead + behind[::-1]
+    return jnp.concatenate([p[0] for p in pieces], axis=1), [p[1] for p in pieces]
+
+
+def ordered_sum(by_offset, axis):
+    size = lax.axis_size(axis)
+    stacked = jnp.stack(by_offset, axis=0)
+    place = (jnp.arange(size) - lax.axis_index(axis)) % size
+    in_order = jnp.take(stacked, place, axis=0)
+    total = in_order[0]
+    for index in range(1, size):
+        total = total + in_order[index]
+    return total
 
 
 def orthogonalize(blocks, carried, rounds):
@@ -125,16 +137,18 @@
     padded = jnp.pad(nesterov, ((0, slots * inner - count_all), (0, 0), (0, 0)))
     by_owner = padded.reshape(inner, slots, rows_piece, cols_full)
     here = lax.axis_index("inner")
-    strip = jnp.concatenate(
-        [shift(lax.dynamic_index_in_dim(by_owner, (here + k) % inner, 0, keepdims=False), "inner", k)
-         for k in range(inner)],
-        axis=1,
-    )
-    blocks = ring_gather(strip, "outer")
     local = vector_partials(normed, ln_gain, ln_bias, ln_cotangent, router_cotangent)
-    steps = [step for axis in ("section",) + SHARD for step in butterfly_rounds(axis)]
-    rounds = [steps[:2]] + [[step] for step in steps[2:]]
-    result, vec_grad = orthogonalize(blocks, local, rounds)
+    moved = [
+        shift((lax.dynamic_index_in_dim(by_owner, (here + k) % inner, 0, keepdims=False), local),
+              "inner", k)
+        for k in range(inner)
+    ]
+    strip = jnp.concatenate([piece for piece, _ in moved], axis=1)
+    inner_sum = ordered_sum([moved[(-k) % inner][1] for k in range(inner)], "inner")
+    blocks, outer_sums = ring_gather(strip, inner_sum, "outer")
+    outer_sum = ordered_sum(outer_sums, "outer")
+    rounds = [butterfly_rounds("section")]
+    result, vec_grad = orthogonalize(blocks, outer_sum, rounds)
     next_first, next_second, adam_step = adam(vec_grad, first_moment, second_moment)
     back = jnp.stack(
         [shift(result[:, k * rows_piece:(k + 1) * rows_piece], "inner", -k) for k in range(inner)],

time: 97.4 us -> 112 us (1.15)
  starting transfers between devices: 33.2 us -> 38.9 us
  waiting for transfers between devices: 26.6 us -> 30.7 us
  local copies, waits for them, and re-layouts: 0.29 us -> 2.63 us
  matrix products: 29.6 us -> 30.9 us
  other arithmetic: 5.81 us -> 6.95 us
    ppermute x14 -> x24, starting transfers between devices: 25 us -> 38.9 us  [shift(): return lax.ppermute(value, axis, [(i, (i + k) % size) for i in range(size)])]
    ppermute x6 -> x1, starting transfers between devices: 8.19 us -> 0.09 us  [butterfly_rounds(): lax.ppermute(value, axis, perm)]
    ppermute x14 -> x24, waiting for transfers between devices: 25.8 us -> 30.7 us  [shift(): return lax.ppermute(value, axis, [(i, (i + k) % size) for i in range(size)])]
    unnamed x35 -> x33, local copies, waits for them, and re-layouts: 0.21 us -> 1.43 us
  transfers between devices with their start and end apart: 20 -> 25, of which waited for: 14 -> 15; matrix products, arithmetic and copies ran while one was open for 24% -> 8% of each run, Pallas kernels for 0% -> 0%
where the time goes in v7:
time: 112 us
  starting transfers between devices  38.9 us (35%)
  matrix products  30.9 us (28%)
  waiting for transfers between devices  30.7 us (27%)
  other arithmetic  6.95 us (6%)
  local copies, waits for them, and re-layouts  2.63 us (2%)
  between operations  1.77 us (2%)
    ppermute x24, starting transfers between devices, shift(): return lax.ppermute(value, axis, [(i, (i + k) % size) for i in range(size)])  38.9 us
    ppermute x24, waiting for transfers between devices, shift(): return lax.ppermute(value, axis, [(i, (i + k) % size) for i in range(size)])  30.7 us
    dot_general x5, matrix products, orthogonalize(): jnp.einsum('kij,kjl->kil', poly, iterate, preferred_element_type=jnp.floa...  16.5 us
    dot_general x5, matrix products, orthogonalize(): jnp.einsum('kij,klj->kil', iterate, iterate, preferred_element_type=jnp.f...  13.4 us
  transfers between devices with their start and end apart: 25, of which 15 were waited for; matrix products, arithmetic and copies ran while one was open for 8% of the time, Pallas kernels for 0%

profile of v7, /device:TPU:16, one launch (start us, length us, event | category | flops | bytes accessed | tf_op | source)
XLA Modules:
  0.0 111.9 jit_solution(15607268754403658839)
XLA Ops:
  4.4 2.7 %collective-permute-start.1 = (f32[34,128]{1,0:T(8,128)S(1)}, f32[34,128]{1,0:T(8,128)S(1)}, u32[]{:S(2)}, u32[]{:S(2)}) collective-permute-start(f32[34,128]{1,0:T(8,128)S(1)} %get-tuple-element.45), channel_id=1, source_target_pairs={{0,16},{8,24},{16,0},{24,8},{1,17},{9,25},{17,1},{25,9},{2,18},{10... | collective-permute-start | bytes 52232 | tf_op jit(solution)/shard_map/ppermute | solution.py:30
  8.5 2.0 %fusion.32 = (bf16[4,16,2048]{2,1,0:T(8,128)(2,1)S(1)}, f32[4,16,2048]{2,1,0:T(8,128)}) fusion(bf16[4,16,2048]{2,1,0:T(8,128)(2,1)} %param.9, f32[4,16,2048]{2,1,0:T(8,128)} %param.10), kind=kLoop, calls=%fused_computation.49 | loop fusion | flops 786432 | bytes 1572864 | tf_op jit(solution)/shard_map/convert_element_type | solution.py:133
  12.2 2.0 %collective-permute-start.12 = (bf16[1,16,2048]{2,1,0:T(8,128)(2,1)S(1)}, bf16[1,16,2048]{2,1,0:T(8,128)(2,1)S(1)}, u32[]{:S(2)}, u32[]{:S(2)}) collective-permute-start(bf16[1,16,2048]{2,1,0:T(8,128)(2,1)S(1)} %get-tuple-element.39), channel_id=1, source_target_pairs={{0,24},{8,0},{16,8},{24,16},{1,25},{9,1},{17,9},{25,17},{2,26},{10... | collective-permute-start | bytes 196616 | tf_op jit(solution)/shard_map/ppermute | solution.py:30
  14.9 5.9 %collective-permute-start.3 = (f32[34,128]{1,0:T(8,128)S(1)}, f32[34,128]{1,0:T(8,128)S(1)}, u32[]{:S(2)}, u32[]{:S(2)}) collective-permute-start(f32[34,128]{1,0:T(8,128)S(1)} %bitcast.96), channel_id=1, source_target_pairs={{0,224},{32,0},{64,32},{96,64},{128,96},{160,128},{192,160},{224,1... | collective-permute-start | bytes 52232 | tf_op jit(solution)/shard_map/ppermute | solution.py:30
  22.3 3.5 %collective-permute-start.4 = (f32[34,128]{1,0:T(8,128)S(1)}, f32[34,128]{1,0:T(8,128)S(1)}, u32[]{:S(2)}, u32[]{:S(2)}) collective-permute-start(f32[34,128]{1,0:T(8,128)S(1)} %collective-permute-done.3), channel_id=1, source_target_pairs={{0,224},{32,0},{64,32},{96,64},{128,96},{160,128},{192,160},{224,1... | collective-permute-start | bytes 52232 | tf_op jit(solution)/shard_map/ppermute | solution.py:30
  27.3 3.6 %collective-permute-start.5 = (f32[34,128]{1,0:T(8,128)S(1)}, f32[34,128]{1,0:T(8,128)S(1)}, u32[]{:S(2)}, u32[]{:S(2)}) collective-permute-start(f32[34,128]{1,0:T(8,128)S(1)} %collective-permute-done.4), channel_id=1, source_target_pairs={{0,224},{32,0},{64,32},{96,64},{128,96},{160,128},{192,160},{224,1... | collective-permute-start | bytes 52232 | tf_op jit(solution)/shard_map/ppermute | solution.py:30
  31.0 3.3 %collective-permute-start.13 = (bf16[1,64,2048]{2,1,0:T(8,128)(2,1)S(1)}, bf16[1,64,2048]{2,1,0:T(8,128)(2,1)S(1)}, u32[]{:S(2)}, u32[]{:S(2)}) collective-permute-start(bf16[1,64,2048]{2,1,0:T(8,128)(2,1)S(1)} %pad_maximum_fusion), channel_id=1, source_target_pairs={{0,224},{32,0},{64,32},{96,64},{128,96},{160,128},{192,160},{224,1... | collective-permute-start | bytes 786440 | tf_op jit(solution)/shard_map/ppermute | solution.py:30
  36.2 6.9 %collective-permute-done.9 = f32[34,128]{1,0:T(8,128)S(1)} collective-permute-done((f32[34,128]{1,0:T(8,128)S(1)}, f32[34,128]{1,0:T(8,128)S(1)}, u32[]{:S(2)}, u32[]{:S(2)}) %collective-permute-start.9) | collective-permute-done | bytes 17440 | tf_op jit(solution)/shard_map/ppermute | solution.py:30
  44.0 2.0 %collective-permute-start.17 = (bf16[1,64,2048]{2,1,0:T(8,128)(2,1)S(1)}, bf16[1,64,2048]{2,1,0:T(8,128)(2,1)S(1)}, u32[]{:S(2)}, u32[]{:S(2)}) collective-permute-start(bf16[1,64,2048]{2,1,0:T(8,128)(2,1)S(1)} %collective-permute-done.16), channel_id=1, source_target_pairs={{0,32},{32,64},{64,96},{96,128},{128,160},{160,192},{192,224},{224... | collective-permute-start | bytes 786440 | tf_op jit(solution)/shard_map/ppermute | solution.py:30
  46.1 4.9 %collective-permute-done.14 = bf16[1,64,2048]{2,1,0:T(8,128)(2,1)S(1)} collective-permute-done((bf16[1,64,2048]{2,1,0:T(8,128)(2,1)S(1)}, bf16[1,64,2048]{2,1,0:T(8,128)(2,1)S(1)}, u32[]{:S(2)}, u32[]{:S(2)}) %collective-permute-start.14) | collective-permute-done | bytes 262176 | tf_op jit(solution)/shard_map/ppermute | solution.py:30
  51.0 3.0 %collective-permute-start.15 = (bf16[1,64,2048]{2,1,0:T(8,128)(2,1)S(1)}, bf16[1,64,2048]{2,1,0:T(8,128)(2,1)S(1)}, u32[]{:S(2)}, u32[]{:S(2)}) collective-permute-start(bf16[1,64,2048]{2,1,0:T(8,128)(2,1)S(1)} %collective-permute-done.14), channel_id=1, source_target_pairs={{0,224},{32,0},{64,32},{96,64},{128,96},{160,128},{192,160},{224,1... | collective-permute-start | bytes 786440 | tf_op jit(solution)/shard_map/ppermute | solution.py:30
  54.2 3.9 %collective-permute-done.15 = bf16[1,64,2048]{2,1,0:T(8,128)(2,1)S(1)} collective-permute-done((bf16[1,64,2048]{2,1,0:T(8,128)(2,1)S(1)}, bf16[1,64,2048]{2,1,0:T(8,128)(2,1)S(1)}, u32[]{:S(2)}, u32[]{:S(2)}) %collective-permute-start.15) | collective-permute-done | bytes 262176 | tf_op jit(solution)/shard_map/ppermute | solution.py:30
  58.1 3.8 %collective-permute-start.20 = (bf16[1,64,1024]{2,1,0:T(8,128)(2,1)S(1)}, bf16[1,64,1024]{2,1,0:T(8,128)(2,1)S(1)}, u32[]{:S(2)}, u32[]{:S(2)}) collective-permute-start(bf16[1,64,1024]{2,1,0:T(8,128)(2,1)S(1)} %slice.89), channel_id=1, source_target_pairs={{0,224},{32,0},{64,32},{96,64},{128,96},{160,128},{192,160},{224,1... | collective-permute-start | bytes 393224 | tf_op jit(solution)/shard_map/ppermute | solution.py:30
  62.3 2.1 %collective-permute-done.20 = bf16[1,64,1024]{2,1,0:T(8,128)(2,1)S(1)} collective-permute-done((bf16[1,64,1024]{2,1,0:T(8,128)(2,1)S(1)}, bf16[1,64,1024]{2,1,0:T(8,128)(2,1)S(1)}, u32[]{:S(2)}, u32[]{:S(2)}) %collective-permute-start.20) | collective-permute-done | bytes 131104 | tf_op jit(solution)/shard_map/ppermute | solution.py:30
  64.4 4.0 %collective-permute-done.19 = bf16[1,64,1024]{2,1,0:T(8,128)(2,1)S(1)} collective-permute-done((bf16[1,64,1024]{2,1,0:T(8,128)(2,1)S(1)}, bf16[1,64,1024]{2,1,0:T(8,128)(2,1)S(1)}, u32[]{:S(2)}, u32[]{:S(2)}) %collective-permute-start.19) | collective-permute-done | bytes 131104 | tf_op jit(solution)/shard_map/ppermute | solution.py:30
  73.9 3.8 %fusion.6 = bf16[1,512,2048]{2,1,0:T(8,128)(2,1)S(1)} fusion(bf16[1,512,2048]{2,1,0:T(8,128)(2,1)} %copy-done.1, f32[512,512]{1,0:T(8,128)S(1)} %fusion.20), kind=kOutput, calls=%fused_computation.15 | convolution fusion | flops 1347682304 | bytes 5242880 | tf_op jit(solution)/shard_map/kij,kjl->kil/dot_general | solution.py:80
  79.1 2.9 %fusion.5 = bf16[1,512,2048]{2,1,0:T(8,128)(2,1)} fusion(bf16[1,512,2048]{2,1,0:T(8,128)(2,1)S(1)} %fusion.6, f32[512,512]{1,0:T(8,128)S(1)} %fusion.17), kind=kOutput, calls=%fused_computation.13 | convolution fusion | flops 1347682304 | bytes 5242880 | tf_op jit(solution)/shard_map/kij,kjl->kil/dot_general | solution.py:80
  82.0 3.6 %fusion.14 = f32[512,512]{1,0:T(8,128)S(1)} fusion(bf16[1,512,2048]{2,1,0:T(8,128)(2,1)} %fusion.5), kind=kOutput, calls=%fused_computation.23 | convolution fusion | flops 1073741824 | bytes 3145728 | tf_op jit(solution)/shard_map/kij,klj->kil/dot_general | solution.py:74
  85.7 2.9 %fusion.4 = bf16[1,512,2048]{2,1,0:T(8,128)(2,1)} fusion(bf16[1,512,2048]{2,1,0:T(8,128)(2,1)S(1)} %copy-done.4, f32[512,512]{1,0:T(8,128)S(1)} %fusion.14), kind=kOutput, calls=%fused_computation.11 | convolution fusion | flops 1347682304 | bytes 5242880 | tf_op jit(solution)/shard_map/kij,kjl->kil/dot_general | solution.py:80
  88.6 3.6 %fusion.11 = f32[512,512]{1,0:T(8,128)S(1)} fusion(bf16[1,512,2048]{2,1,0:T(8,128)(2,1)} %fusion.4), kind=kOutput, calls=%fused_computation.20 | convolution fusion | flops 1073741824 | bytes 3145728 | tf_op jit(solution)/shard_map/kij,klj->kil/dot_general | solution.py:74
  92.3 2.9 %fusion.3 = bf16[1,512,2048]{2,1,0:T(8,128)(2,1)} fusion(bf16[1,512,2048]{2,1,0:T(8,128)(2,1)S(1)} %copy-done.5, f32[512,512]{1,0:T(8,128)S(1)} %fusion.11), kind=kOutput, calls=%fused_computation.9 | convolution fusion | flops 1347682304 | bytes 5242880 | tf_op jit(solution)/shard_map/kij,kjl->kil/dot_general | solution.py:80
  95.2 3.5 %fusion.8 = f32[512,512]{1,0:T(8,128)S(1)} fusion(bf16[1,512,2048]{2,1,0:T(8,128)(2,1)} %fusion.3), kind=kOutput, calls=%fused_computation.17 | convolution fusion | flops 1073741824 | bytes 3145728 | tf_op jit(solution)/shard_map/kij,klj->kil/dot_general | solution.py:74
  98.7 3.8 %fusion.2 = bf16[1,512,2048]{2,1,0:T(8,128)(2,1)S(1)} fusion(bf16[1,512,2048]{2,1,0:T(8,128)(2,1)} %fusion.3, f32[512,512]{1,0:T(8,128)S(1)} %fusion.8), kind=kOutput, calls=%fused_computation.7 | convolution fusion | flops 1347682304 | bytes 5242880 | tf_op jit(solution)/shard_map/kij,kjl->kil/dot_general | solution.py:80
  107.6 2.0 %collective-permute-done.23 = bf16[1,16,2048]{2,1,0:T(8,128)(2,1)S(1)} collective-permute-done((bf16[1,16,2048]{2,1,0:T(8,128)(2,1)S(1)}, bf16[1,16,2048]{2,1,0:T(8,128)(2,1)S(1)}, u32[]{:S(2)}, u32[]{:S(2)}) %collective-permute-start.23) | collective-permute-done | bytes 65568 | tf_op jit(solution)/shard_map/ppermute | solution.py:30
  (100 shorter events, 27.4 us)
Async XLA Ops:
  2.8 9.4 %collective-permute-start.2 = (f32[34,128]{1,0:T(8,128)S(1)}, f32[34,128]{1,0:T(8,128)S(1)}, u32[]{:S(2)}, u32[]{:S(2)}) collective-permute-start(f32[34,128]{1,0:T(8,128)S(1)} %get-tuple-element.45), channel_id=1, source_target_pairs={{0,8},{8,16},{16,24},{24,0},{1,9},{9,17},{17,25},{25,1},{2,10},{10... | collective-permute-start | bytes 52232 | tf_op jit(solution)/shard_map/ppermute | solution.py:30
  4.4 9.8 %collective-permute-start.1 = (f32[34,128]{1,0:T(8,128)S(1)}, f32[34,128]{1,0:T(8,128)S(1)}, u32[]{:S(2)}, u32[]{:S(2)}) collective-permute-start(f32[34,128]{1,0:T(8,128)S(1)} %get-tuple-element.45), channel_id=1, source_target_pairs={{0,16},{8,24},{16,0},{24,8},{1,17},{9,25},{17,1},{25,9},{2,18},{10... | collective-permute-start | bytes 52232 | tf_op jit(solution)/shard_map/ppermute | solution.py:30
  7.1 7.1 %collective-permute-start = (f32[34,128]{1,0:T(8,128)S(1)}, f32[34,128]{1,0:T(8,128)S(1)}, u32[]{:S(2)}, u32[]{:S(2)}) collective-permute-start(f32[34,128]{1,0:T(8,128)S(1)} %get-tuple-element.45), channel_id=1, source_target_pairs={{0,24},{8,0},{16,8},{24,16},{1,25},{9,1},{17,9},{25,17},{2,26},{10... | collective-permute-start | bytes 52232 | tf_op jit(solution)/shard_map/ppermute | solution.py:30
  10.6 20.4 %collective-permute-start.10 = (bf16[1,16,2048]{2,1,0:T(8,128)(2,1)S(1)}, bf16[1,16,2048]{2,1,0:T(8,128)(2,1)S(1)}, u32[]{:S(2)}, u32[]{:S(2)}) collective-permute-start(bf16[1,16,2048]{2,1,0:T(8,128)(2,1)S(1)} %get-tuple-element.41), channel_id=1, source_target_pairs={{0,8},{8,16},{16,24},{24,0},{1,9},{9,17},{17,25},{25,1},{2,10},{10... | collective-permute-start | bytes 196616 | tf_op jit(solution)/shard_map/ppermute | solution.py:30
  11.3 19.7 %collective-permute-start.11 = (bf16[1,16,2048]{2,1,0:T(8,128)(2,1)S(1)}, bf16[1,16,2048]{2,1,0:T(8,128)(2,1)S(1)}, u32[]{:S(2)}, u32[]{:S(2)}) collective-permute-start(bf16[1,16,2048]{2,1,0:T(8,128)(2,1)S(1)} %get-tuple-element.40), channel_id=1, source_target_pairs={{0,16},{8,24},{16,0},{24,8},{1,17},{9,25},{17,1},{25,9},{2,18},{10... | collective-permute-start | bytes 196616 | tf_op jit(solution)/shard_map/ppermute | solution.py:30
  12.2 18.8 %collective-permute-start.12 = (bf16[1,16,2048]{2,1,0:T(8,128)(2,1)S(1)}, bf16[1,16,2048]{2,1,0:T(8,128)(2,1)S(1)}, u32[]{:S(2)}, u32[]{:S(2)}) collective-permute-start(bf16[1,16,2048]{2,1,0:T(8,128)(2,1)S(1)} %get-tuple-element.39), channel_id=1, source_target_pairs={{0,24},{8,0},{16,8},{24,16},{1,25},{9,1},{17,9},{25,17},{2,26},{10... | collective-permute-start | bytes 196616 | tf_op jit(solution)/shard_map/ppermute | solution.py:30
  14.9 7.4 %collective-permute-start.3 = (f32[34,128]{1,0:T(8,128)S(1)}, f32[34,128]{1,0:T(8,128)S(1)}, u32[]{:S(2)}, u32[]{:S(2)}) collective-permute-start(f32[34,128]{1,0:T(8,128)S(1)} %bitcast.96), channel_id=1, source_target_pairs={{0,224},{32,0},{64,32},{96,64},{128,96},{160,128},{192,160},{224,1... | collective-permute-start | bytes 52232 | tf_op jit(solution)/shard_map/ppermute | solution.py:30
  20.8 5.1 %collective-permute-start.6 = (f32[34,128]{1,0:T(8,128)S(1)}, f32[34,128]{1,0:T(8,128)S(1)}, u32[]{:S(2)}, u32[]{:S(2)}) collective-permute-start(f32[34,128]{1,0:T(8,128)S(1)} %bitcast.97), channel_id=1, source_target_pairs={{0,32},{32,64},{64,96},{96,128},{128,160},{160,192},{192,224},{224... | collective-permute-start | bytes 52232 | tf_op jit(solution)/shard_map/ppermute | solution.py:30
  25.9 5.1 %collective-permute-start.7 = (f32[34,128]{1,0:T(8,128)S(1)}, f32[34,128]{1,0:T(8,128)S(1)}, u32[]{:S(2)}, u32[]{:S(2)}) collective-permute-start(f32[34,128]{1,0:T(8,128)S(1)} %collective-permute-done.6), channel_id=1, source_target_pairs={{0,32},{32,64},{64,96},{96,128},{128,160},{160,192},{192,224},{224... | collective-permute-start | bytes 52232 | tf_op jit(solution)/shard_map/ppermute | solution.py:30
  27.3 8.9 %collective-permute-start.5 = (f32[34,128]{1,0:T(8,128)S(1)}, f32[34,128]{1,0:T(8,128)S(1)}, u32[]{:S(2)}, u32[]{:S(2)}) collective-permute-start(f32[34,128]{1,0:T(8,128)S(1)} %collective-permute-done.4), channel_id=1, source_target_pairs={{0,224},{32,0},{64,32},{96,64},{128,96},{160,128},{192,160},{224,1... | collective-permute-start | bytes 52232 | tf_op jit(solution)/shard_map/ppermute | solution.py:30
  31.0 5.2 %collective-permute-start.8 = (f32[34,128]{1,0:T(8,128)S(1)}, f32[34,128]{1,0:T(8,128)S(1)}, u32[]{:S(2)}, u32[]{:S(2)}) collective-permute-start(f32[34,128]{1,0:T(8,128)S(1)} %collective-permute-done.7), channel_id=1, source_target_pairs={{0,32},{32,64},{64,96},{96,128},{128,160},{160,192},{192,224},{224... | collective-permute-start | bytes 52232 | tf_op jit(solution)/shard_map/ppermute | solution.py:30
  31.0 12.7 %collective-permute-start.13 = (bf16[1,64,2048]{2,1,0:T(8,128)(2,1)S(1)}, bf16[1,64,2048]{2,1,0:T(8,128)(2,1)S(1)}, u32[]{:S(2)}, u32[]{:S(2)}) collective-permute-start(bf16[1,64,2048]{2,1,0:T(8,128)(2,1)S(1)} %pad_maximum_fusion), channel_id=1, source_target_pairs={{0,224},{32,0},{64,32},{96,64},{128,96},{160,128},{192,160},{224,1... | collective-permute-start | bytes 786440 | tf_op jit(solution)/shard_map/ppermute | solution.py:30
  34.3 9.6 %collective-permute-start.16 = (bf16[1,64,2048]{2,1,0:T(8,128)(2,1)S(1)}, bf16[1,64,2048]{2,1,0:T(8,128)(2,1)S(1)}, u32[]{:S(2)}, u32[]{:S(2)}) collective-permute-start(bf16[1,64,2048]{2,1,0:T(8,128)(2,1)S(1)} %pad_maximum_fusion), channel_id=1, source_target_pairs={{0,32},{32,64},{64,96},{96,128},{128,160},{160,192},{192,224},{224... | collective-permute-start | bytes 786440 | tf_op jit(solution)/shard_map/ppermute | solution.py:30
  36.2 6.9 %collective-permute-start.9 = (f32[34,128]{1,0:T(8,128)S(1)}, f32[34,128]{1,0:T(8,128)S(1)}, u32[]{:S(2)}, u32[]{:S(2)}) collective-permute-start(f32[34,128]{1,0:T(8,128)S(1)} %collective-permute-done.8), channel_id=1, source_target_pairs={{0,32},{32,64},{64,96},{96,128},{128,160},{160,192},{192,224},{224... | collective-permute-start | bytes 52232 | tf_op jit(solution)/shard_map/ppermute | solution.py:30
  43.7 7.3 %collective-permute-start.14 = (bf16[1,64,2048]{2,1,0:T(8,128)(2,1)S(1)}, bf16[1,64,2048]{2,1,0:T(8,128)(2,1)S(1)}, u32[]{:S(2)}, u32[]{:S(2)}) collective-permute-start(bf16[1,64,2048]{2,1,0:T(8,128)(2,1)S(1)} %collective-permute-done.13), channel_id=1, source_target_pairs={{0,224},{32,0},{64,32},{96,64},{128,96},{160,128},{192,160},{224,1... | collective-permute-start | bytes 786440 | tf_op jit(solution)/shard_map/ppermute | solution.py:30
  44.0 10.2 %collective-permute-start.17 = (bf16[1,64,2048]{2,1,0:T(8,128)(2,1)S(1)}, bf16[1,64,2048]{2,1,0:T(8,128)(2,1)S(1)}, u32[]{:S(2)}, u32[]{:S(2)}) collective-permute-start(bf16[1,64,2048]{2,1,0:T(8,128)(2,1)S(1)} %collective-permute-done.16), channel_id=1, source_target_pairs={{0,32},{32,64},{64,96},{96,128},{128,160},{160,192},{192,224},{224... | collective-permute-start | bytes 786440 | tf_op jit(solution)/shard_map/ppermute | solution.py:30
  51.0 7.1 %collective-permute-start.15 = (bf16[1,64,2048]{2,1,0:T(8,128)(2,1)S(1)}, bf16[1,64,2048]{2,1,0:T(8,128)(2,1)S(1)}, u32[]{:S(2)}, u32[]{:S(2)}) collective-permute-start(bf16[1,64,2048]{2,1,0:T(8,128)(2,1)S(1)} %collective-permute-done.14), channel_id=1, source_target_pairs={{0,224},{32,0},{64,32},{96,64},{128,96},{160,128},{192,160},{224,1... | collective-permute-start | bytes 786440 | tf_op jit(solution)/shard_map/ppermute | solution.py:30
  54.2 8.0 %collective-permute-start.18 = (bf16[1,64,2048]{2,1,0:T(8,128)(2,1)S(1)}, bf16[1,64,2048]{2,1,0:T(8,128)(2,1)S(1)}, u32[]{:S(2)}, u32[]{:S(2)}) collective-permute-start(bf16[1,64,2048]{2,1,0:T(8,128)(2,1)S(1)} %collective-permute-done.17), channel_id=1, source_target_pairs={{0,32},{32,64},{64,96},{96,128},{128,160},{160,192},{192,224},{224... | collective-permute-start | bytes 786440 | tf_op jit(solution)/shard_map/ppermute | solution.py:30
  58.1 6.3 %collective-permute-start.20 = (bf16[1,64,1024]{2,1,0:T(8,128)(2,1)S(1)}, bf16[1,64,1024]{2,1,0:T(8,128)(2,1)S(1)}, u32[]{:S(2)}, u32[]{:S(2)}) collective-permute-start(bf16[1,64,1024]{2,1,0:T(8,128)(2,1)S(1)} %slice.89), channel_id=1, source_target_pairs={{0,224},{32,0},{64,32},{96,64},{128,96},{160,128},{192,160},{224,1... | collective-permute-start | bytes 393224 | tf_op jit(solution)/shard_map/ppermute | solution.py:30
  62.2 6.3 %collective-permute-start.19 = (bf16[1,64,1024]{2,1,0:T(8,128)(2,1)S(1)}, bf16[1,64,1024]{2,1,0:T(8,128)(2,1)S(1)}, u32[]{:S(2)}, u32[]{:S(2)}) collective-permute-start(bf16[1,64,1024]{2,1,0:T(8,128)(2,1)S(1)} %slice.88), channel_id=1, source_target_pairs={{0,32},{32,64},{64,96},{96,128},{128,160},{160,192},{192,224},{224... | collective-permute-start | bytes 393224 | tf_op jit(solution)/shard_map/ppermute | solution.py:30
  71.3 6.4 %collective-permute-start.21 = (f32[34,128]{1,0:T(8,128)S(1)}, f32[34,128]{1,0:T(8,128)S(1)}, u32[]{:S(2)}, u32[]{:S(2)}) collective-permute-start(f32[34,128]{1,0:T(8,128)S(1)} %fusion.60), channel_id=1, source_target_pairs={{0,1},{1,0},{2,3},{3,2},{4,5},{5,4},{6,7},{7,6},{8,9},{9,8},{10,11... | collective-permute-start | bytes 52232 | tf_op jit(solution)/shard_map/ppermute | solution.py:96
  102.6 5.0 %collective-permute-start.22 = (bf16[1,16,2048]{2,1,0:T(8,128)(2,1)S(1)}, bf16[1,16,2048]{2,1,0:T(8,128)(2,1)S(1)}, u32[]{:S(2)}, u32[]{:S(2)}) collective-permute-start(bf16[1,16,2048]{2,1,0:T(8,128)(2,1)S(1)} %get-tuple-element.38), channel_id=1, source_target_pairs={{0,24},{8,0},{16,8},{24,16},{1,25},{9,1},{17,9},{25,17},{2,26},{10... | collective-permute-start | bytes 196616 | tf_op jit(solution)/shard_map/ppermute | solution.py:30
  103.8 5.8 %collective-permute-start.23 = (bf16[1,16,2048]{2,1,0:T(8,128)(2,1)S(1)}, bf16[1,16,2048]{2,1,0:T(8,128)(2,1)S(1)}, u32[]{:S(2)}, u32[]{:S(2)}) collective-permute-start(bf16[1,16,2048]{2,1,0:T(8,128)(2,1)S(1)} %get-tuple-element.37), channel_id=1, source_target_pairs={{0,16},{8,24},{16,0},{24,8},{1,17},{9,25},{17,1},{25,9},{2,18},{10... | collective-permute-start | bytes 196616 | tf_op jit(solution)/shard_map/ppermute | solution.py:30
  105.5 5.5 %collective-permute-start.24 = (bf16[1,16,2048]{2,1,0:T(8,128)(2,1)S(1)}, bf16[1,16,2048]{2,1,0:T(8,128)(2,1)S(1)}, u32[]{:S(2)}, u32[]{:S(2)}) collective-permute-start(bf16[1,16,2048]{2,1,0:T(8,128)(2,1)S(1)} %get-tuple-element.36), channel_id=1, source_target_pairs={{0,8},{8,16},{16,24},{24,0},{1,9},{9,17},{17,25},{25,1},{2,10},{10... | collective-permute-start | bytes 196616 | tf_op jit(solution)/shard_map/ppermute | solution.py:30
  (7 other events, 30.7 us)

commit v8 on v6

--- a/solution.py
+++ b/solution.py
@@ -5,6 +5,7 @@
 import numpy as np
 from jax import lax
 from jax.experimental import pallas as pl
+from jax.experimental.pallas import tpu as pltpu
 from jax.sharding import Mesh
 from jax.sharding import PartitionSpec as P
 
@@ -50,8 +51,7 @@
     return jnp.concatenate([strip] + ahead + behind[::-1], axis=1)
 
 
-def ns_step_kernel(iterate_ref, out_ref):
-    iterate = iterate_ref[...]
+def ns_update(iterate):
     gram = lax.dot_general(
         iterate, iterate, (((1,), (1,)), ((), ())), preferred_element_type=jnp.float32
     )
@@ -59,32 +59,44 @@
     square_term = jnp.dot(gram_half, gram_half, preferred_element_type=jnp.float32)
     poly = (CUBIC_TERM * gram + QUINTIC_TERM * square_term).astype(jnp.bfloat16)
     product = jnp.dot(poly, iterate, preferred_element_type=jnp.float32)
-    out_ref[...] = (LINEAR_TERM * iterate.astype(jnp.float32) + product).astype(jnp.bfloat16)
-
-
-def ns_step(iterate):
-    count, rows, cols = iterate.shape
-    spec = pl.BlockSpec((None, rows, cols), lambda k: (k, 0, 0))
+    return (LINEAR_TERM * iterate.astype(jnp.float32) + product).astype(jnp.bfloat16)
+
+
+def first_step_kernel(blocks_ref, out_ref):
+    for k in range(blocks_ref.shape[0]):
+        wide = blocks_ref[k].astype(jnp.float32)
+        total = jnp.sqrt(jnp.sum(wide * wide))
+        out_ref[k] = ns_update((wide / (total + NORM_EPSILON)).astype(jnp.bfloat16))
+
+
+def later_step_kernel(iterate_ref, out_ref):
+    for k in range(iterate_ref.shape[0]):
+        out_ref[k] = ns_update(iterate_ref[k])
+
+
+def in_vmem(resident):
+    return pl.BlockSpec(memory_space=pltpu.VMEM) if resident else pl.BlockSpec()
+
+
+def ns_call(kernel, value, source, target):
     return pl.pallas_call(
-        ns_step_kernel,
-        out_shape=jax.ShapeDtypeStruct(iterate.shape, iterate.dtype),
-        grid=(count,),
-        in_specs=[spec],
-        out_specs=spec,
-    )(iterate)
+        kernel,
+        out_shape=jax.ShapeDtypeStruct(value.shape, jnp.bfloat16),
+        in_specs=[in_vmem(source)],
+        out_specs=in_vmem(target),
+    )(value)
 
 
 def orthogonalize(blocks, carried, rounds):
-    squares = jnp.sum(jnp.square(blocks.astype(jnp.float32)), axis=(1, 2))
-    total = jnp.sqrt(squares)
-    iterate = (blocks.astype(jnp.float32) / (total + NORM_EPSILON)[:, None, None]).astype(
-        jnp.bfloat16
-    )
+    iterate = blocks
     for repeat in range(ITERS):
         carried, iterate = lax.optimization_barrier((carried, iterate))
         for step in rounds[repeat] if repeat < len(rounds) else ():
             carried = step(carried)
-        iterate = ns_step(iterate)
+        kernel = first_step_kernel if repeat == 0 else later_step_kernel
+        source = repeat > 0
+        target = repeat < ITERS - 1
+        iterate = ns_call(kernel, iterate, source, target)
     for group in rounds[ITERS:]:
         for step in group:
             carried = step(carried)

time: 101 us -> 97.8 us (0.968)
  other arithmetic: 7.11 us -> 3.71 us
  Pallas kernels: 28.2 us -> 29.4 us
    convert_element_type x1 -> x0, other arithmetic: 1.72 us -> none  [orthogonalize(): (blocks.astype(jnp.float32) / (total + NORM_EPSILON)[:, None, None]).asty...]
    reduce_sum x1 -> x0, other arithmetic: 1.68 us -> none  [orthogonalize(): squares = jnp.sum(jnp.square(blocks.astype(jnp.float32)), axis=(1, 2))]
    pallas_call x5, Pallas kernels: 28.2 us -> 29.4 us  [ns_call(): pl.pallas_call(kernel, out_shape=jax.ShapeDtypeStruct(value.shape, jnp.bf...]
  transfers between devices with their start and end apart: 20 -> 20, of which waited for: 13 -> 13; matrix products, arithmetic and copies ran while one was open for 3% -> 3% of each run, Pallas kernels for 28% -> 30%
where the time goes in v8:
time: 97.8 us; the launch traced here: 97.4 us
  starting transfers between devices  33.4 us (34%)
  Pallas kernels  29.4 us (30%)
  waiting for transfers between devices  27 us (28%)
  other arithmetic  3.71 us (4%)
  local copies, waits for them, and re-layouts  2.86 us (3%)
    pallas_call x5, Pallas kernels, ns_call(): pl.pallas_call(kernel, out_shape=jax.ShapeDtypeStruct(value.shape, jnp.bf...  29.4 us
    ppermute x14, waiting for transfers between devices, shift(): return lax.ppermute(value, axis, [(i, (i + k) % size) for i in range(size)])  25.8 us
    ppermute x14, starting transfers between devices, shift(): return lax.ppermute(value, axis, [(i, (i + k) % size) for i in range(size)])  25 us
    ppermute x6, starting transfers between devices, butterfly_rounds(): lax.ppermute(value, axis, perm)  8.38 us
    convert_element_type x1, other arithmetic, on_device(): nesterov = (grad_float + MUON_DECAY * next_momentum).astype(jnp.bfloat16)  2.08 us
  transfers between devices with their start and end apart: 20, of which 13 were waited for; matrix products, arithmetic and copies ran while one was open for 3% of the time, Pallas kernels for 30%

profile of v8, /device:TPU:16, one launch (start us, length us, event | category | flops | bytes accessed | tf_op | source)
XLA Modules:
  0.0 97.4 jit_solution(10058079628415349677)
XLA Ops:
  0.7 2.1 %fusion = (bf16[4,16,2048]{2,1,0:T(8,128)(2,1)S(1)}, f32[4,16,2048]{2,1,0:T(8,128)}) fusion(bf16[4,16,2048]{2,1,0:T(8,128)(2,1)} %param.9, f32[4,16,2048]{2,1,0:T(8,128)} %param.10), kind=kLoop, calls=%fused_computation.3 | loop fusion | flops 786432 | bytes 1572864 | tf_op jit(solution)/shard_map/convert_element_type | solution.py:151
  2.8 1.6 %collective-permute-start = (bf16[1,16,2048]{2,1,0:T(8,128)(2,1)S(1)}, bf16[1,16,2048]{2,1,0:T(8,128)(2,1)S(1)}, u32[]{:S(2)}, u32[]{:S(2)}) collective-permute-start(bf16[1,16,2048]{2,1,0:T(8,128)(2,1)S(1)} %get-tuple-element.39), channel_id=1, source_target_pairs={{0,8},{8,16},{16,24},{24,0},{1,9},{9,17},{17,25},{25,1},{2,10},{10... | collective-permute-start | bytes 196616 | tf_op jit(solution)/shard_map/ppermute | solution.py:32
  4.4 2.7 %collective-permute-start.1 = (bf16[1,16,2048]{2,1,0:T(8,128)(2,1)S(1)}, bf16[1,16,2048]{2,1,0:T(8,128)(2,1)S(1)}, u32[]{:S(2)}, u32[]{:S(2)}) collective-permute-start(bf16[1,16,2048]{2,1,0:T(8,128)(2,1)S(1)} %get-tuple-element.38), channel_id=1, source_target_pairs={{0,16},{8,24},{16,0},{24,8},{1,17},{9,25},{17,1},{25,9},{2,18},{10... | collective-permute-start | bytes 196616 | tf_op jit(solution)/shard_map/ppermute | solution.py:32
  7.1 1.4 %collective-permute-start.2 = (bf16[1,16,2048]{2,1,0:T(8,128)(2,1)S(1)}, bf16[1,16,2048]{2,1,0:T(8,128)(2,1)S(1)}, u32[]{:S(2)}, u32[]{:S(2)}) collective-permute-start(bf16[1,16,2048]{2,1,0:T(8,128)(2,1)S(1)} %get-tuple-element.37), channel_id=1, source_target_pairs={{0,24},{8,0},{16,8},{24,16},{1,25},{9,1},{17,9},{25,17},{2,26},{10... | collective-permute-start | bytes 196616 | tf_op jit(solution)/shard_map/ppermute | solution.py:32
  9.0 1.4 %collective-permute-done.1 = bf16[1,16,2048]{2,1,0:T(8,128)(2,1)S(1)} collective-permute-done((bf16[1,16,2048]{2,1,0:T(8,128)(2,1)S(1)}, bf16[1,16,2048]{2,1,0:T(8,128)(2,1)S(1)}, u32[]{:S(2)}, u32[]{:S(2)}) %collective-permute-start.1) | collective-permute-done | bytes 65568 | tf_op jit(solution)/shard_map/ppermute | solution.py:32
  11.4 5.9 %collective-permute-start.3 = (bf16[1,64,2048]{2,1,0:T(8,128)(2,1)S(1)}, bf16[1,64,2048]{2,1,0:T(8,128)(2,1)S(1)}, u32[]{:S(2)}, u32[]{:S(2)}) collective-permute-start(bf16[1,64,2048]{2,1,0:T(8,128)(2,1)S(1)} %pad_maximum_fusion), channel_id=1, source_target_pairs={{0,224},{32,0},{64,32},{96,64},{128,96},{160,128},{192,160},{224,1... | collective-permute-start | bytes 786440 | tf_op jit(solution)/shard_map/ppermute | solution.py:32
  17.4 4.4 %collective-permute-done.3 = bf16[1,64,2048]{2,1,0:T(8,128)(2,1)S(1)} collective-permute-done((bf16[1,64,2048]{2,1,0:T(8,128)(2,1)S(1)}, bf16[1,64,2048]{2,1,0:T(8,128)(2,1)S(1)}, u32[]{:S(2)}, u32[]{:S(2)}) %collective-permute-start.3) | collective-permute-done | bytes 262176 | tf_op jit(solution)/shard_map/ppermute | solution.py:32
  21.8 3.7 %collective-permute-start.4 = (bf16[1,64,2048]{2,1,0:T(8,128)(2,1)S(1)}, bf16[1,64,2048]{2,1,0:T(8,128)(2,1)S(1)}, u32[]{:S(2)}, u32[]{:S(2)}) collective-permute-start(bf16[1,64,2048]{2,1,0:T(8,128)(2,1)S(1)} %collective-permute-done.3), channel_id=1, source_target_pairs={{0,224},{32,0},{64,32},{96,64},{128,96},{160,128},{192,160},{224,1... | collective-permute-start | bytes 786440 | tf_op jit(solution)/shard_map/ppermute | solution.py:32
  25.5 3.9 %collective-permute-done.4 = bf16[1,64,2048]{2,1,0:T(8,128)(2,1)S(1)} collective-permute-done((bf16[1,64,2048]{2,1,0:T(8,128)(2,1)S(1)}, bf16[1,64,2048]{2,1,0:T(8,128)(2,1)S(1)}, u32[]{:S(2)}, u32[]{:S(2)}) %collective-permute-start.4) | collective-permute-done | bytes 262176 | tf_op jit(solution)/shard_map/ppermute | solution.py:32
  29.3 3.7 %collective-permute-start.5 = (bf16[1,64,2048]{2,1,0:T(8,128)(2,1)S(1)}, bf16[1,64,2048]{2,1,0:T(8,128)(2,1)S(1)}, u32[]{:S(2)}, u32[]{:S(2)}) collective-permute-start(bf16[1,64,2048]{2,1,0:T(8,128)(2,1)S(1)} %collective-permute-done.4), channel_id=1, source_target_pairs={{0,224},{32,0},{64,32},{96,64},{128,96},{160,128},{192,160},{224,1... | collective-permute-start | bytes 786440 | tf_op jit(solution)/shard_map/ppermute | solution.py:32
  33.1 4.4 %collective-permute-done.5 = bf16[1,64,2048]{2,1,0:T(8,128)(2,1)S(1)} collective-permute-done((bf16[1,64,2048]{2,1,0:T(8,128)(2,1)S(1)}, bf16[1,64,2048]{2,1,0:T(8,128)(2,1)S(1)}, u32[]{:S(2)}, u32[]{:S(2)}) %collective-permute-start.5) | collective-permute-done | bytes 262176 | tf_op jit(solution)/shard_map/ppermute | solution.py:32
  37.5 3.8 %collective-permute-start.10 = (bf16[1,64,1024]{2,1,0:T(8,128)(2,1)S(1)}, bf16[1,64,1024]{2,1,0:T(8,128)(2,1)S(1)}, u32[]{:S(2)}, u32[]{:S(2)}) collective-permute-start(bf16[1,64,1024]{2,1,0:T(8,128)(2,1)S(1)} %slice.25), channel_id=1, source_target_pairs={{0,224},{32,0},{64,32},{96,64},{128,96},{160,128},{192,160},{224,1... | collective-permute-start | bytes 393224 | tf_op jit(solution)/shard_map/ppermute | solution.py:32
  41.5 2.3 %collective-permute-done.10 = bf16[1,64,1024]{2,1,0:T(8,128)(2,1)S(1)} collective-permute-done((bf16[1,64,1024]{2,1,0:T(8,128)(2,1)S(1)}, bf16[1,64,1024]{2,1,0:T(8,128)(2,1)S(1)}, u32[]{:S(2)}, u32[]{:S(2)}) %collective-permute-start.10) | collective-permute-done | bytes 131104 | tf_op jit(solution)/shard_map/ppermute | solution.py:32
  43.8 3.8 %collective-permute-done.9 = bf16[1,64,1024]{2,1,0:T(8,128)(2,1)S(1)} collective-permute-done((bf16[1,64,1024]{2,1,0:T(8,128)(2,1)S(1)}, bf16[1,64,1024]{2,1,0:T(8,128)(2,1)S(1)}, u32[]{:S(2)}, u32[]{:S(2)}) %collective-permute-start.9) | collective-permute-done | bytes 131104 | tf_op jit(solution)/shard_map/ppermute | solution.py:32
  49.1 6.9 %shard_map.128.iterate_ref = bf16[1,512,2048]{2,1,0:T(8,128)(2,1)} custom-call(bf16[1,512,2048]{2,1,0:T(8,128)(2,1)} %copy-done.1), custom_call_target="tpu_custom_call" | custom-call | tf_op jit(solution)/shard_map/pallas_call | solution.py:82
  56.1 5.6 %shard_map.129.iterate_ref = bf16[1,512,2048]{2,1,0:T(8,128)(2,1)} custom-call(bf16[1,512,2048]{2,1,0:T(8,128)(2,1)} %shard_map.128.iterate_ref), custom_call_target="tpu_custom_call" | custom-call | tf_op jit(solution)/shard_map/pallas_call | solution.py:82
  61.7 3.7 %collective-permute-start.14 = (f32[34,128]{1,0:T(8,128)S(1)}, f32[34,128]{1,0:T(8,128)S(1)}, u32[]{:S(2)}, u32[]{:S(2)}) collective-permute-start(f32[34,128]{1,0:T(8,128)S(1)} %add.102), channel_id=1, source_target_pairs={{0,128},{32,160},{64,192},{96,224},{128,0},{160,32},{192,64},{224,... | collective-permute-start | bytes 52232 | tf_op jit(solution)/shard_map/ppermute | solution.py:114
  65.4 5.6 %shard_map.130.iterate_ref = bf16[1,512,2048]{2,1,0:T(8,128)(2,1)} custom-call(bf16[1,512,2048]{2,1,0:T(8,128)(2,1)} %shard_map.129.iterate_ref), custom_call_target="tpu_custom_call" | custom-call | tf_op jit(solution)/shard_map/pallas_call | solution.py:82
  71.1 1.3 %collective-permute-start.15 = (f32[34,128]{1,0:T(8,128)S(1)}, f32[34,128]{1,0:T(8,128)S(1)}, u32[]{:S(2)}, u32[]{:S(2)}) collective-permute-start(f32[34,128]{1,0:T(8,128)S(1)} %add.103), channel_id=1, source_target_pairs={{0,8},{8,0},{16,24},{24,16},{1,9},{9,1},{17,25},{25,17},{2,10},{10... | collective-permute-start | bytes 52232 | tf_op jit(solution)/shard_map/ppermute | solution.py:114
  72.4 5.6 %shard_map.131.iterate_ref = bf16[1,512,2048]{2,1,0:T(8,128)(2,1)} custom-call(bf16[1,512,2048]{2,1,0:T(8,128)(2,1)} %shard_map.130.iterate_ref), custom_call_target="tpu_custom_call" | custom-call | tf_op jit(solution)/shard_map/pallas_call | solution.py:82
  78.0 3.2 %collective-permute-start.19 = (f32[34,128]{1,0:T(8,128)S(1)}, f32[34,128]{1,0:T(8,128)S(1)}, u32[]{:S(2)}, u32[]{:S(2)}) collective-permute-start(f32[34,128]{1,0:T(8,128)S(1)} %add.104), channel_id=1, source_target_pairs={{0,16},{8,24},{16,0},{24,8},{1,17},{9,25},{17,1},{25,9},{2,18},{10... | collective-permute-start | bytes 52232 | tf_op jit(solution)/shard_map/ppermute | solution.py:114
  81.2 5.7 %shard_map.132 = bf16[1,512,2048]{2,1,0:T(8,128)(2,1)} custom-call(bf16[1,512,2048]{2,1,0:T(8,128)(2,1)} %shard_map.131.iterate_ref), custom_call_target="tpu_custom_call" | custom-call | tf_op jit(solution)/shard_map/pallas_call | solution.py:82
  91.4 1.5 %collective-permute-done.16 = bf16[1,16,2048]{2,1,0:T(8,128)(2,1)S(1)} collective-permute-done((bf16[1,16,2048]{2,1,0:T(8,128)(2,1)S(1)}, bf16[1,16,2048]{2,1,0:T(8,128)(2,1)S(1)}, u32[]{:S(2)}, u32[]{:S(2)}) %collective-permute-start.16) | collective-permute-done | bytes 65568 | tf_op jit(solution)/shard_map/ppermute | solution.py:32
  92.9 2.1 %collective-permute-done.17 = bf16[1,16,2048]{2,1,0:T(8,128)(2,1)S(1)} collective-permute-done((bf16[1,16,2048]{2,1,0:T(8,128)(2,1)S(1)}, bf16[1,16,2048]{2,1,0:T(8,128)(2,1)S(1)}, u32[]{:S(2)}, u32[]{:S(2)}) %collective-permute-start.17) | collective-permute-done | bytes 65568 | tf_op jit(solution)/shard_map/ppermute | solution.py:32
  (71 shorter events, 10.2 us)
Async XLA Ops:
  0.6 8.0 %copy-start = (bf16[512,32]{0,1:T(8,128)(2,1)S(1)}, bf16[512,32]{0,1:T(8,128)(2,1)}, u32[]{:S(2)}) copy-start(bf16[512,32]{0,1:T(8,128)(2,1)} %param.15) | copy-start | bytes 98308
  0.7 8.1 %copy-start.3 = (bf16[512,128]{1,0:T(8,128)(2,1)S(1)}, bf16[512,128]{1,0:T(8,128)(2,1)}, u32[]{:S(2)}) copy-start(bf16[512,128]{1,0:T(8,128)(2,1)} %param.14) | copy-start | bytes 393220
  2.8 6.1 %collective-permute-start = (bf16[1,16,2048]{2,1,0:T(8,128)(2,1)S(1)}, bf16[1,16,2048]{2,1,0:T(8,128)(2,1)S(1)}, u32[]{:S(2)}, u32[]{:S(2)}) collective-permute-start(bf16[1,16,2048]{2,1,0:T(8,128)(2,1)S(1)} %get-tuple-element.39), channel_id=1, source_target_pairs={{0,8},{8,16},{16,24},{24,0},{1,9},{9,17},{17,25},{25,1},{2,10},{10... | collective-permute-start | bytes 196616 | tf_op jit(solution)/shard_map/ppermute | solution.py:32
  4.4 5.9 %collective-permute-start.1 = (bf16[1,16,2048]{2,1,0:T(8,128)(2,1)S(1)}, bf16[1,16,2048]{2,1,0:T(8,128)(2,1)S(1)}, u32[]{:S(2)}, u32[]{:S(2)}) collective-permute-start(bf16[1,16,2048]{2,1,0:T(8,128)(2,1)S(1)} %get-tuple-element.38), channel_id=1, source_target_pairs={{0,16},{8,24},{16,0},{24,8},{1,17},{9,25},{17,1},{25,9},{2,18},{10... | collective-permute-start | bytes 196616 | tf_op jit(solution)/shard_map/ppermute | solution.py:32
  7.1 4.3 %collective-permute-start.2 = (bf16[1,16,2048]{2,1,0:T(8,128)(2,1)S(1)}, bf16[1,16,2048]{2,1,0:T(8,128)(2,1)S(1)}, u32[]{:S(2)}, u32[]{:S(2)}) collective-permute-start(bf16[1,16,2048]{2,1,0:T(8,128)(2,1)S(1)} %get-tuple-element.37), channel_id=1, source_target_pairs={{0,24},{8,0},{16,8},{24,16},{1,25},{9,1},{17,9},{25,17},{2,26},{10... | collective-permute-start | bytes 196616 | tf_op jit(solution)/shard_map/ppermute | solution.py:32
  11.4 10.3 %collective-permute-start.3 = (bf16[1,64,2048]{2,1,0:T(8,128)(2,1)S(1)}, bf16[1,64,2048]{2,1,0:T(8,128)(2,1)S(1)}, u32[]{:S(2)}, u32[]{:S(2)}) collective-permute-start(bf16[1,64,2048]{2,1,0:T(8,128)(2,1)S(1)} %pad_maximum_fusion), channel_id=1, source_target_pairs={{0,224},{32,0},{64,32},{96,64},{128,96},{160,128},{192,160},{224,1... | collective-permute-start | bytes 786440 | tf_op jit(solution)/shard_map/ppermute | solution.py:32
  17.4 8.1 %collective-permute-start.6 = (bf16[1,64,2048]{2,1,0:T(8,128)(2,1)S(1)}, bf16[1,64,2048]{2,1,0:T(8,128)(2,1)S(1)}, u32[]{:S(2)}, u32[]{:S(2)}) collective-permute-start(bf16[1,64,2048]{2,1,0:T(8,128)(2,1)S(1)} %pad_maximum_fusion), channel_id=1, source_target_pairs={{0,32},{32,64},{64,96},{96,128},{128,160},{160,192},{192,224},{224... | collective-permute-start | bytes 786440 | tf_op jit(solution)/shard_map/ppermute | solution.py:32
  21.8 7.6 %collective-permute-start.4 = (bf16[1,64,2048]{2,1,0:T(8,128)(2,1)S(1)}, bf16[1,64,2048]{2,1,0:T(8,128)(2,1)S(1)}, u32[]{:S(2)}, u32[]{:S(2)}) collective-permute-start(bf16[1,64,2048]{2,1,0:T(8,128)(2,1)S(1)} %collective-permute-done.3), channel_id=1, source_target_pairs={{0,224},{32,0},{64,32},{96,64},{128,96},{160,128},{192,160},{224,1... | collective-permute-start | bytes 786440 | tf_op jit(solution)/shard_map/ppermute | solution.py:32
  25.5 7.6 %collective-permute-start.7 = (bf16[1,64,2048]{2,1,0:T(8,128)(2,1)S(1)}, bf16[1,64,2048]{2,1,0:T(8,128)(2,1)S(1)}, u32[]{:S(2)}, u32[]{:S(2)}) collective-permute-start(bf16[1,64,2048]{2,1,0:T(8,128)(2,1)S(1)} %collective-permute-done.6), channel_id=1, source_target_pairs={{0,32},{32,64},{64,96},{96,128},{128,160},{160,192},{192,224},{224... | collective-permute-start | bytes 786440 | tf_op jit(solution)/shard_map/ppermute | solution.py:32
  29.3 8.2 %collective-permute-start.5 = (bf16[1,64,2048]{2,1,0:T(8,128)(2,1)S(1)}, bf16[1,64,2048]{2,1,0:T(8,128)(2,1)S(1)}, u32[]{:S(2)}, u32[]{:S(2)}) collective-permute-start(bf16[1,64,2048]{2,1,0:T(8,128)(2,1)S(1)} %collective-permute-done.4), channel_id=1, source_target_pairs={{0,224},{32,0},{64,32},{96,64},{128,96},{160,128},{192,160},{224,1... | collective-permute-start | bytes 786440 | tf_op jit(solution)/shard_map/ppermute | solution.py:32
  33.0 8.4 %collective-permute-start.8 = (bf16[1,64,2048]{2,1,0:T(8,128)(2,1)S(1)}, bf16[1,64,2048]{2,1,0:T(8,128)(2,1)S(1)}, u32[]{:S(2)}, u32[]{:S(2)}) collective-permute-start(bf16[1,64,2048]{2,1,0:T(8,128)(2,1)S(1)} %collective-permute-done.7), channel_id=1, source_target_pairs={{0,32},{32,64},{64,96},{96,128},{128,160},{160,192},{192,224},{224... | collective-permute-start | bytes 786440 | tf_op jit(solution)/shard_map/ppermute | solution.py:32
  37.5 6.3 %collective-permute-start.10 = (bf16[1,64,1024]{2,1,0:T(8,128)(2,1)S(1)}, bf16[1,64,1024]{2,1,0:T(8,128)(2,1)S(1)}, u32[]{:S(2)}, u32[]{:S(2)}) collective-permute-start(bf16[1,64,1024]{2,1,0:T(8,128)(2,1)S(1)} %slice.25), channel_id=1, source_target_pairs={{0,224},{32,0},{64,32},{96,64},{128,96},{160,128},{192,160},{224,1... | collective-permute-start | bytes 393224 | tf_op jit(solution)/shard_map/ppermute | solution.py:32
  41.4 6.3 %collective-permute-start.9 = (bf16[1,64,1024]{2,1,0:T(8,128)(2,1)S(1)}, bf16[1,64,1024]{2,1,0:T(8,128)(2,1)S(1)}, u32[]{:S(2)}, u32[]{:S(2)}) collective-permute-start(bf16[1,64,1024]{2,1,0:T(8,128)(2,1)S(1)} %slice.24), channel_id=1, source_target_pairs={{0,32},{32,64},{64,96},{96,128},{128,160},{160,192},{192,224},{224... | collective-permute-start | bytes 393224 | tf_op jit(solution)/shard_map/ppermute | solution.py:32
  47.8 1.3 %collective-permute-start.11 = (f32[34,128]{1,0:T(8,128)S(1)}, f32[34,128]{1,0:T(8,128)S(1)}, u32[]{:S(2)}, u32[]{:S(2)}) collective-permute-start(f32[34,128]{1,0:T(8,128)S(1)} %pad_maximum_fusion.1), channel_id=1, source_target_pairs={{0,1},{1,0},{2,3},{3,2},{4,5},{5,4},{6,7},{7,6},{8,9},{9,8},{10,11... | collective-permute-start | bytes 52232 | tf_op jit(solution)/shard_map/ppermute | solution.py:114
  49.1 6.9 %collective-permute-start.12 = (f32[34,128]{1,0:T(8,128)S(1)}, f32[34,128]{1,0:T(8,128)S(1)}, u32[]{:S(2)}, u32[]{:S(2)}) collective-permute-start(f32[34,128]{1,0:T(8,128)S(1)} %add.100), channel_id=1, source_target_pairs={{0,32},{32,0},{64,96},{96,64},{128,160},{160,128},{192,224},{224,1... | collective-permute-start | bytes 52232 | tf_op jit(solution)/shard_map/ppermute | solution.py:114
  56.0 5.7 %collective-permute-start.13 = (f32[34,128]{1,0:T(8,128)S(1)}, f32[34,128]{1,0:T(8,128)S(1)}, u32[]{:S(2)}, u32[]{:S(2)}) collective-permute-start(f32[34,128]{1,0:T(8,128)S(1)} %add.101), channel_id=1, source_target_pairs={{0,64},{32,96},{64,0},{96,32},{128,192},{160,224},{192,128},{224,1... | collective-permute-start | bytes 52232 | tf_op jit(solution)/shard_map/ppermute | solution.py:114
  61.7 9.3 %collective-permute-start.14 = (f32[34,128]{1,0:T(8,128)S(1)}, f32[34,128]{1,0:T(8,128)S(1)}, u32[]{:S(2)}, u32[]{:S(2)}) collective-permute-start(f32[34,128]{1,0:T(8,128)S(1)} %add.102), channel_id=1, source_target_pairs={{0,128},{32,160},{64,192},{96,224},{128,0},{160,32},{192,64},{224,... | collective-permute-start | bytes 52232 | tf_op jit(solution)/shard_map/ppermute | solution.py:114
  71.1 6.9 %collective-permute-start.15 = (f32[34,128]{1,0:T(8,128)S(1)}, f32[34,128]{1,0:T(8,128)S(1)}, u32[]{:S(2)}, u32[]{:S(2)}) collective-permute-start(f32[34,128]{1,0:T(8,128)S(1)} %add.103), channel_id=1, source_target_pairs={{0,8},{8,0},{16,24},{24,16},{1,9},{9,1},{17,25},{25,17},{2,10},{10... | collective-permute-start | bytes 52232 | tf_op jit(solution)/shard_map/ppermute | solution.py:114
  78.0 12.7 %copy-start.4 = (f32[34,128]{1,0:T(8,128)S(1)}, f32[34,128]{1,0:T(8,128)}, u32[]{:S(2)}) copy-start(f32[34,128]{1,0:T(8,128)} %param.17) | copy-start | bytes 52228
  78.0 12.7 %copy-start.5 = (f32[34,128]{1,0:T(8,128)S(1)}, f32[34,128]{1,0:T(8,128)}, u32[]{:S(2)}) copy-start(f32[34,128]{1,0:T(8,128)} %param.16) | copy-start | bytes 52228
  78.0 12.7 %collective-permute-start.19 = (f32[34,128]{1,0:T(8,128)S(1)}, f32[34,128]{1,0:T(8,128)S(1)}, u32[]{:S(2)}, u32[]{:S(2)}) collective-permute-start(f32[34,128]{1,0:T(8,128)S(1)} %add.104), channel_id=1, source_target_pairs={{0,16},{8,24},{16,0},{24,8},{1,17},{9,25},{17,1},{25,9},{2,18},{10... | collective-permute-start | bytes 52232 | tf_op jit(solution)/shard_map/ppermute | solution.py:114
  88.6 4.3 %collective-permute-start.16 = (bf16[1,16,2048]{2,1,0:T(8,128)(2,1)S(1)}, bf16[1,16,2048]{2,1,0:T(8,128)(2,1)S(1)}, u32[]{:S(2)}, u32[]{:S(2)}) collective-permute-start(bf16[1,16,2048]{2,1,0:T(8,128)(2,1)S(1)} %get-tuple-element.36), channel_id=1, source_target_pairs={{0,24},{8,0},{16,8},{24,16},{1,25},{9,1},{17,9},{25,17},{2,26},{10... | collective-permute-start | bytes 196616 | tf_op jit(solution)/shard_map/ppermute | solution.py:32
  89.2 5.8 %collective-permute-start.17 = (bf16[1,16,2048]{2,1,0:T(8,128)(2,1)S(1)}, bf16[1,16,2048]{2,1,0:T(8,128)(2,1)S(1)}, u32[]{:S(2)}, u32[]{:S(2)}) collective-permute-start(bf16[1,16,2048]{2,1,0:T(8,128)(2,1)S(1)} %get-tuple-element.35), channel_id=1, source_target_pairs={{0,16},{8,24},{16,0},{24,8},{1,17},{9,25},{17,1},{25,9},{2,18},{10... | collective-permute-start | bytes 196616 | tf_op jit(solution)/shard_map/ppermute | solution.py:32
  90.1 5.6 %collective-permute-start.18 = (bf16[1,16,2048]{2,1,0:T(8,128)(2,1)S(1)}, bf16[1,16,2048]{2,1,0:T(8,128)(2,1)S(1)}, u32[]{:S(2)}, u32[]{:S(2)}) collective-permute-start(bf16[1,16,2048]{2,1,0:T(8,128)(2,1)S(1)} %get-tuple-element.34), channel_id=1, source_target_pairs={{0,8},{8,16},{16,24},{24,0},{1,9},{9,17},{17,25},{25,1},{2,10},{10... | collective-permute-start | bytes 196616 | tf_op jit(solution)/shard_map/ppermute | solution.py:32
  (4 other events, 25.1 us)

commit v9 on v5

--- a/solution.py
+++ b/solution.py
@@ -49,7 +49,7 @@
     return jnp.concatenate([strip] + ahead + behind[::-1], axis=1)
 
 
-def orthogonalize(blocks, carried, rounds):
+def orthogonalize(blocks, carried, rounds, keep):
     squares = jnp.sum(jnp.square(blocks.astype(jnp.float32)), axis=(1, 2))
     total = jnp.sqrt(squares)
     iterate = (blocks.astype(jnp.float32) / (total + NORM_EPSILON)[:, None, None]).astype(
@@ -61,12 +61,15 @@
             carried = step(carried)
         gram = jnp.einsum("kij,klj->kil", iterate, iterate, preferred_element_type=jnp.float32)
         gram_half = gram.astype(jnp.bfloat16)
+        rows = keep if repeat == ITERS - 1 else iterate.shape[1]
         square_term = jnp.einsum(
-            "kij,kjl->kil", gram_half, gram_half, preferred_element_type=jnp.float32
+            "kij,kjl->kil", gram_half[:, :rows], gram_half, preferred_element_type=jnp.float32
         )
-        poly = (CUBIC_TERM * gram + QUINTIC_TERM * square_term).astype(jnp.bfloat16)
+        poly = (CUBIC_TERM * gram[:, :rows] + QUINTIC_TERM * square_term).astype(jnp.bfloat16)
         product = jnp.einsum("kij,kjl->kil", poly, iterate, preferred_element_type=jnp.float32)
-        iterate = (LINEAR_TERM * iterate.astype(jnp.float32) + product).astype(jnp.bfloat16)
+        iterate = (LINEAR_TERM * iterate[:, :rows].astype(jnp.float32) + product).astype(
+            jnp.bfloat16
+        )
     for group in rounds[ITERS:]:
         for step in group:
             carried = step(carried)
@@ -134,7 +137,7 @@
     local = vector_partials(normed, ln_gain, ln_bias, ln_cotangent, router_cotangent)
     steps = [step for axis in ("section",) + SHARD for step in butterfly_rounds(axis)]
     rounds = [steps[:2]] + [[step] for step in steps[2:]]
-    result, vec_grad = orthogonalize(blocks, local, rounds)
+    result, vec_grad = orthogonalize(blocks, local, rounds, inner * rows_piece)
     next_first, next_second, adam_step = adam(vec_grad, first_moment, second_moment)
     back = jnp.stack(
         [shift(result[:, k * rows_piece:(k + 1) * rows_piece], "inner", -k) for k in range(inner)],

time: 97.4 us -> 94.4 us (0.969)
  matrix products: 29.6 us -> 26 us
    dot_general x5, matrix products: 13.1 us -> 10.8 us  [orthogonalize(): jnp.einsum('kij,klj->kil', iterate, iterate, preferred_element_type=jnp.f...]
    dot_general x5, matrix products: 16.4 us -> 15 us  [orthogonalize(): jnp.einsum('kij,kjl->kil', poly, iterate, preferred_element_type=jnp.floa...]
  transfers between devices with their start and end apart: 20 -> 20, of which waited for: 14 -> 14; matrix products, arithmetic and copies ran while one was open for 24% -> 26% of each run, Pallas kernels for 0% -> 0%
where the time goes in v9:
time: 94.4 us; the launch traced here: 94.2 us
  starting transfers between devices  33 us (35%)
  waiting for transfers between devices  26.6 us (28%)
  matrix products  26 us (28%)
  other arithmetic  6.67 us (7%)
  between operations  1.75 us (2%)
    ppermute x14, waiting for transfers between devices, shift(): return lax.ppermute(value, axis, [(i, (i + k) % size) for i in range(size)])  25.8 us
    ppermute x14, starting transfers between devices, shift(): return lax.ppermute(value, axis, [(i, (i + k) % size) for i in range(size)])  25 us
    dot_general x5, matrix products, orthogonalize(): jnp.einsum('kij,kjl->kil', poly, iterate, preferred_element_type=jnp.floa...  15 us
    dot_general x5, matrix products, orthogonalize(): jnp.einsum('kij,klj->kil', iterate, iterate, preferred_element_type=jnp.f...  10.8 us
    ppermute x6, starting transfers between devices, butterfly_rounds(): lax.ppermute(value, axis, perm)  7.97 us
    convert_element_type x1, other arithmetic, on_device(): nesterov = (grad_float + MUON_DECAY * next_momentum).astype(jnp.bfloat16)  2.08 us
  transfers between devices with their start and end apart: 20, of which 14 were waited for; matrix products, arithmetic and copies ran while one was open for 26% of the time, Pallas kernels for 0%

profile of v9, /device:TPU:16, one launch (start us, length us, event | category | flops | bytes accessed | tf_op | source)
XLA Modules:
  0.0 94.2 jit_solution(16738011733695660181)
XLA Ops:
  0.7 2.1 %fusion.35 = (bf16[4,16,2048]{2,1,0:T(8,128)(2,1)S(1)}, f32[4,16,2048]{2,1,0:T(8,128)}) fusion(bf16[4,16,2048]{2,1,0:T(8,128)(2,1)} %param.9, f32[4,16,2048]{2,1,0:T(8,128)} %param.10), kind=kLoop, calls=%fused_computation.50 | loop fusion | flops 786432 | bytes 1572864 | tf_op jit(solution)/shard_map/convert_element_type | solution.py:124
  2.9 1.6 %collective-permute-start = (bf16[1,16,2048]{2,1,0:T(8,128)(2,1)S(1)}, bf16[1,16,2048]{2,1,0:T(8,128)(2,1)S(1)}, u32[]{:S(2)}, u32[]{:S(2)}) collective-permute-start(bf16[1,16,2048]{2,1,0:T(8,128)(2,1)S(1)} %get-tuple-element.39), channel_id=1, source_target_pairs={{0,8},{8,16},{16,24},{24,0},{1,9},{9,17},{17,25},{25,1},{2,10},{10... | collective-permute-start | bytes 196616 | tf_op jit(solution)/shard_map/ppermute | solution.py:30
  4.4 2.7 %collective-permute-start.1 = (bf16[1,16,2048]{2,1,0:T(8,128)(2,1)S(1)}, bf16[1,16,2048]{2,1,0:T(8,128)(2,1)S(1)}, u32[]{:S(2)}, u32[]{:S(2)}) collective-permute-start(bf16[1,16,2048]{2,1,0:T(8,128)(2,1)S(1)} %get-tuple-element.38), channel_id=1, source_target_pairs={{0,16},{8,24},{16,0},{24,8},{1,17},{9,25},{17,1},{25,9},{2,18},{10... | collective-permute-start | bytes 196616 | tf_op jit(solution)/shard_map/ppermute | solution.py:30
  7.1 1.4 %collective-permute-start.2 = (bf16[1,16,2048]{2,1,0:T(8,128)(2,1)S(1)}, bf16[1,16,2048]{2,1,0:T(8,128)(2,1)S(1)}, u32[]{:S(2)}, u32[]{:S(2)}) collective-permute-start(bf16[1,16,2048]{2,1,0:T(8,128)(2,1)S(1)} %get-tuple-element.37), channel_id=1, source_target_pairs={{0,24},{8,0},{16,8},{24,16},{1,25},{9,1},{17,9},{25,17},{2,26},{10... | collective-permute-start | bytes 196616 | tf_op jit(solution)/shard_map/ppermute | solution.py:30
  11.4 5.9 %collective-permute-start.3 = (bf16[1,64,2048]{2,1,0:T(8,128)(2,1)S(1)}, bf16[1,64,2048]{2,1,0:T(8,128)(2,1)S(1)}, u32[]{:S(2)}, u32[]{:S(2)}) collective-permute-start(bf16[1,64,2048]{2,1,0:T(8,128)(2,1)S(1)} %pad_maximum_fusion), channel_id=1, source_target_pairs={{0,224},{32,0},{64,32},{96,64},{128,96},{160,128},{192,160},{224,1... | collective-permute-start | bytes 786440 | tf_op jit(solution)/shard_map/ppermute | solution.py:30
  17.4 4.3 %collective-permute-done.3 = bf16[1,64,2048]{2,1,0:T(8,128)(2,1)S(1)} collective-permute-done((bf16[1,64,2048]{2,1,0:T(8,128)(2,1)S(1)}, bf16[1,64,2048]{2,1,0:T(8,128)(2,1)S(1)}, u32[]{:S(2)}, u32[]{:S(2)}) %collective-permute-start.3) | collective-permute-done | bytes 262176 | tf_op jit(solution)/shard_map/ppermute | solution.py:30
  21.8 3.7 %collective-permute-start.4 = (bf16[1,64,2048]{2,1,0:T(8,128)(2,1)S(1)}, bf16[1,64,2048]{2,1,0:T(8,128)(2,1)S(1)}, u32[]{:S(2)}, u32[]{:S(2)}) collective-permute-start(bf16[1,64,2048]{2,1,0:T(8,128)(2,1)S(1)} %collective-permute-done.3), channel_id=1, source_target_pairs={{0,224},{32,0},{64,32},{96,64},{128,96},{160,128},{192,160},{224,1... | collective-permute-start | bytes 786440 | tf_op jit(solution)/shard_map/ppermute | solution.py:30
  25.5 3.9 %collective-permute-done.4 = bf16[1,64,2048]{2,1,0:T(8,128)(2,1)S(1)} collective-permute-done((bf16[1,64,2048]{2,1,0:T(8,128)(2,1)S(1)}, bf16[1,64,2048]{2,1,0:T(8,128)(2,1)S(1)}, u32[]{:S(2)}, u32[]{:S(2)}) %collective-permute-start.4) | collective-permute-done | bytes 262176 | tf_op jit(solution)/shard_map/ppermute | solution.py:30
  29.3 3.7 %collective-permute-start.5 = (bf16[1,64,2048]{2,1,0:T(8,128)(2,1)S(1)}, bf16[1,64,2048]{2,1,0:T(8,128)(2,1)S(1)}, u32[]{:S(2)}, u32[]{:S(2)}) collective-permute-start(bf16[1,64,2048]{2,1,0:T(8,128)(2,1)S(1)} %collective-permute-done.4), channel_id=1, source_target_pairs={{0,224},{32,0},{64,32},{96,64},{128,96},{160,128},{192,160},{224,1... | collective-permute-start | bytes 786440 | tf_op jit(solution)/shard_map/ppermute | solution.py:30
  33.1 4.4 %collective-permute-done.5 = bf16[1,64,2048]{2,1,0:T(8,128)(2,1)S(1)} collective-permute-done((bf16[1,64,2048]{2,1,0:T(8,128)(2,1)S(1)}, bf16[1,64,2048]{2,1,0:T(8,128)(2,1)S(1)}, u32[]{:S(2)}, u32[]{:S(2)}) %collective-permute-start.5) | collective-permute-done | bytes 262176 | tf_op jit(solution)/shard_map/ppermute | solution.py:30
  37.5 3.8 %collective-permute-start.10 = (bf16[1,64,1024]{2,1,0:T(8,128)(2,1)S(1)}, bf16[1,64,1024]{2,1,0:T(8,128)(2,1)S(1)}, u32[]{:S(2)}, u32[]{:S(2)}) collective-permute-start(bf16[1,64,1024]{2,1,0:T(8,128)(2,1)S(1)} %slice.37), channel_id=1, source_target_pairs={{0,224},{32,0},{64,32},{96,64},{128,96},{160,128},{192,160},{224,1... | collective-permute-start | bytes 393224 | tf_op jit(solution)/shard_map/ppermute | solution.py:30
  41.5 2.3 %collective-permute-done.10 = bf16[1,64,1024]{2,1,0:T(8,128)(2,1)S(1)} collective-permute-done((bf16[1,64,1024]{2,1,0:T(8,128)(2,1)S(1)}, bf16[1,64,1024]{2,1,0:T(8,128)(2,1)S(1)}, u32[]{:S(2)}, u32[]{:S(2)}) %collective-permute-start.10) | collective-permute-done | bytes 131104 | tf_op jit(solution)/shard_map/ppermute | solution.py:30
  43.8 3.8 %collective-permute-done.9 = bf16[1,64,1024]{2,1,0:T(8,128)(2,1)S(1)} collective-permute-done((bf16[1,64,1024]{2,1,0:T(8,128)(2,1)S(1)}, bf16[1,64,1024]{2,1,0:T(8,128)(2,1)S(1)}, u32[]{:S(2)}, u32[]{:S(2)}) %collective-permute-start.9) | collective-permute-done | bytes 131104 | tf_op jit(solution)/shard_map/ppermute | solution.py:30
  47.8 1.7 %fusion = f32[]{:T(128)} fusion(bf16[1,512,2048]{2,1,0:T(8,128)(2,1)S(1)} %constant_dynamic-update-slice_fusion), kind=kLoop, calls=%fused_computation.2 | loop fusion | flops 3145727 | bytes 2097156 | tf_op jit(solution)/shard_map/reduce_sum | solution.py:53
  52.3 3.8 %fusion.5 = bf16[1,512,2048]{2,1,0:T(8,128)(2,1)S(1)} fusion(bf16[1,512,2048]{2,1,0:T(8,128)(2,1)} %copy-done.1, f32[512,512]{1,0:T(8,128)S(1)} %fusion.21), kind=kOutput, calls=%fused_computation.11 | convolution fusion | flops 1347682304 | bytes 5242880 | tf_op jit(solution)/shard_map/kij,kjl->kil/dot_general | solution.py:69
  57.5 2.9 %fusion.4 = bf16[1,512,2048]{2,1,0:T(8,128)(2,1)} fusion(bf16[1,512,2048]{2,1,0:T(8,128)(2,1)S(1)} %fusion.5, f32[512,512]{1,0:T(8,128)S(1)} %fusion.18), kind=kOutput, calls=%fused_computation.9 | convolution fusion | flops 1347682304 | bytes 5242880 | tf_op jit(solution)/shard_map/kij,kjl->kil/dot_general | solution.py:69
  60.9 3.2 %collective-permute-start.14 = (f32[34,128]{1,0:T(8,128)S(1)}, f32[34,128]{1,0:T(8,128)S(1)}, u32[]{:S(2)}, u32[]{:S(2)}) collective-permute-start(f32[34,128]{1,0:T(8,128)S(1)} %add.143), channel_id=1, source_target_pairs={{0,128},{32,160},{64,192},{96,224},{128,0},{160,32},{192,64},{224,... | collective-permute-start | bytes 52232 | tf_op jit(solution)/shard_map/ppermute | solution.py:87
  64.1 3.5 %fusion.15 = f32[512,512]{1,0:T(8,128)S(1)} fusion(bf16[1,512,2048]{2,1,0:T(8,128)(2,1)} %fusion.4), kind=kOutput, calls=%fused_computation.22 | convolution fusion | flops 1073741824 | bytes 3145728 | tf_op jit(solution)/shard_map/kij,klj->kil/dot_general | solution.py:62
  67.7 2.9 %fusion.3 = bf16[1,512,2048]{2,1,0:T(8,128)(2,1)} fusion(bf16[1,512,2048]{2,1,0:T(8,128)(2,1)S(1)} %copy-done.8, f32[512,512]{1,0:T(8,128)S(1)} %fusion.15), kind=kOutput, calls=%fused_computation.7 | convolution fusion | flops 1347682304 | bytes 5242880 | tf_op jit(solution)/shard_map/kij,kjl->kil/dot_general | solution.py:69
  71.9 3.5 %fusion.12 = f32[512,512]{1,0:T(8,128)S(1)} fusion(bf16[1,512,2048]{2,1,0:T(8,128)(2,1)} %fusion.3), kind=kOutput, calls=%fused_computation.19 | convolution fusion | flops 1073741824 | bytes 3145728 | tf_op jit(solution)/shard_map/kij,klj->kil/dot_general | solution.py:62
  75.4 3.8 %fusion.2 = bf16[1,512,2048]{2,1,0:T(8,128)(2,1)S(1)} fusion(bf16[1,512,2048]{2,1,0:T(8,128)(2,1)} %fusion.3, f32[512,512]{1,0:T(8,128)S(1)} %fusion.12), kind=kOutput, calls=%fused_computation.5 | convolution fusion | flops 1347682304 | bytes 5242880 | tf_op jit(solution)/shard_map/kij,kjl->kil/dot_general | solution.py:69
  81.4 1.5 %fusion.7 = bf16[1,64,2048]{2,1,0:T(8,128)(2,1)S(1)} fusion(bf16[1,512,2048]{2,1,0:T(8,128)(2,1)S(1)} %fusion.2, f32[512,512]{1,0:T(8,128)S(1)} %fusion.9, f32[1,512,512]{2,1,0:T(8,128)S(1)} %bitcast.90, bf16[1,512,512]{2,1,0:T(8,128)(2,1)} %convert_bitcast_fusion), kind=kOutput, calls=%fused_computation.14 | convolution fusion | flops 168689664 | bytes 3866624 | tf_op jit(solution)/shard_map/kij,kjl->kil/dot_general | solution.py:69
  83.0 3.0 %collective-permute-start.19 = (f32[34,128]{1,0:T(8,128)S(1)}, f32[34,128]{1,0:T(8,128)S(1)}, u32[]{:S(2)}, u32[]{:S(2)}) collective-permute-start(f32[34,128]{1,0:T(8,128)S(1)} %add.149), channel_id=1, source_target_pairs={{0,16},{8,24},{16,0},{24,8},{1,17},{9,25},{17,1},{25,9},{2,18},{10... | collective-permute-start | bytes 52232 | tf_op jit(solution)/shard_map/ppermute | solution.py:87
  90.2 2.5 %collective-permute-done.17 = bf16[1,16,2048]{2,1,0:T(8,128)(2,1)S(1)} collective-permute-done((bf16[1,16,2048]{2,1,0:T(8,128)(2,1)S(1)}, bf16[1,16,2048]{2,1,0:T(8,128)(2,1)S(1)}, u32[]{:S(2)}, u32[]{:S(2)}) %collective-permute-start.17) | collective-permute-done | bytes 65568 | tf_op jit(solution)/shard_map/ppermute | solution.py:30
  (81 shorter events, 16.4 us)
Async XLA Ops:
  0.6 8.0 %copy-start = (bf16[512,32]{0,1:T(8,128)(2,1)S(1)}, bf16[512,32]{0,1:T(8,128)(2,1)}, u32[]{:S(2)}) copy-start(bf16[512,32]{0,1:T(8,128)(2,1)} %param.15) | copy-start | bytes 98308
  0.6 7.9 %copy-start.2 = (bf16[512,128]{1,0:T(8,128)(2,1)S(1)}, bf16[512,128]{1,0:T(8,128)(2,1)}, u32[]{:S(2)}) copy-start(bf16[512,128]{1,0:T(8,128)(2,1)} %param.11) | copy-start | bytes 393220
  0.7 7.9 %copy-start.6 = (f32[128]{0:T(128)S(1)}, f32[128]{0:T(128)}, u32[]{:S(2)}) copy-start(f32[128]{0:T(128)} %param.13) | copy-start | bytes 1540
  0.7 8.1 %copy-start.3 = (bf16[512,128]{1,0:T(8,128)(2,1)S(1)}, bf16[512,128]{1,0:T(8,128)(2,1)}, u32[]{:S(2)}) copy-start(bf16[512,128]{1,0:T(8,128)(2,1)} %param.14) | copy-start | bytes 393220
  2.9 6.1 %collective-permute-start = (bf16[1,16,2048]{2,1,0:T(8,128)(2,1)S(1)}, bf16[1,16,2048]{2,1,0:T(8,128)(2,1)S(1)}, u32[]{:S(2)}, u32[]{:S(2)}) collective-permute-start(bf16[1,16,2048]{2,1,0:T(8,128)(2,1)S(1)} %get-tuple-element.39), channel_id=1, source_target_pairs={{0,8},{8,16},{16,24},{24,0},{1,9},{9,17},{17,25},{25,1},{2,10},{10... | collective-permute-start | bytes 196616 | tf_op jit(solution)/shard_map/ppermute | solution.py:30
  4.4 5.9 %collective-permute-start.1 = (bf16[1,16,2048]{2,1,0:T(8,128)(2,1)S(1)}, bf16[1,16,2048]{2,1,0:T(8,128)(2,1)S(1)}, u32[]{:S(2)}, u32[]{:S(2)}) collective-permute-start(bf16[1,16,2048]{2,1,0:T(8,128)(2,1)S(1)} %get-tuple-element.38), channel_id=1, source_target_pairs={{0,16},{8,24},{16,0},{24,8},{1,17},{9,25},{17,1},{25,9},{2,18},{10... | collective-permute-start | bytes 196616 | tf_op jit(solution)/shard_map/ppermute | solution.py:30
  7.1 4.3 %collective-permute-start.2 = (bf16[1,16,2048]{2,1,0:T(8,128)(2,1)S(1)}, bf16[1,16,2048]{2,1,0:T(8,128)(2,1)S(1)}, u32[]{:S(2)}, u32[]{:S(2)}) collective-permute-start(bf16[1,16,2048]{2,1,0:T(8,128)(2,1)S(1)} %get-tuple-element.37), channel_id=1, source_target_pairs={{0,24},{8,0},{16,8},{24,16},{1,25},{9,1},{17,9},{25,17},{2,26},{10... | collective-permute-start | bytes 196616 | tf_op jit(solution)/shard_map/ppermute | solution.py:30
  11.4 10.3 %collective-permute-start.3 = (bf16[1,64,2048]{2,1,0:T(8,128)(2,1)S(1)}, bf16[1,64,2048]{2,1,0:T(8,128)(2,1)S(1)}, u32[]{:S(2)}, u32[]{:S(2)}) collective-permute-start(bf16[1,64,2048]{2,1,0:T(8,128)(2,1)S(1)} %pad_maximum_fusion), channel_id=1, source_target_pairs={{0,224},{32,0},{64,32},{96,64},{128,96},{160,128},{192,160},{224,1... | collective-permute-start | bytes 786440 | tf_op jit(solution)/shard_map/ppermute | solution.py:30
  17.4 8.1 %collective-permute-start.6 = (bf16[1,64,2048]{2,1,0:T(8,128)(2,1)S(1)}, bf16[1,64,2048]{2,1,0:T(8,128)(2,1)S(1)}, u32[]{:S(2)}, u32[]{:S(2)}) collective-permute-start(bf16[1,64,2048]{2,1,0:T(8,128)(2,1)S(1)} %pad_maximum_fusion), channel_id=1, source_target_pairs={{0,32},{32,64},{64,96},{96,128},{128,160},{160,192},{192,224},{224... | collective-permute-start | bytes 786440 | tf_op jit(solution)/shard_map/ppermute | solution.py:30
  21.8 7.6 %collective-permute-start.4 = (bf16[1,64,2048]{2,1,0:T(8,128)(2,1)S(1)}, bf16[1,64,2048]{2,1,0:T(8,128)(2,1)S(1)}, u32[]{:S(2)}, u32[]{:S(2)}) collective-permute-start(bf16[1,64,2048]{2,1,0:T(8,128)(2,1)S(1)} %collective-permute-done.3), channel_id=1, source_target_pairs={{0,224},{32,0},{64,32},{96,64},{128,96},{160,128},{192,160},{224,1... | collective-permute-start | bytes 786440 | tf_op jit(solution)/shard_map/ppermute | solution.py:30
  25.5 7.6 %collective-permute-start.7 = (bf16[1,64,2048]{2,1,0:T(8,128)(2,1)S(1)}, bf16[1,64,2048]{2,1,0:T(8,128)(2,1)S(1)}, u32[]{:S(2)}, u32[]{:S(2)}) collective-permute-start(bf16[1,64,2048]{2,1,0:T(8,128)(2,1)S(1)} %collective-permute-done.6), channel_id=1, source_target_pairs={{0,32},{32,64},{64,96},{96,128},{128,160},{160,192},{192,224},{224... | collective-permute-start | bytes 786440 | tf_op jit(solution)/shard_map/ppermute | solution.py:30
  29.3 8.2 %collective-permute-start.5 = (bf16[1,64,2048]{2,1,0:T(8,128)(2,1)S(1)}, bf16[1,64,2048]{2,1,0:T(8,128)(2,1)S(1)}, u32[]{:S(2)}, u32[]{:S(2)}) collective-permute-start(bf16[1,64,2048]{2,1,0:T(8,128)(2,1)S(1)} %collective-permute-done.4), channel_id=1, source_target_pairs={{0,224},{32,0},{64,32},{96,64},{128,96},{160,128},{192,160},{224,1... | collective-permute-start | bytes 786440 | tf_op jit(solution)/shard_map/ppermute | solution.py:30
  33.0 8.4 %collective-permute-start.8 = (bf16[1,64,2048]{2,1,0:T(8,128)(2,1)S(1)}, bf16[1,64,2048]{2,1,0:T(8,128)(2,1)S(1)}, u32[]{:S(2)}, u32[]{:S(2)}) collective-permute-start(bf16[1,64,2048]{2,1,0:T(8,128)(2,1)S(1)} %collective-permute-done.7), channel_id=1, source_target_pairs={{0,32},{32,64},{64,96},{96,128},{128,160},{160,192},{192,224},{224... | collective-permute-start | bytes 786440 | tf_op jit(solution)/shard_map/ppermute | solution.py:30
  37.5 6.3 %collective-permute-start.10 = (bf16[1,64,1024]{2,1,0:T(8,128)(2,1)S(1)}, bf16[1,64,1024]{2,1,0:T(8,128)(2,1)S(1)}, u32[]{:S(2)}, u32[]{:S(2)}) collective-permute-start(bf16[1,64,1024]{2,1,0:T(8,128)(2,1)S(1)} %slice.37), channel_id=1, source_target_pairs={{0,224},{32,0},{64,32},{96,64},{128,96},{160,128},{192,160},{224,1... | collective-permute-start | bytes 393224 | tf_op jit(solution)/shard_map/ppermute | solution.py:30
  41.4 6.3 %collective-permute-start.9 = (bf16[1,64,1024]{2,1,0:T(8,128)(2,1)S(1)}, bf16[1,64,1024]{2,1,0:T(8,128)(2,1)S(1)}, u32[]{:S(2)}, u32[]{:S(2)}) collective-permute-start(bf16[1,64,1024]{2,1,0:T(8,128)(2,1)S(1)} %slice.36), channel_id=1, source_target_pairs={{0,32},{32,64},{64,96},{96,128},{128,160},{160,192},{192,224},{224... | collective-permute-start | bytes 393224 | tf_op jit(solution)/shard_map/ppermute | solution.py:30
  50.6 1.4 %collective-permute-start.11 = (f32[34,128]{1,0:T(8,128)S(1)}, f32[34,128]{1,0:T(8,128)S(1)}, u32[]{:S(2)}, u32[]{:S(2)}) collective-permute-start(f32[34,128]{1,0:T(8,128)S(1)} %pad_maximum_fusion.1), channel_id=1, source_target_pairs={{0,1},{1,0},{2,3},{3,2},{4,5},{5,4},{6,7},{7,6},{8,9},{9,8},{10,11... | collective-permute-start | bytes 52232 | tf_op jit(solution)/shard_map/ppermute | solution.py:87
  52.0 4.1 %collective-permute-start.12 = (f32[34,128]{1,0:T(8,128)S(1)}, f32[34,128]{1,0:T(8,128)S(1)}, u32[]{:S(2)}, u32[]{:S(2)}) collective-permute-start(f32[34,128]{1,0:T(8,128)S(1)} %add.139), channel_id=1, source_target_pairs={{0,32},{32,0},{64,96},{96,64},{128,160},{160,128},{192,224},{224,1... | collective-permute-start | bytes 52232 | tf_op jit(solution)/shard_map/ppermute | solution.py:87
  56.1 4.8 %collective-permute-start.13 = (f32[34,128]{1,0:T(8,128)S(1)}, f32[34,128]{1,0:T(8,128)S(1)}, u32[]{:S(2)}, u32[]{:S(2)}) collective-permute-start(f32[34,128]{1,0:T(8,128)S(1)} %add.140), channel_id=1, source_target_pairs={{0,64},{32,96},{64,0},{96,32},{128,192},{160,224},{192,128},{224,1... | collective-permute-start | bytes 52232 | tf_op jit(solution)/shard_map/ppermute | solution.py:87
  60.9 9.7 %collective-permute-start.14 = (f32[34,128]{1,0:T(8,128)S(1)}, f32[34,128]{1,0:T(8,128)S(1)}, u32[]{:S(2)}, u32[]{:S(2)}) collective-permute-start(f32[34,128]{1,0:T(8,128)S(1)} %add.143), channel_id=1, source_target_pairs={{0,128},{32,160},{64,192},{96,224},{128,0},{160,32},{192,64},{224,... | collective-permute-start | bytes 52232 | tf_op jit(solution)/shard_map/ppermute | solution.py:87
  70.6 8.6 %collective-permute-start.15 = (f32[34,128]{1,0:T(8,128)S(1)}, f32[34,128]{1,0:T(8,128)S(1)}, u32[]{:S(2)}, u32[]{:S(2)}) collective-permute-start(f32[34,128]{1,0:T(8,128)S(1)} %add.146), channel_id=1, source_target_pairs={{0,8},{8,0},{16,24},{24,16},{1,9},{9,1},{17,25},{25,17},{2,10},{10... | collective-permute-start | bytes 52232 | tf_op jit(solution)/shard_map/ppermute | solution.py:87
  83.0 5.4 %collective-permute-start.19 = (f32[34,128]{1,0:T(8,128)S(1)}, f32[34,128]{1,0:T(8,128)S(1)}, u32[]{:S(2)}, u32[]{:S(2)}) collective-permute-start(f32[34,128]{1,0:T(8,128)S(1)} %add.149), channel_id=1, source_target_pairs={{0,16},{8,24},{16,0},{24,8},{1,17},{9,25},{17,1},{25,9},{2,18},{10... | collective-permute-start | bytes 52232 | tf_op jit(solution)/shard_map/ppermute | solution.py:87
  85.9 4.3 %collective-permute-start.16 = (bf16[1,16,2048]{2,1,0:T(8,128)(2,1)S(1)}, bf16[1,16,2048]{2,1,0:T(8,128)(2,1)S(1)}, u32[]{:S(2)}, u32[]{:S(2)}) collective-permute-start(bf16[1,16,2048]{2,1,0:T(8,128)(2,1)S(1)} %get-tuple-element.36), channel_id=1, source_target_pairs={{0,24},{8,0},{16,8},{24,16},{1,25},{9,1},{17,9},{25,17},{2,26},{10... | collective-permute-start | bytes 196616 | tf_op jit(solution)/shard_map/ppermute | solution.py:30
  86.5 6.2 %collective-permute-start.17 = (bf16[1,16,2048]{2,1,0:T(8,128)(2,1)S(1)}, bf16[1,16,2048]{2,1,0:T(8,128)(2,1)S(1)}, u32[]{:S(2)}, u32[]{:S(2)}) collective-permute-start(bf16[1,16,2048]{2,1,0:T(8,128)(2,1)S(1)} %get-tuple-element.35), channel_id=1, source_target_pairs={{0,16},{8,24},{16,0},{24,8},{1,17},{9,25},{17,1},{25,9},{2,18},{10... | collective-permute-start | bytes 196616 | tf_op jit(solution)/shard_map/ppermute | solution.py:30
  87.4 5.9 %collective-permute-start.18 = (bf16[1,16,2048]{2,1,0:T(8,128)(2,1)S(1)}, bf16[1,16,2048]{2,1,0:T(8,128)(2,1)S(1)}, u32[]{:S(2)}, u32[]{:S(2)}) collective-permute-start(bf16[1,16,2048]{2,1,0:T(8,128)(2,1)S(1)} %get-tuple-element.34), channel_id=1, source_target_pairs={{0,8},{8,16},{16,24},{24,0},{1,9},{9,17},{17,25},{25,1},{2,10},{10... | collective-permute-start | bytes 196616 | tf_op jit(solution)/shard_map/ppermute | solution.py:30
  (5 other events, 29.9 us)

commit v10 on v9

--- a/solution.py
+++ b/solution.py
@@ -47,6 +47,38 @@
         ahead.append(from_ahead)
         behind.append(from_behind)
     return jnp.concatenate([strip] + ahead + behind[::-1], axis=1)
+
+
+EXTRA_ROWS = 8
+
+
+def encode(value, like):
+    flat = value.reshape(-1)
+    high = flat.astype(jnp.bfloat16)
+    low = (flat - high.astype(jnp.float32)).astype(jnp.bfloat16)
+    slots, _, cols = like.shape
+    room = EXTRA_ROWS * cols - 2 * flat.size
+    packed = jnp.concatenate([high, low, jnp.zeros((room,), jnp.bfloat16)])
+    return jnp.broadcast_to(packed.reshape(1, EXTRA_ROWS, cols), (slots, EXTRA_ROWS, cols))
+
+
+def decode(rows, shape):
+    flat = rows[0].reshape(-1)
+    size = math.prod(shape)
+    high = flat[:size].astype(jnp.float32)
+    low = flat[size:2 * size].astype(jnp.float32)
+    return (high + low).reshape(shape)
+
+
+def ordered_sum(by_offset, axis):
+    size = lax.axis_size(axis)
+    stacked = jnp.stack(by_offset, axis=0)
+    place = (jnp.arange(size) - lax.axis_index(axis)) % size
+    in_order = jnp.take(stacked, place, axis=0)
+    total = in_order[0]
+    for index in range(1, size):
+        total = total + in_order[index]
+    return total
 
 
 def orthogonalize(blocks, carried, rounds, keep):
@@ -128,16 +160,28 @@
     padded = jnp.pad(nesterov, ((0, slots * inner - count_all), (0, 0), (0, 0)))
     by_owner = padded.reshape(inner, slots, rows_piece, cols_full)
     here = lax.axis_index("inner")
-    strip = jnp.concatenate(
-        [shift(lax.dynamic_index_in_dim(by_owner, (here + k) % inner, 0, keepdims=False), "inner", k)
-         for k in range(inner)],
-        axis=1,
-    )
-    blocks = ring_gather(strip, "outer")
     local = vector_partials(normed, ln_gain, ln_bias, ln_cotangent, router_cotangent)
-    steps = [step for axis in ("section",) + SHARD for step in butterfly_rounds(axis)]
-    rounds = [steps[:2]] + [[step] for step in steps[2:]]
-    result, vec_grad = orthogonalize(blocks, local, rounds, inner * rows_piece)
+    shape = local.shape
+    extra = encode(local, by_owner[0])
+    moved = [
+        shift(jnp.concatenate(
+            [lax.dynamic_index_in_dim(by_owner, (here + k) % inner, 0, keepdims=False), extra],
+            axis=1), "inner", k)
+        for k in range(inner)
+    ]
+    strip = jnp.concatenate([piece[:, :rows_piece] for piece in moved], axis=1)
+    inner_sum = ordered_sum(
+        [decode(moved[(-k) % inner][:, rows_piece:], shape) for k in range(inner)], "inner"
+    )
+    strip_rows = inner * rows_piece
+    gathered = ring_gather(jnp.concatenate([strip, encode(inner_sum, strip)], axis=1), "outer")
+    size = lax.axis_size("outer")
+    whole = strip_rows + EXTRA_ROWS
+    pieces = [gathered[:, k * whole:(k + 1) * whole] for k in range(size)]
+    blocks = jnp.concatenate([piece[:, :strip_rows] for piece in pieces], axis=1)
+    outer_sum = ordered_sum([decode(piece[:, strip_rows:], shape) for piece in pieces], "outer")
+    rounds = [butterfly_rounds("section")]
+    result, vec_grad = orthogonalize(blocks, outer_sum, rounds, strip_rows)
     next_first, next_second, adam_step = adam(vec_grad, first_moment, second_moment)
     back = jnp.stack(
         [shift(result[:, k * rows_piece:(k + 1) * rows_piece], "inner", -k) for k in range(inner)],

time: 94.4 us -> 101 us (1.070)
  starting transfers between devices: 33 us -> 23.8 us
  local copies, waits for them, and re-layouts: 0.28 us -> 8.45 us
  matrix products: 26 us -> 30.8 us
  other arithmetic: 6.67 us -> 10.8 us
  waiting for transfers between devices: 26.6 us -> 24.3 us
    ppermute x6 -> x1, starting transfers between devices: 7.97 us -> 0.27 us  [butterfly_rounds(): lax.ppermute(value, axis, perm)]
    dot_general x5, matrix products: 10.8 us -> 15.7 us  [orthogonalize(): jnp.einsum('kij,klj->kil', iterate, iterate, preferred_element_type=jnp.f...]
    slice x0 -> x20, local copies, waits for them, and re-layouts: none -> 2.84 us  [the longest x10 2.05 us: decode(): high = flat[:size].astype(jnp.float32)]
    unnamed x33 -> x32, local copies, waits for them, and re-layouts: 0.2 us -> 2.15 us
    unnamed x1 -> x7, other arithmetic: 0.02 us -> 1.61 us
    ppermute x14, starting transfers between devices: 25 us -> 23.6 us  [shift(): return lax.ppermute(value, axis, [(i, (i + k) % size) for i in range(size)])]
    ppermute x14, waiting for transfers between devices: 25.8 us -> 24.3 us  [shift(): return lax.ppermute(value, axis, [(i, (i + k) % size) for i in range(size)])]
    convert_element_type x1, other arithmetic: 0.42 us -> 1.76 us  [orthogonalize(): (blocks.astype(jnp.float32) / (total + NORM_EPSILON)[:, None, None]).asty...]
  transfers between devices with their start and end apart: 20 -> 15, of which waited for: 14 -> 8; matrix products, arithmetic and copies ran while one was open for 26% -> 15% of each run, Pallas kernels for 0% -> 0%
where the time goes in v10:
time: 101 us; the launch traced here: 100 us
  matrix products  30.8 us (30%)
  waiting for transfers between devices  24.3 us (24%)
  starting transfers between devices  23.8 us (24%)
  other arithmetic  10.8 us (11%)
  local copies, waits for them, and re-layouts  8.45 us (8%)
  between operations  2.01 us (2%)
    ppermute x14, waiting for transfers between devices, shift(): return lax.ppermute(value, axis, [(i, (i + k) % size) for i in range(size)])  24.3 us
    ppermute x14, starting transfers between devices, shift(): return lax.ppermute(value, axis, [(i, (i + k) % size) for i in range(size)])  23.6 us
    dot_general x5, matrix products, orthogonalize(): jnp.einsum('kij,klj->kil', iterate, iterate, preferred_element_type=jnp.f...  15.7 us
    dot_general x5, matrix products, orthogonalize(): jnp.einsum('kij,kjl->kil', poly, iterate, preferred_element_type=jnp.floa...  14 us
    unnamed x32, local copies, waits for them, and re-layouts  2.15 us
    slice x10, local copies, waits for them, and re-layouts, decode(): high = flat[:size].astype(jnp.float32)  2.05 us
  transfers between devices with their start and end apart: 15, of which 8 were waited for; matrix products, arithmetic and copies ran while one was open for 15% of the time, Pallas kernels for 0%

profile of v10, /device:TPU:16, one launch (start us, length us, event | category | flops | bytes accessed | tf_op | source)
XLA Modules:
  0.0 100.3 jit_solution(9724220606318386153)
XLA Ops:
  3.0 2.0 %fusion.35 = (bf16[4,16,2048]{2,1,0:T(8,128)(2,1)S(1)}, f32[4,16,2048]{2,1,0:T(8,128)}) fusion(bf16[4,16,2048]{2,1,0:T(8,128)(2,1)} %param.9, f32[4,16,2048]{2,1,0:T(8,128)} %param.10), kind=kLoop, calls=%fused_computation.51 | loop fusion | flops 786432 | bytes 1572864 | tf_op jit(solution)/shard_map/convert_element_type | solution.py:156
  5.0 2.8 %collective-permute-start = (bf16[1,24,2048]{2,1,0:T(8,128)(2,1)S(1)}, bf16[1,24,2048]{2,1,0:T(8,128)(2,1)S(1)}, u32[]{:S(2)}, u32[]{:S(2)}) collective-permute-start(bf16[1,24,2048]{2,1,0:T(8,128)(2,1)S(1)} %get-tuple-element.49), channel_id=1, source_target_pairs={{0,24},{8,0},{16,8},{24,16},{1,25},{9,1},{17,9},{25,17},{2,26},{10... | collective-permute-start | bytes 294920 | tf_op jit(solution)/shard_map/ppermute | solution.py:30
  9.7 2.4 %collective-permute-done = bf16[1,24,2048]{2,1,0:T(8,128)(2,1)S(1)} collective-permute-done((bf16[1,24,2048]{2,1,0:T(8,128)(2,1)S(1)}, bf16[1,24,2048]{2,1,0:T(8,128)(2,1)S(1)}, u32[]{:S(2)}, u32[]{:S(2)}) %collective-permute-start) | collective-permute-done | bytes 98336 | tf_op jit(solution)/shard_map/ppermute | solution.py:30
  12.1 2.6 %collective-permute-done.1 = bf16[1,24,2048]{2,1,0:T(8,128)(2,1)S(1)} collective-permute-done((bf16[1,24,2048]{2,1,0:T(8,128)(2,1)S(1)}, bf16[1,24,2048]{2,1,0:T(8,128)(2,1)S(1)}, u32[]{:S(2)}, u32[]{:S(2)}) %collective-permute-start.1) | collective-permute-done | bytes 98336 | tf_op jit(solution)/shard_map/ppermute | solution.py:30
  16.6 2.0 %collective-permute-start.6 = (bf16[1,72,2048]{2,1,0:T(8,128)(2,1)S(1)}, bf16[1,72,2048]{2,1,0:T(8,128)(2,1)S(1)}, u32[]{:S(2)}, u32[]{:S(2)}) collective-permute-start(bf16[1,72,2048]{2,1,0:T(8,128)(2,1)S(1)} %constant_dynamic-update-slice_fusion), channel_id=1, source_target_pairs={{0,32},{32,64},{64,96},{96,128},{128,160},{160,192},{192,224},{224... | collective-permute-start | bytes 884744 | tf_op jit(solution)/shard_map/ppermute | solution.py:30
  18.6 4.0 %collective-permute-start.3 = (bf16[1,72,2048]{2,1,0:T(8,128)(2,1)S(1)}, bf16[1,72,2048]{2,1,0:T(8,128)(2,1)S(1)}, u32[]{:S(2)}, u32[]{:S(2)}) collective-permute-start(bf16[1,72,2048]{2,1,0:T(8,128)(2,1)S(1)} %constant_dynamic-update-slice_fusion), channel_id=1, source_target_pairs={{0,224},{32,0},{64,32},{96,64},{128,96},{160,128},{192,160},{224,1... | collective-permute-start | bytes 884744 | tf_op jit(solution)/shard_map/ppermute | solution.py:30
  22.6 6.6 %collective-permute-done.6 = bf16[1,72,2048]{2,1,0:T(8,128)(2,1)S(1)} collective-permute-done((bf16[1,72,2048]{2,1,0:T(8,128)(2,1)S(1)}, bf16[1,72,2048]{2,1,0:T(8,128)(2,1)S(1)}, u32[]{:S(2)}, u32[]{:S(2)}) %collective-permute-start.6) | collective-permute-done | bytes 294944 | tf_op jit(solution)/shard_map/ppermute | solution.py:30
  29.2 3.2 %collective-permute-start.4 = (bf16[1,72,2048]{2,1,0:T(8,128)(2,1)S(1)}, bf16[1,72,2048]{2,1,0:T(8,128)(2,1)}, u32[]{:S(2)}, u32[]{:S(2)}) collective-permute-start(bf16[1,72,2048]{2,1,0:T(8,128)(2,1)S(1)} %collective-permute-done.3), channel_id=1, source_target_pairs={{0,224},{32,0},{64,32},{96,64},{128,96},{160,128},{192,160},{224,1... | collective-permute-start | bytes 884744 | tf_op jit(solution)/shard_map/ppermute | solution.py:30
  32.5 5.7 %collective-permute-done.7 = bf16[1,72,2048]{2,1,0:T(8,128)(2,1)S(1)} collective-permute-done((bf16[1,72,2048]{2,1,0:T(8,128)(2,1)S(1)}, bf16[1,72,2048]{2,1,0:T(8,128)(2,1)S(1)}, u32[]{:S(2)}, u32[]{:S(2)}) %collective-permute-start.7) | collective-permute-done | bytes 294944 | tf_op jit(solution)/shard_map/ppermute | solution.py:30
  38.2 3.2 %collective-permute-start.5 = (bf16[1,72,2048]{2,1,0:T(8,128)(2,1)}, bf16[1,72,2048]{2,1,0:T(8,128)(2,1)S(1)}, u32[]{:S(2)}, u32[]{:S(2)}) collective-permute-start(bf16[1,72,2048]{2,1,0:T(8,128)(2,1)} %collective-permute-done.4), channel_id=1, source_target_pairs={{0,224},{32,0},{64,32},{96,64},{128,96},{160,128},{192,160},{224,1... | collective-permute-start | bytes 884744 | tf_op jit(solution)/shard_map/ppermute | solution.py:30
  48.4 3.2 %collective-permute-start.10 = (bf16[1,72,1024]{2,1,0:T(8,128)(2,1)}, bf16[1,72,1024]{2,1,0:T(8,128)(2,1)}, u32[]{:S(2)}, u32[]{:S(2)}) collective-permute-start(bf16[1,72,1024]{2,1,0:T(8,128)(2,1)} %slice.324), channel_id=1, source_target_pairs={{0,224},{32,0},{64,32},{96,64},{128,96},{160,128},{192,160},{224,1... | collective-permute-start | bytes 442376 | tf_op jit(solution)/shard_map/ppermute | solution.py:30
  55.7 1.7 %fusion = f32[]{:T(128)} fusion(bf16[1,512,2048]{2,1,0:T(8,128)(2,1)S(1)} %slice_dynamic-update-slice_fusion), kind=kLoop, calls=%fused_computation.4 | loop fusion | flops 3145727 | bytes 2097156 | tf_op jit(solution)/shard_map/reduce_sum | solution.py:85
  58.1 1.8 %fusion.1 = bf16[1,512,2048]{2,1,0:T(8,128)(2,1)} fusion(bf16[1,512,2048]{2,1,0:T(8,128)(2,1)S(1)} %slice_dynamic-update-slice_fusion, f32[]{:T(128)S(6)} %add.360), kind=kLoop, calls=%fused_computation.5 | loop fusion | flops 3145728 | bytes 4194308 | tf_op jit(solution)/shard_map/convert_element_type | solution.py:87
  61.0 3.6 %fusion.21 = f32[512,512]{1,0:T(8,128)S(1)} fusion(bf16[1,512,2048]{2,1,0:T(8,128)(2,1)} %fusion.1), kind=kOutput, calls=%fused_computation.30 | convolution fusion | flops 1073741824 | bytes 3145728 | tf_op jit(solution)/shard_map/kij,klj->kil/dot_general | solution.py:94
  64.6 2.9 %fusion.5 = bf16[1,512,2048]{2,1,0:T(8,128)(2,1)} fusion(bf16[1,512,2048]{2,1,0:T(8,128)(2,1)S(1)} %copy-done.1, f32[512,512]{1,0:T(8,128)S(1)} %fusion.21), kind=kOutput, calls=%fused_computation.13 | convolution fusion | flops 1347682304 | bytes 5242880 | tf_op jit(solution)/shard_map/kij,kjl->kil/dot_general | solution.py:101
  67.5 3.6 %fusion.18 = f32[512,512]{1,0:T(8,128)S(1)} fusion(bf16[1,512,2048]{2,1,0:T(8,128)(2,1)} %fusion.5), kind=kOutput, calls=%fused_computation.27 | convolution fusion | flops 1073741824 | bytes 3145728 | tf_op jit(solution)/shard_map/kij,klj->kil/dot_general | solution.py:94
  71.2 2.9 %fusion.4 = bf16[1,512,2048]{2,1,0:T(8,128)(2,1)} fusion(bf16[1,512,2048]{2,1,0:T(8,128)(2,1)S(1)} %copy-done.5, f32[512,512]{1,0:T(8,128)S(1)} %fusion.18), kind=kOutput, calls=%fused_computation.11 | convolution fusion | flops 1347682304 | bytes 5242880 | tf_op jit(solution)/shard_map/kij,kjl->kil/dot_general | solution.py:101
  74.1 3.6 %fusion.15 = f32[512,512]{1,0:T(8,128)S(1)} fusion(bf16[1,512,2048]{2,1,0:T(8,128)(2,1)} %fusion.4), kind=kOutput, calls=%fused_computation.24 | convolution fusion | flops 1073741824 | bytes 3145728 | tf_op jit(solution)/shard_map/kij,klj->kil/dot_general | solution.py:94
  77.8 2.9 %fusion.3 = bf16[1,512,2048]{2,1,0:T(8,128)(2,1)} fusion(bf16[1,512,2048]{2,1,0:T(8,128)(2,1)S(1)} %copy-done.6, f32[512,512]{1,0:T(8,128)S(1)} %fusion.15), kind=kOutput, calls=%fused_computation.9 | convolution fusion | flops 1347682304 | bytes 5242880 | tf_op jit(solution)/shard_map/kij,kjl->kil/dot_general | solution.py:101
  80.7 3.5 %fusion.12 = f32[512,512]{1,0:T(8,128)S(1)} fusion(bf16[1,512,2048]{2,1,0:T(8,128)(2,1)} %fusion.3), kind=kOutput, calls=%fused_computation.21 | convolution fusion | flops 1073741824 | bytes 3145728 | tf_op jit(solution)/shard_map/kij,klj->kil/dot_general | solution.py:94
  84.2 3.8 %fusion.2 = bf16[1,512,2048]{2,1,0:T(8,128)(2,1)S(1)} fusion(bf16[1,512,2048]{2,1,0:T(8,128)(2,1)} %fusion.3, f32[512,512]{1,0:T(8,128)S(1)} %fusion.12), kind=kOutput, calls=%fused_computation.7 | convolution fusion | flops 1347682304 | bytes 5242880 | tf_op jit(solution)/shard_map/kij,kjl->kil/dot_general | solution.py:101
  90.1 1.5 %fusion.7 = bf16[1,64,2048]{2,1,0:T(8,128)(2,1)S(1)} fusion(bf16[1,512,2048]{2,1,0:T(8,128)(2,1)S(1)} %fusion.2, f32[512,512]{1,0:T(8,128)S(1)} %fusion.9, f32[1,512,512]{2,1,0:T(8,128)S(1)} %bitcast.133, bf16[1,512,512]{2,1,0:T(8,128)(2,1)} %convert_bitcast_fusion), kind=kOutput, calls=%fused_computation.16 | convolution fusion | flops 168689664 | bytes 3866624 | tf_op jit(solution)/shard_map/kij,kjl->kil/dot_general | solution.py:101
  91.9 3.1 %collective-permute-start.12 = (bf16[1,16,2048]{2,1,0:T(8,128)(2,1)S(1)}, bf16[1,16,2048]{2,1,0:T(8,128)(2,1)S(1)}, u32[]{:S(2)}, u32[]{:S(2)}) collective-permute-start(bf16[1,16,2048]{2,1,0:T(8,128)(2,1)S(1)} %get-tuple-element.37), channel_id=1, source_target_pairs={{0,24},{8,0},{16,8},{24,16},{1,25},{9,1},{17,9},{25,17},{2,26},{10... | collective-permute-start | bytes 196616 | tf_op jit(solution)/shard_map/ppermute | solution.py:30
  95.6 3.7 %collective-permute-done.12 = bf16[1,16,2048]{2,1,0:T(8,128)(2,1)S(1)} collective-permute-done((bf16[1,16,2048]{2,1,0:T(8,128)(2,1)S(1)}, bf16[1,16,2048]{2,1,0:T(8,128)(2,1)S(1)}, u32[]{:S(2)}, u32[]{:S(2)}) %collective-permute-start.12) | collective-permute-done | bytes 65568 | tf_op jit(solution)/shard_map/ppermute | solution.py:30
  (115 shorter events, 21.8 us)
Async XLA Ops:
  0.6 1.1 %copy-start = (bf16[512,32]{0,1:T(8,128)(2,1)S(1)}, bf16[512,32]{0,1:T(8,128)(2,1)}, u32[]{:S(2)}) copy-start(bf16[512,32]{0,1:T(8,128)(2,1)} %param.15) | copy-start | bytes 98308
  5.0 7.0 %collective-permute-start = (bf16[1,24,2048]{2,1,0:T(8,128)(2,1)S(1)}, bf16[1,24,2048]{2,1,0:T(8,128)(2,1)S(1)}, u32[]{:S(2)}, u32[]{:S(2)}) collective-permute-start(bf16[1,24,2048]{2,1,0:T(8,128)(2,1)S(1)} %get-tuple-element.49), channel_id=1, source_target_pairs={{0,24},{8,0},{16,8},{24,16},{1,25},{9,1},{17,9},{25,17},{2,26},{10... | collective-permute-start | bytes 294920 | tf_op jit(solution)/shard_map/ppermute | solution.py:30
  7.9 6.8 %collective-permute-start.1 = (bf16[1,24,2048]{2,1,0:T(8,128)(2,1)S(1)}, bf16[1,24,2048]{2,1,0:T(8,128)(2,1)S(1)}, u32[]{:S(2)}, u32[]{:S(2)}) collective-permute-start(bf16[1,24,2048]{2,1,0:T(8,128)(2,1)S(1)} %get-tuple-element.50), channel_id=1, source_target_pairs={{0,16},{8,24},{16,0},{24,8},{1,17},{9,25},{17,1},{25,9},{2,18},{10... | collective-permute-start | bytes 294920 | tf_op jit(solution)/shard_map/ppermute | solution.py:30
  8.7 7.1 %collective-permute-start.2 = (bf16[1,24,2048]{2,1,0:T(8,128)(2,1)S(1)}, bf16[1,24,2048]{2,1,0:T(8,128)(2,1)S(1)}, u32[]{:S(2)}, u32[]{:S(2)}) collective-permute-start(bf16[1,24,2048]{2,1,0:T(8,128)(2,1)S(1)} %get-tuple-element.51), channel_id=1, source_target_pairs={{0,8},{8,16},{16,24},{24,0},{1,9},{9,17},{17,25},{25,1},{2,10},{10... | collective-permute-start | bytes 294920 | tf_op jit(solution)/shard_map/ppermute | solution.py:30
  16.6 12.6 %collective-permute-start.6 = (bf16[1,72,2048]{2,1,0:T(8,128)(2,1)S(1)}, bf16[1,72,2048]{2,1,0:T(8,128)(2,1)S(1)}, u32[]{:S(2)}, u32[]{:S(2)}) collective-permute-start(bf16[1,72,2048]{2,1,0:T(8,128)(2,1)S(1)} %constant_dynamic-update-slice_fusion), channel_id=1, source_target_pairs={{0,32},{32,64},{64,96},{96,128},{128,160},{160,192},{192,224},{224... | collective-permute-start | bytes 884744 | tf_op jit(solution)/shard_map/ppermute | solution.py:30
  18.6 10.6 %collective-permute-start.3 = (bf16[1,72,2048]{2,1,0:T(8,128)(2,1)S(1)}, bf16[1,72,2048]{2,1,0:T(8,128)(2,1)S(1)}, u32[]{:S(2)}, u32[]{:S(2)}) collective-permute-start(bf16[1,72,2048]{2,1,0:T(8,128)(2,1)S(1)} %constant_dynamic-update-slice_fusion), channel_id=1, source_target_pairs={{0,224},{32,0},{64,32},{96,64},{128,96},{160,128},{192,160},{224,1... | collective-permute-start | bytes 884744 | tf_op jit(solution)/shard_map/ppermute | solution.py:30
  29.2 9.0 %collective-permute-start.7 = (bf16[1,72,2048]{2,1,0:T(8,128)(2,1)S(1)}, bf16[1,72,2048]{2,1,0:T(8,128)(2,1)S(1)}, u32[]{:S(2)}, u32[]{:S(2)}) collective-permute-start(bf16[1,72,2048]{2,1,0:T(8,128)(2,1)S(1)} %collective-permute-done.6), channel_id=1, source_target_pairs={{0,32},{32,64},{64,96},{96,128},{128,160},{160,192},{192,224},{224... | collective-permute-start | bytes 884744 | tf_op jit(solution)/shard_map/ppermute | solution.py:30
  29.2 9.0 %collective-permute-start.4 = (bf16[1,72,2048]{2,1,0:T(8,128)(2,1)S(1)}, bf16[1,72,2048]{2,1,0:T(8,128)(2,1)}, u32[]{:S(2)}, u32[]{:S(2)}) collective-permute-start(bf16[1,72,2048]{2,1,0:T(8,128)(2,1)S(1)} %collective-permute-done.3), channel_id=1, source_target_pairs={{0,224},{32,0},{64,32},{96,64},{128,96},{160,128},{192,160},{224,1... | collective-permute-start | bytes 884744 | tf_op jit(solution)/shard_map/ppermute | solution.py:30
  38.2 8.2 %collective-permute-start.8 = (bf16[1,72,2048]{2,1,0:T(8,128)(2,1)S(1)}, bf16[1,72,2048]{2,1,0:T(8,128)(2,1)S(1)}, u32[]{:S(2)}, u32[]{:S(2)}) collective-permute-start(bf16[1,72,2048]{2,1,0:T(8,128)(2,1)S(1)} %collective-permute-done.7), channel_id=1, source_target_pairs={{0,32},{32,64},{64,96},{96,128},{128,160},{160,192},{192,224},{224... | collective-permute-start | bytes 884744 | tf_op jit(solution)/shard_map/ppermute | solution.py:30
  38.2 8.9 %collective-permute-start.5 = (bf16[1,72,2048]{2,1,0:T(8,128)(2,1)}, bf16[1,72,2048]{2,1,0:T(8,128)(2,1)S(1)}, u32[]{:S(2)}, u32[]{:S(2)}) collective-permute-start(bf16[1,72,2048]{2,1,0:T(8,128)(2,1)} %collective-permute-done.4), channel_id=1, source_target_pairs={{0,224},{32,0},{64,32},{96,64},{128,96},{160,128},{192,160},{224,1... | collective-permute-start | bytes 884744 | tf_op jit(solution)/shard_map/ppermute | solution.py:30
  47.1 6.7 %collective-permute-start.9 = (bf16[1,72,1024]{2,1,0:T(8,128)(2,1)}, bf16[1,72,1024]{2,1,0:T(8,128)(2,1)}, u32[]{:S(2)}, u32[]{:S(2)}) collective-permute-start(bf16[1,72,1024]{2,1,0:T(8,128)(2,1)} %slice.323), channel_id=1, source_target_pairs={{0,32},{32,64},{64,96},{96,128},{128,160},{160,192},{192,224},{224... | collective-permute-start | bytes 442376 | tf_op jit(solution)/shard_map/ppermute | solution.py:30
  48.4 6.3 %collective-permute-start.10 = (bf16[1,72,1024]{2,1,0:T(8,128)(2,1)}, bf16[1,72,1024]{2,1,0:T(8,128)(2,1)}, u32[]{:S(2)}, u32[]{:S(2)}) collective-permute-start(bf16[1,72,1024]{2,1,0:T(8,128)(2,1)} %slice.324), channel_id=1, source_target_pairs={{0,224},{32,0},{64,32},{96,64},{128,96},{160,128},{192,160},{224,1... | collective-permute-start | bytes 442376 | tf_op jit(solution)/shard_map/ppermute | solution.py:30
  58.1 1.8 %copy-start.2 = (bf16[128,128]{1,0:T(8,128)(2,1)S(1)}, bf16[128,128]{1,0:T(8,128)(2,1)}, u32[]{:S(2)}) copy-start(bf16[128,128]{1,0:T(8,128)(2,1)} %slice.265) | copy-start | bytes 98308
  60.7 3.9 %copy-start.1 = (bf16[1,512,2048]{2,1,0:T(8,128)(2,1)S(1)}, bf16[1,512,2048]{2,1,0:T(8,128)(2,1)}, u32[]{:S(2)}) copy-start(bf16[1,512,2048]{2,1,0:T(8,128)(2,1)} %fusion.1) | copy-start | bytes 6291460
  60.7 6.9 %collective-permute-start.11 = (f32[34,128]{1,0:T(8,128)S(1)}, f32[34,128]{1,0:T(8,128)S(1)}, u32[]{:S(2)}, u32[]{:S(2)}) collective-permute-start(f32[34,128]{1,0:T(8,128)S(1)} %fusion.66), channel_id=1, source_target_pairs={{0,1},{1,0},{2,3},{3,2},{4,5},{5,4},{6,7},{7,6},{8,9},{9,8},{10,11... | collective-permute-start | bytes 52232 | tf_op jit(solution)/shard_map/ppermute | solution.py:119
  67.5 3.7 %copy-start.5 = (bf16[1,512,2048]{2,1,0:T(8,128)(2,1)S(1)}, bf16[1,512,2048]{2,1,0:T(8,128)(2,1)}, u32[]{:S(2)}) copy-start(bf16[1,512,2048]{2,1,0:T(8,128)(2,1)} %fusion.5) | copy-start | bytes 6291460
  74.1 3.7 %copy-start.6 = (bf16[1,512,2048]{2,1,0:T(8,128)(2,1)S(1)}, bf16[1,512,2048]{2,1,0:T(8,128)(2,1)}, u32[]{:S(2)}) copy-start(bf16[1,512,2048]{2,1,0:T(8,128)(2,1)} %fusion.4) | copy-start | bytes 6291460
  90.1 4.9 %copy-start.3 = (f32[34,128]{1,0:T(8,128)S(1)}, f32[34,128]{1,0:T(8,128)}, u32[]{:S(2)}) copy-start(f32[34,128]{1,0:T(8,128)} %param.17) | copy-start | bytes 52228
  90.1 4.9 %copy-start.4 = (f32[34,128]{1,0:T(8,128)S(1)}, f32[34,128]{1,0:T(8,128)}, u32[]{:S(2)}) copy-start(f32[34,128]{1,0:T(8,128)} %param.16) | copy-start | bytes 52228
  91.7 7.6 %collective-permute-start.14 = (bf16[1,16,2048]{2,1,0:T(8,128)(2,1)S(1)}, bf16[1,16,2048]{2,1,0:T(8,128)(2,1)S(1)}, u32[]{:S(2)}, u32[]{:S(2)}) collective-permute-start(bf16[1,16,2048]{2,1,0:T(8,128)(2,1)S(1)} %get-tuple-element.35), channel_id=1, source_target_pairs={{0,8},{8,16},{16,24},{24,0},{1,9},{9,17},{17,25},{25,1},{2,10},{10... | collective-permute-start | bytes 196616 | tf_op jit(solution)/shard_map/ppermute | solution.py:30
  91.8 7.5 %collective-permute-start.13 = (bf16[1,16,2048]{2,1,0:T(8,128)(2,1)S(1)}, bf16[1,16,2048]{2,1,0:T(8,128)(2,1)S(1)}, u32[]{:S(2)}, u32[]{:S(2)}) collective-permute-start(bf16[1,16,2048]{2,1,0:T(8,128)(2,1)S(1)} %get-tuple-element.36), channel_id=1, source_target_pairs={{0,16},{8,24},{16,0},{24,8},{1,17},{9,25},{17,1},{25,9},{2,18},{10... | collective-permute-start | bytes 196616 | tf_op jit(solution)/shard_map/ppermute | solution.py:30
  91.9 7.4 %collective-permute-start.12 = (bf16[1,16,2048]{2,1,0:T(8,128)(2,1)S(1)}, bf16[1,16,2048]{2,1,0:T(8,128)(2,1)S(1)}, u32[]{:S(2)}, u32[]{:S(2)}) collective-permute-start(bf16[1,16,2048]{2,1,0:T(8,128)(2,1)S(1)} %get-tuple-element.37), channel_id=1, source_target_pairs={{0,24},{8,0},{16,8},{24,16},{1,25},{9,1},{17,9},{25,17},{2,26},{10... | collective-permute-start | bytes 196616 | tf_op jit(solution)/shard_map/ppermute | solution.py:30

commit v11 on v9

--- a/solution.py
+++ b/solution.py
@@ -136,7 +136,7 @@
     blocks = ring_gather(strip, "outer")
     local = vector_partials(normed, ln_gain, ln_bias, ln_cotangent, router_cotangent)
     steps = [step for axis in ("section",) + SHARD for step in butterfly_rounds(axis)]
-    rounds = [steps[:2]] + [[step] for step in steps[2:]]
+    rounds = [steps[:2], steps[2:4]] + [[step] for step in steps[4:]]
     result, vec_grad = orthogonalize(blocks, local, rounds, inner * rows_piece)
     next_first, next_second, adam_step = adam(vec_grad, first_moment, second_moment)
     back = jnp.stack(

time: 94.4 us -> 99 us (1.049)
  waiting for transfers between devices: 26.6 us -> 32.6 us
  starting transfers between devices: 33 us -> 31.5 us
    ppermute x6, waiting for transfers between devices: 0.8 us -> 6.72 us  [butterfly_rounds(): lax.ppermute(value, axis, perm)]
    ppermute x6, starting transfers between devices: 7.97 us -> 6.47 us  [butterfly_rounds(): lax.ppermute(value, axis, perm)]
  transfers between devices with their start and end apart: 20 -> 20, of which waited for: 14 -> 14; matrix products, arithmetic and copies ran while one was open for 26% -> 24% of each run, Pallas kernels for 0% -> 0%
where the time goes in v11:
time: 99 us; the launch traced here: 98.8 us
  waiting for transfers between devices  32.6 us (33%)
  starting transfers between devices  31.5 us (32%)
  matrix products  26 us (26%)
  other arithmetic  6.67 us (7%)
  between operations  1.76 us (2%)
    ppermute x14, waiting for transfers between devices, shift(): return lax.ppermute(value, axis, [(i, (i + k) % size) for i in range(size)])  25.9 us
    ppermute x14, starting transfers between devices, shift(): return lax.ppermute(value, axis, [(i, (i + k) % size) for i in range(size)])  25 us
    dot_general x5, matrix products, orthogonalize(): jnp.einsum('kij,kjl->kil', poly, iterate, preferred_element_type=jnp.floa...  15 us
    dot_general x5, matrix products, orthogonalize(): jnp.einsum('kij,klj->kil', iterate, iterate, preferred_element_type=jnp.f...  10.8 us
    ppermute x6, waiting for transfers between devices, butterfly_rounds(): lax.ppermute(value, axis, perm)  6.72 us
    ppermute x6, starting transfers between devices, butterfly_rounds(): lax.ppermute(value, axis, perm)  6.47 us
    convert_element_type x1, other arithmetic, on_device(): nesterov = (grad_float + MUON_DECAY * next_momentum).astype(jnp.bfloat16)  2.08 us
  transfers between devices with their start and end apart: 20, of which 14 were waited for; matrix products, arithmetic and copies ran while one was open for 24% of the time, Pallas kernels for 0%

profile of v11, /device:TPU:16, one launch (start us, length us, event | category | flops | bytes accessed | tf_op | source)
XLA Modules:
  0.0 98.8 jit_solution(11991157912538336128)
XLA Ops:
  0.7 2.1 %fusion.35 = (bf16[4,16,2048]{2,1,0:T(8,128)(2,1)S(1)}, f32[4,16,2048]{2,1,0:T(8,128)}) fusion(bf16[4,16,2048]{2,1,0:T(8,128)(2,1)} %param.9, f32[4,16,2048]{2,1,0:T(8,128)} %param.10), kind=kLoop, calls=%fused_computation.50 | loop fusion | flops 786432 | bytes 1572864 | tf_op jit(solution)/shard_map/convert_element_type | solution.py:124
  2.9 1.6 %collective-permute-start = (bf16[1,16,2048]{2,1,0:T(8,128)(2,1)S(1)}, bf16[1,16,2048]{2,1,0:T(8,128)(2,1)S(1)}, u32[]{:S(2)}, u32[]{:S(2)}) collective-permute-start(bf16[1,16,2048]{2,1,0:T(8,128)(2,1)S(1)} %get-tuple-element.39), channel_id=1, source_target_pairs={{0,8},{8,16},{16,24},{24,0},{1,9},{9,17},{17,25},{25,1},{2,10},{10... | collective-permute-start | bytes 196616 | tf_op jit(solution)/shard_map/ppermute | solution.py:30
  4.4 2.7 %collective-permute-start.1 = (bf16[1,16,2048]{2,1,0:T(8,128)(2,1)S(1)}, bf16[1,16,2048]{2,1,0:T(8,128)(2,1)S(1)}, u32[]{:S(2)}, u32[]{:S(2)}) collective-permute-start(bf16[1,16,2048]{2,1,0:T(8,128)(2,1)S(1)} %get-tuple-element.38), channel_id=1, source_target_pairs={{0,16},{8,24},{16,0},{24,8},{1,17},{9,25},{17,1},{25,9},{2,18},{10... | collective-permute-start | bytes 196616 | tf_op jit(solution)/shard_map/ppermute | solution.py:30
  11.4 5.9 %collective-permute-start.3 = (bf16[1,64,2048]{2,1,0:T(8,128)(2,1)S(1)}, bf16[1,64,2048]{2,1,0:T(8,128)(2,1)S(1)}, u32[]{:S(2)}, u32[]{:S(2)}) collective-permute-start(bf16[1,64,2048]{2,1,0:T(8,128)(2,1)S(1)} %pad_maximum_fusion), channel_id=1, source_target_pairs={{0,224},{32,0},{64,32},{96,64},{128,96},{160,128},{192,160},{224,1... | collective-permute-start | bytes 786440 | tf_op jit(solution)/shard_map/ppermute | solution.py:30
  17.4 4.3 %collective-permute-done.3 = bf16[1,64,2048]{2,1,0:T(8,128)(2,1)S(1)} collective-permute-done((bf16[1,64,2048]{2,1,0:T(8,128)(2,1)S(1)}, bf16[1,64,2048]{2,1,0:T(8,128)(2,1)S(1)}, u32[]{:S(2)}, u32[]{:S(2)}) %collective-permute-start.3) | collective-permute-done | bytes 262176 | tf_op jit(solution)/shard_map/ppermute | solution.py:30
  21.8 3.7 %collective-permute-start.4 = (bf16[1,64,2048]{2,1,0:T(8,128)(2,1)S(1)}, bf16[1,64,2048]{2,1,0:T(8,128)(2,1)S(1)}, u32[]{:S(2)}, u32[]{:S(2)}) collective-permute-start(bf16[1,64,2048]{2,1,0:T(8,128)(2,1)S(1)} %collective-permute-done.3), channel_id=1, source_target_pairs={{0,224},{32,0},{64,32},{96,64},{128,96},{160,128},{192,160},{224,1... | collective-permute-start | bytes 786440 | tf_op jit(solution)/shard_map/ppermute | solution.py:30
  25.5 3.9 %collective-permute-done.4 = bf16[1,64,2048]{2,1,0:T(8,128)(2,1)S(1)} collective-permute-done((bf16[1,64,2048]{2,1,0:T(8,128)(2,1)S(1)}, bf16[1,64,2048]{2,1,0:T(8,128)(2,1)S(1)}, u32[]{:S(2)}, u32[]{:S(2)}) %collective-permute-start.4) | collective-permute-done | bytes 262176 | tf_op jit(solution)/shard_map/ppermute | solution.py:30
  29.3 3.7 %collective-permute-start.5 = (bf16[1,64,2048]{2,1,0:T(8,128)(2,1)S(1)}, bf16[1,64,2048]{2,1,0:T(8,128)(2,1)S(1)}, u32[]{:S(2)}, u32[]{:S(2)}) collective-permute-start(bf16[1,64,2048]{2,1,0:T(8,128)(2,1)S(1)} %collective-permute-done.4), channel_id=1, source_target_pairs={{0,224},{32,0},{64,32},{96,64},{128,96},{160,128},{192,160},{224,1... | collective-permute-start | bytes 786440 | tf_op jit(solution)/shard_map/ppermute | solution.py:30
  33.1 4.4 %collective-permute-done.5 = bf16[1,64,2048]{2,1,0:T(8,128)(2,1)S(1)} collective-permute-done((bf16[1,64,2048]{2,1,0:T(8,128)(2,1)S(1)}, bf16[1,64,2048]{2,1,0:T(8,128)(2,1)S(1)}, u32[]{:S(2)}, u32[]{:S(2)}) %collective-permute-start.5) | collective-permute-done | bytes 262176 | tf_op jit(solution)/shard_map/ppermute | solution.py:30
  37.5 3.8 %collective-permute-start.10 = (bf16[1,64,1024]{2,1,0:T(8,128)(2,1)S(1)}, bf16[1,64,1024]{2,1,0:T(8,128)(2,1)S(1)}, u32[]{:S(2)}, u32[]{:S(2)}) collective-permute-start(bf16[1,64,1024]{2,1,0:T(8,128)(2,1)S(1)} %slice.37), channel_id=1, source_target_pairs={{0,224},{32,0},{64,32},{96,64},{128,96},{160,128},{192,160},{224,1... | collective-permute-start | bytes 393224 | tf_op jit(solution)/shard_map/ppermute | solution.py:30
  41.5 2.3 %collective-permute-done.10 = bf16[1,64,1024]{2,1,0:T(8,128)(2,1)S(1)} collective-permute-done((bf16[1,64,1024]{2,1,0:T(8,128)(2,1)S(1)}, bf16[1,64,1024]{2,1,0:T(8,128)(2,1)S(1)}, u32[]{:S(2)}, u32[]{:S(2)}) %collective-permute-start.10) | collective-permute-done | bytes 131104 | tf_op jit(solution)/shard_map/ppermute | solution.py:30
  43.8 3.8 %collective-permute-done.9 = bf16[1,64,1024]{2,1,0:T(8,128)(2,1)S(1)} collective-permute-done((bf16[1,64,1024]{2,1,0:T(8,128)(2,1)S(1)}, bf16[1,64,1024]{2,1,0:T(8,128)(2,1)S(1)}, u32[]{:S(2)}, u32[]{:S(2)}) %collective-permute-start.9) | collective-permute-done | bytes 131104 | tf_op jit(solution)/shard_map/ppermute | solution.py:30
  47.8 1.7 %fusion = f32[]{:T(128)} fusion(bf16[1,512,2048]{2,1,0:T(8,128)(2,1)S(1)} %constant_dynamic-update-slice_fusion), kind=kLoop, calls=%fused_computation.2 | loop fusion | flops 3145727 | bytes 2097156 | tf_op jit(solution)/shard_map/reduce_sum | solution.py:53
  52.3 3.8 %fusion.5 = bf16[1,512,2048]{2,1,0:T(8,128)(2,1)S(1)} fusion(bf16[1,512,2048]{2,1,0:T(8,128)(2,1)} %copy-done.1, f32[512,512]{1,0:T(8,128)S(1)} %fusion.21), kind=kOutput, calls=%fused_computation.11 | convolution fusion | flops 1347682304 | bytes 5242880 | tf_op jit(solution)/shard_map/kij,kjl->kil/dot_general | solution.py:69
  57.5 3.4 %collective-permute-done.13 = f32[34,128]{1,0:T(8,128)S(1)} collective-permute-done((f32[34,128]{1,0:T(8,128)S(1)}, f32[34,128]{1,0:T(8,128)S(1)}, u32[]{:S(2)}, u32[]{:S(2)}) %collective-permute-start.13) | collective-permute-done | bytes 17440 | tf_op jit(solution)/shard_map/ppermute | solution.py:87
  62.3 2.9 %fusion.4 = bf16[1,512,2048]{2,1,0:T(8,128)(2,1)} fusion(bf16[1,512,2048]{2,1,0:T(8,128)(2,1)S(1)} %fusion.5, f32[512,512]{1,0:T(8,128)S(1)} %fusion.18), kind=kOutput, calls=%fused_computation.9 | convolution fusion | flops 1347682304 | bytes 5242880 | tf_op jit(solution)/shard_map/kij,kjl->kil/dot_general | solution.py:69
  65.3 3.3 %collective-permute-done.14 = f32[34,128]{1,0:T(8,128)S(1)} collective-permute-done((f32[34,128]{1,0:T(8,128)S(1)}, f32[34,128]{1,0:T(8,128)S(1)}, u32[]{:S(2)}, u32[]{:S(2)}) %collective-permute-start.14) | collective-permute-done | bytes 17440 | tf_op jit(solution)/shard_map/ppermute | solution.py:87
  69.9 3.5 %fusion.15 = f32[512,512]{1,0:T(8,128)S(1)} fusion(bf16[1,512,2048]{2,1,0:T(8,128)(2,1)} %fusion.4), kind=kOutput, calls=%fused_computation.22 | convolution fusion | flops 1073741824 | bytes 3145728 | tf_op jit(solution)/shard_map/kij,klj->kil/dot_general | solution.py:62
  73.5 2.9 %fusion.3 = bf16[1,512,2048]{2,1,0:T(8,128)(2,1)} fusion(bf16[1,512,2048]{2,1,0:T(8,128)(2,1)S(1)} %copy-done.8, f32[512,512]{1,0:T(8,128)S(1)} %fusion.15), kind=kOutput, calls=%fused_computation.7 | convolution fusion | flops 1347682304 | bytes 5242880 | tf_op jit(solution)/shard_map/kij,kjl->kil/dot_general | solution.py:69
  76.4 3.2 %collective-permute-start.16 = (f32[34,128]{1,0:T(8,128)S(1)}, f32[34,128]{1,0:T(8,128)S(1)}, u32[]{:S(2)}, u32[]{:S(2)}) collective-permute-start(f32[34,128]{1,0:T(8,128)S(1)} %add.147), channel_id=1, source_target_pairs={{0,16},{8,24},{16,0},{24,8},{1,17},{9,25},{17,1},{25,9},{2,18},{10... | collective-permute-start | bytes 52232 | tf_op jit(solution)/shard_map/ppermute | solution.py:87
  79.6 3.5 %fusion.12 = f32[512,512]{1,0:T(8,128)S(1)} fusion(bf16[1,512,2048]{2,1,0:T(8,128)(2,1)} %fusion.3), kind=kOutput, calls=%fused_computation.19 | convolution fusion | flops 1073741824 | bytes 3145728 | tf_op jit(solution)/shard_map/kij,klj->kil/dot_general | solution.py:62
  83.1 3.8 %fusion.2 = bf16[1,512,2048]{2,1,0:T(8,128)(2,1)S(1)} fusion(bf16[1,512,2048]{2,1,0:T(8,128)(2,1)} %fusion.3, f32[512,512]{1,0:T(8,128)S(1)} %fusion.12), kind=kOutput, calls=%fused_computation.5 | convolution fusion | flops 1347682304 | bytes 5242880 | tf_op jit(solution)/shard_map/kij,kjl->kil/dot_general | solution.py:69
  93.4 1.6 %collective-permute-done.17 = bf16[1,16,2048]{2,1,0:T(8,128)(2,1)S(1)} collective-permute-done((bf16[1,16,2048]{2,1,0:T(8,128)(2,1)S(1)}, bf16[1,16,2048]{2,1,0:T(8,128)(2,1)S(1)}, u32[]{:S(2)}, u32[]{:S(2)}) %collective-permute-start.17) | collective-permute-done | bytes 65568 | tf_op jit(solution)/shard_map/ppermute | solution.py:30
  95.0 1.9 %collective-permute-done.18 = bf16[1,16,2048]{2,1,0:T(8,128)(2,1)S(1)} collective-permute-done((bf16[1,16,2048]{2,1,0:T(8,128)(2,1)S(1)}, bf16[1,16,2048]{2,1,0:T(8,128)(2,1)S(1)}, u32[]{:S(2)}, u32[]{:S(2)}) %collective-permute-start.18) | collective-permute-done | bytes 65568 | tf_op jit(solution)/shard_map/ppermute | solution.py:30
  (82 shorter events, 19.1 us)
Async XLA Ops:
  0.6 8.0 %copy-start = (bf16[512,32]{0,1:T(8,128)(2,1)S(1)}, bf16[512,32]{0,1:T(8,128)(2,1)}, u32[]{:S(2)}) copy-start(bf16[512,32]{0,1:T(8,128)(2,1)} %param.15) | copy-start | bytes 98308
  0.6 7.9 %copy-start.2 = (bf16[512,128]{1,0:T(8,128)(2,1)S(1)}, bf16[512,128]{1,0:T(8,128)(2,1)}, u32[]{:S(2)}) copy-start(bf16[512,128]{1,0:T(8,128)(2,1)} %param.11) | copy-start | bytes 393220
  0.7 7.9 %copy-start.6 = (f32[128]{0:T(128)S(1)}, f32[128]{0:T(128)}, u32[]{:S(2)}) copy-start(f32[128]{0:T(128)} %param.13) | copy-start | bytes 1540
  0.7 8.1 %copy-start.3 = (bf16[512,128]{1,0:T(8,128)(2,1)S(1)}, bf16[512,128]{1,0:T(8,128)(2,1)}, u32[]{:S(2)}) copy-start(bf16[512,128]{1,0:T(8,128)(2,1)} %param.14) | copy-start | bytes 393220
  2.9 6.1 %collective-permute-start = (bf16[1,16,2048]{2,1,0:T(8,128)(2,1)S(1)}, bf16[1,16,2048]{2,1,0:T(8,128)(2,1)S(1)}, u32[]{:S(2)}, u32[]{:S(2)}) collective-permute-start(bf16[1,16,2048]{2,1,0:T(8,128)(2,1)S(1)} %get-tuple-element.39), channel_id=1, source_target_pairs={{0,8},{8,16},{16,24},{24,0},{1,9},{9,17},{17,25},{25,1},{2,10},{10... | collective-permute-start | bytes 196616 | tf_op jit(solution)/shard_map/ppermute | solution.py:30
  4.4 5.9 %collective-permute-start.1 = (bf16[1,16,2048]{2,1,0:T(8,128)(2,1)S(1)}, bf16[1,16,2048]{2,1,0:T(8,128)(2,1)S(1)}, u32[]{:S(2)}, u32[]{:S(2)}) collective-permute-start(bf16[1,16,2048]{2,1,0:T(8,128)(2,1)S(1)} %get-tuple-element.38), channel_id=1, source_target_pairs={{0,16},{8,24},{16,0},{24,8},{1,17},{9,25},{17,1},{25,9},{2,18},{10... | collective-permute-start | bytes 196616 | tf_op jit(solution)/shard_map/ppermute | solution.py:30
  7.1 4.3 %collective-permute-start.2 = (bf16[1,16,2048]{2,1,0:T(8,128)(2,1)S(1)}, bf16[1,16,2048]{2,1,0:T(8,128)(2,1)S(1)}, u32[]{:S(2)}, u32[]{:S(2)}) collective-permute-start(bf16[1,16,2048]{2,1,0:T(8,128)(2,1)S(1)} %get-tuple-element.37), channel_id=1, source_target_pairs={{0,24},{8,0},{16,8},{24,16},{1,25},{9,1},{17,9},{25,17},{2,26},{10... | collective-permute-start | bytes 196616 | tf_op jit(solution)/shard_map/ppermute | solution.py:30
  11.4 10.3 %collective-permute-start.3 = (bf16[1,64,2048]{2,1,0:T(8,128)(2,1)S(1)}, bf16[1,64,2048]{2,1,0:T(8,128)(2,1)S(1)}, u32[]{:S(2)}, u32[]{:S(2)}) collective-permute-start(bf16[1,64,2048]{2,1,0:T(8,128)(2,1)S(1)} %pad_maximum_fusion), channel_id=1, source_target_pairs={{0,224},{32,0},{64,32},{96,64},{128,96},{160,128},{192,160},{224,1... | collective-permute-start | bytes 786440 | tf_op jit(solution)/shard_map/ppermute | solution.py:30
  17.4 8.1 %collective-permute-start.6 = (bf16[1,64,2048]{2,1,0:T(8,128)(2,1)S(1)}, bf16[1,64,2048]{2,1,0:T(8,128)(2,1)S(1)}, u32[]{:S(2)}, u32[]{:S(2)}) collective-permute-start(bf16[1,64,2048]{2,1,0:T(8,128)(2,1)S(1)} %pad_maximum_fusion), channel_id=1, source_target_pairs={{0,32},{32,64},{64,96},{96,128},{128,160},{160,192},{192,224},{224... | collective-permute-start | bytes 786440 | tf_op jit(solution)/shard_map/ppermute | solution.py:30
  21.8 7.6 %collective-permute-start.4 = (bf16[1,64,2048]{2,1,0:T(8,128)(2,1)S(1)}, bf16[1,64,2048]{2,1,0:T(8,128)(2,1)S(1)}, u32[]{:S(2)}, u32[]{:S(2)}) collective-permute-start(bf16[1,64,2048]{2,1,0:T(8,128)(2,1)S(1)} %collective-permute-done.3), channel_id=1, source_target_pairs={{0,224},{32,0},{64,32},{96,64},{128,96},{160,128},{192,160},{224,1... | collective-permute-start | bytes 786440 | tf_op jit(solution)/shard_map/ppermute | solution.py:30
  25.5 7.6 %collective-permute-start.7 = (bf16[1,64,2048]{2,1,0:T(8,128)(2,1)S(1)}, bf16[1,64,2048]{2,1,0:T(8,128)(2,1)S(1)}, u32[]{:S(2)}, u32[]{:S(2)}) collective-permute-start(bf16[1,64,2048]{2,1,0:T(8,128)(2,1)S(1)} %collective-permute-done.6), channel_id=1, source_target_pairs={{0,32},{32,64},{64,96},{96,128},{128,160},{160,192},{192,224},{224... | collective-permute-start | bytes 786440 | tf_op jit(solution)/shard_map/ppermute | solution.py:30
  29.3 8.2 %collective-permute-start.5 = (bf16[1,64,2048]{2,1,0:T(8,128)(2,1)S(1)}, bf16[1,64,2048]{2,1,0:T(8,128)(2,1)S(1)}, u32[]{:S(2)}, u32[]{:S(2)}) collective-permute-start(bf16[1,64,2048]{2,1,0:T(8,128)(2,1)S(1)} %collective-permute-done.4), channel_id=1, source_target_pairs={{0,224},{32,0},{64,32},{96,64},{128,96},{160,128},{192,160},{224,1... | collective-permute-start | bytes 786440 | tf_op jit(solution)/shard_map/ppermute | solution.py:30
  33.0 8.4 %collective-permute-start.8 = (bf16[1,64,2048]{2,1,0:T(8,128)(2,1)S(1)}, bf16[1,64,2048]{2,1,0:T(8,128)(2,1)S(1)}, u32[]{:S(2)}, u32[]{:S(2)}) collective-permute-start(bf16[1,64,2048]{2,1,0:T(8,128)(2,1)S(1)} %collective-permute-done.7), channel_id=1, source_target_pairs={{0,32},{32,64},{64,96},{96,128},{128,160},{160,192},{192,224},{224... | collective-permute-start | bytes 786440 | tf_op jit(solution)/shard_map/ppermute | solution.py:30
  37.5 6.3 %collective-permute-start.10 = (bf16[1,64,1024]{2,1,0:T(8,128)(2,1)S(1)}, bf16[1,64,1024]{2,1,0:T(8,128)(2,1)S(1)}, u32[]{:S(2)}, u32[]{:S(2)}) collective-permute-start(bf16[1,64,1024]{2,1,0:T(8,128)(2,1)S(1)} %slice.37), channel_id=1, source_target_pairs={{0,224},{32,0},{64,32},{96,64},{128,96},{160,128},{192,160},{224,1... | collective-permute-start | bytes 393224 | tf_op jit(solution)/shard_map/ppermute | solution.py:30
  41.4 6.3 %collective-permute-start.9 = (bf16[1,64,1024]{2,1,0:T(8,128)(2,1)S(1)}, bf16[1,64,1024]{2,1,0:T(8,128)(2,1)S(1)}, u32[]{:S(2)}, u32[]{:S(2)}) collective-permute-start(bf16[1,64,1024]{2,1,0:T(8,128)(2,1)S(1)} %slice.36), channel_id=1, source_target_pairs={{0,32},{32,64},{64,96},{96,128},{128,160},{160,192},{192,224},{224... | collective-permute-start | bytes 393224 | tf_op jit(solution)/shard_map/ppermute | solution.py:30
  50.6 1.4 %collective-permute-start.11 = (f32[34,128]{1,0:T(8,128)S(1)}, f32[34,128]{1,0:T(8,128)S(1)}, u32[]{:S(2)}, u32[]{:S(2)}) collective-permute-start(f32[34,128]{1,0:T(8,128)S(1)} %pad_maximum_fusion.1), channel_id=1, source_target_pairs={{0,1},{1,0},{2,3},{3,2},{4,5},{5,4},{6,7},{7,6},{8,9},{9,8},{10,11... | collective-permute-start | bytes 52232 | tf_op jit(solution)/shard_map/ppermute | solution.py:87
  52.0 4.1 %collective-permute-start.12 = (f32[34,128]{1,0:T(8,128)S(1)}, f32[34,128]{1,0:T(8,128)S(1)}, u32[]{:S(2)}, u32[]{:S(2)}) collective-permute-start(f32[34,128]{1,0:T(8,128)S(1)} %add.139), channel_id=1, source_target_pairs={{0,32},{32,0},{64,96},{96,64},{128,160},{160,128},{192,224},{224,1... | collective-permute-start | bytes 52232 | tf_op jit(solution)/shard_map/ppermute | solution.py:87
  56.1 4.8 %collective-permute-start.13 = (f32[34,128]{1,0:T(8,128)S(1)}, f32[34,128]{1,0:T(8,128)S(1)}, u32[]{:S(2)}, u32[]{:S(2)}) collective-permute-start(f32[34,128]{1,0:T(8,128)S(1)} %add.140), channel_id=1, source_target_pairs={{0,64},{32,96},{64,0},{96,32},{128,192},{160,224},{192,128},{224,1... | collective-permute-start | bytes 52232 | tf_op jit(solution)/shard_map/ppermute | solution.py:87
  60.9 7.7 %collective-permute-start.14 = (f32[34,128]{1,0:T(8,128)S(1)}, f32[34,128]{1,0:T(8,128)S(1)}, u32[]{:S(2)}, u32[]{:S(2)}) collective-permute-start(f32[34,128]{1,0:T(8,128)S(1)} %add.143), channel_id=1, source_target_pairs={{0,128},{32,160},{64,192},{96,224},{128,0},{160,32},{192,64},{224,... | collective-permute-start | bytes 52232 | tf_op jit(solution)/shard_map/ppermute | solution.py:87
  68.6 7.8 %collective-permute-start.15 = (f32[34,128]{1,0:T(8,128)S(1)}, f32[34,128]{1,0:T(8,128)S(1)}, u32[]{:S(2)}, u32[]{:S(2)}) collective-permute-start(f32[34,128]{1,0:T(8,128)S(1)} %add.144), channel_id=1, source_target_pairs={{0,8},{8,0},{16,24},{24,16},{1,9},{9,1},{17,25},{25,17},{2,10},{10... | collective-permute-start | bytes 52232 | tf_op jit(solution)/shard_map/ppermute | solution.py:87
  76.4 10.6 %collective-permute-start.16 = (f32[34,128]{1,0:T(8,128)S(1)}, f32[34,128]{1,0:T(8,128)S(1)}, u32[]{:S(2)}, u32[]{:S(2)}) collective-permute-start(f32[34,128]{1,0:T(8,128)S(1)} %add.147), channel_id=1, source_target_pairs={{0,16},{8,24},{16,0},{24,8},{1,17},{9,25},{17,1},{25,9},{2,18},{10... | collective-permute-start | bytes 52232 | tf_op jit(solution)/shard_map/ppermute | solution.py:87
  90.7 4.3 %collective-permute-start.17 = (bf16[1,16,2048]{2,1,0:T(8,128)(2,1)S(1)}, bf16[1,16,2048]{2,1,0:T(8,128)(2,1)S(1)}, u32[]{:S(2)}, u32[]{:S(2)}) collective-permute-start(bf16[1,16,2048]{2,1,0:T(8,128)(2,1)S(1)} %get-tuple-element.36), channel_id=1, source_target_pairs={{0,24},{8,0},{16,8},{24,16},{1,25},{9,1},{17,9},{25,17},{2,26},{10... | collective-permute-start | bytes 196616 | tf_op jit(solution)/shard_map/ppermute | solution.py:30
  91.2 5.8 %collective-permute-start.18 = (bf16[1,16,2048]{2,1,0:T(8,128)(2,1)S(1)}, bf16[1,16,2048]{2,1,0:T(8,128)(2,1)S(1)}, u32[]{:S(2)}, u32[]{:S(2)}) collective-permute-start(bf16[1,16,2048]{2,1,0:T(8,128)(2,1)S(1)} %get-tuple-element.35), channel_id=1, source_target_pairs={{0,16},{8,24},{16,0},{24,8},{1,17},{9,25},{17,1},{25,9},{2,18},{10... | collective-permute-start | bytes 196616 | tf_op jit(solution)/shard_map/ppermute | solution.py:30
  92.4 5.5 %collective-permute-start.19 = (bf16[1,16,2048]{2,1,0:T(8,128)(2,1)S(1)}, bf16[1,16,2048]{2,1,0:T(8,128)(2,1)S(1)}, u32[]{:S(2)}, u32[]{:S(2)}) collective-permute-start(bf16[1,16,2048]{2,1,0:T(8,128)(2,1)S(1)} %get-tuple-element.34), channel_id=1, source_target_pairs={{0,8},{8,16},{16,24},{24,0},{1,9},{9,17},{17,25},{25,1},{2,10},{10... | collective-permute-start | bytes 196616 | tf_op jit(solution)/shard_map/ppermute | solution.py:30
  (5 other events, 21.5 us)

commit v12 on v9

--- a/solution.py
+++ b/solution.py
@@ -135,7 +135,7 @@
     )
     blocks = ring_gather(strip, "outer")
     local = vector_partials(normed, ln_gain, ln_bias, ln_cotangent, router_cotangent)
-    steps = [step for axis in ("section",) + SHARD for step in butterfly_rounds(axis)]
+    steps = [step for axis in SHARD[::-1] + ("section",) for step in butterfly_rounds(axis)]
     rounds = [steps[:2]] + [[step] for step in steps[2:]]
     result, vec_grad = orthogonalize(blocks, local, rounds, inner * rows_piece)
     next_first, next_second, adam_step = adam(vec_grad, first_moment, second_moment)

time: 94.4 us -> 96.9 us (1.026)
  waiting for transfers between devices: 26.6 us -> 27.6 us
    ppermute x14, starting transfers between devices: 25 us -> 26.5 us  [shift(): return lax.ppermute(value, axis, [(i, (i + k) % size) for i in range(size)])]
  transfers between devices with their start and end apart: 20 -> 20, of which waited for: 14 -> 13; matrix products, arithmetic and copies ran while one was open for 26% -> 25% of each run, Pallas kernels for 0% -> 0%
where the time goes in v12:
time: 96.9 us; the launch traced here: 96.3 us
  starting transfers between devices  33.8 us (35%)
  waiting for transfers between devices  27.6 us (28%)
  matrix products  26.1 us (27%)
  other arithmetic  6.67 us (7%)
  between operations  1.76 us (2%)
    ppermute x14, waiting for transfers between devices, shift(): return lax.ppermute(value, axis, [(i, (i + k) % size) for i in range(size)])  26.5 us
    ppermute x14, starting transfers between devices, shift(): return lax.ppermute(value, axis, [(i, (i + k) % size) for i in range(size)])  26.5 us
    dot_general x5, matrix products, orthogonalize(): jnp.einsum('kij,kjl->kil', poly, iterate, preferred_element_type=jnp.floa...  15 us
    dot_general x5, matrix products, orthogonalize(): jnp.einsum('kij,klj->kil', iterate, iterate, preferred_element_type=jnp.f...  11 us
    ppermute x6, starting transfers between devices, butterfly_rounds(): lax.ppermute(value, axis, perm)  7.34 us
    convert_element_type x1, other arithmetic, on_device(): nesterov = (grad_float + MUON_DECAY * next_momentum).astype(jnp.bfloat16)  2.08 us
  transfers between devices with their start and end apart: 20, of which 13 were waited for; matrix products, arithmetic and copies ran while one was open for 25% of the time, Pallas kernels for 0%

profile of v12, /device:TPU:16, one launch (start us, length us, event | category | flops | bytes accessed | tf_op | source)
XLA Modules:
  0.0 96.3 jit_solution(15807115704156752828)
XLA Ops:
  0.7 2.1 %fusion.35 = (bf16[4,16,2048]{2,1,0:T(8,128)(2,1)S(1)}, f32[4,16,2048]{2,1,0:T(8,128)}) fusion(bf16[4,16,2048]{2,1,0:T(8,128)(2,1)} %param.9, f32[4,16,2048]{2,1,0:T(8,128)} %param.10), kind=kLoop, calls=%fused_computation.50 | loop fusion | flops 786432 | bytes 1572864 | tf_op jit(solution)/shard_map/convert_element_type | solution.py:124
  2.9 1.6 %collective-permute-start = (bf16[1,16,2048]{2,1,0:T(8,128)(2,1)S(1)}, bf16[1,16,2048]{2,1,0:T(8,128)(2,1)S(1)}, u32[]{:S(2)}, u32[]{:S(2)}) collective-permute-start(bf16[1,16,2048]{2,1,0:T(8,128)(2,1)S(1)} %get-tuple-element.39), channel_id=1, source_target_pairs={{0,8},{8,16},{16,24},{24,0},{1,9},{9,17},{17,25},{25,1},{2,10},{10... | collective-permute-start | bytes 196616 | tf_op jit(solution)/shard_map/ppermute | solution.py:30
  4.4 2.7 %collective-permute-start.1 = (bf16[1,16,2048]{2,1,0:T(8,128)(2,1)S(1)}, bf16[1,16,2048]{2,1,0:T(8,128)(2,1)S(1)}, u32[]{:S(2)}, u32[]{:S(2)}) collective-permute-start(bf16[1,16,2048]{2,1,0:T(8,128)(2,1)S(1)} %get-tuple-element.38), channel_id=1, source_target_pairs={{0,16},{8,24},{16,0},{24,8},{1,17},{9,25},{17,1},{25,9},{2,18},{10... | collective-permute-start | bytes 196616 | tf_op jit(solution)/shard_map/ppermute | solution.py:30
  11.4 5.9 %collective-permute-start.3 = (bf16[1,64,2048]{2,1,0:T(8,128)(2,1)S(1)}, bf16[1,64,2048]{2,1,0:T(8,128)(2,1)S(1)}, u32[]{:S(2)}, u32[]{:S(2)}) collective-permute-start(bf16[1,64,2048]{2,1,0:T(8,128)(2,1)S(1)} %pad_maximum_fusion), channel_id=1, source_target_pairs={{0,224},{32,0},{64,32},{96,64},{128,96},{160,128},{192,160},{224,1... | collective-permute-start | bytes 786440 | tf_op jit(solution)/shard_map/ppermute | solution.py:30
  17.4 4.3 %collective-permute-done.3 = bf16[1,64,2048]{2,1,0:T(8,128)(2,1)S(1)} collective-permute-done((bf16[1,64,2048]{2,1,0:T(8,128)(2,1)S(1)}, bf16[1,64,2048]{2,1,0:T(8,128)(2,1)S(1)}, u32[]{:S(2)}, u32[]{:S(2)}) %collective-permute-start.3) | collective-permute-done | bytes 262176 | tf_op jit(solution)/shard_map/ppermute | solution.py:30
  21.8 3.7 %collective-permute-start.4 = (bf16[1,64,2048]{2,1,0:T(8,128)(2,1)S(1)}, bf16[1,64,2048]{2,1,0:T(8,128)(2,1)S(1)}, u32[]{:S(2)}, u32[]{:S(2)}) collective-permute-start(bf16[1,64,2048]{2,1,0:T(8,128)(2,1)S(1)} %collective-permute-done.3), channel_id=1, source_target_pairs={{0,224},{32,0},{64,32},{96,64},{128,96},{160,128},{192,160},{224,1... | collective-permute-start | bytes 786440 | tf_op jit(solution)/shard_map/ppermute | solution.py:30
  25.5 3.9 %collective-permute-done.4 = bf16[1,64,2048]{2,1,0:T(8,128)(2,1)S(1)} collective-permute-done((bf16[1,64,2048]{2,1,0:T(8,128)(2,1)S(1)}, bf16[1,64,2048]{2,1,0:T(8,128)(2,1)S(1)}, u32[]{:S(2)}, u32[]{:S(2)}) %collective-permute-start.4) | collective-permute-done | bytes 262176 | tf_op jit(solution)/shard_map/ppermute | solution.py:30
  29.3 3.7 %collective-permute-start.5 = (bf16[1,64,2048]{2,1,0:T(8,128)(2,1)S(1)}, bf16[1,64,2048]{2,1,0:T(8,128)(2,1)S(1)}, u32[]{:S(2)}, u32[]{:S(2)}) collective-permute-start(bf16[1,64,2048]{2,1,0:T(8,128)(2,1)S(1)} %collective-permute-done.4), channel_id=1, source_target_pairs={{0,224},{32,0},{64,32},{96,64},{128,96},{160,128},{192,160},{224,1... | collective-permute-start | bytes 786440 | tf_op jit(solution)/shard_map/ppermute | solution.py:30
  33.1 4.4 %collective-permute-done.5 = bf16[1,64,2048]{2,1,0:T(8,128)(2,1)S(1)} collective-permute-done((bf16[1,64,2048]{2,1,0:T(8,128)(2,1)S(1)}, bf16[1,64,2048]{2,1,0:T(8,128)(2,1)S(1)}, u32[]{:S(2)}, u32[]{:S(2)}) %collective-permute-start.5) | collective-permute-done | bytes 262176 | tf_op jit(solution)/shard_map/ppermute | solution.py:30
  37.5 3.8 %collective-permute-start.10 = (bf16[1,64,1024]{2,1,0:T(8,128)(2,1)S(1)}, bf16[1,64,1024]{2,1,0:T(8,128)(2,1)S(1)}, u32[]{:S(2)}, u32[]{:S(2)}) collective-permute-start(bf16[1,64,1024]{2,1,0:T(8,128)(2,1)S(1)} %slice.37), channel_id=1, source_target_pairs={{0,224},{32,0},{64,32},{96,64},{128,96},{160,128},{192,160},{224,1... | collective-permute-start | bytes 393224 | tf_op jit(solution)/shard_map/ppermute | solution.py:30
  41.5 2.3 %collective-permute-done.10 = bf16[1,64,1024]{2,1,0:T(8,128)(2,1)S(1)} collective-permute-done((bf16[1,64,1024]{2,1,0:T(8,128)(2,1)S(1)}, bf16[1,64,1024]{2,1,0:T(8,128)(2,1)S(1)}, u32[]{:S(2)}, u32[]{:S(2)}) %collective-permute-start.10) | collective-permute-done | bytes 131104 | tf_op jit(solution)/shard_map/ppermute | solution.py:30
  43.8 3.8 %collective-permute-done.9 = bf16[1,64,1024]{2,1,0:T(8,128)(2,1)S(1)} collective-permute-done((bf16[1,64,1024]{2,1,0:T(8,128)(2,1)S(1)}, bf16[1,64,1024]{2,1,0:T(8,128)(2,1)S(1)}, u32[]{:S(2)}, u32[]{:S(2)}) %collective-permute-start.9) | collective-permute-done | bytes 131104 | tf_op jit(solution)/shard_map/ppermute | solution.py:30
  47.8 1.7 %fusion = f32[]{:T(128)} fusion(bf16[1,512,2048]{2,1,0:T(8,128)(2,1)S(1)} %constant_dynamic-update-slice_fusion), kind=kLoop, calls=%fused_computation.2 | loop fusion | flops 3145727 | bytes 2097156 | tf_op jit(solution)/shard_map/reduce_sum | solution.py:53
  54.5 2.2 %collective-permute-start.12 = (f32[34,128]{1,0:T(8,128)S(1)}, f32[34,128]{1,0:T(8,128)S(1)}, u32[]{:S(2)}, u32[]{:S(2)}) collective-permute-start(f32[34,128]{1,0:T(8,128)S(1)} %add.139), channel_id=1, source_target_pairs={{0,16},{8,24},{16,0},{24,8},{1,17},{9,25},{17,1},{25,9},{2,18},{10... | collective-permute-start | bytes 52232 | tf_op jit(solution)/shard_map/ppermute | solution.py:87
  56.7 3.8 %fusion.5 = bf16[1,512,2048]{2,1,0:T(8,128)(2,1)S(1)} fusion(bf16[1,512,2048]{2,1,0:T(8,128)(2,1)} %copy-done.1, f32[512,512]{1,0:T(8,128)S(1)} %fusion.21), kind=kOutput, calls=%fused_computation.11 | convolution fusion | flops 1347682304 | bytes 5242880 | tf_op jit(solution)/shard_map/kij,kjl->kil/dot_general | solution.py:69
  61.9 2.9 %fusion.4 = bf16[1,512,2048]{2,1,0:T(8,128)(2,1)} fusion(bf16[1,512,2048]{2,1,0:T(8,128)(2,1)S(1)} %fusion.5, f32[512,512]{1,0:T(8,128)S(1)} %fusion.18), kind=kOutput, calls=%fused_computation.9 | convolution fusion | flops 1347682304 | bytes 5242880 | tf_op jit(solution)/shard_map/kij,kjl->kil/dot_general | solution.py:69
  65.0 3.6 %fusion.15 = f32[512,512]{1,0:T(8,128)S(1)} fusion(bf16[1,512,2048]{2,1,0:T(8,128)(2,1)} %fusion.4), kind=kOutput, calls=%fused_computation.22 | convolution fusion | flops 1073741824 | bytes 3145728 | tf_op jit(solution)/shard_map/kij,klj->kil/dot_general | solution.py:62
  68.6 2.9 %fusion.3 = bf16[1,512,2048]{2,1,0:T(8,128)(2,1)} fusion(bf16[1,512,2048]{2,1,0:T(8,128)(2,1)S(1)} %copy-done.8, f32[512,512]{1,0:T(8,128)S(1)} %fusion.15), kind=kOutput, calls=%fused_computation.7 | convolution fusion | flops 1347682304 | bytes 5242880 | tf_op jit(solution)/shard_map/kij,kjl->kil/dot_general | solution.py:69
  71.6 3.4 %collective-permute-start.15 = (f32[34,128]{1,0:T(8,128)S(1)}, f32[34,128]{1,0:T(8,128)S(1)}, u32[]{:S(2)}, u32[]{:S(2)}) collective-permute-start(f32[34,128]{1,0:T(8,128)S(1)} %add.146), channel_id=1, source_target_pairs={{0,128},{32,160},{64,192},{96,224},{128,0},{160,32},{192,64},{224,... | collective-permute-start | bytes 52232 | tf_op jit(solution)/shard_map/ppermute | solution.py:87
  75.0 3.5 %fusion.12 = f32[512,512]{1,0:T(8,128)S(1)} fusion(bf16[1,512,2048]{2,1,0:T(8,128)(2,1)} %fusion.3), kind=kOutput, calls=%fused_computation.19 | convolution fusion | flops 1073741824 | bytes 3145728 | tf_op jit(solution)/shard_map/kij,klj->kil/dot_general | solution.py:62
  78.5 3.8 %fusion.2 = bf16[1,512,2048]{2,1,0:T(8,128)(2,1)S(1)} fusion(bf16[1,512,2048]{2,1,0:T(8,128)(2,1)} %fusion.3, f32[512,512]{1,0:T(8,128)S(1)} %fusion.12), kind=kOutput, calls=%fused_computation.5 | convolution fusion | flops 1347682304 | bytes 5242880 | tf_op jit(solution)/shard_map/kij,kjl->kil/dot_general | solution.py:69
  86.1 2.0 %collective-permute-start.16 = (bf16[1,16,2048]{2,1,0:T(8,128)(2,1)S(1)}, bf16[1,16,2048]{2,1,0:T(8,128)(2,1)S(1)}, u32[]{:S(2)}, u32[]{:S(2)}) collective-permute-start(bf16[1,16,2048]{2,1,0:T(8,128)(2,1)S(1)} %get-tuple-element.36), channel_id=1, source_target_pairs={{0,24},{8,0},{16,8},{24,16},{1,25},{9,1},{17,9},{25,17},{2,26},{10... | collective-permute-start | bytes 196616 | tf_op jit(solution)/shard_map/ppermute | solution.py:30
  88.1 1.5 %collective-permute-start.17 = (bf16[1,16,2048]{2,1,0:T(8,128)(2,1)S(1)}, bf16[1,16,2048]{2,1,0:T(8,128)(2,1)S(1)}, u32[]{:S(2)}, u32[]{:S(2)}) collective-permute-start(bf16[1,16,2048]{2,1,0:T(8,128)(2,1)S(1)} %get-tuple-element.35), channel_id=1, source_target_pairs={{0,16},{8,24},{16,0},{24,8},{1,17},{9,25},{17,1},{25,9},{2,18},{10... | collective-permute-start | bytes 196616 | tf_op jit(solution)/shard_map/ppermute | solution.py:30
  91.5 3.1 %collective-permute-done.17 = bf16[1,16,2048]{2,1,0:T(8,128)(2,1)S(1)} collective-permute-done((bf16[1,16,2048]{2,1,0:T(8,128)(2,1)S(1)}, bf16[1,16,2048]{2,1,0:T(8,128)(2,1)S(1)}, u32[]{:S(2)}, u32[]{:S(2)}) %collective-permute-start.17) | collective-permute-done | bytes 65568 | tf_op jit(solution)/shard_map/ppermute | solution.py:30
  (81 shorter events, 17.7 us)
Async XLA Ops:
  0.6 8.0 %copy-start = (bf16[512,32]{0,1:T(8,128)(2,1)S(1)}, bf16[512,32]{0,1:T(8,128)(2,1)}, u32[]{:S(2)}) copy-start(bf16[512,32]{0,1:T(8,128)(2,1)} %param.15) | copy-start | bytes 98308
  0.6 7.9 %copy-start.2 = (bf16[512,128]{1,0:T(8,128)(2,1)S(1)}, bf16[512,128]{1,0:T(8,128)(2,1)}, u32[]{:S(2)}) copy-start(bf16[512,128]{1,0:T(8,128)(2,1)} %param.11) | copy-start | bytes 393220
  0.7 7.9 %copy-start.6 = (f32[128]{0:T(128)S(1)}, f32[128]{0:T(128)}, u32[]{:S(2)}) copy-start(f32[128]{0:T(128)} %param.13) | copy-start | bytes 1540
  0.7 8.1 %copy-start.3 = (bf16[512,128]{1,0:T(8,128)(2,1)S(1)}, bf16[512,128]{1,0:T(8,128)(2,1)}, u32[]{:S(2)}) copy-start(bf16[512,128]{1,0:T(8,128)(2,1)} %param.14) | copy-start | bytes 393220
  2.9 6.1 %collective-permute-start = (bf16[1,16,2048]{2,1,0:T(8,128)(2,1)S(1)}, bf16[1,16,2048]{2,1,0:T(8,128)(2,1)S(1)}, u32[]{:S(2)}, u32[]{:S(2)}) collective-permute-start(bf16[1,16,2048]{2,1,0:T(8,128)(2,1)S(1)} %get-tuple-element.39), channel_id=1, source_target_pairs={{0,8},{8,16},{16,24},{24,0},{1,9},{9,17},{17,25},{25,1},{2,10},{10... | collective-permute-start | bytes 196616 | tf_op jit(solution)/shard_map/ppermute | solution.py:30
  4.4 5.9 %collective-permute-start.1 = (bf16[1,16,2048]{2,1,0:T(8,128)(2,1)S(1)}, bf16[1,16,2048]{2,1,0:T(8,128)(2,1)S(1)}, u32[]{:S(2)}, u32[]{:S(2)}) collective-permute-start(bf16[1,16,2048]{2,1,0:T(8,128)(2,1)S(1)} %get-tuple-element.38), channel_id=1, source_target_pairs={{0,16},{8,24},{16,0},{24,8},{1,17},{9,25},{17,1},{25,9},{2,18},{10... | collective-permute-start | bytes 196616 | tf_op jit(solution)/shard_map/ppermute | solution.py:30
  7.1 4.3 %collective-permute-start.2 = (bf16[1,16,2048]{2,1,0:T(8,128)(2,1)S(1)}, bf16[1,16,2048]{2,1,0:T(8,128)(2,1)S(1)}, u32[]{:S(2)}, u32[]{:S(2)}) collective-permute-start(bf16[1,16,2048]{2,1,0:T(8,128)(2,1)S(1)} %get-tuple-element.37), channel_id=1, source_target_pairs={{0,24},{8,0},{16,8},{24,16},{1,25},{9,1},{17,9},{25,17},{2,26},{10... | collective-permute-start | bytes 196616 | tf_op jit(solution)/shard_map/ppermute | solution.py:30
  11.4 10.3 %collective-permute-start.3 = (bf16[1,64,2048]{2,1,0:T(8,128)(2,1)S(1)}, bf16[1,64,2048]{2,1,0:T(8,128)(2,1)S(1)}, u32[]{:S(2)}, u32[]{:S(2)}) collective-permute-start(bf16[1,64,2048]{2,1,0:T(8,128)(2,1)S(1)} %pad_maximum_fusion), channel_id=1, source_target_pairs={{0,224},{32,0},{64,32},{96,64},{128,96},{160,128},{192,160},{224,1... | collective-permute-start | bytes 786440 | tf_op jit(solution)/shard_map/ppermute | solution.py:30
  17.4 8.1 %collective-permute-start.6 = (bf16[1,64,2048]{2,1,0:T(8,128)(2,1)S(1)}, bf16[1,64,2048]{2,1,0:T(8,128)(2,1)S(1)}, u32[]{:S(2)}, u32[]{:S(2)}) collective-permute-start(bf16[1,64,2048]{2,1,0:T(8,128)(2,1)S(1)} %pad_maximum_fusion), channel_id=1, source_target_pairs={{0,32},{32,64},{64,96},{96,128},{128,160},{160,192},{192,224},{224... | collective-permute-start | bytes 786440 | tf_op jit(solution)/shard_map/ppermute | solution.py:30
  21.8 7.6 %collective-permute-start.4 = (bf16[1,64,2048]{2,1,0:T(8,128)(2,1)S(1)}, bf16[1,64,2048]{2,1,0:T(8,128)(2,1)S(1)}, u32[]{:S(2)}, u32[]{:S(2)}) collective-permute-start(bf16[1,64,2048]{2,1,0:T(8,128)(2,1)S(1)} %collective-permute-done.3), channel_id=1, source_target_pairs={{0,224},{32,0},{64,32},{96,64},{128,96},{160,128},{192,160},{224,1... | collective-permute-start | bytes 786440 | tf_op jit(solution)/shard_map/ppermute | solution.py:30
  25.5 7.6 %collective-permute-start.7 = (bf16[1,64,2048]{2,1,0:T(8,128)(2,1)S(1)}, bf16[1,64,2048]{2,1,0:T(8,128)(2,1)S(1)}, u32[]{:S(2)}, u32[]{:S(2)}) collective-permute-start(bf16[1,64,2048]{2,1,0:T(8,128)(2,1)S(1)} %collective-permute-done.6), channel_id=1, source_target_pairs={{0,32},{32,64},{64,96},{96,128},{128,160},{160,192},{192,224},{224... | collective-permute-start | bytes 786440 | tf_op jit(solution)/shard_map/ppermute | solution.py:30
  29.3 8.2 %collective-permute-start.5 = (bf16[1,64,2048]{2,1,0:T(8,128)(2,1)S(1)}, bf16[1,64,2048]{2,1,0:T(8,128)(2,1)S(1)}, u32[]{:S(2)}, u32[]{:S(2)}) collective-permute-start(bf16[1,64,2048]{2,1,0:T(8,128)(2,1)S(1)} %collective-permute-done.4), channel_id=1, source_target_pairs={{0,224},{32,0},{64,32},{96,64},{128,96},{160,128},{192,160},{224,1... | collective-permute-start | bytes 786440 | tf_op jit(solution)/shard_map/ppermute | solution.py:30
  33.0 8.4 %collective-permute-start.8 = (bf16[1,64,2048]{2,1,0:T(8,128)(2,1)S(1)}, bf16[1,64,2048]{2,1,0:T(8,128)(2,1)S(1)}, u32[]{:S(2)}, u32[]{:S(2)}) collective-permute-start(bf16[1,64,2048]{2,1,0:T(8,128)(2,1)S(1)} %collective-permute-done.7), channel_id=1, source_target_pairs={{0,32},{32,64},{64,96},{96,128},{128,160},{160,192},{192,224},{224... | collective-permute-start | bytes 786440 | tf_op jit(solution)/shard_map/ppermute | solution.py:30
  37.5 6.3 %collective-permute-start.10 = (bf16[1,64,1024]{2,1,0:T(8,128)(2,1)S(1)}, bf16[1,64,1024]{2,1,0:T(8,128)(2,1)S(1)}, u32[]{:S(2)}, u32[]{:S(2)}) collective-permute-start(bf16[1,64,1024]{2,1,0:T(8,128)(2,1)S(1)} %slice.37), channel_id=1, source_target_pairs={{0,224},{32,0},{64,32},{96,64},{128,96},{160,128},{192,160},{224,1... | collective-permute-start | bytes 393224 | tf_op jit(solution)/shard_map/ppermute | solution.py:30
  41.4 6.3 %collective-permute-start.9 = (bf16[1,64,1024]{2,1,0:T(8,128)(2,1)S(1)}, bf16[1,64,1024]{2,1,0:T(8,128)(2,1)S(1)}, u32[]{:S(2)}, u32[]{:S(2)}) collective-permute-start(bf16[1,64,1024]{2,1,0:T(8,128)(2,1)S(1)} %slice.36), channel_id=1, source_target_pairs={{0,32},{32,64},{64,96},{96,128},{128,160},{160,192},{192,224},{224... | collective-permute-start | bytes 393224 | tf_op jit(solution)/shard_map/ppermute | solution.py:30
  50.6 3.9 %collective-permute-start.11 = (f32[34,128]{1,0:T(8,128)S(1)}, f32[34,128]{1,0:T(8,128)S(1)}, u32[]{:S(2)}, u32[]{:S(2)}) collective-permute-start(f32[34,128]{1,0:T(8,128)S(1)} %pad_maximum_fusion.1), channel_id=1, source_target_pairs={{0,8},{8,0},{16,24},{24,16},{1,9},{9,1},{17,25},{25,17},{2,10},{10... | collective-permute-start | bytes 52232 | tf_op jit(solution)/shard_map/ppermute | solution.py:87
  54.5 6.1 %collective-permute-start.12 = (f32[34,128]{1,0:T(8,128)S(1)}, f32[34,128]{1,0:T(8,128)S(1)}, u32[]{:S(2)}, u32[]{:S(2)}) collective-permute-start(f32[34,128]{1,0:T(8,128)S(1)} %add.139), channel_id=1, source_target_pairs={{0,16},{8,24},{16,0},{24,8},{1,17},{9,25},{17,1},{25,9},{2,18},{10... | collective-permute-start | bytes 52232 | tf_op jit(solution)/shard_map/ppermute | solution.py:87
  60.5 4.3 %collective-permute-start.13 = (f32[34,128]{1,0:T(8,128)S(1)}, f32[34,128]{1,0:T(8,128)S(1)}, u32[]{:S(2)}, u32[]{:S(2)}) collective-permute-start(f32[34,128]{1,0:T(8,128)S(1)} %add.140), channel_id=1, source_target_pairs={{0,32},{32,0},{64,96},{96,64},{128,160},{160,128},{192,224},{224,1... | collective-permute-start | bytes 52232 | tf_op jit(solution)/shard_map/ppermute | solution.py:87
  64.9 6.7 %collective-permute-start.14 = (f32[34,128]{1,0:T(8,128)S(1)}, f32[34,128]{1,0:T(8,128)S(1)}, u32[]{:S(2)}, u32[]{:S(2)}) collective-permute-start(f32[34,128]{1,0:T(8,128)S(1)} %add.143), channel_id=1, source_target_pairs={{0,64},{32,96},{64,0},{96,32},{128,192},{160,224},{192,128},{224,1... | collective-permute-start | bytes 52232 | tf_op jit(solution)/shard_map/ppermute | solution.py:87
  71.6 10.7 %collective-permute-start.15 = (f32[34,128]{1,0:T(8,128)S(1)}, f32[34,128]{1,0:T(8,128)S(1)}, u32[]{:S(2)}, u32[]{:S(2)}) collective-permute-start(f32[34,128]{1,0:T(8,128)S(1)} %add.146), channel_id=1, source_target_pairs={{0,128},{32,160},{64,192},{96,224},{128,0},{160,32},{192,64},{224,... | collective-permute-start | bytes 52232 | tf_op jit(solution)/shard_map/ppermute | solution.py:87
  86.0 3.7 %collective-permute-start.19 = (f32[34,128]{1,0:T(8,128)S(1)}, f32[34,128]{1,0:T(8,128)S(1)}, u32[]{:S(2)}, u32[]{:S(2)}) collective-permute-start(f32[34,128]{1,0:T(8,128)S(1)} %add.149), channel_id=1, source_target_pairs={{0,1},{1,0},{2,3},{3,2},{4,5},{5,4},{6,7},{7,6},{8,9},{9,8},{10,11... | collective-permute-start | bytes 52232 | tf_op jit(solution)/shard_map/ppermute | solution.py:87
  86.1 5.4 %collective-permute-start.16 = (bf16[1,16,2048]{2,1,0:T(8,128)(2,1)S(1)}, bf16[1,16,2048]{2,1,0:T(8,128)(2,1)S(1)}, u32[]{:S(2)}, u32[]{:S(2)}) collective-permute-start(bf16[1,16,2048]{2,1,0:T(8,128)(2,1)S(1)} %get-tuple-element.36), channel_id=1, source_target_pairs={{0,24},{8,0},{16,8},{24,16},{1,25},{9,1},{17,9},{25,17},{2,26},{10... | collective-permute-start | bytes 196616 | tf_op jit(solution)/shard_map/ppermute | solution.py:30
  88.1 6.4 %collective-permute-start.17 = (bf16[1,16,2048]{2,1,0:T(8,128)(2,1)S(1)}, bf16[1,16,2048]{2,1,0:T(8,128)(2,1)S(1)}, u32[]{:S(2)}, u32[]{:S(2)}) collective-permute-start(bf16[1,16,2048]{2,1,0:T(8,128)(2,1)S(1)} %get-tuple-element.35), channel_id=1, source_target_pairs={{0,16},{8,24},{16,0},{24,8},{1,17},{9,25},{17,1},{25,9},{2,18},{10... | collective-permute-start | bytes 196616 | tf_op jit(solution)/shard_map/ppermute | solution.py:30
  89.7 5.7 %collective-permute-start.18 = (bf16[1,16,2048]{2,1,0:T(8,128)(2,1)S(1)}, bf16[1,16,2048]{2,1,0:T(8,128)(2,1)S(1)}, u32[]{:S(2)}, u32[]{:S(2)}) collective-permute-start(bf16[1,16,2048]{2,1,0:T(8,128)(2,1)S(1)} %get-tuple-element.34), channel_id=1, source_target_pairs={{0,8},{8,16},{16,24},{24,0},{1,9},{9,17},{17,25},{25,1},{2,10},{10... | collective-permute-start | bytes 196616 | tf_op jit(solution)/shard_map/ppermute | solution.py:30
  (5 other events, 24.8 us)

commit v13 on v9

--- a/solution.py
+++ b/solution.py
@@ -46,11 +46,12 @@
         from_ahead = shift(from_ahead, axis, -1)
         ahead.append(from_ahead)
         behind.append(from_behind)
-    return jnp.concatenate([strip] + ahead + behind[::-1], axis=1)
+    pieces = [strip] + ahead + behind[::-1]
+    squares = sum(jnp.sum(jnp.square(piece.astype(jnp.float32)), axis=(1, 2)) for piece in pieces)
+    return jnp.concatenate(pieces, axis=1), squares
 
 
-def orthogonalize(blocks, carried, rounds, keep):
-    squares = jnp.sum(jnp.square(blocks.astype(jnp.float32)), axis=(1, 2))
+def orthogonalize(blocks, squares, carried, rounds, keep):
     total = jnp.sqrt(squares)
     iterate = (blocks.astype(jnp.float32) / (total + NORM_EPSILON)[:, None, None]).astype(
         jnp.bfloat16
@@ -133,11 +134,11 @@
          for k in range(inner)],
         axis=1,
     )
-    blocks = ring_gather(strip, "outer")
+    blocks, squares = ring_gather(strip, "outer")
     local = vector_partials(normed, ln_gain, ln_bias, ln_cotangent, router_cotangent)
     steps = [step for axis in ("section",) + SHARD for step in butterfly_rounds(axis)]
     rounds = [steps[:2]] + [[step] for step in steps[2:]]
-    result, vec_grad = orthogonalize(blocks, local, rounds, inner * rows_piece)
+    result, vec_grad = orthogonalize(blocks, squares, local, rounds, inner * rows_piece)
     next_first, next_second, adam_step = adam(vec_grad, first_moment, second_moment)
     back = jnp.stack(
         [shift(result[:, k * rows_piece:(k + 1) * rows_piece], "inner", -k) for k in range(inner)],

time: 94.4 us -> 98.9 us (1.048)
  waiting for transfers between devices: 26.6 us -> 17.6 us
  other arithmetic: 6.67 us -> 11.7 us
  between operations: 1.75 us -> 6.24 us
  starting transfers between devices: 33 us -> 35.3 us
  local copies, waits for them, and re-layouts: 0.28 us -> 1.86 us
    ppermute x14, waiting for transfers between devices: 25.8 us -> 17.6 us  [shift(): return lax.ppermute(value, axis, [(i, (i + k) % size) for i in range(size)])]
    reduce_sum x1 -> x8, other arithmetic: 1.68 us -> 6.79 us  [ring_gather(): jnp.sum(jnp.square(piece.astype(jnp.float32)), axis=(1, 2))]
    ppermute x6, starting transfers between devices: 7.97 us -> 10.4 us  [butterfly_rounds(): lax.ppermute(value, axis, perm)]
  transfers between devices with their start and end apart: 20 -> 20, of which waited for: 14 -> 10; matrix products, arithmetic and copies ran while one was open for 26% -> 33% of each run, Pallas kernels for 0% -> 0%
where the time goes in v13:
time: 98.9 us; the launch traced here: 98.6 us
  starting transfers between devices  35.3 us (36%)
  matrix products  26 us (26%)
  waiting for transfers between devices  17.6 us (18%)
  other arithmetic  11.7 us (12%)
  between operations  6.24 us (6%)
  local copies, waits for them, and re-layouts  1.86 us (2%)
    ppermute x14, starting transfers between devices, shift(): return lax.ppermute(value, axis, [(i, (i + k) % size) for i in range(size)])  24.9 us
    ppermute x14, waiting for transfers between devices, shift(): return lax.ppermute(value, axis, [(i, (i + k) % size) for i in range(size)])  17.6 us
    dot_general x5, matrix products, orthogonalize(): jnp.einsum('kij,kjl->kil', poly, iterate, preferred_element_type=jnp.floa...  15 us
    dot_general x5, matrix products, orthogonalize(): jnp.einsum('kij,klj->kil', iterate, iterate, preferred_element_type=jnp.f...  10.8 us
    ppermute x6, starting transfers between devices, butterfly_rounds(): lax.ppermute(value, axis, perm)  10.4 us
    reduce_sum x8, other arithmetic, ring_gather(): jnp.sum(jnp.square(piece.astype(jnp.float32)), axis=(1, 2))  6.79 us
    convert_element_type x1, other arithmetic, on_device(): nesterov = (grad_float + MUON_DECAY * next_momentum).astype(jnp.bfloat16)  2.04 us
  transfers between devices with their start and end apart: 20, of which 10 were waited for; matrix products, arithmetic and copies ran while one was open for 33% of the time, Pallas kernels for 0%

profile of v13, /device:TPU:16, one launch (start us, length us, event | category | flops | bytes accessed | tf_op | source)
XLA Modules:
  0.0 98.6 jit_solution(13233726184924255665)
XLA Ops:
  0.7 2.0 %fusion.33 = (bf16[4,16,2048]{2,1,0:T(8,128)(2,1)S(1)}, f32[4,16,2048]{2,1,0:T(8,128)}) fusion(bf16[4,16,2048]{2,1,0:T(8,128)(2,1)} %param.9, f32[4,16,2048]{2,1,0:T(8,128)} %param.10), kind=kLoop, calls=%fused_computation.47 | loop fusion | flops 786432 | bytes 1572864 | tf_op jit(solution)/shard_map/convert_element_type | solution.py:125
  2.8 2.8 %collective-permute-start.2 = (bf16[1,16,2048]{2,1,0:T(8,128)(2,1)S(1)}, bf16[1,16,2048]{2,1,0:T(8,128)(2,1)S(1)}, u32[]{:S(2)}, u32[]{:S(2)}) collective-permute-start(bf16[1,16,2048]{2,1,0:T(8,128)(2,1)S(1)} %get-tuple-element.39), channel_id=1, source_target_pairs={{0,24},{8,0},{16,8},{24,16},{1,25},{9,1},{17,9},{25,17},{2,26},{10... | collective-permute-start | bytes 196616 | tf_op jit(solution)/shard_map/ppermute | solution.py:30
  7.9 3.5 %collective-permute-done.1 = bf16[1,16,2048]{2,1,0:T(8,128)(2,1)S(1)} collective-permute-done((bf16[1,16,2048]{2,1,0:T(8,128)(2,1)S(1)}, bf16[1,16,2048]{2,1,0:T(8,128)(2,1)S(1)}, u32[]{:S(2)}, u32[]{:S(2)}) %collective-permute-start.1) | collective-permute-done | bytes 65568 | tf_op jit(solution)/shard_map/ppermute | solution.py:30
  12.9 1.9 %collective-permute-start.6 = (bf16[1,64,2048]{2,1,0:T(8,128)(2,1)S(1)}, bf16[1,64,2048]{2,1,0:T(8,128)(2,1)S(1)}, u32[]{:S(2)}, u32[]{:S(2)}) collective-permute-start(bf16[1,64,2048]{2,1,0:T(8,128)(2,1)S(1)} %get-tuple-element.31), channel_id=1, source_target_pairs={{0,32},{32,64},{64,96},{96,128},{128,160},{160,192},{192,224},{224... | collective-permute-start | bytes 786440 | tf_op jit(solution)/shard_map/ppermute | solution.py:30
  14.8 3.9 %collective-permute-start.3 = (bf16[1,64,2048]{2,1,0:T(8,128)(2,1)S(1)}, bf16[1,64,2048]{2,1,0:T(8,128)(2,1)S(1)}, u32[]{:S(2)}, u32[]{:S(2)}) collective-permute-start(bf16[1,64,2048]{2,1,0:T(8,128)(2,1)S(1)} %get-tuple-element.31), channel_id=1, source_target_pairs={{0,224},{32,0},{64,32},{96,64},{128,96},{160,128},{192,160},{224,1... | collective-permute-start | bytes 786440 | tf_op jit(solution)/shard_map/ppermute | solution.py:30
  18.7 4.8 %collective-permute-done.6 = bf16[1,64,2048]{2,1,0:T(8,128)(2,1)S(1)} collective-permute-done((bf16[1,64,2048]{2,1,0:T(8,128)(2,1)S(1)}, bf16[1,64,2048]{2,1,0:T(8,128)(2,1)S(1)}, u32[]{:S(2)}, u32[]{:S(2)}) %collective-permute-start.6) | collective-permute-done | bytes 262176 | tf_op jit(solution)/shard_map/ppermute | solution.py:30
  23.6 3.2 %collective-permute-start.4 = (bf16[1,64,2048]{2,1,0:T(8,128)(2,1)S(1)}, bf16[1,64,2048]{2,1,0:T(8,128)(2,1)S(1)}, u32[]{:S(2)}, u32[]{:S(2)}) collective-permute-start(bf16[1,64,2048]{2,1,0:T(8,128)(2,1)S(1)} %collective-permute-done.3), channel_id=1, source_target_pairs={{0,224},{32,0},{64,32},{96,64},{128,96},{160,128},{192,160},{224,1... | collective-permute-start | bytes 786440 | tf_op jit(solution)/shard_map/ppermute | solution.py:30
  29.6 1.5 %collective-permute-done.7 = bf16[1,64,2048]{2,1,0:T(8,128)(2,1)S(1)} collective-permute-done((bf16[1,64,2048]{2,1,0:T(8,128)(2,1)S(1)}, bf16[1,64,2048]{2,1,0:T(8,128)(2,1)S(1)}, u32[]{:S(2)}, u32[]{:S(2)}) %collective-permute-start.7) | collective-permute-done | bytes 262176 | tf_op jit(solution)/shard_map/ppermute | solution.py:30
  31.9 3.2 %collective-permute-start.5 = (bf16[1,64,2048]{2,1,0:T(8,128)(2,1)S(1)}, bf16[1,64,2048]{2,1,0:T(8,128)(2,1)S(1)}, u32[]{:S(2)}, u32[]{:S(2)}) collective-permute-start(bf16[1,64,2048]{2,1,0:T(8,128)(2,1)S(1)} %collective-permute-done.4), channel_id=1, source_target_pairs={{0,224},{32,0},{64,32},{96,64},{128,96},{160,128},{192,160},{224,1... | collective-permute-start | bytes 786440 | tf_op jit(solution)/shard_map/ppermute | solution.py:30
  36.6 2.2 %collective-permute-done.8 = bf16[1,64,2048]{2,1,0:T(8,128)(2,1)S(1)} collective-permute-done((bf16[1,64,2048]{2,1,0:T(8,128)(2,1)S(1)}, bf16[1,64,2048]{2,1,0:T(8,128)(2,1)S(1)}, u32[]{:S(2)}, u32[]{:S(2)}) %collective-permute-start.8) | collective-permute-done | bytes 262176 | tf_op jit(solution)/shard_map/ppermute | solution.py:30
  39.9 3.8 %collective-permute-start.10 = (bf16[1,64,1024]{2,1,0:T(8,128)(2,1)S(1)}, bf16[1,64,1024]{2,1,0:T(8,128)(2,1)S(1)}, u32[]{:S(2)}, u32[]{:S(2)}) collective-permute-start(bf16[1,64,1024]{2,1,0:T(8,128)(2,1)S(1)} %slice.37), channel_id=1, source_target_pairs={{0,224},{32,0},{64,32},{96,64},{128,96},{160,128},{192,160},{224,1... | collective-permute-start | bytes 393224 | tf_op jit(solution)/shard_map/ppermute | solution.py:30
  46.2 1.6 %multiply_reduce_fusion.3 = f32[]{:T(128)} fusion(bf16[1,64,1024]{2,1,0:T(8,128)(2,1)S(1)} %collective-permute-done.10, bf16[1,64,1024]{2,1,0:T(8,128)(2,1)} %collective-permute-done.9), kind=kLoop, calls=%fused_computation.64 | loop fusion | flops 786431 | bytes 262148 | tf_op jit(solution)/shard_map/reduce_sum | solution.py:50
  53.5 3.8 %fusion.3 = bf16[1,512,2048]{2,1,0:T(8,128)(2,1)S(1)} fusion(bf16[1,512,2048]{2,1,0:T(8,128)(2,1)} %copy-done.1, f32[512,512]{1,0:T(8,128)S(1)} %fusion.19), kind=kOutput, calls=%fused_computation.7 | convolution fusion | flops 1347682304 | bytes 5242880 | tf_op jit(solution)/shard_map/kij,kjl->kil/dot_general | solution.py:70
  57.4 6.2 %collective-permute-start.13 = (f32[34,128]{1,0:T(8,128)S(1)}, f32[34,128]{1,0:T(8,128)S(1)}, u32[]{:S(2)}, u32[]{:S(2)}) collective-permute-start(f32[34,128]{1,0:T(8,128)S(1)} %add.174), channel_id=1, source_target_pairs={{0,64},{32,96},{64,0},{96,32},{128,192},{160,224},{192,128},{224,1... | collective-permute-start | bytes 52232 | tf_op jit(solution)/shard_map/ppermute | solution.py:88
  64.8 2.9 %fusion.2 = bf16[1,512,2048]{2,1,0:T(8,128)(2,1)} fusion(bf16[1,512,2048]{2,1,0:T(8,128)(2,1)S(1)} %fusion.3, f32[512,512]{1,0:T(8,128)S(1)} %fusion.16), kind=kOutput, calls=%fused_computation.5 | convolution fusion | flops 1347682304 | bytes 5242880 | tf_op jit(solution)/shard_map/kij,kjl->kil/dot_general | solution.py:70
  67.8 1.5 %collective-permute-start.14 = (f32[34,128]{1,0:T(8,128)S(1)}, f32[34,128]{1,0:T(8,128)S(1)}, u32[]{:S(2)}, u32[]{:S(2)}) collective-permute-start(f32[34,128]{1,0:T(8,128)S(1)} %add.177), channel_id=1, source_target_pairs={{0,128},{32,160},{64,192},{96,224},{128,0},{160,32},{192,64},{224,... | collective-permute-start | bytes 52232 | tf_op jit(solution)/shard_map/ppermute | solution.py:88
  69.3 3.5 %fusion.13 = f32[512,512]{1,0:T(8,128)S(1)} fusion(bf16[1,512,2048]{2,1,0:T(8,128)(2,1)} %fusion.2), kind=kOutput, calls=%fused_computation.19 | convolution fusion | flops 1073741824 | bytes 3145728 | tf_op jit(solution)/shard_map/kij,klj->kil/dot_general | solution.py:63
  72.8 2.9 %fusion.1 = bf16[1,512,2048]{2,1,0:T(8,128)(2,1)} fusion(bf16[1,512,2048]{2,1,0:T(8,128)(2,1)S(1)} %copy-done.8, f32[512,512]{1,0:T(8,128)S(1)} %fusion.13), kind=kOutput, calls=%fused_computation.3 | convolution fusion | flops 1347682304 | bytes 5242880 | tf_op jit(solution)/shard_map/kij,kjl->kil/dot_general | solution.py:70
  75.8 3.5 %fusion.10 = f32[512,512]{1,0:T(8,128)S(1)} fusion(bf16[1,512,2048]{2,1,0:T(8,128)(2,1)} %fusion.1), kind=kOutput, calls=%fused_computation.16 | convolution fusion | flops 1073741824 | bytes 3145728 | tf_op jit(solution)/shard_map/kij,klj->kil/dot_general | solution.py:63
  79.3 3.8 %fusion = bf16[1,512,2048]{2,1,0:T(8,128)(2,1)S(1)} fusion(bf16[1,512,2048]{2,1,0:T(8,128)(2,1)} %fusion.1, f32[512,512]{1,0:T(8,128)S(1)} %fusion.10), kind=kOutput, calls=%fused_computation.1 | convolution fusion | flops 1347682304 | bytes 5242880 | tf_op jit(solution)/shard_map/kij,kjl->kil/dot_general | solution.py:70
  83.2 2.3 %collective-permute-start.19 = (f32[34,128]{1,0:T(8,128)S(1)}, f32[34,128]{1,0:T(8,128)S(1)}, u32[]{:S(2)}, u32[]{:S(2)}) collective-permute-start(f32[34,128]{1,0:T(8,128)S(1)} %add.183), channel_id=1, source_target_pairs={{0,16},{8,24},{16,0},{24,8},{1,17},{9,25},{17,1},{25,9},{2,18},{10... | collective-permute-start | bytes 52232 | tf_op jit(solution)/shard_map/ppermute | solution.py:88
  87.6 1.5 %fusion.5 = bf16[1,64,2048]{2,1,0:T(8,128)(2,1)S(1)} fusion(bf16[1,512,2048]{2,1,0:T(8,128)(2,1)S(1)} %fusion, f32[512,512]{1,0:T(8,128)S(1)} %fusion.7, f32[1,512,512]{2,1,0:T(8,128)S(1)} %bitcast.90, bf16[1,512,512]{2,1,0:T(8,128)(2,1)} %convert_bitcast_fusion), kind=kOutput, calls=%fused_computation.11 | convolution fusion | flops 168689664 | bytes 3866624 | tf_op jit(solution)/shard_map/kij,kjl->kil/dot_general | solution.py:70
  89.8 3.6 %collective-permute-start.17 = (bf16[1,16,2048]{2,1,0:T(8,128)(2,1)S(1)}, bf16[1,16,2048]{2,1,0:T(8,128)(2,1)S(1)}, u32[]{:S(2)}, u32[]{:S(2)}) collective-permute-start(bf16[1,16,2048]{2,1,0:T(8,128)(2,1)S(1)} %get-tuple-element.37), channel_id=1, source_target_pairs={{0,16},{8,24},{16,0},{24,8},{1,17},{9,25},{17,1},{25,9},{2,18},{10... | collective-permute-start | bytes 196616 | tf_op jit(solution)/shard_map/ppermute | solution.py:30
  94.0 3.6 %collective-permute-done.16 = bf16[1,16,2048]{2,1,0:T(8,128)(2,1)S(1)} collective-permute-done((bf16[1,16,2048]{2,1,0:T(8,128)(2,1)S(1)}, bf16[1,16,2048]{2,1,0:T(8,128)(2,1)S(1)}, u32[]{:S(2)}, u32[]{:S(2)}) %collective-permute-start.16) | collective-permute-done | bytes 65568 | tf_op jit(solution)/shard_map/ppermute | solution.py:30
  (88 shorter events, 18.5 us)
Async XLA Ops:
  0.6 6.8 %copy-start = (bf16[512,32]{0,1:T(8,128)(2,1)S(1)}, bf16[512,32]{0,1:T(8,128)(2,1)}, u32[]{:S(2)}) copy-start(bf16[512,32]{0,1:T(8,128)(2,1)} %param.15) | copy-start | bytes 98308
  0.6 6.7 %copy-start.3 = (bf16[512,128]{1,0:T(8,128)(2,1)S(1)}, bf16[512,128]{1,0:T(8,128)(2,1)}, u32[]{:S(2)}) copy-start(bf16[512,128]{1,0:T(8,128)(2,1)} %param.11) | copy-start | bytes 393220
  0.7 6.8 %copy-start.6 = (f32[128]{0:T(128)S(1)}, f32[128]{0:T(128)}, u32[]{:S(2)}) copy-start(f32[128]{0:T(128)} %param.13) | copy-start | bytes 1540
  0.7 6.8 %copy-start.7 = (f32[128]{0:T(128)S(1)}, f32[128]{0:T(128)}, u32[]{:S(2)}) copy-start(f32[128]{0:T(128)} %param.12) | copy-start | bytes 1540
  2.8 5.1 %collective-permute-start.2 = (bf16[1,16,2048]{2,1,0:T(8,128)(2,1)S(1)}, bf16[1,16,2048]{2,1,0:T(8,128)(2,1)S(1)}, u32[]{:S(2)}, u32[]{:S(2)}) collective-permute-start(bf16[1,16,2048]{2,1,0:T(8,128)(2,1)S(1)} %get-tuple-element.39), channel_id=1, source_target_pairs={{0,24},{8,0},{16,8},{24,16},{1,25},{9,1},{17,9},{25,17},{2,26},{10... | collective-permute-start | bytes 196616 | tf_op jit(solution)/shard_map/ppermute | solution.py:30
  5.7 5.8 %collective-permute-start.1 = (bf16[1,16,2048]{2,1,0:T(8,128)(2,1)S(1)}, bf16[1,16,2048]{2,1,0:T(8,128)(2,1)S(1)}, u32[]{:S(2)}, u32[]{:S(2)}) collective-permute-start(bf16[1,16,2048]{2,1,0:T(8,128)(2,1)S(1)} %get-tuple-element.40), channel_id=1, source_target_pairs={{0,16},{8,24},{16,0},{24,8},{1,17},{9,25},{17,1},{25,9},{2,18},{10... | collective-permute-start | bytes 196616 | tf_op jit(solution)/shard_map/ppermute | solution.py:30
  6.5 5.7 %collective-permute-start = (bf16[1,16,2048]{2,1,0:T(8,128)(2,1)S(1)}, bf16[1,16,2048]{2,1,0:T(8,128)(2,1)S(1)}, u32[]{:S(2)}, u32[]{:S(2)}) collective-permute-start(bf16[1,16,2048]{2,1,0:T(8,128)(2,1)S(1)} %get-tuple-element.41), channel_id=1, source_target_pairs={{0,8},{8,16},{16,24},{24,0},{1,9},{9,17},{17,25},{25,1},{2,10},{10... | collective-permute-start | bytes 196616 | tf_op jit(solution)/shard_map/ppermute | solution.py:30
  12.9 10.7 %collective-permute-start.6 = (bf16[1,64,2048]{2,1,0:T(8,128)(2,1)S(1)}, bf16[1,64,2048]{2,1,0:T(8,128)(2,1)S(1)}, u32[]{:S(2)}, u32[]{:S(2)}) collective-permute-start(bf16[1,64,2048]{2,1,0:T(8,128)(2,1)S(1)} %get-tuple-element.31), channel_id=1, source_target_pairs={{0,32},{32,64},{64,96},{96,128},{128,160},{160,192},{192,224},{224... | collective-permute-start | bytes 786440 | tf_op jit(solution)/shard_map/ppermute | solution.py:30
  14.8 8.8 %collective-permute-start.3 = (bf16[1,64,2048]{2,1,0:T(8,128)(2,1)S(1)}, bf16[1,64,2048]{2,1,0:T(8,128)(2,1)S(1)}, u32[]{:S(2)}, u32[]{:S(2)}) collective-permute-start(bf16[1,64,2048]{2,1,0:T(8,128)(2,1)S(1)} %get-tuple-element.31), channel_id=1, source_target_pairs={{0,224},{32,0},{64,32},{96,64},{128,96},{160,128},{192,160},{224,1... | collective-permute-start | bytes 786440 | tf_op jit(solution)/shard_map/ppermute | solution.py:30
  23.6 7.6 %collective-permute-start.7 = (bf16[1,64,2048]{2,1,0:T(8,128)(2,1)S(1)}, bf16[1,64,2048]{2,1,0:T(8,128)(2,1)S(1)}, u32[]{:S(2)}, u32[]{:S(2)}) collective-permute-start(bf16[1,64,2048]{2,1,0:T(8,128)(2,1)S(1)} %collective-permute-done.6), channel_id=1, source_target_pairs={{0,32},{32,64},{64,96},{96,128},{128,160},{160,192},{192,224},{224... | collective-permute-start | bytes 786440 | tf_op jit(solution)/shard_map/ppermute | solution.py:30
  23.6 8.3 %collective-permute-start.4 = (bf16[1,64,2048]{2,1,0:T(8,128)(2,1)S(1)}, bf16[1,64,2048]{2,1,0:T(8,128)(2,1)S(1)}, u32[]{:S(2)}, u32[]{:S(2)}) collective-permute-start(bf16[1,64,2048]{2,1,0:T(8,128)(2,1)S(1)} %collective-permute-done.3), channel_id=1, source_target_pairs={{0,224},{32,0},{64,32},{96,64},{128,96},{160,128},{192,160},{224,1... | collective-permute-start | bytes 786440 | tf_op jit(solution)/shard_map/ppermute | solution.py:30
  31.2 7.6 %collective-permute-start.8 = (bf16[1,64,2048]{2,1,0:T(8,128)(2,1)S(1)}, bf16[1,64,2048]{2,1,0:T(8,128)(2,1)S(1)}, u32[]{:S(2)}, u32[]{:S(2)}) collective-permute-start(bf16[1,64,2048]{2,1,0:T(8,128)(2,1)S(1)} %collective-permute-done.7), channel_id=1, source_target_pairs={{0,32},{32,64},{64,96},{96,128},{128,160},{160,192},{192,224},{224... | collective-permute-start | bytes 786440 | tf_op jit(solution)/shard_map/ppermute | solution.py:30
  31.9 8.0 %collective-permute-start.5 = (bf16[1,64,2048]{2,1,0:T(8,128)(2,1)S(1)}, bf16[1,64,2048]{2,1,0:T(8,128)(2,1)S(1)}, u32[]{:S(2)}, u32[]{:S(2)}) collective-permute-start(bf16[1,64,2048]{2,1,0:T(8,128)(2,1)S(1)} %collective-permute-done.4), channel_id=1, source_target_pairs={{0,224},{32,0},{64,32},{96,64},{128,96},{160,128},{192,160},{224,1... | collective-permute-start | bytes 786440 | tf_op jit(solution)/shard_map/ppermute | solution.py:30
  39.4 6.5 %collective-permute-start.9 = (bf16[1,64,1024]{2,1,0:T(8,128)(2,1)}, bf16[1,64,1024]{2,1,0:T(8,128)(2,1)}, u32[]{:S(2)}, u32[]{:S(2)}) collective-permute-start(bf16[1,64,1024]{2,1,0:T(8,128)(2,1)} %slice.36), channel_id=1, source_target_pairs={{0,32},{32,64},{64,96},{96,128},{128,160},{160,192},{192,224},{224... | collective-permute-start | bytes 393224 | tf_op jit(solution)/shard_map/ppermute | solution.py:30
  39.9 6.3 %collective-permute-start.10 = (bf16[1,64,1024]{2,1,0:T(8,128)(2,1)S(1)}, bf16[1,64,1024]{2,1,0:T(8,128)(2,1)S(1)}, u32[]{:S(2)}, u32[]{:S(2)}) collective-permute-start(bf16[1,64,1024]{2,1,0:T(8,128)(2,1)S(1)} %slice.37), channel_id=1, source_target_pairs={{0,224},{32,0},{64,32},{96,64},{128,96},{160,128},{192,160},{224,1... | collective-permute-start | bytes 393224 | tf_op jit(solution)/shard_map/ppermute | solution.py:30
  51.8 1.4 %collective-permute-start.11 = (f32[34,128]{1,0:T(8,128)S(1)}, f32[34,128]{1,0:T(8,128)S(1)}, u32[]{:S(2)}, u32[]{:S(2)}) collective-permute-start(f32[34,128]{1,0:T(8,128)S(1)} %pad_maximum_fusion.1), channel_id=1, source_target_pairs={{0,1},{1,0},{2,3},{3,2},{4,5},{5,4},{6,7},{7,6},{8,9},{9,8},{10,11... | collective-permute-start | bytes 52232 | tf_op jit(solution)/shard_map/ppermute | solution.py:88
  53.3 4.1 %collective-permute-start.12 = (f32[34,128]{1,0:T(8,128)S(1)}, f32[34,128]{1,0:T(8,128)S(1)}, u32[]{:S(2)}, u32[]{:S(2)}) collective-permute-start(f32[34,128]{1,0:T(8,128)S(1)} %add.173), channel_id=1, source_target_pairs={{0,32},{32,0},{64,96},{96,64},{128,160},{160,128},{192,224},{224,1... | collective-permute-start | bytes 52232 | tf_op jit(solution)/shard_map/ppermute | solution.py:88
  57.4 10.4 %collective-permute-start.13 = (f32[34,128]{1,0:T(8,128)S(1)}, f32[34,128]{1,0:T(8,128)S(1)}, u32[]{:S(2)}, u32[]{:S(2)}) collective-permute-start(f32[34,128]{1,0:T(8,128)S(1)} %add.174), channel_id=1, source_target_pairs={{0,64},{32,96},{64,0},{96,32},{128,192},{160,224},{192,128},{224,1... | collective-permute-start | bytes 52232 | tf_op jit(solution)/shard_map/ppermute | solution.py:88
  67.8 7.9 %collective-permute-start.14 = (f32[34,128]{1,0:T(8,128)S(1)}, f32[34,128]{1,0:T(8,128)S(1)}, u32[]{:S(2)}, u32[]{:S(2)}) collective-permute-start(f32[34,128]{1,0:T(8,128)S(1)} %add.177), channel_id=1, source_target_pairs={{0,128},{32,160},{64,192},{96,224},{128,0},{160,32},{192,64},{224,... | collective-permute-start | bytes 52232 | tf_op jit(solution)/shard_map/ppermute | solution.py:88
  75.7 7.4 %collective-permute-start.15 = (f32[34,128]{1,0:T(8,128)S(1)}, f32[34,128]{1,0:T(8,128)S(1)}, u32[]{:S(2)}, u32[]{:S(2)}) collective-permute-start(f32[34,128]{1,0:T(8,128)S(1)} %add.180), channel_id=1, source_target_pairs={{0,8},{8,0},{16,24},{24,16},{1,9},{9,1},{17,25},{25,17},{2,10},{10... | collective-permute-start | bytes 52232 | tf_op jit(solution)/shard_map/ppermute | solution.py:88
  83.2 10.2 %collective-permute-start.19 = (f32[34,128]{1,0:T(8,128)S(1)}, f32[34,128]{1,0:T(8,128)S(1)}, u32[]{:S(2)}, u32[]{:S(2)}) collective-permute-start(f32[34,128]{1,0:T(8,128)S(1)} %add.183), channel_id=1, source_target_pairs={{0,16},{8,24},{16,0},{24,8},{1,17},{9,25},{17,1},{25,9},{2,18},{10... | collective-permute-start | bytes 52232 | tf_op jit(solution)/shard_map/ppermute | solution.py:88
  89.2 8.5 %collective-permute-start.18 = (bf16[1,16,2048]{2,1,0:T(8,128)(2,1)S(1)}, bf16[1,16,2048]{2,1,0:T(8,128)(2,1)S(1)}, u32[]{:S(2)}, u32[]{:S(2)}) collective-permute-start(bf16[1,16,2048]{2,1,0:T(8,128)(2,1)S(1)} %get-tuple-element.36), channel_id=1, source_target_pairs={{0,8},{8,16},{16,24},{24,0},{1,9},{9,17},{17,25},{25,1},{2,10},{10... | collective-permute-start | bytes 196616 | tf_op jit(solution)/shard_map/ppermute | solution.py:30
  89.8 7.8 %collective-permute-start.17 = (bf16[1,16,2048]{2,1,0:T(8,128)(2,1)S(1)}, bf16[1,16,2048]{2,1,0:T(8,128)(2,1)S(1)}, u32[]{:S(2)}, u32[]{:S(2)}) collective-permute-start(bf16[1,16,2048]{2,1,0:T(8,128)(2,1)S(1)} %get-tuple-element.37), channel_id=1, source_target_pairs={{0,16},{8,24},{16,0},{24,8},{1,17},{9,25},{17,1},{25,9},{2,18},{10... | collective-permute-start | bytes 196616 | tf_op jit(solution)/shard_map/ppermute | solution.py:30
  93.4 4.3 %collective-permute-start.16 = (bf16[1,16,2048]{2,1,0:T(8,128)(2,1)S(1)}, bf16[1,16,2048]{2,1,0:T(8,128)(2,1)S(1)}, u32[]{:S(2)}, u32[]{:S(2)}) collective-permute-start(bf16[1,16,2048]{2,1,0:T(8,128)(2,1)S(1)} %get-tuple-element.38), channel_id=1, source_target_pairs={{0,24},{8,0},{16,8},{24,16},{1,25},{9,1},{17,9},{25,17},{2,26},{10... | collective-permute-start | bytes 196616 | tf_op jit(solution)/shard_map/ppermute | solution.py:30
  (5 other events, 24.6 us)

commit v14 on v9

--- a/solution.py
+++ b/solution.py
@@ -120,8 +120,7 @@
     second_moment,
 ):
     grad_float = gradient.astype(jnp.float32)
-    next_momentum = MUON_DECAY * momentum + grad_float
-    nesterov = (grad_float + MUON_DECAY * next_momentum).astype(jnp.bfloat16)
+    nesterov = (grad_float + MUON_DECAY * (MUON_DECAY * momentum + grad_float)).astype(jnp.bfloat16)
     count_all, rows_piece, cols_full = nesterov.shape
     inner = lax.axis_size("inner")
     slots = -(-count_all // inner)
@@ -133,6 +132,8 @@
          for k in range(inner)],
         axis=1,
     )
+    momentum, grad_float, strip = lax.optimization_barrier((momentum, grad_float, strip))
+    next_momentum = MUON_DECAY * momentum + grad_float
     blocks = ring_gather(strip, "outer")
     local = vector_partials(normed, ln_gain, ln_bias, ln_cotangent, router_cotangent)
     steps = [step for axis in ("section",) + SHARD for step in butterfly_rounds(axis)]

time: 94.4 us -> 99.2 us (1.051)
  matrix products: 26 us -> 29.8 us
  starting transfers between devices: 33 us -> 31.3 us
  local copies, waits for them, and re-layouts: 0.28 us -> 1.51 us
  other arithmetic: 6.67 us -> 7.75 us
    ppermute x6, starting transfers between devices: 7.97 us -> 5.96 us  [butterfly_rounds(): lax.ppermute(value, axis, perm)]
    dot_general x5, matrix products: 10.8 us -> 12.8 us  [orthogonalize(): jnp.einsum('kij,klj->kil', iterate, iterate, preferred_element_type=jnp.f...]
    dot_general x5, matrix products: 15 us -> 16.9 us  [orthogonalize(): jnp.einsum('kij,kjl->kil', poly, iterate, preferred_element_type=jnp.floa...]
    unnamed x33, local copies, waits for them, and re-layouts: 0.2 us -> 1.42 us
    convert_element_type x1 -> x2, other arithmetic: 2.08 us -> 2.32 us  [the longest x1 1.33 us: on_device(): (grad_float + MUON_DECAY * (MUON_DECAY * momentum + grad_float)).astype(j...]
  transfers between devices with their start and end apart: 20 -> 20, of which waited for: 14 -> 13; matrix products, arithmetic and copies ran while one was open for 26% -> 30% of each run, Pallas kernels for 0% -> 0%
where the time goes in v14:
time: 99.2 us; the launch traced here: 99 us
  starting transfers between devices  31.3 us (32%)
  matrix products  29.8 us (30%)
  waiting for transfers between devices  26.9 us (27%)
  other arithmetic  7.75 us (8%)
  between operations  1.76 us (2%)
  local copies, waits for them, and re-layouts  1.51 us (2%)
    ppermute x14, waiting for transfers between devices, shift(): return lax.ppermute(value, axis, [(i, (i + k) % size) for i in range(size)])  26.4 us
    ppermute x14, starting transfers between devices, shift(): return lax.ppermute(value, axis, [(i, (i + k) % size) for i in range(size)])  25.3 us
    dot_general x5, matrix products, orthogonalize(): jnp.einsum('kij,kjl->kil', poly, iterate, preferred_element_type=jnp.floa...  16.9 us
    dot_general x5, matrix products, orthogonalize(): jnp.einsum('kij,klj->kil', iterate, iterate, preferred_element_type=jnp.f...  12.8 us
    ppermute x6, starting transfers between devices, butterfly_rounds(): lax.ppermute(value, axis, perm)  5.96 us
  transfers between devices with their start and end apart: 20, of which 13 were waited for; matrix products, arithmetic and copies ran while one was open for 30% of the time, Pallas kernels for 0%

profile of v14, /device:TPU:16, one launch (start us, length us, event | category | flops | bytes accessed | tf_op | source)
XLA Modules:
  0.0 99.0 jit_solution(7678259148368731470)
XLA Ops:
  2.1 2.8 %collective-permute-start.2 = (bf16[1,16,2048]{2,1,0:T(8,128)(2,1)S(1)}, bf16[1,16,2048]{2,1,0:T(8,128)(2,1)S(1)}, u32[]{:S(2)}, u32[]{:S(2)}) collective-permute-start(bf16[1,16,2048]{2,1,0:T(8,128)(2,1)S(1)} %get-tuple-element.40), channel_id=1, source_target_pairs={{0,24},{8,0},{16,8},{24,16},{1,25},{9,1},{17,9},{25,17},{2,26},{10... | collective-permute-start | bytes 196616 | tf_op jit(solution)/shard_map/ppermute | solution.py:30
  7.7 3.1 %collective-permute-done.1 = bf16[1,16,2048]{2,1,0:T(8,128)(2,1)S(1)} collective-permute-done((bf16[1,16,2048]{2,1,0:T(8,128)(2,1)S(1)}, bf16[1,16,2048]{2,1,0:T(8,128)(2,1)S(1)}, u32[]{:S(2)}, u32[]{:S(2)}) %collective-permute-start.1) | collective-permute-done | bytes 65568 | tf_op jit(solution)/shard_map/ppermute | solution.py:30
  11.5 5.9 %collective-permute-start.3 = (bf16[1,64,2048]{2,1,0:T(8,128)(2,1)S(1)}, bf16[1,64,2048]{2,1,0:T(8,128)(2,1)S(1)}, u32[]{:S(2)}, u32[]{:S(2)}) collective-permute-start(bf16[1,64,2048]{2,1,0:T(8,128)(2,1)S(1)} %pad_maximum_fusion), channel_id=1, source_target_pairs={{0,224},{32,0},{64,32},{96,64},{128,96},{160,128},{192,160},{224,1... | collective-permute-start | bytes 786440 | tf_op jit(solution)/shard_map/ppermute | solution.py:30
  17.7 3.8 %collective-permute-done.3 = bf16[1,64,2048]{2,1,0:T(8,128)(2,1)S(1)} collective-permute-done((bf16[1,64,2048]{2,1,0:T(8,128)(2,1)S(1)}, bf16[1,64,2048]{2,1,0:T(8,128)(2,1)S(1)}, u32[]{:S(2)}, u32[]{:S(2)}) %collective-permute-start.3) | collective-permute-done | bytes 262176 | tf_op jit(solution)/shard_map/ppermute | solution.py:30
  21.5 3.7 %collective-permute-start.4 = (bf16[1,64,2048]{2,1,0:T(8,128)(2,1)S(1)}, bf16[1,64,2048]{2,1,0:T(8,128)(2,1)S(1)}, u32[]{:S(2)}, u32[]{:S(2)}) collective-permute-start(bf16[1,64,2048]{2,1,0:T(8,128)(2,1)S(1)} %collective-permute-done.3), channel_id=1, source_target_pairs={{0,224},{32,0},{64,32},{96,64},{128,96},{160,128},{192,160},{224,1... | collective-permute-start | bytes 786440 | tf_op jit(solution)/shard_map/ppermute | solution.py:30
  26.1 3.0 %collective-permute-done.4 = bf16[1,64,2048]{2,1,0:T(8,128)(2,1)S(1)} collective-permute-done((bf16[1,64,2048]{2,1,0:T(8,128)(2,1)S(1)}, bf16[1,64,2048]{2,1,0:T(8,128)(2,1)S(1)}, u32[]{:S(2)}, u32[]{:S(2)}) %collective-permute-start.4) | collective-permute-done | bytes 262176 | tf_op jit(solution)/shard_map/ppermute | solution.py:30
  29.1 3.7 %collective-permute-start.5 = (bf16[1,64,2048]{2,1,0:T(8,128)(2,1)S(1)}, bf16[1,64,2048]{2,1,0:T(8,128)(2,1)S(1)}, u32[]{:S(2)}, u32[]{:S(2)}) collective-permute-start(bf16[1,64,2048]{2,1,0:T(8,128)(2,1)S(1)} %collective-permute-done.4), channel_id=1, source_target_pairs={{0,224},{32,0},{64,32},{96,64},{128,96},{160,128},{192,160},{224,1... | collective-permute-start | bytes 786440 | tf_op jit(solution)/shard_map/ppermute | solution.py:30
  32.9 4.6 %collective-permute-done.5 = bf16[1,64,2048]{2,1,0:T(8,128)(2,1)S(1)} collective-permute-done((bf16[1,64,2048]{2,1,0:T(8,128)(2,1)S(1)}, bf16[1,64,2048]{2,1,0:T(8,128)(2,1)S(1)}, u32[]{:S(2)}, u32[]{:S(2)}) %collective-permute-start.5) | collective-permute-done | bytes 262176 | tf_op jit(solution)/shard_map/ppermute | solution.py:30
  37.6 3.8 %collective-permute-start.10 = (bf16[1,64,1024]{2,1,0:T(8,128)(2,1)S(1)}, bf16[1,64,1024]{2,1,0:T(8,128)(2,1)S(1)}, u32[]{:S(2)}, u32[]{:S(2)}) collective-permute-start(bf16[1,64,1024]{2,1,0:T(8,128)(2,1)S(1)} %slice.37), channel_id=1, source_target_pairs={{0,224},{32,0},{64,32},{96,64},{128,96},{160,128},{192,160},{224,1... | collective-permute-start | bytes 393224 | tf_op jit(solution)/shard_map/ppermute | solution.py:30
  41.7 2.1 %collective-permute-done.10 = bf16[1,64,1024]{2,1,0:T(8,128)(2,1)S(1)} collective-permute-done((bf16[1,64,1024]{2,1,0:T(8,128)(2,1)S(1)}, bf16[1,64,1024]{2,1,0:T(8,128)(2,1)S(1)}, u32[]{:S(2)}, u32[]{:S(2)}) %collective-permute-start.10) | collective-permute-done | bytes 131104 | tf_op jit(solution)/shard_map/ppermute | solution.py:30
  43.9 4.0 %collective-permute-done.9 = bf16[1,64,1024]{2,1,0:T(8,128)(2,1)S(1)} collective-permute-done((bf16[1,64,1024]{2,1,0:T(8,128)(2,1)S(1)}, bf16[1,64,1024]{2,1,0:T(8,128)(2,1)S(1)}, u32[]{:S(2)}, u32[]{:S(2)}) %collective-permute-start.9) | collective-permute-done | bytes 131104 | tf_op jit(solution)/shard_map/ppermute | solution.py:30
  48.0 1.7 %fusion = f32[]{:T(128)} fusion(bf16[1,512,2048]{2,1,0:T(8,128)(2,1)S(1)} %constant_dynamic-update-slice_fusion), kind=kLoop, calls=%fused_computation.2 | loop fusion | flops 3145727 | bytes 2097156 | tf_op jit(solution)/shard_map/reduce_sum | solution.py:53
  52.1 2.3 %fusion.21 = f32[512,512]{1,0:T(8,128)} fusion(bf16[1,512,2048]{2,1,0:T(8,128)(2,1)S(1)} %fusion.1), kind=kOutput, calls=%fused_computation.28 | convolution fusion | flops 1073741824 | bytes 3145728 | tf_op jit(solution)/shard_map/kij,klj->kil/dot_general | solution.py:62
  54.6 4.7 %fusion.5 = bf16[1,512,2048]{2,1,0:T(8,128)(2,1)S(1)} fusion(bf16[1,512,2048]{2,1,0:T(8,128)(2,1)} %copy-done.2, f32[512,512]{1,0:T(8,128)} %fusion.21), kind=kOutput, calls=%fused_computation.11 | convolution fusion | flops 1347682304 | bytes 5242880 | tf_op jit(solution)/shard_map/kij,kjl->kil/dot_general | solution.py:69
  60.8 2.9 %fusion.4 = bf16[1,512,2048]{2,1,0:T(8,128)(2,1)} fusion(bf16[1,512,2048]{2,1,0:T(8,128)(2,1)S(1)} %fusion.5, f32[512,512]{1,0:T(8,128)S(1)} %fusion.18), kind=kOutput, calls=%fused_computation.9 | convolution fusion | flops 1347682304 | bytes 5242880 | tf_op jit(solution)/shard_map/kij,kjl->kil/dot_general | solution.py:69
  64.2 3.1 %collective-permute-start.14 = (f32[34,128]{1,0:T(8,128)S(1)}, f32[34,128]{1,0:T(8,128)S(1)}, u32[]{:S(2)}, u32[]{:S(2)}) collective-permute-start(f32[34,128]{1,0:T(8,128)S(1)} %add.147), channel_id=1, source_target_pairs={{0,128},{32,160},{64,192},{96,224},{128,0},{160,32},{192,64},{224,... | collective-permute-start | bytes 52232 | tf_op jit(solution)/shard_map/ppermute | solution.py:87
  67.3 3.5 %fusion.15 = f32[512,512]{1,0:T(8,128)S(1)} fusion(bf16[1,512,2048]{2,1,0:T(8,128)(2,1)} %fusion.4), kind=kOutput, calls=%fused_computation.22 | convolution fusion | flops 1073741824 | bytes 3145728 | tf_op jit(solution)/shard_map/kij,klj->kil/dot_general | solution.py:62
  70.8 2.9 %fusion.3 = bf16[1,512,2048]{2,1,0:T(8,128)(2,1)} fusion(bf16[1,512,2048]{2,1,0:T(8,128)(2,1)S(1)} %copy-done.9, f32[512,512]{1,0:T(8,128)S(1)} %fusion.15), kind=kOutput, calls=%fused_computation.7 | convolution fusion | flops 1347682304 | bytes 5242880 | tf_op jit(solution)/shard_map/kij,kjl->kil/dot_general | solution.py:69
  73.9 4.5 %fusion.12 = f32[512,512]{1,0:T(8,128)} fusion(bf16[1,512,2048]{2,1,0:T(8,128)(2,1)} %fusion.3), kind=kOutput, calls=%fused_computation.19 | convolution fusion | flops 1073741824 | bytes 3145728 | tf_op jit(solution)/shard_map/kij,klj->kil/dot_general | solution.py:62
  78.3 4.7 %fusion.2 = bf16[1,512,2048]{2,1,0:T(8,128)(2,1)S(1)} fusion(bf16[1,512,2048]{2,1,0:T(8,128)(2,1)} %fusion.3, f32[512,512]{1,0:T(8,128)} %fusion.12), kind=kOutput, calls=%fused_computation.5 | convolution fusion | flops 1347682304 | bytes 5242880 | tf_op jit(solution)/shard_map/kij,kjl->kil/dot_general | solution.py:69
  85.3 1.5 %fusion.7 = bf16[1,64,2048]{2,1,0:T(8,128)(2,1)S(1)} fusion(bf16[1,512,2048]{2,1,0:T(8,128)(2,1)S(1)} %fusion.2, f32[512,512]{1,0:T(8,128)S(1)} %fusion.9, f32[1,512,512]{2,1,0:T(8,128)S(1)} %bitcast.90, bf16[1,512,512]{2,1,0:T(8,128)(2,1)} %convert_bitcast_fusion), kind=kOutput, calls=%fused_computation.14 | convolution fusion | flops 168689664 | bytes 3866624 | tf_op jit(solution)/shard_map/kij,kjl->kil/dot_general | solution.py:69
  86.8 2.3 %collective-permute-start.19 = (f32[34,128]{1,0:T(8,128)S(1)}, f32[34,128]{1,0:T(8,128)S(1)}, u32[]{:S(2)}, u32[]{:S(2)}) collective-permute-start(f32[34,128]{1,0:T(8,128)S(1)} %add.153), channel_id=1, source_target_pairs={{0,16},{8,24},{16,0},{24,8},{1,17},{9,25},{17,1},{25,9},{2,18},{10... | collective-permute-start | bytes 52232 | tf_op jit(solution)/shard_map/ppermute | solution.py:87
  89.1 2.7 %collective-permute-start.16 = (bf16[1,16,2048]{2,1,0:T(8,128)(2,1)S(1)}, bf16[1,16,2048]{2,1,0:T(8,128)(2,1)S(1)}, u32[]{:S(2)}, u32[]{:S(2)}) collective-permute-start(bf16[1,16,2048]{2,1,0:T(8,128)(2,1)S(1)} %get-tuple-element.38), channel_id=1, source_target_pairs={{0,24},{8,0},{16,8},{24,16},{1,25},{9,1},{17,9},{25,17},{2,26},{10... | collective-permute-start | bytes 196616 | tf_op jit(solution)/shard_map/ppermute | solution.py:30
  94.3 3.3 %collective-permute-done.17 = bf16[1,16,2048]{2,1,0:T(8,128)(2,1)S(1)} collective-permute-done((bf16[1,16,2048]{2,1,0:T(8,128)(2,1)S(1)}, bf16[1,16,2048]{2,1,0:T(8,128)(2,1)S(1)}, u32[]{:S(2)}, u32[]{:S(2)}) %collective-permute-start.17) | collective-permute-done | bytes 65568 | tf_op jit(solution)/shard_map/ppermute | solution.py:30
  (83 shorter events, 16.4 us)
Async XLA Ops:
  0.6 16.8 %copy-start = (bf16[512,32]{0,1:T(8,128)(2,1)S(1)}, bf16[512,32]{0,1:T(8,128)(2,1)}, u32[]{:S(2)}) copy-start(bf16[512,32]{0,1:T(8,128)(2,1)} %param.15) | copy-start | bytes 98308
  0.6 24.6 %copy-start.1 = (f32[4,16,2048]{2,1,0:T(8,128)S(1)}, f32[4,16,2048]{2,1,0:T(8,128)}, u32[]{:S(2)}) copy-start(f32[4,16,2048]{2,1,0:T(8,128)} %param.10) | copy-start | bytes 1572868
  0.7 16.8 %copy-start.3 = (bf16[512,128]{1,0:T(8,128)(2,1)S(1)}, bf16[512,128]{1,0:T(8,128)(2,1)}, u32[]{:S(2)}) copy-start(bf16[512,128]{1,0:T(8,128)(2,1)} %param.11) | copy-start | bytes 393220
  0.7 16.9 %copy-start.4 = (bf16[512,128]{1,0:T(8,128)(2,1)S(1)}, bf16[512,128]{1,0:T(8,128)(2,1)}, u32[]{:S(2)}) copy-start(bf16[512,128]{1,0:T(8,128)(2,1)} %param.14) | copy-start | bytes 393220
  2.1 5.5 %collective-permute-start.2 = (bf16[1,16,2048]{2,1,0:T(8,128)(2,1)S(1)}, bf16[1,16,2048]{2,1,0:T(8,128)(2,1)S(1)}, u32[]{:S(2)}, u32[]{:S(2)}) collective-permute-start(bf16[1,16,2048]{2,1,0:T(8,128)(2,1)S(1)} %get-tuple-element.40), channel_id=1, source_target_pairs={{0,24},{8,0},{16,8},{24,16},{1,25},{9,1},{17,9},{25,17},{2,26},{10... | collective-permute-start | bytes 196616 | tf_op jit(solution)/shard_map/ppermute | solution.py:30
  5.0 5.8 %collective-permute-start.1 = (bf16[1,16,2048]{2,1,0:T(8,128)(2,1)S(1)}, bf16[1,16,2048]{2,1,0:T(8,128)(2,1)S(1)}, u32[]{:S(2)}, u32[]{:S(2)}) collective-permute-start(bf16[1,16,2048]{2,1,0:T(8,128)(2,1)S(1)} %get-tuple-element.41), channel_id=1, source_target_pairs={{0,16},{8,24},{16,0},{24,8},{1,17},{9,25},{17,1},{25,9},{2,18},{10... | collective-permute-start | bytes 196616 | tf_op jit(solution)/shard_map/ppermute | solution.py:30
  5.8 5.7 %collective-permute-start = (bf16[1,16,2048]{2,1,0:T(8,128)(2,1)S(1)}, bf16[1,16,2048]{2,1,0:T(8,128)(2,1)S(1)}, u32[]{:S(2)}, u32[]{:S(2)}) collective-permute-start(bf16[1,16,2048]{2,1,0:T(8,128)(2,1)S(1)} %get-tuple-element.42), channel_id=1, source_target_pairs={{0,8},{8,16},{16,24},{24,0},{1,9},{9,17},{17,25},{25,1},{2,10},{10... | collective-permute-start | bytes 196616 | tf_op jit(solution)/shard_map/ppermute | solution.py:30
  11.5 10.1 %collective-permute-start.3 = (bf16[1,64,2048]{2,1,0:T(8,128)(2,1)S(1)}, bf16[1,64,2048]{2,1,0:T(8,128)(2,1)S(1)}, u32[]{:S(2)}, u32[]{:S(2)}) collective-permute-start(bf16[1,64,2048]{2,1,0:T(8,128)(2,1)S(1)} %pad_maximum_fusion), channel_id=1, source_target_pairs={{0,224},{32,0},{64,32},{96,64},{128,96},{160,128},{192,160},{224,1... | collective-permute-start | bytes 786440 | tf_op jit(solution)/shard_map/ppermute | solution.py:30
  17.4 7.8 %collective-permute-start.6 = (bf16[1,64,2048]{2,1,0:T(8,128)(2,1)S(1)}, bf16[1,64,2048]{2,1,0:T(8,128)(2,1)S(1)}, u32[]{:S(2)}, u32[]{:S(2)}) collective-permute-start(bf16[1,64,2048]{2,1,0:T(8,128)(2,1)S(1)} %pad_maximum_fusion), channel_id=1, source_target_pairs={{0,32},{32,64},{64,96},{96,128},{128,160},{160,192},{192,224},{224... | collective-permute-start | bytes 786440 | tf_op jit(solution)/shard_map/ppermute | solution.py:30
  21.5 7.6 %collective-permute-start.4 = (bf16[1,64,2048]{2,1,0:T(8,128)(2,1)S(1)}, bf16[1,64,2048]{2,1,0:T(8,128)(2,1)S(1)}, u32[]{:S(2)}, u32[]{:S(2)}) collective-permute-start(bf16[1,64,2048]{2,1,0:T(8,128)(2,1)S(1)} %collective-permute-done.3), channel_id=1, source_target_pairs={{0,224},{32,0},{64,32},{96,64},{128,96},{160,128},{192,160},{224,1... | collective-permute-start | bytes 786440 | tf_op jit(solution)/shard_map/ppermute | solution.py:30
  25.2 7.7 %collective-permute-start.7 = (bf16[1,64,2048]{2,1,0:T(8,128)(2,1)S(1)}, bf16[1,64,2048]{2,1,0:T(8,128)(2,1)S(1)}, u32[]{:S(2)}, u32[]{:S(2)}) collective-permute-start(bf16[1,64,2048]{2,1,0:T(8,128)(2,1)S(1)} %collective-permute-done.6), channel_id=1, source_target_pairs={{0,32},{32,64},{64,96},{96,128},{128,160},{160,192},{192,224},{224... | collective-permute-start | bytes 786440 | tf_op jit(solution)/shard_map/ppermute | solution.py:30
  29.1 8.4 %collective-permute-start.5 = (bf16[1,64,2048]{2,1,0:T(8,128)(2,1)S(1)}, bf16[1,64,2048]{2,1,0:T(8,128)(2,1)S(1)}, u32[]{:S(2)}, u32[]{:S(2)}) collective-permute-start(bf16[1,64,2048]{2,1,0:T(8,128)(2,1)S(1)} %collective-permute-done.4), channel_id=1, source_target_pairs={{0,224},{32,0},{64,32},{96,64},{128,96},{160,128},{192,160},{224,1... | collective-permute-start | bytes 786440 | tf_op jit(solution)/shard_map/ppermute | solution.py:30
  32.9 8.7 %collective-permute-start.8 = (bf16[1,64,2048]{2,1,0:T(8,128)(2,1)S(1)}, bf16[1,64,2048]{2,1,0:T(8,128)(2,1)S(1)}, u32[]{:S(2)}, u32[]{:S(2)}) collective-permute-start(bf16[1,64,2048]{2,1,0:T(8,128)(2,1)S(1)} %collective-permute-done.7), channel_id=1, source_target_pairs={{0,32},{32,64},{64,96},{96,128},{128,160},{160,192},{192,224},{224... | collective-permute-start | bytes 786440 | tf_op jit(solution)/shard_map/ppermute | solution.py:30
  37.6 6.3 %collective-permute-start.10 = (bf16[1,64,1024]{2,1,0:T(8,128)(2,1)S(1)}, bf16[1,64,1024]{2,1,0:T(8,128)(2,1)S(1)}, u32[]{:S(2)}, u32[]{:S(2)}) collective-permute-start(bf16[1,64,1024]{2,1,0:T(8,128)(2,1)S(1)} %slice.37), channel_id=1, source_target_pairs={{0,224},{32,0},{64,32},{96,64},{128,96},{160,128},{192,160},{224,1... | collective-permute-start | bytes 393224 | tf_op jit(solution)/shard_map/ppermute | solution.py:30
  41.6 6.3 %collective-permute-start.9 = (bf16[1,64,1024]{2,1,0:T(8,128)(2,1)S(1)}, bf16[1,64,1024]{2,1,0:T(8,128)(2,1)S(1)}, u32[]{:S(2)}, u32[]{:S(2)}) collective-permute-start(bf16[1,64,1024]{2,1,0:T(8,128)(2,1)S(1)} %slice.36), channel_id=1, source_target_pairs={{0,32},{32,64},{64,96},{96,128},{128,160},{160,192},{192,224},{224... | collective-permute-start | bytes 393224 | tf_op jit(solution)/shard_map/ppermute | solution.py:30
  50.8 3.6 %collective-permute-start.11 = (f32[34,128]{1,0:T(8,128)S(1)}, f32[34,128]{1,0:T(8,128)S(1)}, u32[]{:S(2)}, u32[]{:S(2)}) collective-permute-start(f32[34,128]{1,0:T(8,128)S(1)} %pad_maximum_fusion.1), channel_id=1, source_target_pairs={{0,1},{1,0},{2,3},{3,2},{4,5},{5,4},{6,7},{7,6},{8,9},{9,8},{10,11... | collective-permute-start | bytes 52232 | tf_op jit(solution)/shard_map/ppermute | solution.py:87
  54.4 5.0 %collective-permute-start.12 = (f32[34,128]{1,0:T(8,128)S(1)}, f32[34,128]{1,0:T(8,128)S(1)}, u32[]{:S(2)}, u32[]{:S(2)}) collective-permute-start(f32[34,128]{1,0:T(8,128)S(1)} %add.143), channel_id=1, source_target_pairs={{0,32},{32,0},{64,96},{96,64},{128,160},{160,128},{192,224},{224,1... | collective-permute-start | bytes 52232 | tf_op jit(solution)/shard_map/ppermute | solution.py:87
  59.4 4.8 %collective-permute-start.13 = (f32[34,128]{1,0:T(8,128)S(1)}, f32[34,128]{1,0:T(8,128)S(1)}, u32[]{:S(2)}, u32[]{:S(2)}) collective-permute-start(f32[34,128]{1,0:T(8,128)S(1)} %add.144), channel_id=1, source_target_pairs={{0,64},{32,96},{64,0},{96,32},{128,192},{160,224},{192,128},{224,1... | collective-permute-start | bytes 52232 | tf_op jit(solution)/shard_map/ppermute | solution.py:87
  64.2 9.6 %collective-permute-start.14 = (f32[34,128]{1,0:T(8,128)S(1)}, f32[34,128]{1,0:T(8,128)S(1)}, u32[]{:S(2)}, u32[]{:S(2)}) collective-permute-start(f32[34,128]{1,0:T(8,128)S(1)} %add.147), channel_id=1, source_target_pairs={{0,128},{32,160},{64,192},{96,224},{128,0},{160,32},{192,64},{224,... | collective-permute-start | bytes 52232 | tf_op jit(solution)/shard_map/ppermute | solution.py:87
  73.8 9.3 %collective-permute-start.15 = (f32[34,128]{1,0:T(8,128)S(1)}, f32[34,128]{1,0:T(8,128)S(1)}, u32[]{:S(2)}, u32[]{:S(2)}) collective-permute-start(f32[34,128]{1,0:T(8,128)S(1)} %add.150), channel_id=1, source_target_pairs={{0,8},{8,0},{16,24},{24,16},{1,9},{9,1},{17,25},{25,17},{2,10},{10... | collective-permute-start | bytes 52232 | tf_op jit(solution)/shard_map/ppermute | solution.py:87
  86.8 6.0 %collective-permute-start.19 = (f32[34,128]{1,0:T(8,128)S(1)}, f32[34,128]{1,0:T(8,128)S(1)}, u32[]{:S(2)}, u32[]{:S(2)}) collective-permute-start(f32[34,128]{1,0:T(8,128)S(1)} %add.153), channel_id=1, source_target_pairs={{0,16},{8,24},{16,0},{24,8},{1,17},{9,25},{17,1},{25,9},{2,18},{10... | collective-permute-start | bytes 52232 | tf_op jit(solution)/shard_map/ppermute | solution.py:87
  89.1 5.2 %collective-permute-start.16 = (bf16[1,16,2048]{2,1,0:T(8,128)(2,1)S(1)}, bf16[1,16,2048]{2,1,0:T(8,128)(2,1)S(1)}, u32[]{:S(2)}, u32[]{:S(2)}) collective-permute-start(bf16[1,16,2048]{2,1,0:T(8,128)(2,1)S(1)} %get-tuple-element.38), channel_id=1, source_target_pairs={{0,24},{8,0},{16,8},{24,16},{1,25},{9,1},{17,9},{25,17},{2,26},{10... | collective-permute-start | bytes 196616 | tf_op jit(solution)/shard_map/ppermute | solution.py:30
  91.8 5.9 %collective-permute-start.17 = (bf16[1,16,2048]{2,1,0:T(8,128)(2,1)S(1)}, bf16[1,16,2048]{2,1,0:T(8,128)(2,1)S(1)}, u32[]{:S(2)}, u32[]{:S(2)}) collective-permute-start(bf16[1,16,2048]{2,1,0:T(8,128)(2,1)S(1)} %get-tuple-element.37), channel_id=1, source_target_pairs={{0,16},{8,24},{16,0},{24,8},{1,17},{9,25},{17,1},{25,9},{2,18},{10... | collective-permute-start | bytes 196616 | tf_op jit(solution)/shard_map/ppermute | solution.py:30
  91.9 6.2 %collective-permute-start.18 = (bf16[1,16,2048]{2,1,0:T(8,128)(2,1)S(1)}, bf16[1,16,2048]{2,1,0:T(8,128)(2,1)S(1)}, u32[]{:S(2)}, u32[]{:S(2)}) collective-permute-start(bf16[1,16,2048]{2,1,0:T(8,128)(2,1)S(1)} %get-tuple-element.36), channel_id=1, source_target_pairs={{0,8},{8,16},{16,24},{24,0},{1,9},{9,17},{17,25},{25,1},{2,10},{10... | collective-permute-start | bytes 196616 | tf_op jit(solution)/shard_map/ppermute | solution.py:30
  (6 other events, 56.4 us)

commit v15 on v9

--- a/solution.py
+++ b/solution.py
@@ -66,6 +66,8 @@
             "kij,kjl->kil", gram_half[:, :rows], gram_half, preferred_element_type=jnp.float32
         )
         poly = (CUBIC_TERM * gram[:, :rows] + QUINTIC_TERM * square_term).astype(jnp.bfloat16)
+        if repeat == ITERS - 1:
+            carried, poly = lax.optimization_barrier((carried, poly))
         product = jnp.einsum("kij,kjl->kil", poly, iterate, preferred_element_type=jnp.float32)
         iterate = (LINEAR_TERM * iterate[:, :rows].astype(jnp.float32) + product).astype(
             jnp.bfloat16

time: 94.4 us -> 95 us (level)
  starting transfers between devices: 33 us -> 35.5 us
    ppermute x14, starting transfers between devices: 25 us -> 27.3 us  [shift(): return lax.ppermute(value, axis, [(i, (i + k) % size) for i in range(size)])]
    dot_general x5, matrix products: 15 us -> 14 us  [orthogonalize(): jnp.einsum('kij,kjl->kil', poly, iterate, preferred_element_type=jnp.floa...]
  transfers between devices with their start and end apart: 20 -> 20, of which waited for: 14 -> 13; matrix products, arithmetic and copies ran while one was open for 26% -> 27% of each run, Pallas kernels for 0% -> 0%
where the time goes in v15:
time: 95 us; the launch traced here: 94.8 us
  starting transfers between devices  35.5 us (37%)
  waiting for transfers between devices  26.2 us (28%)
  matrix products  25.2 us (27%)
  other arithmetic  5.88 us (6%)
  between operations  1.79 us (2%)
    ppermute x14, starting transfers between devices, shift(): return lax.ppermute(value, axis, [(i, (i + k) % size) for i in range(size)])  27.3 us
    ppermute x14, waiting for transfers between devices, shift(): return lax.ppermute(value, axis, [(i, (i + k) % size) for i in range(size)])  25 us
    dot_general x5, matrix products, orthogonalize(): jnp.einsum('kij,kjl->kil', poly, iterate, preferred_element_type=jnp.floa...  14 us
    dot_general x5, matrix products, orthogonalize(): jnp.einsum('kij,klj->kil', iterate, iterate, preferred_element_type=jnp.f...  10.8 us
    ppermute x6, starting transfers between devices, butterfly_rounds(): lax.ppermute(value, axis, perm)  8.19 us
    convert_element_type x1, other arithmetic, on_device(): nesterov = (grad_float + MUON_DECAY * next_momentum).astype(jnp.bfloat16)  2.08 us
  transfers between devices with their start and end apart: 20, of which 13 were waited for; matrix products, arithmetic and copies ran while one was open for 27% of the time, Pallas kernels for 0%

profile of v15, /device:TPU:16, one launch (start us, length us, event | category | flops | bytes accessed | tf_op | source)
XLA Modules:
  0.0 94.8 jit_solution(7457947896753348688)
XLA Ops:
  0.7 2.1 %fusion.34 = (bf16[4,16,2048]{2,1,0:T(8,128)(2,1)S(1)}, f32[4,16,2048]{2,1,0:T(8,128)}) fusion(bf16[4,16,2048]{2,1,0:T(8,128)(2,1)} %param.9, f32[4,16,2048]{2,1,0:T(8,128)} %param.10), kind=kLoop, calls=%fused_computation.49 | loop fusion | flops 786432 | bytes 1572864 | tf_op jit(solution)/shard_map/convert_element_type | solution.py:126
  2.9 1.6 %collective-permute-start = (bf16[1,16,2048]{2,1,0:T(8,128)(2,1)S(1)}, bf16[1,16,2048]{2,1,0:T(8,128)(2,1)S(1)}, u32[]{:S(2)}, u32[]{:S(2)}) collective-permute-start(bf16[1,16,2048]{2,1,0:T(8,128)(2,1)S(1)} %get-tuple-element.43), channel_id=1, source_target_pairs={{0,8},{8,16},{16,24},{24,0},{1,9},{9,17},{17,25},{25,1},{2,10},{10... | collective-permute-start | bytes 196616 | tf_op jit(solution)/shard_map/ppermute | solution.py:30
  4.4 2.7 %collective-permute-start.1 = (bf16[1,16,2048]{2,1,0:T(8,128)(2,1)S(1)}, bf16[1,16,2048]{2,1,0:T(8,128)(2,1)S(1)}, u32[]{:S(2)}, u32[]{:S(2)}) collective-permute-start(bf16[1,16,2048]{2,1,0:T(8,128)(2,1)S(1)} %get-tuple-element.42), channel_id=1, source_target_pairs={{0,16},{8,24},{16,0},{24,8},{1,17},{9,25},{17,1},{25,9},{2,18},{10... | collective-permute-start | bytes 196616 | tf_op jit(solution)/shard_map/ppermute | solution.py:30
  11.4 5.9 %collective-permute-start.3 = (bf16[1,64,2048]{2,1,0:T(8,128)(2,1)S(1)}, bf16[1,64,2048]{2,1,0:T(8,128)(2,1)S(1)}, u32[]{:S(2)}, u32[]{:S(2)}) collective-permute-start(bf16[1,64,2048]{2,1,0:T(8,128)(2,1)S(1)} %pad_maximum_fusion), channel_id=1, source_target_pairs={{0,224},{32,0},{64,32},{96,64},{128,96},{160,128},{192,160},{224,1... | collective-permute-start | bytes 786440 | tf_op jit(solution)/shard_map/ppermute | solution.py:30
  17.4 4.3 %collective-permute-done.3 = bf16[1,64,2048]{2,1,0:T(8,128)(2,1)S(1)} collective-permute-done((bf16[1,64,2048]{2,1,0:T(8,128)(2,1)S(1)}, bf16[1,64,2048]{2,1,0:T(8,128)(2,1)S(1)}, u32[]{:S(2)}, u32[]{:S(2)}) %collective-permute-start.3) | collective-permute-done | bytes 262176 | tf_op jit(solution)/shard_map/ppermute | solution.py:30
  21.8 3.7 %collective-permute-start.4 = (bf16[1,64,2048]{2,1,0:T(8,128)(2,1)S(1)}, bf16[1,64,2048]{2,1,0:T(8,128)(2,1)S(1)}, u32[]{:S(2)}, u32[]{:S(2)}) collective-permute-start(bf16[1,64,2048]{2,1,0:T(8,128)(2,1)S(1)} %collective-permute-done.3), channel_id=1, source_target_pairs={{0,224},{32,0},{64,32},{96,64},{128,96},{160,128},{192,160},{224,1... | collective-permute-start | bytes 786440 | tf_op jit(solution)/shard_map/ppermute | solution.py:30
  25.5 3.9 %collective-permute-done.4 = bf16[1,64,2048]{2,1,0:T(8,128)(2,1)S(1)} collective-permute-done((bf16[1,64,2048]{2,1,0:T(8,128)(2,1)S(1)}, bf16[1,64,2048]{2,1,0:T(8,128)(2,1)S(1)}, u32[]{:S(2)}, u32[]{:S(2)}) %collective-permute-start.4) | collective-permute-done | bytes 262176 | tf_op jit(solution)/shard_map/ppermute | solution.py:30
  29.3 3.7 %collective-permute-start.5 = (bf16[1,64,2048]{2,1,0:T(8,128)(2,1)S(1)}, bf16[1,64,2048]{2,1,0:T(8,128)(2,1)S(1)}, u32[]{:S(2)}, u32[]{:S(2)}) collective-permute-start(bf16[1,64,2048]{2,1,0:T(8,128)(2,1)S(1)} %collective-permute-done.4), channel_id=1, source_target_pairs={{0,224},{32,0},{64,32},{96,64},{128,96},{160,128},{192,160},{224,1... | collective-permute-start | bytes 786440 | tf_op jit(solution)/shard_map/ppermute | solution.py:30
  33.1 4.4 %collective-permute-done.5 = bf16[1,64,2048]{2,1,0:T(8,128)(2,1)S(1)} collective-permute-done((bf16[1,64,2048]{2,1,0:T(8,128)(2,1)S(1)}, bf16[1,64,2048]{2,1,0:T(8,128)(2,1)S(1)}, u32[]{:S(2)}, u32[]{:S(2)}) %collective-permute-start.5) | collective-permute-done | bytes 262176 | tf_op jit(solution)/shard_map/ppermute | solution.py:30
  37.5 3.8 %collective-permute-start.10 = (bf16[1,64,1024]{2,1,0:T(8,128)(2,1)S(1)}, bf16[1,64,1024]{2,1,0:T(8,128)(2,1)S(1)}, u32[]{:S(2)}, u32[]{:S(2)}) collective-permute-start(bf16[1,64,1024]{2,1,0:T(8,128)(2,1)S(1)} %slice.37), channel_id=1, source_target_pairs={{0,224},{32,0},{64,32},{96,64},{128,96},{160,128},{192,160},{224,1... | collective-permute-start | bytes 393224 | tf_op jit(solution)/shard_map/ppermute | solution.py:30
  41.5 2.3 %collective-permute-done.10 = bf16[1,64,1024]{2,1,0:T(8,128)(2,1)S(1)} collective-permute-done((bf16[1,64,1024]{2,1,0:T(8,128)(2,1)S(1)}, bf16[1,64,1024]{2,1,0:T(8,128)(2,1)S(1)}, u32[]{:S(2)}, u32[]{:S(2)}) %collective-permute-start.10) | collective-permute-done | bytes 131104 | tf_op jit(solution)/shard_map/ppermute | solution.py:30
  43.8 3.8 %collective-permute-done.9 = bf16[1,64,1024]{2,1,0:T(8,128)(2,1)S(1)} collective-permute-done((bf16[1,64,1024]{2,1,0:T(8,128)(2,1)S(1)}, bf16[1,64,1024]{2,1,0:T(8,128)(2,1)S(1)}, u32[]{:S(2)}, u32[]{:S(2)}) %collective-permute-start.9) | collective-permute-done | bytes 131104 | tf_op jit(solution)/shard_map/ppermute | solution.py:30
  47.8 1.7 %fusion = f32[]{:T(128)} fusion(bf16[1,512,2048]{2,1,0:T(8,128)(2,1)S(1)} %constant_dynamic-update-slice_fusion), kind=kLoop, calls=%fused_computation.2 | loop fusion | flops 3145727 | bytes 2097156 | tf_op jit(solution)/shard_map/reduce_sum | solution.py:53
  52.3 3.8 %fusion.5 = bf16[1,512,2048]{2,1,0:T(8,128)(2,1)S(1)} fusion(bf16[1,512,2048]{2,1,0:T(8,128)(2,1)} %copy-done.1, f32[512,512]{1,0:T(8,128)S(1)} %fusion.21), kind=kOutput, calls=%fused_computation.11 | convolution fusion | flops 1347682304 | bytes 5242880 | tf_op jit(solution)/shard_map/kij,kjl->kil/dot_general | solution.py:71
  57.5 2.9 %fusion.4 = bf16[1,512,2048]{2,1,0:T(8,128)(2,1)} fusion(bf16[1,512,2048]{2,1,0:T(8,128)(2,1)S(1)} %fusion.5, f32[512,512]{1,0:T(8,128)S(1)} %fusion.18), kind=kOutput, calls=%fused_computation.9 | convolution fusion | flops 1347682304 | bytes 5242880 | tf_op jit(solution)/shard_map/kij,kjl->kil/dot_general | solution.py:71
  60.9 3.2 %collective-permute-start.14 = (f32[34,128]{1,0:T(8,128)S(1)}, f32[34,128]{1,0:T(8,128)S(1)}, u32[]{:S(2)}, u32[]{:S(2)}) collective-permute-start(f32[34,128]{1,0:T(8,128)S(1)} %add.143), channel_id=1, source_target_pairs={{0,128},{32,160},{64,192},{96,224},{128,0},{160,32},{192,64},{224,... | collective-permute-start | bytes 52232 | tf_op jit(solution)/shard_map/ppermute | solution.py:89
  64.1 3.5 %fusion.15 = f32[512,512]{1,0:T(8,128)S(1)} fusion(bf16[1,512,2048]{2,1,0:T(8,128)(2,1)} %fusion.4), kind=kOutput, calls=%fused_computation.22 | convolution fusion | flops 1073741824 | bytes 3145728 | tf_op jit(solution)/shard_map/kij,klj->kil/dot_general | solution.py:62
  67.7 2.9 %fusion.3 = bf16[1,512,2048]{2,1,0:T(8,128)(2,1)} fusion(bf16[1,512,2048]{2,1,0:T(8,128)(2,1)S(1)} %copy-done.8, f32[512,512]{1,0:T(8,128)S(1)} %fusion.15), kind=kOutput, calls=%fused_computation.7 | convolution fusion | flops 1347682304 | bytes 5242880 | tf_op jit(solution)/shard_map/kij,kjl->kil/dot_general | solution.py:71
  71.9 3.5 %fusion.12 = f32[512,512]{1,0:T(8,128)S(1)} fusion(bf16[1,512,2048]{2,1,0:T(8,128)(2,1)} %fusion.3), kind=kOutput, calls=%fused_computation.19 | convolution fusion | flops 1073741824 | bytes 3145728 | tf_op jit(solution)/shard_map/kij,klj->kil/dot_general | solution.py:62
  75.4 3.8 %fusion.2 = bf16[1,512,2048]{2,1,0:T(8,128)(2,1)S(1)} fusion(bf16[1,512,2048]{2,1,0:T(8,128)(2,1)} %fusion.3, f32[512,512]{1,0:T(8,128)S(1)} %fusion.12), kind=kOutput, calls=%fused_computation.5 | convolution fusion | flops 1347682304 | bytes 5242880 | tf_op jit(solution)/shard_map/kij,kjl->kil/dot_general | solution.py:71
  79.3 3.2 %collective-permute-start.16 = (f32[34,128]{1,0:T(8,128)S(1)}, f32[34,128]{1,0:T(8,128)S(1)}, u32[]{:S(2)}, u32[]{:S(2)}) collective-permute-start(f32[34,128]{1,0:T(8,128)S(1)} %add.149), channel_id=1, source_target_pairs={{0,16},{8,24},{16,0},{24,8},{1,17},{9,25},{17,1},{25,9},{2,18},{10... | collective-permute-start | bytes 52232 | tf_op jit(solution)/shard_map/ppermute | solution.py:89
  85.4 1.5 %collective-permute-start.17 = (bf16[1,16,2048]{2,1,0:T(8,128)(2,1)S(1)}, bf16[1,16,2048]{2,1,0:T(8,128)(2,1)S(1)}, u32[]{:S(2)}, u32[]{:S(2)}) collective-permute-start(bf16[1,16,2048]{2,1,0:T(8,128)(2,1)S(1)} %get-tuple-element.40), channel_id=1, source_target_pairs={{0,24},{8,0},{16,8},{24,16},{1,25},{9,1},{17,9},{25,17},{2,26},{10... | collective-permute-start | bytes 196616 | tf_op jit(solution)/shard_map/ppermute | solution.py:30
  86.9 1.5 %collective-permute-start.18 = (bf16[1,16,2048]{2,1,0:T(8,128)(2,1)S(1)}, bf16[1,16,2048]{2,1,0:T(8,128)(2,1)S(1)}, u32[]{:S(2)}, u32[]{:S(2)}) collective-permute-start(bf16[1,16,2048]{2,1,0:T(8,128)(2,1)S(1)} %get-tuple-element.39), channel_id=1, source_target_pairs={{0,16},{8,24},{16,0},{24,8},{1,17},{9,25},{17,1},{25,9},{2,18},{10... | collective-permute-start | bytes 196616 | tf_op jit(solution)/shard_map/ppermute | solution.py:30
  90.4 2.3 %collective-permute-done.18 = bf16[1,16,2048]{2,1,0:T(8,128)(2,1)S(1)} collective-permute-done((bf16[1,16,2048]{2,1,0:T(8,128)(2,1)S(1)}, bf16[1,16,2048]{2,1,0:T(8,128)(2,1)S(1)}, u32[]{:S(2)}, u32[]{:S(2)}) %collective-permute-start.18) | collective-permute-done | bytes 65568 | tf_op jit(solution)/shard_map/ppermute | solution.py:30
  (83 shorter events, 16.9 us)
Async XLA Ops:
  0.6 8.0 %copy-start = (bf16[512,32]{0,1:T(8,128)(2,1)S(1)}, bf16[512,32]{0,1:T(8,128)(2,1)}, u32[]{:S(2)}) copy-start(bf16[512,32]{0,1:T(8,128)(2,1)} %param.15) | copy-start | bytes 98308
  0.6 7.9 %copy-start.2 = (bf16[512,128]{1,0:T(8,128)(2,1)S(1)}, bf16[512,128]{1,0:T(8,128)(2,1)}, u32[]{:S(2)}) copy-start(bf16[512,128]{1,0:T(8,128)(2,1)} %param.11) | copy-start | bytes 393220
  0.7 7.9 %copy-start.6 = (f32[128]{0:T(128)S(1)}, f32[128]{0:T(128)}, u32[]{:S(2)}) copy-start(f32[128]{0:T(128)} %param.13) | copy-start | bytes 1540
  0.7 8.1 %copy-start.3 = (bf16[512,128]{1,0:T(8,128)(2,1)S(1)}, bf16[512,128]{1,0:T(8,128)(2,1)}, u32[]{:S(2)}) copy-start(bf16[512,128]{1,0:T(8,128)(2,1)} %param.14) | copy-start | bytes 393220
  2.9 6.1 %collective-permute-start = (bf16[1,16,2048]{2,1,0:T(8,128)(2,1)S(1)}, bf16[1,16,2048]{2,1,0:T(8,128)(2,1)S(1)}, u32[]{:S(2)}, u32[]{:S(2)}) collective-permute-start(bf16[1,16,2048]{2,1,0:T(8,128)(2,1)S(1)} %get-tuple-element.43), channel_id=1, source_target_pairs={{0,8},{8,16},{16,24},{24,0},{1,9},{9,17},{17,25},{25,1},{2,10},{10... | collective-permute-start | bytes 196616 | tf_op jit(solution)/shard_map/ppermute | solution.py:30
  4.4 5.9 %collective-permute-start.1 = (bf16[1,16,2048]{2,1,0:T(8,128)(2,1)S(1)}, bf16[1,16,2048]{2,1,0:T(8,128)(2,1)S(1)}, u32[]{:S(2)}, u32[]{:S(2)}) collective-permute-start(bf16[1,16,2048]{2,1,0:T(8,128)(2,1)S(1)} %get-tuple-element.42), channel_id=1, source_target_pairs={{0,16},{8,24},{16,0},{24,8},{1,17},{9,25},{17,1},{25,9},{2,18},{10... | collective-permute-start | bytes 196616 | tf_op jit(solution)/shard_map/ppermute | solution.py:30
  7.1 4.3 %collective-permute-start.2 = (bf16[1,16,2048]{2,1,0:T(8,128)(2,1)S(1)}, bf16[1,16,2048]{2,1,0:T(8,128)(2,1)S(1)}, u32[]{:S(2)}, u32[]{:S(2)}) collective-permute-start(bf16[1,16,2048]{2,1,0:T(8,128)(2,1)S(1)} %get-tuple-element.41), channel_id=1, source_target_pairs={{0,24},{8,0},{16,8},{24,16},{1,25},{9,1},{17,9},{25,17},{2,26},{10... | collective-permute-start | bytes 196616 | tf_op jit(solution)/shard_map/ppermute | solution.py:30
  11.4 10.3 %collective-permute-start.3 = (bf16[1,64,2048]{2,1,0:T(8,128)(2,1)S(1)}, bf16[1,64,2048]{2,1,0:T(8,128)(2,1)S(1)}, u32[]{:S(2)}, u32[]{:S(2)}) collective-permute-start(bf16[1,64,2048]{2,1,0:T(8,128)(2,1)S(1)} %pad_maximum_fusion), channel_id=1, source_target_pairs={{0,224},{32,0},{64,32},{96,64},{128,96},{160,128},{192,160},{224,1... | collective-permute-start | bytes 786440 | tf_op jit(solution)/shard_map/ppermute | solution.py:30
  17.4 8.1 %collective-permute-start.6 = (bf16[1,64,2048]{2,1,0:T(8,128)(2,1)S(1)}, bf16[1,64,2048]{2,1,0:T(8,128)(2,1)S(1)}, u32[]{:S(2)}, u32[]{:S(2)}) collective-permute-start(bf16[1,64,2048]{2,1,0:T(8,128)(2,1)S(1)} %pad_maximum_fusion), channel_id=1, source_target_pairs={{0,32},{32,64},{64,96},{96,128},{128,160},{160,192},{192,224},{224... | collective-permute-start | bytes 786440 | tf_op jit(solution)/shard_map/ppermute | solution.py:30
  21.8 7.6 %collective-permute-start.4 = (bf16[1,64,2048]{2,1,0:T(8,128)(2,1)S(1)}, bf16[1,64,2048]{2,1,0:T(8,128)(2,1)S(1)}, u32[]{:S(2)}, u32[]{:S(2)}) collective-permute-start(bf16[1,64,2048]{2,1,0:T(8,128)(2,1)S(1)} %collective-permute-done.3), channel_id=1, source_target_pairs={{0,224},{32,0},{64,32},{96,64},{128,96},{160,128},{192,160},{224,1... | collective-permute-start | bytes 786440 | tf_op jit(solution)/shard_map/ppermute | solution.py:30
  25.5 7.6 %collective-permute-start.7 = (bf16[1,64,2048]{2,1,0:T(8,128)(2,1)S(1)}, bf16[1,64,2048]{2,1,0:T(8,128)(2,1)S(1)}, u32[]{:S(2)}, u32[]{:S(2)}) collective-permute-start(bf16[1,64,2048]{2,1,0:T(8,128)(2,1)S(1)} %collective-permute-done.6), channel_id=1, source_target_pairs={{0,32},{32,64},{64,96},{96,128},{128,160},{160,192},{192,224},{224... | collective-permute-start | bytes 786440 | tf_op jit(solution)/shard_map/ppermute | solution.py:30
  29.3 8.2 %collective-permute-start.5 = (bf16[1,64,2048]{2,1,0:T(8,128)(2,1)S(1)}, bf16[1,64,2048]{2,1,0:T(8,128)(2,1)S(1)}, u32[]{:S(2)}, u32[]{:S(2)}) collective-permute-start(bf16[1,64,2048]{2,1,0:T(8,128)(2,1)S(1)} %collective-permute-done.4), channel_id=1, source_target_pairs={{0,224},{32,0},{64,32},{96,64},{128,96},{160,128},{192,160},{224,1... | collective-permute-start | bytes 786440 | tf_op jit(solution)/shard_map/ppermute | solution.py:30
  33.0 8.4 %collective-permute-start.8 = (bf16[1,64,2048]{2,1,0:T(8,128)(2,1)S(1)}, bf16[1,64,2048]{2,1,0:T(8,128)(2,1)S(1)}, u32[]{:S(2)}, u32[]{:S(2)}) collective-permute-start(bf16[1,64,2048]{2,1,0:T(8,128)(2,1)S(1)} %collective-permute-done.7), channel_id=1, source_target_pairs={{0,32},{32,64},{64,96},{96,128},{128,160},{160,192},{192,224},{224... | collective-permute-start | bytes 786440 | tf_op jit(solution)/shard_map/ppermute | solution.py:30
  37.5 6.3 %collective-permute-start.10 = (bf16[1,64,1024]{2,1,0:T(8,128)(2,1)S(1)}, bf16[1,64,1024]{2,1,0:T(8,128)(2,1)S(1)}, u32[]{:S(2)}, u32[]{:S(2)}) collective-permute-start(bf16[1,64,1024]{2,1,0:T(8,128)(2,1)S(1)} %slice.37), channel_id=1, source_target_pairs={{0,224},{32,0},{64,32},{96,64},{128,96},{160,128},{192,160},{224,1... | collective-permute-start | bytes 393224 | tf_op jit(solution)/shard_map/ppermute | solution.py:30
  41.4 6.3 %collective-permute-start.9 = (bf16[1,64,1024]{2,1,0:T(8,128)(2,1)S(1)}, bf16[1,64,1024]{2,1,0:T(8,128)(2,1)S(1)}, u32[]{:S(2)}, u32[]{:S(2)}) collective-permute-start(bf16[1,64,1024]{2,1,0:T(8,128)(2,1)S(1)} %slice.36), channel_id=1, source_target_pairs={{0,32},{32,64},{64,96},{96,128},{128,160},{160,192},{192,224},{224... | collective-permute-start | bytes 393224 | tf_op jit(solution)/shard_map/ppermute | solution.py:30
  50.6 1.4 %collective-permute-start.11 = (f32[34,128]{1,0:T(8,128)S(1)}, f32[34,128]{1,0:T(8,128)S(1)}, u32[]{:S(2)}, u32[]{:S(2)}) collective-permute-start(f32[34,128]{1,0:T(8,128)S(1)} %pad_maximum_fusion.1), channel_id=1, source_target_pairs={{0,1},{1,0},{2,3},{3,2},{4,5},{5,4},{6,7},{7,6},{8,9},{9,8},{10,11... | collective-permute-start | bytes 52232 | tf_op jit(solution)/shard_map/ppermute | solution.py:89
  52.0 4.1 %collective-permute-start.12 = (f32[34,128]{1,0:T(8,128)S(1)}, f32[34,128]{1,0:T(8,128)S(1)}, u32[]{:S(2)}, u32[]{:S(2)}) collective-permute-start(f32[34,128]{1,0:T(8,128)S(1)} %add.139), channel_id=1, source_target_pairs={{0,32},{32,0},{64,96},{96,64},{128,160},{160,128},{192,224},{224,1... | collective-permute-start | bytes 52232 | tf_op jit(solution)/shard_map/ppermute | solution.py:89
  56.1 4.8 %collective-permute-start.13 = (f32[34,128]{1,0:T(8,128)S(1)}, f32[34,128]{1,0:T(8,128)S(1)}, u32[]{:S(2)}, u32[]{:S(2)}) collective-permute-start(f32[34,128]{1,0:T(8,128)S(1)} %add.140), channel_id=1, source_target_pairs={{0,64},{32,96},{64,0},{96,32},{128,192},{160,224},{192,128},{224,1... | collective-permute-start | bytes 52232 | tf_op jit(solution)/shard_map/ppermute | solution.py:89
  60.9 9.7 %collective-permute-start.14 = (f32[34,128]{1,0:T(8,128)S(1)}, f32[34,128]{1,0:T(8,128)S(1)}, u32[]{:S(2)}, u32[]{:S(2)}) collective-permute-start(f32[34,128]{1,0:T(8,128)S(1)} %add.143), channel_id=1, source_target_pairs={{0,128},{32,160},{64,192},{96,224},{128,0},{160,32},{192,64},{224,... | collective-permute-start | bytes 52232 | tf_op jit(solution)/shard_map/ppermute | solution.py:89
  70.6 8.6 %collective-permute-start.15 = (f32[34,128]{1,0:T(8,128)S(1)}, f32[34,128]{1,0:T(8,128)S(1)}, u32[]{:S(2)}, u32[]{:S(2)}) collective-permute-start(f32[34,128]{1,0:T(8,128)S(1)} %add.146), channel_id=1, source_target_pairs={{0,8},{8,0},{16,24},{24,16},{1,9},{9,1},{17,25},{25,17},{2,10},{10... | collective-permute-start | bytes 52232 | tf_op jit(solution)/shard_map/ppermute | solution.py:89
  79.3 5.6 %collective-permute-start.16 = (f32[34,128]{1,0:T(8,128)S(1)}, f32[34,128]{1,0:T(8,128)S(1)}, u32[]{:S(2)}, u32[]{:S(2)}) collective-permute-start(f32[34,128]{1,0:T(8,128)S(1)} %add.149), channel_id=1, source_target_pairs={{0,16},{8,24},{16,0},{24,8},{1,17},{9,25},{17,1},{25,9},{2,18},{10... | collective-permute-start | bytes 52232 | tf_op jit(solution)/shard_map/ppermute | solution.py:89
  85.4 5.0 %collective-permute-start.17 = (bf16[1,16,2048]{2,1,0:T(8,128)(2,1)S(1)}, bf16[1,16,2048]{2,1,0:T(8,128)(2,1)S(1)}, u32[]{:S(2)}, u32[]{:S(2)}) collective-permute-start(bf16[1,16,2048]{2,1,0:T(8,128)(2,1)S(1)} %get-tuple-element.40), channel_id=1, source_target_pairs={{0,24},{8,0},{16,8},{24,16},{1,25},{9,1},{17,9},{25,17},{2,26},{10... | collective-permute-start | bytes 196616 | tf_op jit(solution)/shard_map/ppermute | solution.py:30
  86.9 5.8 %collective-permute-start.18 = (bf16[1,16,2048]{2,1,0:T(8,128)(2,1)S(1)}, bf16[1,16,2048]{2,1,0:T(8,128)(2,1)S(1)}, u32[]{:S(2)}, u32[]{:S(2)}) collective-permute-start(bf16[1,16,2048]{2,1,0:T(8,128)(2,1)S(1)} %get-tuple-element.39), channel_id=1, source_target_pairs={{0,16},{8,24},{16,0},{24,8},{1,17},{9,25},{17,1},{25,9},{2,18},{10... | collective-permute-start | bytes 196616 | tf_op jit(solution)/shard_map/ppermute | solution.py:30
  88.5 5.5 %collective-permute-start.19 = (bf16[1,16,2048]{2,1,0:T(8,128)(2,1)S(1)}, bf16[1,16,2048]{2,1,0:T(8,128)(2,1)S(1)}, u32[]{:S(2)}, u32[]{:S(2)}) collective-permute-start(bf16[1,16,2048]{2,1,0:T(8,128)(2,1)S(1)} %get-tuple-element.38), channel_id=1, source_target_pairs={{0,8},{8,16},{16,24},{24,0},{1,9},{9,17},{17,25},{25,1},{2,10},{10... | collective-permute-start | bytes 196616 | tf_op jit(solution)/shard_map/ppermute | solution.py:30
  (5 other events, 28.0 us)

commit v16 on v9

--- a/solution.py
+++ b/solution.py
@@ -143,8 +143,7 @@
         [shift(result[:, k * rows_piece:(k + 1) * rows_piece], "inner", -k) for k in range(inner)],
         axis=0,
     )
-    twice = jnp.concatenate([back, back], axis=0)
-    ordered = lax.dynamic_slice_in_dim(twice, (inner - here) % inner, inner, axis=0)
+    ordered = jnp.take(back, (jnp.arange(inner) - here) % inner, axis=0)
     ordered = ordered.reshape(inner * slots, rows_piece, cols_full)
     update = ordered[:count_all].astype(jnp.float32) * math.sqrt(FF)
     return (next_momentum, update, next_first, next_second, adam_step)

time: 94.4 us -> 94.6 us (level)
  waiting for transfers between devices: 26.6 us -> 24.9 us
  starting transfers between devices: 33 us -> 34.2 us
    ppermute x14, starting transfers between devices: 25 us -> 26.3 us  [shift(): return lax.ppermute(value, axis, [(i, (i + k) % size) for i in range(size)])]
    ppermute x14, waiting for transfers between devices: 25.8 us -> 24.5 us  [shift(): return lax.ppermute(value, axis, [(i, (i + k) % size) for i in range(size)])]
  transfers between devices with their start and end apart: 20 -> 20, of which waited for: 14 -> 12; matrix products, arithmetic and copies ran while one was open for 26% -> 27% of each run, Pallas kernels for 0% -> 0%
where the time goes in v16:
time: 94.6 us; the launch traced here: 94.4 us
  starting transfers between devices  34.2 us (36%)
  matrix products  26 us (27%)
  waiting for transfers between devices  24.9 us (26%)
  other arithmetic  6.79 us (7%)
  between operations  1.76 us (2%)
    ppermute x14, starting transfers between devices, shift(): return lax.ppermute(value, axis, [(i, (i + k) % size) for i in range(size)])  26.3 us
    ppermute x14, waiting for transfers between devices, shift(): return lax.ppermute(value, axis, [(i, (i + k) % size) for i in range(size)])  24.5 us
    dot_general x5, matrix products, orthogonalize(): jnp.einsum('kij,kjl->kil', poly, iterate, preferred_element_type=jnp.floa...  15 us
    dot_general x5, matrix products, orthogonalize(): jnp.einsum('kij,klj->kil', iterate, iterate, preferred_element_type=jnp.f...  10.8 us
    ppermute x6, starting transfers between devices, butterfly_rounds(): lax.ppermute(value, axis, perm)  7.91 us
    convert_element_type x1, other arithmetic, on_device(): nesterov = (grad_float + MUON_DECAY * next_momentum).astype(jnp.bfloat16)  2.05 us
  transfers between devices with their start and end apart: 20, of which 12 were waited for; matrix products, arithmetic and copies ran while one was open for 27% of the time, Pallas kernels for 0%

profile of v16, /device:TPU:16, one launch (start us, length us, event | category | flops | bytes accessed | tf_op | source)
XLA Modules:
  0.0 94.4 jit_solution(11726065226485436308)
XLA Ops:
  0.7 2.1 %fusion.35 = (bf16[4,16,2048]{2,1,0:T(8,128)(2,1)S(1)}, f32[4,16,2048]{2,1,0:T(8,128)}) fusion(bf16[4,16,2048]{2,1,0:T(8,128)(2,1)} %param.9, f32[4,16,2048]{2,1,0:T(8,128)} %param.10), kind=kLoop, calls=%fused_computation.51 | loop fusion | flops 786432 | bytes 1572864 | tf_op jit(solution)/shard_map/convert_element_type | solution.py:124
  2.8 1.6 %collective-permute-start = (bf16[1,16,2048]{2,1,0:T(8,128)(2,1)S(1)}, bf16[1,16,2048]{2,1,0:T(8,128)(2,1)S(1)}, u32[]{:S(2)}, u32[]{:S(2)}) collective-permute-start(bf16[1,16,2048]{2,1,0:T(8,128)(2,1)S(1)} %get-tuple-element.40), channel_id=1, source_target_pairs={{0,8},{8,16},{16,24},{24,0},{1,9},{9,17},{17,25},{25,1},{2,10},{10... | collective-permute-start | bytes 196616 | tf_op jit(solution)/shard_map/ppermute | solution.py:30
  4.4 2.7 %collective-permute-start.1 = (bf16[1,16,2048]{2,1,0:T(8,128)(2,1)S(1)}, bf16[1,16,2048]{2,1,0:T(8,128)(2,1)S(1)}, u32[]{:S(2)}, u32[]{:S(2)}) collective-permute-start(bf16[1,16,2048]{2,1,0:T(8,128)(2,1)S(1)} %get-tuple-element.39), channel_id=1, source_target_pairs={{0,16},{8,24},{16,0},{24,8},{1,17},{9,25},{17,1},{25,9},{2,18},{10... | collective-permute-start | bytes 196616 | tf_op jit(solution)/shard_map/ppermute | solution.py:30
  11.4 5.9 %collective-permute-start.3 = (bf16[1,64,2048]{2,1,0:T(8,128)(2,1)S(1)}, bf16[1,64,2048]{2,1,0:T(8,128)(2,1)S(1)}, u32[]{:S(2)}, u32[]{:S(2)}) collective-permute-start(bf16[1,64,2048]{2,1,0:T(8,128)(2,1)S(1)} %pad_maximum_fusion), channel_id=1, source_target_pairs={{0,224},{32,0},{64,32},{96,64},{128,96},{160,128},{192,160},{224,1... | collective-permute-start | bytes 786440 | tf_op jit(solution)/shard_map/ppermute | solution.py:30
  17.4 4.4 %collective-permute-done.3 = bf16[1,64,2048]{2,1,0:T(8,128)(2,1)S(1)} collective-permute-done((bf16[1,64,2048]{2,1,0:T(8,128)(2,1)S(1)}, bf16[1,64,2048]{2,1,0:T(8,128)(2,1)S(1)}, u32[]{:S(2)}, u32[]{:S(2)}) %collective-permute-start.3) | collective-permute-done | bytes 262176 | tf_op jit(solution)/shard_map/ppermute | solution.py:30
  21.7 3.7 %collective-permute-start.4 = (bf16[1,64,2048]{2,1,0:T(8,128)(2,1)S(1)}, bf16[1,64,2048]{2,1,0:T(8,128)(2,1)S(1)}, u32[]{:S(2)}, u32[]{:S(2)}) collective-permute-start(bf16[1,64,2048]{2,1,0:T(8,128)(2,1)S(1)} %collective-permute-done.3), channel_id=1, source_target_pairs={{0,224},{32,0},{64,32},{96,64},{128,96},{160,128},{192,160},{224,1... | collective-permute-start | bytes 786440 | tf_op jit(solution)/shard_map/ppermute | solution.py:30
  25.5 3.9 %collective-permute-done.4 = bf16[1,64,2048]{2,1,0:T(8,128)(2,1)S(1)} collective-permute-done((bf16[1,64,2048]{2,1,0:T(8,128)(2,1)S(1)}, bf16[1,64,2048]{2,1,0:T(8,128)(2,1)S(1)}, u32[]{:S(2)}, u32[]{:S(2)}) %collective-permute-start.4) | collective-permute-done | bytes 262176 | tf_op jit(solution)/shard_map/ppermute | solution.py:30
  29.3 3.7 %collective-permute-start.5 = (bf16[1,64,2048]{2,1,0:T(8,128)(2,1)S(1)}, bf16[1,64,2048]{2,1,0:T(8,128)(2,1)S(1)}, u32[]{:S(2)}, u32[]{:S(2)}) collective-permute-start(bf16[1,64,2048]{2,1,0:T(8,128)(2,1)S(1)} %collective-permute-done.4), channel_id=1, source_target_pairs={{0,224},{32,0},{64,32},{96,64},{128,96},{160,128},{192,160},{224,1... | collective-permute-start | bytes 786440 | tf_op jit(solution)/shard_map/ppermute | solution.py:30
  33.1 4.4 %collective-permute-done.5 = bf16[1,64,2048]{2,1,0:T(8,128)(2,1)S(1)} collective-permute-done((bf16[1,64,2048]{2,1,0:T(8,128)(2,1)S(1)}, bf16[1,64,2048]{2,1,0:T(8,128)(2,1)S(1)}, u32[]{:S(2)}, u32[]{:S(2)}) %collective-permute-start.5) | collective-permute-done | bytes 262176 | tf_op jit(solution)/shard_map/ppermute | solution.py:30
  37.5 3.8 %collective-permute-start.10 = (bf16[1,64,1024]{2,1,0:T(8,128)(2,1)S(1)}, bf16[1,64,1024]{2,1,0:T(8,128)(2,1)S(1)}, u32[]{:S(2)}, u32[]{:S(2)}) collective-permute-start(bf16[1,64,1024]{2,1,0:T(8,128)(2,1)S(1)} %slice.39), channel_id=1, source_target_pairs={{0,224},{32,0},{64,32},{96,64},{128,96},{160,128},{192,160},{224,1... | collective-permute-start | bytes 393224 | tf_op jit(solution)/shard_map/ppermute | solution.py:30
  41.5 2.3 %collective-permute-done.10 = bf16[1,64,1024]{2,1,0:T(8,128)(2,1)S(1)} collective-permute-done((bf16[1,64,1024]{2,1,0:T(8,128)(2,1)S(1)}, bf16[1,64,1024]{2,1,0:T(8,128)(2,1)S(1)}, u32[]{:S(2)}, u32[]{:S(2)}) %collective-permute-start.10) | collective-permute-done | bytes 131104 | tf_op jit(solution)/shard_map/ppermute | solution.py:30
  43.8 3.8 %collective-permute-done.9 = bf16[1,64,1024]{2,1,0:T(8,128)(2,1)S(1)} collective-permute-done((bf16[1,64,1024]{2,1,0:T(8,128)(2,1)S(1)}, bf16[1,64,1024]{2,1,0:T(8,128)(2,1)S(1)}, u32[]{:S(2)}, u32[]{:S(2)}) %collective-permute-start.9) | collective-permute-done | bytes 131104 | tf_op jit(solution)/shard_map/ppermute | solution.py:30
  47.8 1.7 %fusion = f32[]{:T(128)} fusion(bf16[1,512,2048]{2,1,0:T(8,128)(2,1)S(1)} %constant_dynamic-update-slice_fusion), kind=kLoop, calls=%fused_computation.3 | loop fusion | flops 3145727 | bytes 2097156 | tf_op jit(solution)/shard_map/reduce_sum | solution.py:53
  52.3 3.8 %fusion.5 = bf16[1,512,2048]{2,1,0:T(8,128)(2,1)S(1)} fusion(bf16[1,512,2048]{2,1,0:T(8,128)(2,1)} %copy-done.1, f32[512,512]{1,0:T(8,128)S(1)} %fusion.21), kind=kOutput, calls=%fused_computation.12 | convolution fusion | flops 1347682304 | bytes 5242880 | tf_op jit(solution)/shard_map/kij,kjl->kil/dot_general | solution.py:69
  57.5 2.9 %fusion.4 = bf16[1,512,2048]{2,1,0:T(8,128)(2,1)} fusion(bf16[1,512,2048]{2,1,0:T(8,128)(2,1)S(1)} %fusion.5, f32[512,512]{1,0:T(8,128)S(1)} %fusion.18), kind=kOutput, calls=%fused_computation.10 | convolution fusion | flops 1347682304 | bytes 5242880 | tf_op jit(solution)/shard_map/kij,kjl->kil/dot_general | solution.py:69
  60.9 3.3 %collective-permute-start.14 = (f32[34,128]{1,0:T(8,128)S(1)}, f32[34,128]{1,0:T(8,128)S(1)}, u32[]{:S(2)}, u32[]{:S(2)}) collective-permute-start(f32[34,128]{1,0:T(8,128)S(1)} %add.171), channel_id=1, source_target_pairs={{0,128},{32,160},{64,192},{96,224},{128,0},{160,32},{192,64},{224,... | collective-permute-start | bytes 52232 | tf_op jit(solution)/shard_map/ppermute | solution.py:87
  64.1 3.5 %fusion.15 = f32[512,512]{1,0:T(8,128)S(1)} fusion(bf16[1,512,2048]{2,1,0:T(8,128)(2,1)} %fusion.4), kind=kOutput, calls=%fused_computation.23 | convolution fusion | flops 1073741824 | bytes 3145728 | tf_op jit(solution)/shard_map/kij,klj->kil/dot_general | solution.py:62
  67.6 2.9 %fusion.3 = bf16[1,512,2048]{2,1,0:T(8,128)(2,1)} fusion(bf16[1,512,2048]{2,1,0:T(8,128)(2,1)S(1)} %copy-done.8, f32[512,512]{1,0:T(8,128)S(1)} %fusion.15), kind=kOutput, calls=%fused_computation.8 | convolution fusion | flops 1347682304 | bytes 5242880 | tf_op jit(solution)/shard_map/kij,kjl->kil/dot_general | solution.py:69
  71.9 3.5 %fusion.12 = f32[512,512]{1,0:T(8,128)S(1)} fusion(bf16[1,512,2048]{2,1,0:T(8,128)(2,1)} %fusion.3), kind=kOutput, calls=%fused_computation.20 | convolution fusion | flops 1073741824 | bytes 3145728 | tf_op jit(solution)/shard_map/kij,klj->kil/dot_general | solution.py:62
  75.4 3.8 %fusion.2 = bf16[1,512,2048]{2,1,0:T(8,128)(2,1)S(1)} fusion(bf16[1,512,2048]{2,1,0:T(8,128)(2,1)} %fusion.3, f32[512,512]{1,0:T(8,128)S(1)} %fusion.12), kind=kOutput, calls=%fused_computation.6 | convolution fusion | flops 1347682304 | bytes 5242880 | tf_op jit(solution)/shard_map/kij,kjl->kil/dot_general | solution.py:69
  81.4 2.9 %collective-permute-start.19 = (f32[34,128]{1,0:T(8,128)S(1)}, f32[34,128]{1,0:T(8,128)S(1)}, u32[]{:S(2)}, u32[]{:S(2)}) collective-permute-start(f32[34,128]{1,0:T(8,128)S(1)} %add.177), channel_id=1, source_target_pairs={{0,16},{8,24},{16,0},{24,8},{1,17},{9,25},{17,1},{25,9},{2,18},{10... | collective-permute-start | bytes 52232 | tf_op jit(solution)/shard_map/ppermute | solution.py:87
  84.3 1.5 %fusion.7 = bf16[1,64,2048]{2,1,0:T(8,128)(2,1)S(1)} fusion(bf16[1,512,2048]{2,1,0:T(8,128)(2,1)S(1)} %fusion.2, f32[512,512]{1,0:T(8,128)S(1)} %fusion.9, f32[1,512,512]{2,1,0:T(8,128)S(1)} %bitcast.82, bf16[1,512,512]{2,1,0:T(8,128)(2,1)} %convert_bitcast_fusion), kind=kOutput, calls=%fused_computation.15 | convolution fusion | flops 168689664 | bytes 3866624 | tf_op jit(solution)/shard_map/kij,kjl->kil/dot_general | solution.py:69
  85.9 2.0 %collective-permute-start.17 = (bf16[1,16,2048]{2,1,0:T(8,128)(2,1)S(1)}, bf16[1,16,2048]{2,1,0:T(8,128)(2,1)S(1)}, u32[]{:S(2)}, u32[]{:S(2)}) collective-permute-start(bf16[1,16,2048]{2,1,0:T(8,128)(2,1)S(1)} %get-tuple-element.36), channel_id=1, source_target_pairs={{0,16},{8,24},{16,0},{24,8},{1,17},{9,25},{17,1},{25,9},{2,18},{10... | collective-permute-start | bytes 196616 | tf_op jit(solution)/shard_map/ppermute | solution.py:30
  89.8 2.2 %collective-permute-done.18 = bf16[1,16,2048]{2,1,0:T(8,128)(2,1)S(1)} collective-permute-done((bf16[1,16,2048]{2,1,0:T(8,128)(2,1)S(1)}, bf16[1,16,2048]{2,1,0:T(8,128)(2,1)S(1)}, u32[]{:S(2)}, u32[]{:S(2)}) %collective-permute-start.18) | collective-permute-done | bytes 65568 | tf_op jit(solution)/shard_map/ppermute | solution.py:30
  (78 shorter events, 16.4 us)
Async XLA Ops:
  0.6 8.0 %copy-start = (bf16[512,32]{0,1:T(8,128)(2,1)S(1)}, bf16[512,32]{0,1:T(8,128)(2,1)}, u32[]{:S(2)}) copy-start(bf16[512,32]{0,1:T(8,128)(2,1)} %param.15) | copy-start | bytes 98308
  0.6 7.9 %copy-start.3 = (bf16[512,128]{1,0:T(8,128)(2,1)S(1)}, bf16[512,128]{1,0:T(8,128)(2,1)}, u32[]{:S(2)}) copy-start(bf16[512,128]{1,0:T(8,128)(2,1)} %param.11) | copy-start | bytes 393220
  0.7 8.0 %copy-start.6 = (f32[128]{0:T(128)S(1)}, f32[128]{0:T(128)}, u32[]{:S(2)}) copy-start(f32[128]{0:T(128)} %param.13) | copy-start | bytes 1540
  0.7 8.0 %copy-start.7 = (f32[128]{0:T(128)S(1)}, f32[128]{0:T(128)}, u32[]{:S(2)}) copy-start(f32[128]{0:T(128)} %param.12) | copy-start | bytes 1540
  2.8 6.1 %collective-permute-start = (bf16[1,16,2048]{2,1,0:T(8,128)(2,1)S(1)}, bf16[1,16,2048]{2,1,0:T(8,128)(2,1)S(1)}, u32[]{:S(2)}, u32[]{:S(2)}) collective-permute-start(bf16[1,16,2048]{2,1,0:T(8,128)(2,1)S(1)} %get-tuple-element.40), channel_id=1, source_target_pairs={{0,8},{8,16},{16,24},{24,0},{1,9},{9,17},{17,25},{25,1},{2,10},{10... | collective-permute-start | bytes 196616 | tf_op jit(solution)/shard_map/ppermute | solution.py:30
  4.4 5.9 %collective-permute-start.1 = (bf16[1,16,2048]{2,1,0:T(8,128)(2,1)S(1)}, bf16[1,16,2048]{2,1,0:T(8,128)(2,1)S(1)}, u32[]{:S(2)}, u32[]{:S(2)}) collective-permute-start(bf16[1,16,2048]{2,1,0:T(8,128)(2,1)S(1)} %get-tuple-element.39), channel_id=1, source_target_pairs={{0,16},{8,24},{16,0},{24,8},{1,17},{9,25},{17,1},{25,9},{2,18},{10... | collective-permute-start | bytes 196616 | tf_op jit(solution)/shard_map/ppermute | solution.py:30
  7.1 4.3 %collective-permute-start.2 = (bf16[1,16,2048]{2,1,0:T(8,128)(2,1)S(1)}, bf16[1,16,2048]{2,1,0:T(8,128)(2,1)S(1)}, u32[]{:S(2)}, u32[]{:S(2)}) collective-permute-start(bf16[1,16,2048]{2,1,0:T(8,128)(2,1)S(1)} %get-tuple-element.38), channel_id=1, source_target_pairs={{0,24},{8,0},{16,8},{24,16},{1,25},{9,1},{17,9},{25,17},{2,26},{10... | collective-permute-start | bytes 196616 | tf_op jit(solution)/shard_map/ppermute | solution.py:30
  11.4 10.3 %collective-permute-start.3 = (bf16[1,64,2048]{2,1,0:T(8,128)(2,1)S(1)}, bf16[1,64,2048]{2,1,0:T(8,128)(2,1)S(1)}, u32[]{:S(2)}, u32[]{:S(2)}) collective-permute-start(bf16[1,64,2048]{2,1,0:T(8,128)(2,1)S(1)} %pad_maximum_fusion), channel_id=1, source_target_pairs={{0,224},{32,0},{64,32},{96,64},{128,96},{160,128},{192,160},{224,1... | collective-permute-start | bytes 786440 | tf_op jit(solution)/shard_map/ppermute | solution.py:30
  17.3 8.1 %collective-permute-start.6 = (bf16[1,64,2048]{2,1,0:T(8,128)(2,1)S(1)}, bf16[1,64,2048]{2,1,0:T(8,128)(2,1)S(1)}, u32[]{:S(2)}, u32[]{:S(2)}) collective-permute-start(bf16[1,64,2048]{2,1,0:T(8,128)(2,1)S(1)} %pad_maximum_fusion), channel_id=1, source_target_pairs={{0,32},{32,64},{64,96},{96,128},{128,160},{160,192},{192,224},{224... | collective-permute-start | bytes 786440 | tf_op jit(solution)/shard_map/ppermute | solution.py:30
  21.7 7.6 %collective-permute-start.4 = (bf16[1,64,2048]{2,1,0:T(8,128)(2,1)S(1)}, bf16[1,64,2048]{2,1,0:T(8,128)(2,1)S(1)}, u32[]{:S(2)}, u32[]{:S(2)}) collective-permute-start(bf16[1,64,2048]{2,1,0:T(8,128)(2,1)S(1)} %collective-permute-done.3), channel_id=1, source_target_pairs={{0,224},{32,0},{64,32},{96,64},{128,96},{160,128},{192,160},{224,1... | collective-permute-start | bytes 786440 | tf_op jit(solution)/shard_map/ppermute | solution.py:30
  25.4 7.6 %collective-permute-start.7 = (bf16[1,64,2048]{2,1,0:T(8,128)(2,1)S(1)}, bf16[1,64,2048]{2,1,0:T(8,128)(2,1)S(1)}, u32[]{:S(2)}, u32[]{:S(2)}) collective-permute-start(bf16[1,64,2048]{2,1,0:T(8,128)(2,1)S(1)} %collective-permute-done.6), channel_id=1, source_target_pairs={{0,32},{32,64},{64,96},{96,128},{128,160},{160,192},{192,224},{224... | collective-permute-start | bytes 786440 | tf_op jit(solution)/shard_map/ppermute | solution.py:30
  29.3 8.2 %collective-permute-start.5 = (bf16[1,64,2048]{2,1,0:T(8,128)(2,1)S(1)}, bf16[1,64,2048]{2,1,0:T(8,128)(2,1)S(1)}, u32[]{:S(2)}, u32[]{:S(2)}) collective-permute-start(bf16[1,64,2048]{2,1,0:T(8,128)(2,1)S(1)} %collective-permute-done.4), channel_id=1, source_target_pairs={{0,224},{32,0},{64,32},{96,64},{128,96},{160,128},{192,160},{224,1... | collective-permute-start | bytes 786440 | tf_op jit(solution)/shard_map/ppermute | solution.py:30
  33.0 8.4 %collective-permute-start.8 = (bf16[1,64,2048]{2,1,0:T(8,128)(2,1)S(1)}, bf16[1,64,2048]{2,1,0:T(8,128)(2,1)S(1)}, u32[]{:S(2)}, u32[]{:S(2)}) collective-permute-start(bf16[1,64,2048]{2,1,0:T(8,128)(2,1)S(1)} %collective-permute-done.7), channel_id=1, source_target_pairs={{0,32},{32,64},{64,96},{96,128},{128,160},{160,192},{192,224},{224... | collective-permute-start | bytes 786440 | tf_op jit(solution)/shard_map/ppermute | solution.py:30
  37.5 6.3 %collective-permute-start.10 = (bf16[1,64,1024]{2,1,0:T(8,128)(2,1)S(1)}, bf16[1,64,1024]{2,1,0:T(8,128)(2,1)S(1)}, u32[]{:S(2)}, u32[]{:S(2)}) collective-permute-start(bf16[1,64,1024]{2,1,0:T(8,128)(2,1)S(1)} %slice.39), channel_id=1, source_target_pairs={{0,224},{32,0},{64,32},{96,64},{128,96},{160,128},{192,160},{224,1... | collective-permute-start | bytes 393224 | tf_op jit(solution)/shard_map/ppermute | solution.py:30
  41.4 6.3 %collective-permute-start.9 = (bf16[1,64,1024]{2,1,0:T(8,128)(2,1)S(1)}, bf16[1,64,1024]{2,1,0:T(8,128)(2,1)S(1)}, u32[]{:S(2)}, u32[]{:S(2)}) collective-permute-start(bf16[1,64,1024]{2,1,0:T(8,128)(2,1)S(1)} %slice.38), channel_id=1, source_target_pairs={{0,32},{32,64},{64,96},{96,128},{128,160},{160,192},{192,224},{224... | collective-permute-start | bytes 393224 | tf_op jit(solution)/shard_map/ppermute | solution.py:30
  50.6 1.4 %collective-permute-start.11 = (f32[34,128]{1,0:T(8,128)S(1)}, f32[34,128]{1,0:T(8,128)S(1)}, u32[]{:S(2)}, u32[]{:S(2)}) collective-permute-start(f32[34,128]{1,0:T(8,128)S(1)} %pad_maximum_fusion.1), channel_id=1, source_target_pairs={{0,1},{1,0},{2,3},{3,2},{4,5},{5,4},{6,7},{7,6},{8,9},{9,8},{10,11... | collective-permute-start | bytes 52232 | tf_op jit(solution)/shard_map/ppermute | solution.py:87
  52.0 4.1 %collective-permute-start.12 = (f32[34,128]{1,0:T(8,128)S(1)}, f32[34,128]{1,0:T(8,128)S(1)}, u32[]{:S(2)}, u32[]{:S(2)}) collective-permute-start(f32[34,128]{1,0:T(8,128)S(1)} %add.167), channel_id=1, source_target_pairs={{0,32},{32,0},{64,96},{96,64},{128,160},{160,128},{192,224},{224,1... | collective-permute-start | bytes 52232 | tf_op jit(solution)/shard_map/ppermute | solution.py:87
  56.1 4.8 %collective-permute-start.13 = (f32[34,128]{1,0:T(8,128)S(1)}, f32[34,128]{1,0:T(8,128)S(1)}, u32[]{:S(2)}, u32[]{:S(2)}) collective-permute-start(f32[34,128]{1,0:T(8,128)S(1)} %add.168), channel_id=1, source_target_pairs={{0,64},{32,96},{64,0},{96,32},{128,192},{160,224},{192,128},{224,1... | collective-permute-start | bytes 52232 | tf_op jit(solution)/shard_map/ppermute | solution.py:87
  60.9 9.7 %collective-permute-start.14 = (f32[34,128]{1,0:T(8,128)S(1)}, f32[34,128]{1,0:T(8,128)S(1)}, u32[]{:S(2)}, u32[]{:S(2)}) collective-permute-start(f32[34,128]{1,0:T(8,128)S(1)} %add.171), channel_id=1, source_target_pairs={{0,128},{32,160},{64,192},{96,224},{128,0},{160,32},{192,64},{224,... | collective-permute-start | bytes 52232 | tf_op jit(solution)/shard_map/ppermute | solution.py:87
  70.6 8.6 %collective-permute-start.15 = (f32[34,128]{1,0:T(8,128)S(1)}, f32[34,128]{1,0:T(8,128)S(1)}, u32[]{:S(2)}, u32[]{:S(2)}) collective-permute-start(f32[34,128]{1,0:T(8,128)S(1)} %add.174), channel_id=1, source_target_pairs={{0,8},{8,0},{16,24},{24,16},{1,9},{9,1},{17,25},{25,17},{2,10},{10... | collective-permute-start | bytes 52232 | tf_op jit(solution)/shard_map/ppermute | solution.py:87
  81.4 7.8 %collective-permute-start.19 = (f32[34,128]{1,0:T(8,128)S(1)}, f32[34,128]{1,0:T(8,128)S(1)}, u32[]{:S(2)}, u32[]{:S(2)}) collective-permute-start(f32[34,128]{1,0:T(8,128)S(1)} %add.177), channel_id=1, source_target_pairs={{0,16},{8,24},{16,0},{24,8},{1,17},{9,25},{17,1},{25,9},{2,18},{10... | collective-permute-start | bytes 52232 | tf_op jit(solution)/shard_map/ppermute | solution.py:87
  85.8 6.3 %collective-permute-start.18 = (bf16[1,16,2048]{2,1,0:T(8,128)(2,1)S(1)}, bf16[1,16,2048]{2,1,0:T(8,128)(2,1)S(1)}, u32[]{:S(2)}, u32[]{:S(2)}) collective-permute-start(bf16[1,16,2048]{2,1,0:T(8,128)(2,1)S(1)} %get-tuple-element.35), channel_id=1, source_target_pairs={{0,8},{8,16},{16,24},{24,0},{1,9},{9,17},{17,25},{25,1},{2,10},{10... | collective-permute-start | bytes 196616 | tf_op jit(solution)/shard_map/ppermute | solution.py:30
  85.9 6.2 %collective-permute-start.17 = (bf16[1,16,2048]{2,1,0:T(8,128)(2,1)S(1)}, bf16[1,16,2048]{2,1,0:T(8,128)(2,1)S(1)}, u32[]{:S(2)}, u32[]{:S(2)}) collective-permute-start(bf16[1,16,2048]{2,1,0:T(8,128)(2,1)S(1)} %get-tuple-element.36), channel_id=1, source_target_pairs={{0,16},{8,24},{16,0},{24,8},{1,17},{9,25},{17,1},{25,9},{2,18},{10... | collective-permute-start | bytes 196616 | tf_op jit(solution)/shard_map/ppermute | solution.py:30
  87.9 5.0 %collective-permute-start.16 = (bf16[1,16,2048]{2,1,0:T(8,128)(2,1)S(1)}, bf16[1,16,2048]{2,1,0:T(8,128)(2,1)S(1)}, u32[]{:S(2)}, u32[]{:S(2)}) collective-permute-start(bf16[1,16,2048]{2,1,0:T(8,128)(2,1)S(1)} %get-tuple-element.37), channel_id=1, source_target_pairs={{0,24},{8,0},{16,8},{24,16},{1,25},{9,1},{17,9},{25,17},{2,26},{10... | collective-permute-start | bytes 196616 | tf_op jit(solution)/shard_map/ppermute | solution.py:30
  (5 other events, 31.6 us)

commit v17 on v9

--- a/solution.py
+++ b/solution.py
@@ -34,19 +34,21 @@
     size = lax.axis_size(axis)
     cols = strip.shape[-1]
     ahead, behind = [], []
+    far = []
+    if size % 2 == 0 and size > 2:
+        half = cols // 2
+        far = [jnp.concatenate(
+            [shift(strip[..., :half], axis, size // 2), shift(strip[..., half:], axis, -(size // 2))],
+            axis=-1)]
     from_behind = from_ahead = strip
-    for distance in range(1, size // 2 + 1):
-        if 2 * distance == size:
-            half = cols // 2
-            first = shift(from_behind[..., :half], axis, 1)
-            second = shift(from_ahead[..., half:], axis, -1)
-            ahead.append(jnp.concatenate([first, second], axis=-1))
-            break
+    for distance in range(1, (size + 1) // 2):
         from_behind = shift(from_behind, axis, 1)
         from_ahead = shift(from_ahead, axis, -1)
         ahead.append(from_ahead)
         behind.append(from_behind)
-    return jnp.concatenate([strip] + ahead + behind[::-1], axis=1)
+    if size == 2:
+        far = [shift(strip, axis, 1)]
+    return jnp.concatenate([strip] + ahead + far + behind[::-1], axis=1)
 
 
 def orthogonalize(blocks, carried, rounds, keep):

time: 94.4 us -> 103 us (1.091)
  waiting for transfers between devices: 26.6 us -> 32.9 us
  starting transfers between devices: 33 us -> 35.2 us
    ppermute x14, waiting for transfers between devices: 25.8 us -> 32.4 us  [shift(): return lax.ppermute(value, axis, [(i, (i + k) % size) for i in range(size)])]
    ppermute x14, starting transfers between devices: 25 us -> 27.3 us  [shift(): return lax.ppermute(value, axis, [(i, (i + k) % size) for i in range(size)])]
  transfers between devices with their start and end apart: 20 -> 20, of which waited for: 14 -> 11; matrix products, arithmetic and copies ran while one was open for 26% -> 23% of each run, Pallas kernels for 0% -> 0%
where the time goes in v17:
time: 103 us
  starting transfers between devices  35.2 us (34%)
  waiting for transfers between devices  32.9 us (32%)
  matrix products  26 us (25%)
  other arithmetic  6.65 us (6%)
  between operations  1.77 us (2%)
    ppermute x14, waiting for transfers between devices, shift(): return lax.ppermute(value, axis, [(i, (i + k) % size) for i in range(size)])  32.4 us
    ppermute x14, starting transfers between devices, shift(): return lax.ppermute(value, axis, [(i, (i + k) % size) for i in range(size)])  27.3 us
    dot_general x5, matrix products, orthogonalize(): jnp.einsum('kij,kjl->kil', poly, iterate, preferred_element_type=jnp.floa...  15 us
    dot_general x5, matrix products, orthogonalize(): jnp.einsum('kij,klj->kil', iterate, iterate, preferred_element_type=jnp.f...  10.8 us
    ppermute x6, starting transfers between devices, butterfly_rounds(): lax.ppermute(value, axis, perm)  7.87 us
  transfers between devices with their start and end apart: 20, of which 11 were waited for; matrix products, arithmetic and copies ran while one was open for 23% of the time, Pallas kernels for 0%

profile of v17, /device:TPU:16, one launch (start us, length us, event | category | flops | bytes accessed | tf_op | source)
XLA Modules:
  0.0 102.8 jit_solution(1495696362945103908)
XLA Ops:
  0.7 2.1 %fusion.35 = (bf16[4,16,2048]{2,1,0:T(8,128)(2,1)S(1)}, f32[4,16,2048]{2,1,0:T(8,128)}) fusion(bf16[4,16,2048]{2,1,0:T(8,128)(2,1)} %param.9, f32[4,16,2048]{2,1,0:T(8,128)} %param.10), kind=kLoop, calls=%fused_computation.50 | loop fusion | flops 786432 | bytes 1572864 | tf_op jit(solution)/shard_map/convert_element_type | solution.py:126
  2.8 1.6 %collective-permute-start = (bf16[1,16,2048]{2,1,0:T(8,128)(2,1)S(1)}, bf16[1,16,2048]{2,1,0:T(8,128)(2,1)S(1)}, u32[]{:S(2)}, u32[]{:S(2)}) collective-permute-start(bf16[1,16,2048]{2,1,0:T(8,128)(2,1)S(1)} %get-tuple-element.41), channel_id=1, source_target_pairs={{0,8},{8,16},{16,24},{24,0},{1,9},{9,17},{17,25},{25,1},{2,10},{10... | collective-permute-start | bytes 196616 | tf_op jit(solution)/shard_map/ppermute | solution.py:30
  4.4 2.7 %collective-permute-start.1 = (bf16[1,16,2048]{2,1,0:T(8,128)(2,1)S(1)}, bf16[1,16,2048]{2,1,0:T(8,128)(2,1)S(1)}, u32[]{:S(2)}, u32[]{:S(2)}) collective-permute-start(bf16[1,16,2048]{2,1,0:T(8,128)(2,1)S(1)} %get-tuple-element.40), channel_id=1, source_target_pairs={{0,16},{8,24},{16,0},{24,8},{1,17},{9,25},{17,1},{25,9},{2,18},{10... | collective-permute-start | bytes 196616 | tf_op jit(solution)/shard_map/ppermute | solution.py:30
  11.4 5.9 %collective-permute-start.3 = (bf16[1,64,2048]{2,1,0:T(8,128)(2,1)S(1)}, bf16[1,64,2048]{2,1,0:T(8,128)(2,1)S(1)}, u32[]{:S(2)}, u32[]{:S(2)}) collective-permute-start(bf16[1,64,2048]{2,1,0:T(8,128)(2,1)S(1)} %pad_maximum_fusion), channel_id=1, source_target_pairs={{0,224},{32,0},{64,32},{96,64},{128,96},{160,128},{192,160},{224,1... | collective-permute-start | bytes 786440 | tf_op jit(solution)/shard_map/ppermute | solution.py:30
  17.4 3.3 %collective-permute-start.7 = (bf16[1,64,1024]{2,1,0:T(8,128)(2,1)S(1)}, bf16[1,64,1024]{2,1,0:T(8,128)(2,1)S(1)}, u32[]{:S(2)}, u32[]{:S(2)}) collective-permute-start(bf16[1,64,1024]{2,1,0:T(8,128)(2,1)S(1)} %get-tuple-element.38), channel_id=1, source_target_pairs={{0,128},{32,160},{64,192},{96,224},{128,0},{160,32},{192,64},{224,... | collective-permute-start | bytes 393224 | tf_op jit(solution)/shard_map/ppermute | solution.py:30
  20.8 2.7 %collective-permute-start.6 = (bf16[1,64,1024]{2,1,0:T(8,128)(2,1)S(1)}, bf16[1,64,1024]{2,1,0:T(8,128)(2,1)S(1)}, u32[]{:S(2)}, u32[]{:S(2)}) collective-permute-start(bf16[1,64,1024]{2,1,0:T(8,128)(2,1)S(1)} %get-tuple-element.37), channel_id=1, source_target_pairs={{0,128},{32,160},{64,192},{96,224},{128,0},{160,32},{192,64},{224,... | collective-permute-start | bytes 393224 | tf_op jit(solution)/shard_map/ppermute | solution.py:30
  23.5 11.7 %collective-permute-done.3 = bf16[1,64,2048]{2,1,0:T(8,128)(2,1)S(1)} collective-permute-done((bf16[1,64,2048]{2,1,0:T(8,128)(2,1)S(1)}, bf16[1,64,2048]{2,1,0:T(8,128)(2,1)S(1)}, u32[]{:S(2)}, u32[]{:S(2)}) %collective-permute-start.3) | collective-permute-done | bytes 262176 | tf_op jit(solution)/shard_map/ppermute | solution.py:30
  35.1 3.7 %collective-permute-start.4 = (bf16[1,64,2048]{2,1,0:T(8,128)(2,1)S(1)}, bf16[1,64,2048]{2,1,0:T(8,128)(2,1)S(1)}, u32[]{:S(2)}, u32[]{:S(2)}) collective-permute-start(bf16[1,64,2048]{2,1,0:T(8,128)(2,1)S(1)} %collective-permute-done.3), channel_id=1, source_target_pairs={{0,224},{32,0},{64,32},{96,64},{128,96},{160,128},{192,160},{224,1... | collective-permute-start | bytes 786440 | tf_op jit(solution)/shard_map/ppermute | solution.py:30
  38.9 6.1 %collective-permute-done.4 = bf16[1,64,2048]{2,1,0:T(8,128)(2,1)S(1)} collective-permute-done((bf16[1,64,2048]{2,1,0:T(8,128)(2,1)S(1)}, bf16[1,64,2048]{2,1,0:T(8,128)(2,1)S(1)}, u32[]{:S(2)}, u32[]{:S(2)}) %collective-permute-start.4) | collective-permute-done | bytes 262176 | tf_op jit(solution)/shard_map/ppermute | solution.py:30
  45.0 3.7 %collective-permute-start.5 = (bf16[1,64,2048]{2,1,0:T(8,128)(2,1)S(1)}, bf16[1,64,2048]{2,1,0:T(8,128)(2,1)S(1)}, u32[]{:S(2)}, u32[]{:S(2)}) collective-permute-start(bf16[1,64,2048]{2,1,0:T(8,128)(2,1)S(1)} %collective-permute-done.4), channel_id=1, source_target_pairs={{0,224},{32,0},{64,32},{96,64},{128,96},{160,128},{192,160},{224,1... | collective-permute-start | bytes 786440 | tf_op jit(solution)/shard_map/ppermute | solution.py:30
  48.9 3.7 %collective-permute-done.5 = bf16[1,64,2048]{2,1,0:T(8,128)(2,1)S(1)} collective-permute-done((bf16[1,64,2048]{2,1,0:T(8,128)(2,1)S(1)}, bf16[1,64,2048]{2,1,0:T(8,128)(2,1)S(1)}, u32[]{:S(2)}, u32[]{:S(2)}) %collective-permute-start.5) | collective-permute-done | bytes 262176 | tf_op jit(solution)/shard_map/ppermute | solution.py:30
  52.7 3.7 %collective-permute-done.10 = bf16[1,64,2048]{2,1,0:T(8,128)(2,1)S(1)} collective-permute-done((bf16[1,64,2048]{2,1,0:T(8,128)(2,1)S(1)}, bf16[1,64,2048]{2,1,0:T(8,128)(2,1)S(1)}, u32[]{:S(2)}, u32[]{:S(2)}) %collective-permute-start.10) | collective-permute-done | bytes 262176 | tf_op jit(solution)/shard_map/ppermute | solution.py:30
  56.5 1.7 %fusion = f32[]{:T(128)} fusion(bf16[1,512,2048]{2,1,0:T(8,128)(2,1)S(1)} %constant_dynamic-update-slice_fusion), kind=kLoop, calls=%fused_computation.2 | loop fusion | flops 3145727 | bytes 2097156 | tf_op jit(solution)/shard_map/reduce_sum | solution.py:55
  61.0 3.8 %fusion.5 = bf16[1,512,2048]{2,1,0:T(8,128)(2,1)S(1)} fusion(bf16[1,512,2048]{2,1,0:T(8,128)(2,1)} %copy-done.1, f32[512,512]{1,0:T(8,128)S(1)} %fusion.21), kind=kOutput, calls=%fused_computation.11 | convolution fusion | flops 1347682304 | bytes 5242880 | tf_op jit(solution)/shard_map/kij,kjl->kil/dot_general | solution.py:71
  66.2 2.9 %fusion.4 = bf16[1,512,2048]{2,1,0:T(8,128)(2,1)} fusion(bf16[1,512,2048]{2,1,0:T(8,128)(2,1)S(1)} %fusion.5, f32[512,512]{1,0:T(8,128)S(1)} %fusion.18), kind=kOutput, calls=%fused_computation.9 | convolution fusion | flops 1347682304 | bytes 5242880 | tf_op jit(solution)/shard_map/kij,kjl->kil/dot_general | solution.py:71
  69.6 3.4 %collective-permute-start.14 = (f32[34,128]{1,0:T(8,128)S(1)}, f32[34,128]{1,0:T(8,128)S(1)}, u32[]{:S(2)}, u32[]{:S(2)}) collective-permute-start(f32[34,128]{1,0:T(8,128)S(1)} %add.143), channel_id=1, source_target_pairs={{0,128},{32,160},{64,192},{96,224},{128,0},{160,32},{192,64},{224,... | collective-permute-start | bytes 52232 | tf_op jit(solution)/shard_map/ppermute | solution.py:89
  73.0 3.5 %fusion.15 = f32[512,512]{1,0:T(8,128)S(1)} fusion(bf16[1,512,2048]{2,1,0:T(8,128)(2,1)} %fusion.4), kind=kOutput, calls=%fused_computation.22 | convolution fusion | flops 1073741824 | bytes 3145728 | tf_op jit(solution)/shard_map/kij,klj->kil/dot_general | solution.py:64
  76.5 2.9 %fusion.3 = bf16[1,512,2048]{2,1,0:T(8,128)(2,1)} fusion(bf16[1,512,2048]{2,1,0:T(8,128)(2,1)S(1)} %copy-done.8, f32[512,512]{1,0:T(8,128)S(1)} %fusion.15), kind=kOutput, calls=%fused_computation.7 | convolution fusion | flops 1347682304 | bytes 5242880 | tf_op jit(solution)/shard_map/kij,kjl->kil/dot_general | solution.py:71
  79.6 3.5 %fusion.12 = f32[512,512]{1,0:T(8,128)S(1)} fusion(bf16[1,512,2048]{2,1,0:T(8,128)(2,1)} %fusion.3), kind=kOutput, calls=%fused_computation.19 | convolution fusion | flops 1073741824 | bytes 3145728 | tf_op jit(solution)/shard_map/kij,klj->kil/dot_general | solution.py:64
  83.1 3.8 %fusion.2 = bf16[1,512,2048]{2,1,0:T(8,128)(2,1)S(1)} fusion(bf16[1,512,2048]{2,1,0:T(8,128)(2,1)} %fusion.3, f32[512,512]{1,0:T(8,128)S(1)} %fusion.12), kind=kOutput, calls=%fused_computation.5 | convolution fusion | flops 1347682304 | bytes 5242880 | tf_op jit(solution)/shard_map/kij,kjl->kil/dot_general | solution.py:71
  89.1 1.5 %fusion.7 = bf16[1,64,2048]{2,1,0:T(8,128)(2,1)S(1)} fusion(bf16[1,512,2048]{2,1,0:T(8,128)(2,1)S(1)} %fusion.2, f32[512,512]{1,0:T(8,128)S(1)} %fusion.9, f32[1,512,512]{2,1,0:T(8,128)S(1)} %bitcast.90, bf16[1,512,512]{2,1,0:T(8,128)(2,1)} %convert_bitcast_fusion), kind=kOutput, calls=%fused_computation.14 | convolution fusion | flops 168689664 | bytes 3866624 | tf_op jit(solution)/shard_map/kij,kjl->kil/dot_general | solution.py:71
  90.6 3.9 %collective-permute-start.19 = (f32[34,128]{1,0:T(8,128)S(1)}, f32[34,128]{1,0:T(8,128)S(1)}, u32[]{:S(2)}, u32[]{:S(2)}) collective-permute-start(f32[34,128]{1,0:T(8,128)S(1)} %add.149), channel_id=1, source_target_pairs={{0,16},{8,24},{16,0},{24,8},{1,17},{9,25},{17,1},{25,9},{2,18},{10... | collective-permute-start | bytes 52232 | tf_op jit(solution)/shard_map/ppermute | solution.py:89
  97.2 1.6 %collective-permute-done.16 = bf16[1,16,2048]{2,1,0:T(8,128)(2,1)S(1)} collective-permute-done((bf16[1,16,2048]{2,1,0:T(8,128)(2,1)S(1)}, bf16[1,16,2048]{2,1,0:T(8,128)(2,1)S(1)}, u32[]{:S(2)}, u32[]{:S(2)}) %collective-permute-start.16) | collective-permute-done | bytes 65568 | tf_op jit(solution)/shard_map/ppermute | solution.py:30
  98.8 2.4 %collective-permute-done.17 = bf16[1,16,2048]{2,1,0:T(8,128)(2,1)S(1)} collective-permute-done((bf16[1,16,2048]{2,1,0:T(8,128)(2,1)S(1)}, bf16[1,16,2048]{2,1,0:T(8,128)(2,1)S(1)}, u32[]{:S(2)}, u32[]{:S(2)}) %collective-permute-start.17) | collective-permute-done | bytes 65568 | tf_op jit(solution)/shard_map/ppermute | solution.py:30
  (80 shorter events, 15.2 us)
Async XLA Ops:
  0.6 8.0 %copy-start = (bf16[512,32]{0,1:T(8,128)(2,1)S(1)}, bf16[512,32]{0,1:T(8,128)(2,1)}, u32[]{:S(2)}) copy-start(bf16[512,32]{0,1:T(8,128)(2,1)} %param.15) | copy-start | bytes 98308
  0.6 7.9 %copy-start.3 = (bf16[512,128]{1,0:T(8,128)(2,1)S(1)}, bf16[512,128]{1,0:T(8,128)(2,1)}, u32[]{:S(2)}) copy-start(bf16[512,128]{1,0:T(8,128)(2,1)} %param.11) | copy-start | bytes 393220
  0.7 8.0 %copy-start.6 = (f32[128]{0:T(128)S(1)}, f32[128]{0:T(128)}, u32[]{:S(2)}) copy-start(f32[128]{0:T(128)} %param.13) | copy-start | bytes 1540
  0.7 8.0 %copy-start.7 = (f32[128]{0:T(128)S(1)}, f32[128]{0:T(128)}, u32[]{:S(2)}) copy-start(f32[128]{0:T(128)} %param.12) | copy-start | bytes 1540
  2.8 6.1 %collective-permute-start = (bf16[1,16,2048]{2,1,0:T(8,128)(2,1)S(1)}, bf16[1,16,2048]{2,1,0:T(8,128)(2,1)S(1)}, u32[]{:S(2)}, u32[]{:S(2)}) collective-permute-start(bf16[1,16,2048]{2,1,0:T(8,128)(2,1)S(1)} %get-tuple-element.41), channel_id=1, source_target_pairs={{0,8},{8,16},{16,24},{24,0},{1,9},{9,17},{17,25},{25,1},{2,10},{10... | collective-permute-start | bytes 196616 | tf_op jit(solution)/shard_map/ppermute | solution.py:30
  4.4 5.9 %collective-permute-start.1 = (bf16[1,16,2048]{2,1,0:T(8,128)(2,1)S(1)}, bf16[1,16,2048]{2,1,0:T(8,128)(2,1)S(1)}, u32[]{:S(2)}, u32[]{:S(2)}) collective-permute-start(bf16[1,16,2048]{2,1,0:T(8,128)(2,1)S(1)} %get-tuple-element.40), channel_id=1, source_target_pairs={{0,16},{8,24},{16,0},{24,8},{1,17},{9,25},{17,1},{25,9},{2,18},{10... | collective-permute-start | bytes 196616 | tf_op jit(solution)/shard_map/ppermute | solution.py:30
  7.1 4.3 %collective-permute-start.2 = (bf16[1,16,2048]{2,1,0:T(8,128)(2,1)S(1)}, bf16[1,16,2048]{2,1,0:T(8,128)(2,1)S(1)}, u32[]{:S(2)}, u32[]{:S(2)}) collective-permute-start(bf16[1,16,2048]{2,1,0:T(8,128)(2,1)S(1)} %get-tuple-element.39), channel_id=1, source_target_pairs={{0,24},{8,0},{16,8},{24,16},{1,25},{9,1},{17,9},{25,17},{2,26},{10... | collective-permute-start | bytes 196616 | tf_op jit(solution)/shard_map/ppermute | solution.py:30
  11.4 23.7 %collective-permute-start.3 = (bf16[1,64,2048]{2,1,0:T(8,128)(2,1)S(1)}, bf16[1,64,2048]{2,1,0:T(8,128)(2,1)S(1)}, u32[]{:S(2)}, u32[]{:S(2)}) collective-permute-start(bf16[1,64,2048]{2,1,0:T(8,128)(2,1)S(1)} %pad_maximum_fusion), channel_id=1, source_target_pairs={{0,224},{32,0},{64,32},{96,64},{128,96},{160,128},{192,160},{224,1... | collective-permute-start | bytes 786440 | tf_op jit(solution)/shard_map/ppermute | solution.py:30
  17.4 21.5 %collective-permute-start.8 = (bf16[1,64,2048]{2,1,0:T(8,128)(2,1)S(1)}, bf16[1,64,2048]{2,1,0:T(8,128)(2,1)S(1)}, u32[]{:S(2)}, u32[]{:S(2)}) collective-permute-start(bf16[1,64,2048]{2,1,0:T(8,128)(2,1)S(1)} %pad_maximum_fusion), channel_id=1, source_target_pairs={{0,32},{32,64},{64,96},{96,128},{128,160},{160,192},{192,224},{224... | collective-permute-start | bytes 786440 | tf_op jit(solution)/shard_map/ppermute | solution.py:30
  17.4 35.2 %collective-permute-start.7 = (bf16[1,64,1024]{2,1,0:T(8,128)(2,1)S(1)}, bf16[1,64,1024]{2,1,0:T(8,128)(2,1)S(1)}, u32[]{:S(2)}, u32[]{:S(2)}) collective-permute-start(bf16[1,64,1024]{2,1,0:T(8,128)(2,1)S(1)} %get-tuple-element.38), channel_id=1, source_target_pairs={{0,128},{32,160},{64,192},{96,224},{128,0},{160,32},{192,64},{224,... | collective-permute-start | bytes 393224 | tf_op jit(solution)/shard_map/ppermute | solution.py:30
  20.8 31.8 %collective-permute-start.6 = (bf16[1,64,1024]{2,1,0:T(8,128)(2,1)S(1)}, bf16[1,64,1024]{2,1,0:T(8,128)(2,1)S(1)}, u32[]{:S(2)}, u32[]{:S(2)}) collective-permute-start(bf16[1,64,1024]{2,1,0:T(8,128)(2,1)S(1)} %get-tuple-element.37), channel_id=1, source_target_pairs={{0,128},{32,160},{64,192},{96,224},{128,0},{160,32},{192,64},{224,... | collective-permute-start | bytes 393224 | tf_op jit(solution)/shard_map/ppermute | solution.py:30
  35.1 9.9 %collective-permute-start.4 = (bf16[1,64,2048]{2,1,0:T(8,128)(2,1)S(1)}, bf16[1,64,2048]{2,1,0:T(8,128)(2,1)S(1)}, u32[]{:S(2)}, u32[]{:S(2)}) collective-permute-start(bf16[1,64,2048]{2,1,0:T(8,128)(2,1)S(1)} %collective-permute-done.3), channel_id=1, source_target_pairs={{0,224},{32,0},{64,32},{96,64},{128,96},{160,128},{192,160},{224,1... | collective-permute-start | bytes 786440 | tf_op jit(solution)/shard_map/ppermute | solution.py:30
  38.8 9.9 %collective-permute-start.9 = (bf16[1,64,2048]{2,1,0:T(8,128)(2,1)S(1)}, bf16[1,64,2048]{2,1,0:T(8,128)(2,1)S(1)}, u32[]{:S(2)}, u32[]{:S(2)}) collective-permute-start(bf16[1,64,2048]{2,1,0:T(8,128)(2,1)S(1)} %collective-permute-done.8), channel_id=1, source_target_pairs={{0,32},{32,64},{64,96},{96,128},{128,160},{160,192},{192,224},{224... | collective-permute-start | bytes 786440 | tf_op jit(solution)/shard_map/ppermute | solution.py:30
  45.0 7.6 %collective-permute-start.5 = (bf16[1,64,2048]{2,1,0:T(8,128)(2,1)S(1)}, bf16[1,64,2048]{2,1,0:T(8,128)(2,1)S(1)}, u32[]{:S(2)}, u32[]{:S(2)}) collective-permute-start(bf16[1,64,2048]{2,1,0:T(8,128)(2,1)S(1)} %collective-permute-done.4), channel_id=1, source_target_pairs={{0,224},{32,0},{64,32},{96,64},{128,96},{160,128},{192,160},{224,1... | collective-permute-start | bytes 786440 | tf_op jit(solution)/shard_map/ppermute | solution.py:30
  48.7 7.7 %collective-permute-start.10 = (bf16[1,64,2048]{2,1,0:T(8,128)(2,1)S(1)}, bf16[1,64,2048]{2,1,0:T(8,128)(2,1)S(1)}, u32[]{:S(2)}, u32[]{:S(2)}) collective-permute-start(bf16[1,64,2048]{2,1,0:T(8,128)(2,1)S(1)} %collective-permute-done.9), channel_id=1, source_target_pairs={{0,32},{32,64},{64,96},{96,128},{128,160},{160,192},{192,224},{224... | collective-permute-start | bytes 786440 | tf_op jit(solution)/shard_map/ppermute | solution.py:30
  59.3 1.4 %collective-permute-start.11 = (f32[34,128]{1,0:T(8,128)S(1)}, f32[34,128]{1,0:T(8,128)S(1)}, u32[]{:S(2)}, u32[]{:S(2)}) collective-permute-start(f32[34,128]{1,0:T(8,128)S(1)} %pad_maximum_fusion.1), channel_id=1, source_target_pairs={{0,1},{1,0},{2,3},{3,2},{4,5},{5,4},{6,7},{7,6},{8,9},{9,8},{10,11... | collective-permute-start | bytes 52232 | tf_op jit(solution)/shard_map/ppermute | solution.py:89
  60.7 4.1 %collective-permute-start.12 = (f32[34,128]{1,0:T(8,128)S(1)}, f32[34,128]{1,0:T(8,128)S(1)}, u32[]{:S(2)}, u32[]{:S(2)}) collective-permute-start(f32[34,128]{1,0:T(8,128)S(1)} %add.139), channel_id=1, source_target_pairs={{0,32},{32,0},{64,96},{96,64},{128,160},{160,128},{192,224},{224,1... | collective-permute-start | bytes 52232 | tf_op jit(solution)/shard_map/ppermute | solution.py:89
  64.8 4.8 %collective-permute-start.13 = (f32[34,128]{1,0:T(8,128)S(1)}, f32[34,128]{1,0:T(8,128)S(1)}, u32[]{:S(2)}, u32[]{:S(2)}) collective-permute-start(f32[34,128]{1,0:T(8,128)S(1)} %add.140), channel_id=1, source_target_pairs={{0,64},{32,96},{64,0},{96,32},{128,192},{160,224},{192,128},{224,1... | collective-permute-start | bytes 52232 | tf_op jit(solution)/shard_map/ppermute | solution.py:89
  69.6 9.9 %collective-permute-start.14 = (f32[34,128]{1,0:T(8,128)S(1)}, f32[34,128]{1,0:T(8,128)S(1)}, u32[]{:S(2)}, u32[]{:S(2)}) collective-permute-start(f32[34,128]{1,0:T(8,128)S(1)} %add.143), channel_id=1, source_target_pairs={{0,128},{32,160},{64,192},{96,224},{128,0},{160,32},{192,64},{224,... | collective-permute-start | bytes 52232 | tf_op jit(solution)/shard_map/ppermute | solution.py:89
  79.5 7.5 %collective-permute-start.15 = (f32[34,128]{1,0:T(8,128)S(1)}, f32[34,128]{1,0:T(8,128)S(1)}, u32[]{:S(2)}, u32[]{:S(2)}) collective-permute-start(f32[34,128]{1,0:T(8,128)S(1)} %add.146), channel_id=1, source_target_pairs={{0,8},{8,0},{16,24},{24,16},{1,9},{9,1},{17,25},{25,17},{2,10},{10... | collective-permute-start | bytes 52232 | tf_op jit(solution)/shard_map/ppermute | solution.py:89
  90.6 5.9 %collective-permute-start.19 = (f32[34,128]{1,0:T(8,128)S(1)}, f32[34,128]{1,0:T(8,128)S(1)}, u32[]{:S(2)}, u32[]{:S(2)}) collective-permute-start(f32[34,128]{1,0:T(8,128)S(1)} %add.149), channel_id=1, source_target_pairs={{0,16},{8,24},{16,0},{24,8},{1,17},{9,25},{17,1},{25,9},{2,18},{10... | collective-permute-start | bytes 52232 | tf_op jit(solution)/shard_map/ppermute | solution.py:89
  94.5 4.3 %collective-permute-start.16 = (bf16[1,16,2048]{2,1,0:T(8,128)(2,1)S(1)}, bf16[1,16,2048]{2,1,0:T(8,128)(2,1)S(1)}, u32[]{:S(2)}, u32[]{:S(2)}) collective-permute-start(bf16[1,16,2048]{2,1,0:T(8,128)(2,1)S(1)} %get-tuple-element.36), channel_id=1, source_target_pairs={{0,24},{8,0},{16,8},{24,16},{1,25},{9,1},{17,9},{25,17},{2,26},{10... | collective-permute-start | bytes 196616 | tf_op jit(solution)/shard_map/ppermute | solution.py:30
  95.4 5.8 %collective-permute-start.17 = (bf16[1,16,2048]{2,1,0:T(8,128)(2,1)S(1)}, bf16[1,16,2048]{2,1,0:T(8,128)(2,1)S(1)}, u32[]{:S(2)}, u32[]{:S(2)}) collective-permute-start(bf16[1,16,2048]{2,1,0:T(8,128)(2,1)S(1)} %get-tuple-element.35), channel_id=1, source_target_pairs={{0,16},{8,24},{16,0},{24,8},{1,17},{9,25},{17,1},{25,9},{2,18},{10... | collective-permute-start | bytes 196616 | tf_op jit(solution)/shard_map/ppermute | solution.py:30
  96.0 5.9 %collective-permute-start.18 = (bf16[1,16,2048]{2,1,0:T(8,128)(2,1)S(1)}, bf16[1,16,2048]{2,1,0:T(8,128)(2,1)S(1)}, u32[]{:S(2)}, u32[]{:S(2)}) collective-permute-start(bf16[1,16,2048]{2,1,0:T(8,128)(2,1)S(1)} %get-tuple-element.34), channel_id=1, source_target_pairs={{0,8},{8,16},{16,24},{24,0},{1,9},{9,17},{17,25},{25,1},{2,10},{10... | collective-permute-start | bytes 196616 | tf_op jit(solution)/shard_map/ppermute | solution.py:30
  (5 other events, 31.1 us)
